TPU v7x, 32 devices: a whole 2x2x4 slice. The times are simulated.
32 devices in a mesh: ctx: 8 (over z, x), tp: 4 (over y, core).
Axes of the slice: x: 2, y: 2, z: 4, core: 2. Of those that a mesh axis runs over, the one named last changes fastest.
Arguments:
- tokens: bfloat16 [2048, 16384], P('ctx', 'tp')
- document: int32 [2048], P('ctx'), may hold values from 0 to 5, as said below
- place: int32 [2048], P('ctx'), may hold values from 0 to 1023, as said below
- w_qkv: bfloat16 [1280, 16384], P(None, 'tp')
- w_out: bfloat16 [1024, 16384], P(None, 'tp'), may hold values from -0.1875 to 0.1875
- grad_out: bfloat16 [2048, 16384], P('ctx', 'tp'), may hold values from -6 to 6
Outputs:
- out: bfloat16 [2048, 16384], P('ctx', 'tp')
- grad_x: bfloat16 [2048, 16384], P('ctx', 'tp')
- grad_w_qkv: float32 [1280, 16384], P('ctx', 'tp')
- grad_w_out: float32 [1024, 16384], P('ctx', 'tp')
Inputs may be any that keep to these rules, and one draw needn't show every extreme that they name: Each document's tokens carry the positions 0 to its length minus 1, each once; one document holds 1024 tokens. `place`: position of a token within its document, as described for document.
All inputs are finite; a program needn't handle non-finite values.
Results may differ from a plain program's by a relative error of at most 0.028.
Values may be sent and summed in bfloat16 or wider, within the bound.
No kernel may reach another device: no remote copies, remote signals or barrier semaphores. Data moves between devices by JAX's collectives and lax.ppermute only.
A program may use at most 128 MiB of HBM per device.

v0:
```python
import math

import jax
import jax.numpy as jnp
from jax import lax
from jax.sharding import PartitionSpec as P

HD = 128
HQ = 8


THETA = 500000.0
NEG = -1e30


def shifted(block, axis, distance):
    devices = range(lax.axis_size(axis))
    route = [((i - distance) % len(devices), i) for i in devices]
    return lax.ppermute(block, axis, route)


def angles(place, width):
    half = width // 2
    freq = THETA ** (-(jnp.arange(half, dtype=jnp.float32) * 2.0 / width))
    turn = place.astype(jnp.float32)[:, None] * freq[None, :]
    return (jnp.cos(turn), jnp.sin(turn))


def rotate(vector, cosine, sine):
    half = vector.shape[-1] // 2
    first = vector[..., :half]
    second = vector[..., half:]
    return jnp.concatenate(
        [first * cosine - second * sine, second * cosine + first * sine], axis=-1
    )


def against(left, right):
    return lax.dot_general(
        left, right, (((1,), (1,)), ((), ())), preferred_element_type=jnp.float32
    )


def across(left, right):
    return lax.dot_general(
        left, right, (((0,), (0,)), ((), ())), preferred_element_type=jnp.float32
    )


def allowed_mask(stack_doc, stack_place, key_doc, key_place):
    return (stack_doc[:, None] == key_doc[None, :]) & (key_place[None, :] <= stack_place[:, None])


def forward_step(state, queries, keys_vals, allowed, head_dim, factor):
    top, total, summed = state
    keys = keys_vals[:, :head_dim]
    values = keys_vals[:, head_dim:]
    scores = jnp.where(allowed, against(queries, keys) * factor, NEG)
    new_top = jnp.maximum(top, jnp.max(scores, axis=1))
    weights = jnp.where(allowed, jnp.exp(scores - new_top[:, None]), 0.0)
    shrink = jnp.exp(top - new_top)
    total = total * shrink + jnp.sum(weights, axis=1)
    summed = summed * shrink[:, None] + jnp.dot(
        weights.astype(jnp.bfloat16), values, preferred_element_type=jnp.float32
    )
    return (new_top, total, summed)


def backward_step(queries, grad_stack, delta, logsum, keys_vals, allowed, head_dim, factor):
    keys = keys_vals[:, :head_dim]
    values = keys_vals[:, head_dim:]
    scores = against(queries, keys) * factor
    prob = jnp.where(allowed, jnp.exp(scores - logsum[:, None]), 0.0)
    dprob = against(grad_stack, values)
    dscore = (prob * (dprob - delta[:, None])).astype(jnp.bfloat16)
    query_part = jnp.dot(dscore, keys, preferred_element_type=jnp.float32)
    key_part = across(dscore, queries) * factor
    value_part = across(prob.astype(jnp.bfloat16), grad_stack)
    return (query_part, jnp.concatenate([key_part, value_part], axis=1))


def shards(tokens, document, place, w_qkv, w_out, grad_out):
    rows_ctx, slice_width = tokens.shape
    ctx_size = lax.axis_size("ctx")
    tp_size = lax.axis_size("tp")
    rows_mine = rows_ctx // tp_size
    ctx_rank = lax.axis_index("ctx")
    tp_rank = lax.axis_index("tp")
    head_dim = HD
    heads = HQ
    heads_width = heads * head_dim
    factor = 1.0 / math.sqrt(head_dim)
    first_row = tp_rank * rows_mine
    all_doc, all_place = (
        lax.all_gather(document, "ctx", axis=0, tiled=True),
        lax.all_gather(place, "ctx", axis=0, tiled=True),
    )
    cosine_all, sine_all = angles(place, head_dim)
    cosine_mine = lax.dynamic_slice_in_dim(cosine_all, first_row, rows_mine, 0)
    sine_mine = lax.dynamic_slice_in_dim(sine_all, first_row, rows_mine, 0)
    query_doc = lax.dynamic_slice_in_dim(document, first_row, rows_mine, 0)
    query_place = lax.dynamic_slice_in_dim(place, first_row, rows_mine, 0)
    stack_doc = jnp.tile(query_doc, heads)
    stack_place = jnp.tile(query_place, heads)
    qkv = lax.psum(against(tokens, w_qkv), "tp")
    mine = lax.dynamic_slice_in_dim(qkv, first_row, rows_mine, 0)
    keys_all = rotate(qkv[:, heads_width : heads_width + head_dim], cosine_all, sine_all).astype(
        jnp.bfloat16
    )
    keys_vals = jnp.concatenate(
        [keys_all, qkv[:, heads_width + head_dim :].astype(jnp.bfloat16)], axis=1
    )
    raw_query = mine[:, :heads_width].reshape(rows_mine, heads, head_dim)
    rotated = rotate(raw_query, cosine_mine[:, None, :], sine_mine[:, None, :]).astype(jnp.bfloat16)
    queries = jnp.transpose(rotated, (1, 0, 2)).reshape(heads * rows_mine, head_dim)

    def mask_for(step):
        source = (ctx_rank - step + ctx_size) % ctx_size
        key_doc = lax.dynamic_slice_in_dim(all_doc, source * rows_ctx, rows_ctx, 0)
        key_place = lax.dynamic_slice_in_dim(all_place, source * rows_ctx, rows_ctx, 0)
        return allowed_mask(stack_doc, stack_place, key_doc, key_place)

    def advance(state, moving, step):
        allowed = mask_for(step)
        return forward_step(state, queries, moving, allowed, head_dim, factor)

    stacked = heads * rows_mine
    state_zero = (
        jnp.full((stacked,), NEG, jnp.float32),
        jnp.zeros((stacked,), jnp.float32),
        jnp.zeros((stacked, head_dim), jnp.float32),
    )
    state = advance(state_zero, keys_vals, 0)

    def turn(step, carry):
        moving, inner = carry
        moving = shifted(moving, "ctx", 1)
        return (moving, advance(inner, moving, step))

    moving, state = lax.fori_loop(1, ctx_size, turn, (keys_vals, state))
    top, total, summed = state
    attended = (summed / total[:, None]).astype(jnp.bfloat16)
    logsum = top + jnp.log(total)
    rows_attended = jnp.transpose(attended.reshape(heads, rows_mine, head_dim), (1, 0, 2)).reshape(
        rows_mine, heads_width
    )
    piece = lax.all_gather(rows_attended, "tp", axis=0, tiled=True)
    out_sum = jnp.dot(piece, w_out, preferred_element_type=jnp.float32)
    weight_sum = across(piece, grad_out)
    out_sum, out_weight_grad = (out_sum, weight_sum)
    out = out_sum.astype(jnp.bfloat16)
    grad_rows = lax.psum_scatter(
        against(grad_out, w_out).astype(jnp.bfloat16), "tp", scatter_dimension=0, tiled=True
    )
    grad_stack = jnp.transpose(grad_rows.reshape(rows_mine, heads, head_dim), (1, 0, 2)).reshape(
        stacked, head_dim
    )
    delta = jnp.sum(grad_stack.astype(jnp.float32) * attended.astype(jnp.float32), axis=1)

    def retreat(step, moving, query_sum, grads):
        allowed = mask_for(step)
        query_part, pair_part = backward_step(
            queries, grad_stack, delta, logsum, moving, allowed, head_dim, factor
        )
        return (query_sum + query_part, grads + pair_part)

    query_zero = jnp.zeros((stacked, head_dim), jnp.float32)
    grads_zero = jnp.zeros((rows_ctx, 2 * head_dim), jnp.float32)

    def back_turn(step, carry):
        moving, grads, query_sum = carry
        query_sum, grads = retreat(step, moving, query_sum, grads)
        moving = shifted(moving, "ctx", 1)
        grads = shifted(grads.astype(jnp.bfloat16), "ctx", 1).astype(grads.dtype)
        return (moving, grads, query_sum)

    moving, grads, query_sum = lax.fori_loop(
        0, ctx_size - 1, back_turn, (keys_vals, grads_zero, query_zero)
    )
    query_sum, grads = retreat(ctx_size - 1, moving, query_sum, grads)
    grads = shifted(grads.astype(jnp.bfloat16), "ctx", 1).astype(grads.dtype)
    pair_grad = lax.psum(grads.astype(jnp.bfloat16), "tp").astype(jnp.float32)
    key_raw = rotate(pair_grad[:, :head_dim], cosine_all, -sine_all)
    pair_rounded = jnp.concatenate([key_raw, pair_grad[:, head_dim:]], axis=1).astype(jnp.bfloat16)
    query_grad = jnp.transpose((query_sum * factor).reshape(heads, rows_mine, head_dim), (1, 0, 2))
    query_raw = (
        rotate(query_grad, cosine_mine[:, None, :], -sine_mine[:, None, :])
        .reshape(rows_mine, heads_width)
        .astype(jnp.bfloat16)
    )
    w_query = w_qkv[:heads_width]
    w_pair = w_qkv[heads_width:]
    piece = lax.all_gather(query_raw, "tp", axis=0, tiled=True)
    grad_sum = jnp.dot(pair_rounded, w_pair, preferred_element_type=jnp.float32)
    current = grad_sum
    grad_sum = current + jnp.dot(piece, w_query, preferred_element_type=jnp.float32)
    weight_sum = across(piece, tokens)
    grad_sum, query_weight = (grad_sum, weight_sum)
    pair_weight = across(pair_rounded, tokens)
    grad_x = grad_sum.astype(jnp.bfloat16)
    joint_weight = jnp.concatenate([query_weight, pair_weight], axis=0)
    grad_w_qkv, grad_w_out = (
        lax.psum_scatter(
            joint_weight.astype(jnp.bfloat16), "ctx", scatter_dimension=0, tiled=True
        ).astype(jnp.float32),
        lax.psum_scatter(
            out_weight_grad.astype(jnp.bfloat16), "ctx", scatter_dimension=0, tiled=True
        ).astype(jnp.float32),
    )
    return (out, grad_x, grad_w_qkv, grad_w_out)


def solution(mesh):
    return jax.shard_map(
        shards,
        mesh=mesh,
        in_specs=(P("ctx", "tp"), P("ctx"), P("ctx"), P(None, "tp"), P(None, "tp"), P("ctx", "tp")),
        out_specs=(P("ctx", "tp"), P("ctx", "tp"), P("ctx", "tp"), P("ctx", "tp")),
        check_vma=False,
    )
```

profile of v0, /device:TPU:0, one launch (start us, length us, event | category | flops | bytes accessed | tf_op | source)
XLA Modules:
  0.0 609.9 jit_solution(15251290335199952771)
XLA Ops:
  8.8 7.9 %fusion.89 = f32[256,1280]{1,0:T(8,128)} fusion(bf16[256,4096]{1,0:T(8,128)(2,1)S(1)} %copy-done, bf16[1280,4096]{1,0:T(8,128)(2,1)} %param.13), kind=kOutput, calls=%fused_computation.133 | convolution fusion | flops 2684354560 | bytes 13893632 | tf_op jit(solution)/shard_map/dot_general | solution.py:39
  16.8 7.2 %convolution_convert_fusion.4 = bf16[256,1024]{1,0:T(8,128)(2,1)} fusion(bf16[256,4096]{1,0:T(8,128)(2,1)} %param.15, bf16[1024,4096]{1,0:T(8,128)(2,1)} %param.14), kind=kOutput, calls=%fused_computation.48 | convolution fusion | flops 2147745792 | bytes 11010048 | tf_op jit(solution)/shard_map/dot_general | solution.py:39
  24.3 23.3 %all-gather = s32[8,1,256]{2,1,0:T(1,128)} all-gather(s32[1,1,256]{2,1,0:T(1,128)S(1)} %bitcast.84), channel_id=1, replica_groups=mesh['ctx'=8,'tp'=4] {'ctx'}, dimensions={0}, use_global_device_ids=true | all-gather | bytes 9216 | tf_op jit(solution)/shard_map/all_gather | solution.py:95
  47.6 17.3 %all-gather.1 = s32[8,1,256]{2,1,0:T(1,128)} all-gather(s32[1,1,256]{2,1,0:T(1,128)S(1)} %bitcast.83), channel_id=1, replica_groups=mesh['ctx'=8,'tp'=4] {'ctx'}, dimensions={0}, use_global_device_ids=true | all-gather | bytes 9216 | tf_op jit(solution)/shard_map/all_gather | solution.py:96
  74.3 61.7 %while.42 = (s32[]{:T(128)}, bf16[256,256]{1,0:T(8,128)(2,1)S(1)}, f32[512]{0:T(512)S(1)}, f32[512]{0:T(512)S(1)}, f32[512,128]{1,0:T(8,128)S(1)}, /*index=5*/s3...) while((s32[]{:T(128)}, bf16[256,256]{1,0:T(8,128)(2,1)S(1)}, ...), condition=%wide.region_6.7_spmd.clone, body=%wide.region_3.6_spmd.clone.sunk | while | flops 69600272 | bytes 3214208 | solution.py:140
  77.4 5.1 collective-permute-done
  85.3 5.9 collective-permute-done
  93.9 5.9 collective-permute-done
  102.6 5.9 collective-permute-done
  111.2 6.0 collective-permute-done
  119.9 6.0 collective-permute-done
  128.5 6.6 %collective-permute-done = bf16[256,256]{1,0:T(8,128)(2,1)S(1)} collective-permute-done((bf16[256,256]{1,0:T(8,128)(2,1)S(1)}, bf16[256,256]{1,0:T(8,128)(2,1)S(1)}, u32[]{:S(2)}, u32[]{:S(2)}) %collective-permute-start) | collective-permute-done | bytes 131104 | tf_op jit(solution)/shard_map/while/body/eval_jaxpr/ppermute | solution.py:19
  138.4 84.7 %while.43 = (s32[]{:T(128)}, bf16[256,256]{1,0:T(8,128)(2,1)S(1)}, f32[256,256]{0,1:T(8,128)S(1)}, f32[512,128]{1,0:T(8,128)S(1)}, s32[]{:T(128)}, /*index=5*/s3...) while((s32[]{:T(128)}, bf16[256,256]{1,0:T(8,128)(2,1)S(1)}, ...), condition=%wide.region_10.11_spmd.clone, body=%wide.region_9.10_spmd.clone.sunk | while | flops 169574416 | bytes 6253507 | solution.py:177
  142.8 7.6 %collective-permute-done.2 = bf16[256,256]{0,1:T(8,128)(2,1)S(1)} collective-permute-done((bf16[256,256]{0,1:T(8,128)(2,1)}, bf16[256,256]{0,1:T(8,128)(2,1)S(1)}, u32[]{:S(2)}, u32[]{:S(2)}) %collective-permute-start.2) | collective-permute-done | bytes 131104 | tf_op jit(solution)/shard_map/while/body/eval_jaxpr/ppermute | solution.py:19
  154.9 7.6 %collective-permute-done.2 = bf16[256,256]{0,1:T(8,128)(2,1)S(1)} collective-permute-done((bf16[256,256]{0,1:T(8,128)(2,1)}, bf16[256,256]{0,1:T(8,128)(2,1)S(1)}, u32[]{:S(2)}, u32[]{:S(2)}) %collective-permute-start.2) | collective-permute-done | bytes 131104 | tf_op jit(solution)/shard_map/while/body/eval_jaxpr/ppermute | solution.py:19
  167.0 7.6 %collective-permute-done.2 = bf16[256,256]{0,1:T(8,128)(2,1)S(1)} collective-permute-done((bf16[256,256]{0,1:T(8,128)(2,1)}, bf16[256,256]{0,1:T(8,128)(2,1)S(1)}, u32[]{:S(2)}, u32[]{:S(2)}) %collective-permute-start.2) | collective-permute-done | bytes 131104 | tf_op jit(solution)/shard_map/while/body/eval_jaxpr/ppermute | solution.py:19
  179.1 7.6 %collective-permute-done.2 = bf16[256,256]{0,1:T(8,128)(2,1)S(1)} collective-permute-done((bf16[256,256]{0,1:T(8,128)(2,1)}, bf16[256,256]{0,1:T(8,128)(2,1)S(1)}, u32[]{:S(2)}, u32[]{:S(2)}) %collective-permute-start.2) | collective-permute-done | bytes 131104 | tf_op jit(solution)/shard_map/while/body/eval_jaxpr/ppermute | solution.py:19
  191.2 7.6 %collective-permute-done.2 = bf16[256,256]{0,1:T(8,128)(2,1)S(1)} collective-permute-done((bf16[256,256]{0,1:T(8,128)(2,1)}, bf16[256,256]{0,1:T(8,128)(2,1)S(1)}, u32[]{:S(2)}, u32[]{:S(2)}) %collective-permute-start.2) | collective-permute-done | bytes 131104 | tf_op jit(solution)/shard_map/while/body/eval_jaxpr/ppermute | solution.py:19
  203.3 7.6 %collective-permute-done.2 = bf16[256,256]{0,1:T(8,128)(2,1)S(1)} collective-permute-done((bf16[256,256]{0,1:T(8,128)(2,1)}, bf16[256,256]{0,1:T(8,128)(2,1)S(1)}, u32[]{:S(2)}, u32[]{:S(2)}) %collective-permute-start.2) | collective-permute-done | bytes 131104 | tf_op jit(solution)/shard_map/while/body/eval_jaxpr/ppermute | solution.py:19
  215.4 7.6 %collective-permute-done.2 = bf16[256,256]{0,1:T(8,128)(2,1)S(1)} collective-permute-done((bf16[256,256]{0,1:T(8,128)(2,1)}, bf16[256,256]{0,1:T(8,128)(2,1)S(1)}, u32[]{:S(2)}, u32[]{:S(2)}) %collective-permute-start.2) | collective-permute-done | bytes 131104 | tf_op jit(solution)/shard_map/while/body/eval_jaxpr/ppermute | solution.py:19
  226.0 7.6 %all_gather.14 = bf16[256,1024]{1,0:T(8,128)(2,1)} all-gather(bf16[64,1024]{1,0:T(8,128)(2,1)S(1)} %bitcast.77), channel_id=1, replica_groups=mesh['ctx'=8,'tp'=4] {'tp'}, dimensions={0}, use_global_device_ids=true | all-gather | bytes 655360 | tf_op jit(solution)/shard_map/all_gather | solution.py:147
  234.6 7.5 %convolution_convert_fusion = bf16[1024,4096]{1,0:T(8,128)(2,1)} fusion(bf16[256,1024]{1,0:T(8,128)(2,1)} %all_gather.14, bf16[256,4096]{1,0:T(8,128)(2,1)} %param.15), kind=kOutput, calls=%fused_computation.41 | convolution fusion | flops 2151677952 | bytes 11010048 | tf_op jit(solution)/shard_map/dot_general | solution.py:45
  243.1 7.5 %all_gather.15 = bf16[256,1024]{1,0:T(8,128)(2,1)S(1)} all-gather(bf16[64,1024]{1,0:T(8,128)(2,1)S(1)} %bitcast.78), channel_id=1, replica_groups=mesh['ctx'=8,'tp'=4] {'tp'}, dimensions={0}, use_global_device_ids=true | all-gather | bytes 655360 | tf_op jit(solution)/shard_map/all_gather | solution.py:193
  250.7 5.7 convolution_convert_fusion.1
  256.4 10.4 %all-reduce.5.cloned.1.call-done = bf16[256,256]{1,0:T(8,128)(2,1)} async-done(((bf16[256,256]{1,0:T(8,128)(2,1)}), bf16[256,256]{1,0:T(8,128)(2,1)}) %all-reduce.5.cloned.1.call-update) | async-done | bytes 131088 | tf_op jit(solution)/shard_map/psum | solution.py:182
  270.0 11.7 %pad_maximum_fusion = bf16[1280,4096]{1,0:T(8,128)(2,1)} fusion(bf16[256,4096]{1,0:T(8,128)(2,1)S(1)} %convolution_convert_fusion.3, bf16[1024,4096]{1,0:T(8,128)(2,1)} %convolution_convert_fusion.1), kind=kLoop, calls=%fused_computation.38 | loop fusion | flops 20971520 | bytes 20971520 | tf_op jit(solution)/shard_map/concatenate | solution.py:201
  282.7 7.1 %convolution_convert_fusion.2 = bf16[256,4096]{1,0:T(8,128)(2,1)} fusion(bf16[256,1024]{1,0:T(8,128)(2,1)S(1)} %copy-done.1, bf16[1024,4096]{1,0:T(8,128)(2,1)} %param.14), kind=kOutput, calls=%fused_computation.44 | convolution fusion | flops 2148532224 | bytes 11010048 | tf_op jit(solution)/shard_map/dot_general | solution.py:148
  289.8 5.8 fusion.32
  295.6 3.8 fusion.34
  299.4 119.9 %reduce-scatter.8.cloned.1.call-done = bf16[128,4096]{1,0:T(8,128)(2,1)} async-done(((bf16[1024,4096]{1,0:T(8,128)(2,1)}), bf16[128,4096]{1,0:T(8,128)(2,1)}) %reduce-scatter.8.cloned.1.call-update) | async-done | bytes 1048592 | tf_op jit(solution)/shard_map/reduce_scatter | solution.py:206
  422.1 178.2 %reduce-scatter.6.cloned.1.call-done = bf16[160,4096]{1,0:T(8,128)(2,1)} async-done(((bf16[1280,4096]{1,0:T(8,128)(2,1)}), bf16[160,4096]{1,0:T(8,128)(2,1)}) %reduce-scatter.6.cloned.1.call-update) | async-done | bytes 1310736 | tf_op jit(solution)/shard_map/reduce_scatter | solution.py:203
  600.3 3.1 convert_element_type.119
  (304 shorter events, 75.6 us)
Async XLA Ops:
  7.2 60.7 %all-reduce.3.cloned.1.call-start = ((), (), s32[]{:S(2)}) async-start(), calls=%async_computation.3 | async-start | bytes 2621440 | tf_op jit(solution)/shard_map/psum | solution.py:105
  16.7 7.4 %copy-start.8 = (s32[256]{0:T(256)S(1)}, s32[256]{0:T(256)}, u32[]{:S(2)}) copy-start(s32[256]{0:T(256)} %param.12) | copy-start | bytes 3076
  16.7 7.5 %copy-start.11 = (s32[256]{0:T(256)S(1)}, s32[256]{0:T(256)}, u32[]{:S(2)}) copy-start(s32[256]{0:T(256)} %param.11) | copy-start | bytes 3076
  16.8 119.8 %reduce-scatter.4.cloned.1.call-start = ((), (), s32[]{:S(2)}) async-start(), calls=%async_computation.4 | async-start | bytes 655360 | tf_op jit(solution)/shard_map/reduce_scatter | solution.py:152
  24.0 242.8 %all-reduce.5.cloned.1.call-start = ((), (), s32[]{:S(2)}) async-start(), calls=%async_computation.5 | async-start | bytes 262144 | tf_op jit(solution)/shard_map/psum | solution.py:182
  24.1 47.6 %copy-start.9 = (f32[64]{0:T(128)}, f32[64]{0:T(128)S(1)}, u32[]{:S(2)}) copy-start(f32[64]{0:T(128)S(1)} %negate_power_fusion) | copy-start | bytes 772
  67.8 6.5 %copy-start.6 = (s32[512]{0:T(512)}, s32[512]{0:T(512)S(1)}, u32[]{:S(2)}) copy-start(s32[512]{0:T(512)S(1)} %eq.141) | copy-start | bytes 6148
  74.3 8.2 %collective-permute-start = (bf16[256,256]{1,0:T(8,128)(2,1)S(1)}, bf16[256,256]{1,0:T(8,128)(2,1)S(1)}, u32[]{:S(2)}, u32[]{:S(2)}) collective-permute-start(bf16[256,256]{1,0:T(8,128)(2,1)S(1)} %get-tuple-element.912), channel_id=1, source_target_pairs={{28,0},{0,4},{4,8},{8,12},{12,16},{16,20},{20,24},{24,28},{29,1},{... | collective-permute-start | bytes 393224 | tf_op jit(solution)/shard_map/while/body/eval_jaxpr/ppermute | solution.py:19
  83.5 7.7 %collective-permute-start = (bf16[256,256]{1,0:T(8,128)(2,1)S(1)}, bf16[256,256]{1,0:T(8,128)(2,1)S(1)}, u32[]{:S(2)}, u32[]{:S(2)}) collective-permute-start(bf16[256,256]{1,0:T(8,128)(2,1)S(1)} %get-tuple-element.912), channel_id=1, source_target_pairs={{28,0},{0,4},{4,8},{8,12},{12,16},{16,20},{20,24},{24,28},{29,1},{... | collective-permute-start | bytes 393224 | tf_op jit(solution)/shard_map/while/body/eval_jaxpr/ppermute | solution.py:19
  92.1 7.7 %collective-permute-start = (bf16[256,256]{1,0:T(8,128)(2,1)S(1)}, bf16[256,256]{1,0:T(8,128)(2,1)S(1)}, u32[]{:S(2)}, u32[]{:S(2)}) collective-permute-start(bf16[256,256]{1,0:T(8,128)(2,1)S(1)} %get-tuple-element.912), channel_id=1, source_target_pairs={{28,0},{0,4},{4,8},{8,12},{12,16},{16,20},{20,24},{24,28},{29,1},{... | collective-permute-start | bytes 393224 | tf_op jit(solution)/shard_map/while/body/eval_jaxpr/ppermute | solution.py:19
  100.8 7.7 %collective-permute-start = (bf16[256,256]{1,0:T(8,128)(2,1)S(1)}, bf16[256,256]{1,0:T(8,128)(2,1)S(1)}, u32[]{:S(2)}, u32[]{:S(2)}) collective-permute-start(bf16[256,256]{1,0:T(8,128)(2,1)S(1)} %get-tuple-element.912), channel_id=1, source_target_pairs={{28,0},{0,4},{4,8},{8,12},{12,16},{16,20},{20,24},{24,28},{29,1},{... | collective-permute-start | bytes 393224 | tf_op jit(solution)/shard_map/while/body/eval_jaxpr/ppermute | solution.py:19
  109.5 7.7 %collective-permute-start = (bf16[256,256]{1,0:T(8,128)(2,1)S(1)}, bf16[256,256]{1,0:T(8,128)(2,1)S(1)}, u32[]{:S(2)}, u32[]{:S(2)}) collective-permute-start(bf16[256,256]{1,0:T(8,128)(2,1)S(1)} %get-tuple-element.912), channel_id=1, source_target_pairs={{28,0},{0,4},{4,8},{8,12},{12,16},{16,20},{20,24},{24,28},{29,1},{... | collective-permute-start | bytes 393224 | tf_op jit(solution)/shard_map/while/body/eval_jaxpr/ppermute | solution.py:19
  118.1 7.7 %collective-permute-start = (bf16[256,256]{1,0:T(8,128)(2,1)S(1)}, bf16[256,256]{1,0:T(8,128)(2,1)S(1)}, u32[]{:S(2)}, u32[]{:S(2)}) collective-permute-start(bf16[256,256]{1,0:T(8,128)(2,1)S(1)} %get-tuple-element.912), channel_id=1, source_target_pairs={{28,0},{0,4},{4,8},{8,12},{12,16},{16,20},{20,24},{24,28},{29,1},{... | collective-permute-start | bytes 393224 | tf_op jit(solution)/shard_map/while/body/eval_jaxpr/ppermute | solution.py:19
  126.8 8.3 %collective-permute-start = (bf16[256,256]{1,0:T(8,128)(2,1)S(1)}, bf16[256,256]{1,0:T(8,128)(2,1)S(1)}, u32[]{:S(2)}, u32[]{:S(2)}) collective-permute-start(bf16[256,256]{1,0:T(8,128)(2,1)S(1)} %get-tuple-element.912), channel_id=1, source_target_pairs={{28,0},{0,4},{4,8},{8,12},{12,16},{16,20},{20,24},{24,28},{29,1},{... | collective-permute-start | bytes 393224 | tf_op jit(solution)/shard_map/while/body/eval_jaxpr/ppermute | solution.py:19
  138.4 12.1 %collective-permute-start.1 = (bf16[256,256]{1,0:T(8,128)(2,1)S(1)}, bf16[256,256]{1,0:T(8,128)(2,1)S(1)}, u32[]{:S(2)}, u32[]{:S(2)}) collective-permute-start(bf16[256,256]{1,0:T(8,128)(2,1)S(1)} %copy.71), channel_id=1, source_target_pairs={{28,0},{0,4},{4,8},{8,12},{12,16},{16,20},{20,24},{24,28},{29,1},{... | collective-permute-start | bytes 393224 | tf_op jit(solution)/shard_map/while/body/eval_jaxpr/ppermute | solution.py:19
  142.5 7.9 %collective-permute-start.2 = (bf16[256,256]{0,1:T(8,128)(2,1)}, bf16[256,256]{0,1:T(8,128)(2,1)S(1)}, u32[]{:S(2)}, u32[]{:S(2)}) collective-permute-start(bf16[256,256]{0,1:T(8,128)(2,1)} %fusion.153), channel_id=1, source_target_pairs={{28,0},{0,4},{4,8},{8,12},{12,16},{16,20},{20,24},{24,28},{29,1},{... | collective-permute-start | bytes 393224 | tf_op jit(solution)/shard_map/while/body/eval_jaxpr/ppermute | solution.py:19
  150.5 12.1 %collective-permute-start.1 = (bf16[256,256]{1,0:T(8,128)(2,1)S(1)}, bf16[256,256]{1,0:T(8,128)(2,1)S(1)}, u32[]{:S(2)}, u32[]{:S(2)}) collective-permute-start(bf16[256,256]{1,0:T(8,128)(2,1)S(1)} %copy.71), channel_id=1, source_target_pairs={{28,0},{0,4},{4,8},{8,12},{12,16},{16,20},{20,24},{24,28},{29,1},{... | collective-permute-start | bytes 393224 | tf_op jit(solution)/shard_map/while/body/eval_jaxpr/ppermute | solution.py:19
  154.6 7.9 %collective-permute-start.2 = (bf16[256,256]{0,1:T(8,128)(2,1)}, bf16[256,256]{0,1:T(8,128)(2,1)S(1)}, u32[]{:S(2)}, u32[]{:S(2)}) collective-permute-start(bf16[256,256]{0,1:T(8,128)(2,1)} %fusion.153), channel_id=1, source_target_pairs={{28,0},{0,4},{4,8},{8,12},{12,16},{16,20},{20,24},{24,28},{29,1},{... | collective-permute-start | bytes 393224 | tf_op jit(solution)/shard_map/while/body/eval_jaxpr/ppermute | solution.py:19
  162.6 12.1 %collective-permute-start.1 = (bf16[256,256]{1,0:T(8,128)(2,1)S(1)}, bf16[256,256]{1,0:T(8,128)(2,1)S(1)}, u32[]{:S(2)}, u32[]{:S(2)}) collective-permute-start(bf16[256,256]{1,0:T(8,128)(2,1)S(1)} %copy.71), channel_id=1, source_target_pairs={{28,0},{0,4},{4,8},{8,12},{12,16},{16,20},{20,24},{24,28},{29,1},{... | collective-permute-start | bytes 393224 | tf_op jit(solution)/shard_map/while/body/eval_jaxpr/ppermute | solution.py:19
  166.8 7.9 %collective-permute-start.2 = (bf16[256,256]{0,1:T(8,128)(2,1)}, bf16[256,256]{0,1:T(8,128)(2,1)S(1)}, u32[]{:S(2)}, u32[]{:S(2)}) collective-permute-start(bf16[256,256]{0,1:T(8,128)(2,1)} %fusion.153), channel_id=1, source_target_pairs={{28,0},{0,4},{4,8},{8,12},{12,16},{16,20},{20,24},{24,28},{29,1},{... | collective-permute-start | bytes 393224 | tf_op jit(solution)/shard_map/while/body/eval_jaxpr/ppermute | solution.py:19
  174.7 12.1 %collective-permute-start.1 = (bf16[256,256]{1,0:T(8,128)(2,1)S(1)}, bf16[256,256]{1,0:T(8,128)(2,1)S(1)}, u32[]{:S(2)}, u32[]{:S(2)}) collective-permute-start(bf16[256,256]{1,0:T(8,128)(2,1)S(1)} %copy.71), channel_id=1, source_target_pairs={{28,0},{0,4},{4,8},{8,12},{12,16},{16,20},{20,24},{24,28},{29,1},{... | collective-permute-start | bytes 393224 | tf_op jit(solution)/shard_map/while/body/eval_jaxpr/ppermute | solution.py:19
  178.9 7.9 %collective-permute-start.2 = (bf16[256,256]{0,1:T(8,128)(2,1)}, bf16[256,256]{0,1:T(8,128)(2,1)S(1)}, u32[]{:S(2)}, u32[]{:S(2)}) collective-permute-start(bf16[256,256]{0,1:T(8,128)(2,1)} %fusion.153), channel_id=1, source_target_pairs={{28,0},{0,4},{4,8},{8,12},{12,16},{16,20},{20,24},{24,28},{29,1},{... | collective-permute-start | bytes 393224 | tf_op jit(solution)/shard_map/while/body/eval_jaxpr/ppermute | solution.py:19
  186.8 12.1 %collective-permute-start.1 = (bf16[256,256]{1,0:T(8,128)(2,1)S(1)}, bf16[256,256]{1,0:T(8,128)(2,1)S(1)}, u32[]{:S(2)}, u32[]{:S(2)}) collective-permute-start(bf16[256,256]{1,0:T(8,128)(2,1)S(1)} %copy.71), channel_id=1, source_target_pairs={{28,0},{0,4},{4,8},{8,12},{12,16},{16,20},{20,24},{24,28},{29,1},{... | collective-permute-start | bytes 393224 | tf_op jit(solution)/shard_map/while/body/eval_jaxpr/ppermute | solution.py:19
  191.0 7.9 %collective-permute-start.2 = (bf16[256,256]{0,1:T(8,128)(2,1)}, bf16[256,256]{0,1:T(8,128)(2,1)S(1)}, u32[]{:S(2)}, u32[]{:S(2)}) collective-permute-start(bf16[256,256]{0,1:T(8,128)(2,1)} %fusion.153), channel_id=1, source_target_pairs={{28,0},{0,4},{4,8},{8,12},{12,16},{16,20},{20,24},{24,28},{29,1},{... | collective-permute-start | bytes 393224 | tf_op jit(solution)/shard_map/while/body/eval_jaxpr/ppermute | solution.py:19
  198.9 12.1 %collective-permute-start.1 = (bf16[256,256]{1,0:T(8,128)(2,1)S(1)}, bf16[256,256]{1,0:T(8,128)(2,1)S(1)}, u32[]{:S(2)}, u32[]{:S(2)}) collective-permute-start(bf16[256,256]{1,0:T(8,128)(2,1)S(1)} %copy.71), channel_id=1, source_target_pairs={{28,0},{0,4},{4,8},{8,12},{12,16},{16,20},{20,24},{24,28},{29,1},{... | collective-permute-start | bytes 393224 | tf_op jit(solution)/shard_map/while/body/eval_jaxpr/ppermute | solution.py:19
  203.1 7.9 %collective-permute-start.2 = (bf16[256,256]{0,1:T(8,128)(2,1)}, bf16[256,256]{0,1:T(8,128)(2,1)S(1)}, u32[]{:S(2)}, u32[]{:S(2)}) collective-permute-start(bf16[256,256]{0,1:T(8,128)(2,1)} %fusion.153), channel_id=1, source_target_pairs={{28,0},{0,4},{4,8},{8,12},{12,16},{16,20},{20,24},{24,28},{29,1},{... | collective-permute-start | bytes 393224 | tf_op jit(solution)/shard_map/while/body/eval_jaxpr/ppermute | solution.py:19
  211.0 12.1 %collective-permute-start.1 = (bf16[256,256]{1,0:T(8,128)(2,1)S(1)}, bf16[256,256]{1,0:T(8,128)(2,1)S(1)}, u32[]{:S(2)}, u32[]{:S(2)}) collective-permute-start(bf16[256,256]{1,0:T(8,128)(2,1)S(1)} %copy.71), channel_id=1, source_target_pairs={{28,0},{0,4},{4,8},{8,12},{12,16},{16,20},{20,24},{24,28},{29,1},{... | collective-permute-start | bytes 393224 | tf_op jit(solution)/shard_map/while/body/eval_jaxpr/ppermute | solution.py:19
  215.2 7.9 %collective-permute-start.2 = (bf16[256,256]{0,1:T(8,128)(2,1)}, bf16[256,256]{0,1:T(8,128)(2,1)S(1)}, u32[]{:S(2)}, u32[]{:S(2)}) collective-permute-start(bf16[256,256]{0,1:T(8,128)(2,1)} %fusion.153), channel_id=1, source_target_pairs={{28,0},{0,4},{4,8},{8,12},{12,16},{16,20},{20,24},{24,28},{29,1},{... | collective-permute-start | bytes 393224 | tf_op jit(solution)/shard_map/while/body/eval_jaxpr/ppermute | solution.py:19
  224.9 8.7 %collective-permute-start.3 = (bf16[256,256]{1,0:T(8,128)(2,1)S(1)}, bf16[256,256]{1,0:T(8,128)(2,1)S(1)}, u32[]{:S(2)}, u32[]{:S(2)}) collective-permute-start(bf16[256,256]{1,0:T(8,128)(2,1)S(1)} %fusion.46), channel_id=1, source_target_pairs={{28,0},{0,4},{4,8},{8,12},{12,16},{16,20},{20,24},{24,28},{29,1},{... | collective-permute-start | bytes 393224 | tf_op jit(solution)/shard_map/ppermute | solution.py:19
  234.3 185.0 %reduce-scatter.8.cloned.1.call-start = ((), (), s32[]{:S(2)}) async-start(), calls=%async_computation.7 | async-start | bytes 9437184 | tf_op jit(solution)/shard_map/reduce_scatter | solution.py:206
  242.1 358.2 %reduce-scatter.6.cloned.1.call-start = ((), (), s32[]{:S(2)}) async-start(), calls=%async_computation.6 | async-start | bytes 11796480 | tf_op jit(solution)/shard_map/reduce_scatter | solution.py:203
  250.7 17.9 %copy-start.10 = (f32[64]{0:T(128)S(1)}, f32[64]{0:T(128)}, u32[]{:S(2)}) copy-start(f32[64]{0:T(128)} %copy-done.9) | copy-start | bytes 772
  (7 other events, 14.5 us)
Sparse Core Ops, SparseCore 0:
  16.9 41.6 all-reduce.2
  61.6 21.6 reduce-scatter.3
  234.5 32.2 all-reduce.4
  270.3 149.0 reduce-scatter.7
  423.2 177.0 reduce-scatter.5
where the time goes:
time: 612 us; the launch traced here: 610 us
  waiting for transfers between devices  403 us (66%)
  matrix products  67.5 us (11%)
  blocking collectives  55.7 us (9%)
  local copies, waits for them, and re-layouts  35.2 us (6%)
  other arithmetic  29.9 us (5%)
  between operations  14.1 us (2%)
    reduce_scatter x1, waiting for transfers between devices, shards(): lax.psum_scatter(joint_weight.astype(jnp.bfloat16), 'ctx', scatter_dimens...  178 us
    reduce_scatter x1, waiting for transfers between devices, shards(): lax.psum_scatter(out_weight_grad.astype(jnp.bfloat16), 'ctx', scatter_dim...  120 us
    ppermute x22, waiting for transfers between devices, shifted(): return lax.ppermute(block, axis, route)  94.8 us
    dot_general x26, matrix products, against(): lax.dot_general(left, right, (((1,), (1,)), ((), ())), preferred_element_...  27 us
    all_gather x1, blocking collectives, shards(): lax.all_gather(document, 'ctx', axis=0, tiled=True)  23.3 us
    dot_general x19, matrix products, across(): lax.dot_general(left, right, (((0,), (0,)), ((), ())), preferred_element_...  17.7 us
    all_gather x1, blocking collectives, shards(): lax.all_gather(place, 'ctx', axis=0, tiled=True)  17.3 us
  transfers between devices with their start and end apart: 27, of which 17 were waited for; matrix products, arithmetic and copies ran while one was open for 19% of the time, Pallas kernels for 0%

commit v1 on v0

v1 whole, which is shorter than its diff:
```python
import math

import jax
import jax.numpy as jnp
from jax import lax
from jax.sharding import PartitionSpec as P

HD = 128
HQ = 8


THETA = 500000.0
NEG = -1e30
PIECE = 64


def angles(place, width):
    half = width // 2
    freq = THETA ** (-(jnp.arange(half, dtype=jnp.float32) * 2.0 / width))
    turn = place.astype(jnp.float32)[:, None] * freq[None, :]
    return (jnp.cos(turn), jnp.sin(turn))


def rotate(vector, cosine, sine):
    half = vector.shape[-1] // 2
    first = vector[..., :half]
    second = vector[..., half:]
    return jnp.concatenate(
        [first * cosine - second * sine, second * cosine + first * sine], axis=-1
    )


def against(left, right):
    return lax.dot_general(
        left, right, (((1,), (1,)), ((), ())), preferred_element_type=jnp.float32
    )


def across(left, right):
    return lax.dot_general(
        left, right, (((0,), (0,)), ((), ())), preferred_element_type=jnp.float32
    )


def shards(tokens, document, place, w_qkv, w_out, grad_out):
    rows_ctx, slice_width = tokens.shape
    ctx_size = lax.axis_size("ctx")
    tp_size = lax.axis_size("tp")
    rows_mine = rows_ctx // tp_size
    tp_rank = lax.axis_index("tp")
    head_dim = HD
    heads = HQ
    heads_width = heads * head_dim
    pair_width = 2 * head_dim
    factor = 1.0 / math.sqrt(head_dim)
    first_row = tp_rank * rows_mine
    stacked = heads * rows_mine
    total_rows = ctx_size * rows_ctx

    grad_rows = lax.psum_scatter(
        against(grad_out, w_out).astype(jnp.bfloat16), "tp", scatter_dimension=0, tiled=True
    )

    cosine_all, sine_all = angles(place, head_dim)
    cosine_mine = lax.dynamic_slice_in_dim(cosine_all, first_row, rows_mine, 0)
    sine_mine = lax.dynamic_slice_in_dim(sine_all, first_row, rows_mine, 0)
    query_doc = lax.dynamic_slice_in_dim(document, first_row, rows_mine, 0)
    query_place = lax.dynamic_slice_in_dim(place, first_row, rows_mine, 0)

    qkv = lax.psum(against(tokens, w_qkv), "tp")
    keys = rotate(qkv[:, heads_width : heads_width + head_dim], cosine_all, sine_all).astype(
        jnp.bfloat16
    )
    values = qkv[:, heads_width + head_dim :].astype(jnp.bfloat16)

    info = jnp.concatenate(
        [document, place // PIECE, place % PIECE], axis=0
    ).astype(jnp.float32)
    info_rows = -(-info.shape[0] // pair_width)
    info = jnp.pad(info, (0, info_rows * pair_width - info.shape[0]))
    info = info.reshape(info_rows, pair_width).astype(jnp.bfloat16)
    packed = jnp.concatenate([keys, values, ], axis=1)
    packed = jnp.concatenate([packed, info], axis=0)
    gathered = lax.all_gather(packed, "ctx", axis=0, tiled=False)
    keys_all = gathered[:, :rows_ctx, :head_dim].reshape(total_rows, head_dim)
    values_all = gathered[:, :rows_ctx, head_dim:].reshape(total_rows, head_dim)
    info_all = gathered[:, rows_ctx:, :].reshape(ctx_size, info_rows * pair_width).astype(
        jnp.float32
    )
    key_doc = info_all[:, :rows_ctx].reshape(total_rows)
    key_place = (
        info_all[:, rows_ctx : 2 * rows_ctx] * PIECE + info_all[:, 2 * rows_ctx : 3 * rows_ctx]
    ).reshape(total_rows)

    allowed = (query_doc.astype(jnp.float32)[:, None] == key_doc[None, :]) & (
        key_place[None, :] <= query_place.astype(jnp.float32)[:, None]
    )
    allowed = jnp.broadcast_to(allowed[None], (heads, rows_mine, total_rows)).reshape(
        stacked, total_rows
    )

    mine = lax.dynamic_slice_in_dim(qkv, first_row, rows_mine, 0)
    raw_query = mine[:, :heads_width].reshape(rows_mine, heads, head_dim)
    rotated = rotate(raw_query, cosine_mine[:, None, :], sine_mine[:, None, :]).astype(jnp.bfloat16)
    queries = jnp.transpose(rotated, (1, 0, 2)).reshape(stacked, head_dim)

    scores = against(queries, keys_all) * factor
    masked = jnp.where(allowed, scores, NEG)
    top = jnp.max(masked, axis=1)
    weights = jnp.where(allowed, jnp.exp(masked - top[:, None]), 0.0)
    total = jnp.sum(weights, axis=1)
    summed = jnp.dot(weights.astype(jnp.bfloat16), values_all, preferred_element_type=jnp.float32)
    attended = (summed / total[:, None]).astype(jnp.bfloat16)
    logsum = top + jnp.log(total)

    rows_attended = jnp.transpose(attended.reshape(heads, rows_mine, head_dim), (1, 0, 2)).reshape(
        rows_mine, heads_width
    )
    piece = lax.all_gather(rows_attended, "tp", axis=0, tiled=True)
    out = jnp.dot(piece, w_out, preferred_element_type=jnp.float32).astype(jnp.bfloat16)
    out_weight_grad = across(piece, grad_out)

    grad_stack = jnp.transpose(grad_rows.reshape(rows_mine, heads, head_dim), (1, 0, 2)).reshape(
        stacked, head_dim
    )
    delta = jnp.sum(grad_stack.astype(jnp.float32) * attended.astype(jnp.float32), axis=1)
    prob = jnp.where(allowed, jnp.exp(scores - logsum[:, None]), 0.0)
    dprob = against(grad_stack, values_all)
    dscore = (prob * (dprob - delta[:, None])).astype(jnp.bfloat16)
    query_sum = jnp.dot(dscore, keys_all, preferred_element_type=jnp.float32)
    key_part = across(dscore, queries) * factor
    value_part = across(prob.astype(jnp.bfloat16), grad_stack)
    pair_all = jnp.concatenate([key_part, value_part], axis=1)
    pair_grad = lax.psum_scatter(pair_all, ("ctx", "tp"), scatter_dimension=0, tiled=True)

    key_raw = rotate(pair_grad[:, :head_dim], cosine_mine, -sine_mine)
    query_grad = jnp.transpose((query_sum * factor).reshape(heads, rows_mine, head_dim), (1, 0, 2))
    query_raw = rotate(query_grad, cosine_mine[:, None, :], -sine_mine[:, None, :]).reshape(
        rows_mine, heads_width
    )
    d_mine = jnp.concatenate([query_raw, key_raw, pair_grad[:, head_dim:]], axis=1).astype(
        jnp.bfloat16
    )
    d_qkv = lax.all_gather(d_mine, "tp", axis=0, tiled=True)
    grad_x = jnp.dot(d_qkv, w_qkv, preferred_element_type=jnp.float32).astype(jnp.bfloat16)
    joint_weight = across(d_qkv, tokens)
    grad_w_qkv = lax.psum_scatter(
        joint_weight.astype(jnp.bfloat16), "ctx", scatter_dimension=0, tiled=True
    ).astype(jnp.float32)
    grad_w_out = lax.psum_scatter(
        out_weight_grad.astype(jnp.bfloat16), "ctx", scatter_dimension=0, tiled=True
    ).astype(jnp.float32)
    return (out, grad_x, grad_w_qkv, grad_w_out)


def solution(mesh):
    return jax.shard_map(
        shards,
        mesh=mesh,
        in_specs=(P("ctx", "tp"), P("ctx"), P("ctx"), P(None, "tp"), P(None, "tp"), P("ctx", "tp")),
        out_specs=(P("ctx", "tp"), P("ctx", "tp"), P("ctx", "tp"), P("ctx", "tp")),
        check_vma=False,
    )
```

time: 612 us -> 613 us (level)
  waiting for transfers between devices: 403 us -> 512 us
  blocking collectives: 55.7 us -> 14.2 us
  local copies, waits for them, and re-layouts: 35.2 us -> 6.82 us
  matrix products: 67.5 us -> 49.5 us
  other arithmetic: 29.9 us -> 14.6 us
    reduce_scatter x0 -> x1, waiting for transfers between devices: none -> 119 us  [shards(): lax.psum_scatter(pair_all, ('ctx', 'tp'), scatter_dimension=0, tiled=True)]
    ppermute x22 -> x0, waiting for transfers between devices: 94.8 us -> none  [shifted(): return lax.ppermute(block, axis, route)]
    all_gather x0 -> x1, waiting for transfers between devices: none -> 42.4 us  [shards(): gathered = lax.all_gather(packed, 'ctx', axis=0, tiled=False)]
    all_gather x3 -> x1, blocking collectives: 48.1 us -> 7.08 us  [shards(): d_qkv = lax.all_gather(d_mine, 'tp', axis=0, tiled=True)]
    psum x1, waiting for transfers between devices: 0.01 us -> 34.4 us  [shards(): qkv = lax.psum(against(tokens, w_qkv), 'tp')]
    dynamic_slice x32 -> x0, local copies, waits for them, and re-layouts: 24 us -> none  [the longest x15 12 us: mask_for(): lax.dynamic_slice_in_dim(all_place, source * rows_ctx, rows_ctx, 0)]
    reduce_scatter x1, waiting for transfers between devices: 0.01 us -> 19.8 us  [shards(): lax.psum_scatter(against(grad_out, w_out).astype(jnp.bfloat16), 'tp', sca...]
    psum x1 -> x0, waiting for transfers between devices: 10.4 us -> none  [shards(): pair_grad = lax.psum(grads.astype(jnp.bfloat16), 'tp').astype(jnp.float32)]
  transfers between devices with their start and end apart: 27 -> 6, of which waited for: 17 -> 6; matrix products, arithmetic and copies ran while one was open for 19% -> 8% of each run, Pallas kernels for 0% -> 0%
where the time goes in v1:
time: 613 us; the launch traced here: 612 us
  waiting for transfers between devices  512 us (84%)
  matrix products  49.5 us (8%)
  other arithmetic  14.6 us (2%)
  between operations  14.3 us (2%)
  blocking collectives  14.2 us (2%)
  local copies, waits for them, and re-layouts  6.82 us (1%)
    reduce_scatter x1, waiting for transfers between devices, shards(): lax.psum_scatter(joint_weight.astype(jnp.bfloat16), 'ctx', scatter_dimens...  178 us
    reduce_scatter x1, waiting for transfers between devices, shards(): lax.psum_scatter(out_weight_grad.astype(jnp.bfloat16), 'ctx', scatter_dim...  119 us
    reduce_scatter x1, waiting for transfers between devices, shards(): lax.psum_scatter(pair_all, ('ctx', 'tp'), scatter_dimension=0, tiled=True)  119 us
    all_gather x1, waiting for transfers between devices, shards(): gathered = lax.all_gather(packed, 'ctx', axis=0, tiled=False)  42.4 us
    psum x1, waiting for transfers between devices, shards(): qkv = lax.psum(against(tokens, w_qkv), 'tp')  34.4 us
    reduce_scatter x1, waiting for transfers between devices, shards(): lax.psum_scatter(against(grad_out, w_out).astype(jnp.bfloat16), 'tp', sca...  19.8 us
    dot_general x4, matrix products, against(): lax.dot_general(left, right, (((1,), (1,)), ((), ())), preferred_element_...  16.8 us
    dot_general x4, matrix products, across(): lax.dot_general(left, right, (((0,), (0,)), ((), ())), preferred_element_...  14.4 us
  transfers between devices with their start and end apart: 6, of which 6 were waited for; matrix products, arithmetic and copies ran while one was open for 8% of the time, Pallas kernels for 0%

profile of v1, /device:TPU:0, one launch (start us, length us, event | category | flops | bytes accessed | tf_op | source)
XLA Modules:
  0.0 612.1 jit_solution(3792446386187774673)
XLA Ops:
  7.2 1.5 copy-done
  8.8 7.9 %fusion.10 = f32[256,1280]{1,0:T(8,128)} fusion(bf16[256,4096]{1,0:T(8,128)(2,1)S(1)} %copy-done, bf16[1280,4096]{1,0:T(8,128)(2,1)} %param.9), kind=kOutput, calls=%fused_computation.62 | convolution fusion | flops 2684354560 | bytes 13893632 | tf_op jit(solution)/shard_map/dot_general | solution.py:34
  16.8 7.2 %convolution_convert_fusion.4 = bf16[256,1024]{1,0:T(8,128)(2,1)} fusion(bf16[256,4096]{1,0:T(8,128)(2,1)} %param.11, bf16[1024,4096]{1,0:T(8,128)(2,1)} %param.10), kind=kOutput, calls=%fused_computation.14 | convolution fusion | flops 2147745792 | bytes 11010048 | tf_op jit(solution)/shard_map/dot_general | solution.py:34
  24.1 34.4 %all-reduce.2.cloned.1.call-done = f32[256,1280]{1,0:T(8,128)} async-done(((f32[256,1280]{1,0:T(8,128)}), f32[256,1280]{1,0:T(8,128)}) %all-reduce.2.cloned.1.call-update) | async-done | bytes 1310736 | tf_op jit(solution)/shard_map/psum | solution.py:70
  58.5 0.9 slice.114
  59.5 1.6 subtract_convert_fusion.2
  61.0 0.8 maximum_bitcast_fusion
  62.1 1.0 dynamic-slice_bitcast_fusion
  63.5 19.8 %reduce-scatter.5.cloned.1.call-done = bf16[64,1024]{1,0:T(8,128)(2,1)} async-done(((bf16[256,1024]{1,0:T(8,128)(2,1)}), bf16[64,1024]{1,0:T(8,128)(2,1)}) %reduce-scatter.5.cloned.1.call-update) | async-done | bytes 131088 | tf_op jit(solution)/shard_map/reduce_scatter | solution.py:60
  83.3 0.9 copy_bitcast_fusion.2
  84.3 42.4 %all-gather.4.cloned.1.call-done = bf16[8,259,256]{2,1,0:T(8,128)(2,1)} async-done(((bf16[1,259,256]{2,1,0:T(8,128)(2,1)}), bf16[8,259,256]{2,1,0:T(8,128)(2,1)}) %all-gather.4.cloned.1.call-update) | async-done | bytes 1060880 | tf_op jit(solution)/shard_map/all_gather | solution.py:84
  126.7 0.8 convert_bitcast_fusion
  127.7 1.3 fusion.8
  128.9 0.9 fusion
  129.9 1.4 fusion.2
  131.3 1.1 fusion.1
  132.4 0.8 multiply_reduce_fusion
  135.5 1.5 pad_maximum_fusion
  137.1 7.2 %all_gather.14 = bf16[256,1024]{1,0:T(8,128)(2,1)S(1)} all-gather(bf16[64,1024]{1,0:T(8,128)(2,1)S(1)} %bitcast.90), channel_id=1, replica_groups=mesh['ctx'=8,'tp'=4] {'tp'}, dimensions={0}, use_global_device_ids=true | all-gather | bytes 655360 | tf_op jit(solution)/shard_map/all_gather | solution.py:119
  144.3 7.3 %convolution_convert_fusion.1 = bf16[1024,4096]{1,0:T(8,128)(2,1)} fusion(bf16[256,1024]{1,0:T(8,128)(2,1)S(1)} %all_gather.14, bf16[256,4096]{1,0:T(8,128)(2,1)} %param.11), kind=kOutput, calls=%fused_computation.4 | convolution fusion | flops 2151677952 | bytes 11010048 | tf_op jit(solution)/shard_map/dot_general | solution.py:40
  151.7 2.3 convolution_multiply_fusion.1
  154.2 118.5 %reduce-scatter.7.cloned.1.call-done = f32[64,256]{1,0:T(8,128)} async-done(((f32[2048,256]{1,0:T(8,128)}), f32[64,256]{1,0:T(8,128)}) %reduce-scatter.7.cloned.1.call-update) | async-done | bytes 65552 | tf_op jit(solution)/shard_map/reduce_scatter | solution.py:134
  272.8 0.8 slice.115
  273.5 0.9 add_convert_fusion.3
  274.5 7.1 %all_gather.15 = bf16[256,1280]{1,0:T(8,128)(2,1)S(1)} all-gather(bf16[64,1280]{1,0:T(8,128)(2,1)S(1)} %concatenate.33), channel_id=1, replica_groups=mesh['ctx'=8,'tp'=4] {'tp'}, dimensions={0}, use_global_device_ids=true | all-gather | bytes 819200 | tf_op jit(solution)/shard_map/all_gather | solution.py:144
  281.6 5.6 convolution_convert_fusion
  287.3 7.1 %convolution_convert_fusion.2 = bf16[256,4096]{1,0:T(8,128)(2,1)} fusion(bf16[256,1024]{1,0:T(8,128)(2,1)S(1)} %all_gather.14, bf16[1024,4096]{1,0:T(8,128)(2,1)} %param.10), kind=kOutput, calls=%fused_computation.5 | convolution fusion | flops 2148532224 | bytes 11010048 | tf_op jit(solution)/shard_map/dot_general | solution.py:120
  294.4 8.1 %convolution_convert_fusion.3 = bf16[256,4096]{1,0:T(8,128)(2,1)} fusion(bf16[256,1280]{1,0:T(8,128)(2,1)S(1)} %all_gather.15, bf16[1280,4096]{1,0:T(8,128)(2,1)} %param.9), kind=kOutput, calls=%fused_computation.6 | convolution fusion | flops 2685403136 | bytes 13238272 | tf_op jit(solution)/shard_map/dot_general | solution.py:145
  302.5 118.7 %reduce-scatter.11.cloned.1.call-done = bf16[128,4096]{1,0:T(8,128)(2,1)} async-done(((bf16[1024,4096]{1,0:T(8,128)(2,1)}), bf16[128,4096]{1,0:T(8,128)(2,1)}) %reduce-scatter.11.cloned.1.call-update) | async-done | bytes 1048592 | tf_op jit(solution)/shard_map/reduce_scatter | solution.py:150
  421.2 2.8 convert_element_type.89
  423.9 178.2 %reduce-scatter.9.cloned.1.call-done = bf16[160,4096]{1,0:T(8,128)(2,1)} async-done(((bf16[1280,4096]{1,0:T(8,128)(2,1)}), bf16[160,4096]{1,0:T(8,128)(2,1)}) %reduce-scatter.9.cloned.1.call-update) | async-done | bytes 1310736 | tf_op jit(solution)/shard_map/reduce_scatter | solution.py:147
  602.1 3.1 convert_element_type.87
  (43 shorter events, 4.0 us)
Async XLA Ops:
  7.2 1.6 copy-start
  7.2 51.4 %all-reduce.2.cloned.1.call-start = ((), (), s32[]{:S(2)}) async-start(), calls=%async_computation.4 | async-start | bytes 2621440 | tf_op jit(solution)/shard_map/psum | solution.py:70
  16.7 7.3 %copy-start.3 = (s32[256]{0:T(256)S(1)}, s32[256]{0:T(256)}, u32[]{:S(2)}) copy-start(s32[256]{0:T(256)} %param.8) | copy-start | bytes 3076
  16.7 7.3 %copy-start.2 = (s32[256]{0:T(256)S(1)}, s32[256]{0:T(256)}, u32[]{:S(2)}) copy-start(s32[256]{0:T(256)} %param.7) | copy-start | bytes 3076
  16.8 66.6 %reduce-scatter.5.cloned.1.call-start = ((), (), s32[]{:S(2)}) async-start(), calls=%async_computation.5 | async-start | bytes 655360 | tf_op jit(solution)/shard_map/reduce_scatter | solution.py:60
  24.0 102.7 %all-gather.4.cloned.1.call-start = ((), (), s32[]{:S(2)}) async-start(), calls=%async_computation.9 | async-start | bytes 1216512 | tf_op jit(solution)/shard_map/all_gather | solution.py:84
  61.8 211.0 %reduce-scatter.7.cloned.1.call-start = ((), (), s32[]{:S(2)}) async-start(), calls=%async_computation.6 | async-start | bytes 2162688 | tf_op jit(solution)/shard_map/reduce_scatter | solution.py:134
  134.0 1.5 copy-start.1
  136.9 284.2 %reduce-scatter.11.cloned.1.call-start = ((), (), s32[]{:S(2)}) async-start(), calls=%async_computation.8 | async-start | bytes 9437184 | tf_op jit(solution)/shard_map/reduce_scatter | solution.py:150
  151.6 450.5 %reduce-scatter.9.cloned.1.call-start = ((), (), s32[]{:S(2)}) async-start(), calls=%async_computation.7 | async-start | bytes 11796480 | tf_op jit(solution)/shard_map/reduce_scatter | solution.py:147
Sparse Core Ops, SparseCore 0:
  16.9 41.6 all-reduce.1
  61.6 21.6 reduce-scatter.4
  86.3 40.2 all-gather.3
  137.1 135.6 reduce-scatter.6
  276.2 144.8 reduce-scatter.10
  425.0 177.0 reduce-scatter.8

commit v2 on v1

--- a/solution.py
+++ b/solution.py
@@ -1,3 +1,4 @@
+import functools
 import math
 
 import jax
@@ -42,7 +43,62 @@
     )
 
 
-def shards(tokens, document, place, w_qkv, w_out, grad_out):
+def ring_of(mesh):
+    count = mesh.shape["ctx"]
+    try:
+        grid = mesh.devices.reshape(count, -1)
+        coords = [tuple(grid[i, 0].coords) for i in range(count)]
+    except Exception:
+        return list(range(count))
+    varying = [d for d in range(len(coords[0])) if len({c[d] for c in coords}) > 1]
+    if len(varying) == 1:
+        return sorted(range(count), key=lambda i: coords[i][varying[0]])
+    if len(varying) != 2:
+        return list(range(count))
+    for short, long in (varying, varying[::-1]):
+        levels = sorted({c[short] for c in coords})
+        if len(levels) == 2:
+            there = sorted(
+                (i for i in range(count) if coords[i][short] == levels[0]),
+                key=lambda i: coords[i][long],
+            )
+            back = sorted(
+                (i for i in range(count) if coords[i][short] == levels[1]),
+                key=lambda i: -coords[i][long],
+            )
+            return there + back
+    return list(range(count))
+
+
+def ring_scatter(partial, ring, axis):
+    count = len(ring)
+    where = [0] * count
+    for spot, member in enumerate(ring):
+        where[member] = spot
+    spot = jnp.asarray(where, jnp.int32)[lax.axis_index(axis)]
+    order = jnp.asarray(ring, jnp.int32)
+    rows = partial.shape[0] // count
+    half = partial.shape[1] // 2
+    blocks = partial.reshape(count, rows, partial.shape[1])
+    left = blocks[:, :, :half]
+    right = blocks[:, :, half:]
+
+    def block(side, offset):
+        return lax.dynamic_index_in_dim(side, order[(spot + offset) % count], 0, keepdims=False)
+
+    forward = [(ring[p], ring[(p + 1) % count]) for p in range(count)]
+    backward = [(ring[p], ring[(p - 1) % count]) for p in range(count)]
+    send_left = block(left, count - 1)
+    send_right = block(right, 1)
+    for step in range(count - 1):
+        got_left = lax.ppermute(send_left.astype(jnp.bfloat16), axis, forward)
+        got_right = lax.ppermute(send_right.astype(jnp.bfloat16), axis, backward)
+        send_left = got_left.astype(jnp.float32) + block(left, 2 * count - step - 2)
+        send_right = got_right.astype(jnp.float32) + block(right, step + 2)
+    return jnp.concatenate([send_left, send_right], axis=1)
+
+
+def shards(ring, tokens, document, place, w_qkv, w_out, grad_out):
     rows_ctx, slice_width = tokens.shape
     ctx_size = lax.axis_size("ctx")
     tp_size = lax.axis_size("tp")
@@ -131,7 +187,10 @@
     key_part = across(dscore, queries) * factor
     value_part = across(prob.astype(jnp.bfloat16), grad_stack)
     pair_all = jnp.concatenate([key_part, value_part], axis=1)
-    pair_grad = lax.psum_scatter(pair_all, ("ctx", "tp"), scatter_dimension=0, tiled=True)
+    pair_grad = lax.psum(
+        lax.psum_scatter(pair_all, "ctx", scatter_dimension=0, tiled=True), "tp"
+    )
+    pair_grad = lax.dynamic_slice_in_dim(pair_grad, first_row, rows_mine, 0)
 
     key_raw = rotate(pair_grad[:, :head_dim], cosine_mine, -sine_mine)
     query_grad = jnp.transpose((query_sum * factor).reshape(heads, rows_mine, head_dim), (1, 0, 2))
@@ -144,18 +203,14 @@
     d_qkv = lax.all_gather(d_mine, "tp", axis=0, tiled=True)
     grad_x = jnp.dot(d_qkv, w_qkv, preferred_element_type=jnp.float32).astype(jnp.bfloat16)
     joint_weight = across(d_qkv, tokens)
-    grad_w_qkv = lax.psum_scatter(
-        joint_weight.astype(jnp.bfloat16), "ctx", scatter_dimension=0, tiled=True
-    ).astype(jnp.float32)
-    grad_w_out = lax.psum_scatter(
-        out_weight_grad.astype(jnp.bfloat16), "ctx", scatter_dimension=0, tiled=True
-    ).astype(jnp.float32)
+    grad_w_qkv = ring_scatter(joint_weight, ring, "ctx")
+    grad_w_out = ring_scatter(out_weight_grad, ring, "ctx")
     return (out, grad_x, grad_w_qkv, grad_w_out)
 
 
 def solution(mesh):
     return jax.shard_map(
-        shards,
+        functools.partial(shards, ring_of(mesh)),
         mesh=mesh,
         in_specs=(P("ctx", "tp"), P("ctx"), P("ctx"), P(None, "tp"), P(None, "tp"), P("ctx", "tp")),
         out_specs=(P("ctx", "tp"), P("ctx", "tp"), P("ctx", "tp"), P("ctx", "tp")),

time: 613 us -> 440 us (0.72)
  waiting for transfers between devices: 512 us -> 226 us
  starting transfers between devices: 0.43 us -> 37.4 us
  between operations: 14.3 us -> 49.4 us
  local copies, waits for them, and re-layouts: 6.82 us -> 31.3 us
  other arithmetic: 14.6 us -> 38 us
  matrix products: 49.5 us -> 40.8 us
    reduce_scatter x3 -> x1, waiting for transfers between devices: 415 us -> 7.43 us  [shards(): lax.psum_scatter(pair_all, 'ctx', scatter_dimension=0, tiled=True)]
    ppermute x0 -> x28, waiting for transfers between devices: none -> 128 us  [the longest x14 76.5 us: ring_scatter(): got_left = lax.ppermute(send_left.astype(jnp.bfloat16), axis, forward)]
    ppermute x0 -> x28, starting transfers between devices: none -> 37.2 us  [the longest x14 22.9 us: ring_scatter(): got_left = lax.ppermute(send_left.astype(jnp.bfloat16), axis, forward)]
    psum x0 -> x1, waiting for transfers between devices: none -> 30.8 us  [shards(): lax.psum(lax.psum_scatter(pair_all, 'ctx', scatter_dimension=0, tiled=Tru...]
    reduce_scatter x1, waiting for transfers between devices: 19.8 us -> 0.02 us  [shards(): lax.psum_scatter(against(grad_out, w_out).astype(jnp.bfloat16), 'tp', sca...]
    all_gather x1, waiting for transfers between devices: 42.4 us -> 26 us  [shards(): gathered = lax.all_gather(packed, 'ctx', axis=0, tiled=False)]
    convert_element_type x2 -> x24, other arithmetic: 5.85 us -> 21.1 us  [the longest x12 13.2 us: ring_scatter(): got_left = lax.ppermute(send_left.astype(jnp.bfloat16), axis, forward)]
    slice x0 -> x2, local copies, waits for them, and re-layouts: none -> 14.6 us  [ring_scatter(): left = blocks[:, :, :half]]
  transfers between devices with their start and end apart: 6 -> 33, of which waited for: 6 -> 24; matrix products, arithmetic and copies ran while one was open for 8% -> 18% of each run, Pallas kernels for 0% -> 0%
where the time goes in v2:
time: 440 us; the launch traced here: 438 us
  waiting for transfers between devices  226 us (51%)
  between operations  49.4 us (11%)
  matrix products  40.8 us (9%)
  other arithmetic  38 us (9%)
  starting transfers between devices  37.4 us (8%)
  local copies, waits for them, and re-layouts  31.3 us (7%)
  blocking collectives  14.4 us (3%)
    ppermute x14, waiting for transfers between devices, ring_scatter(): got_left = lax.ppermute(send_left.astype(jnp.bfloat16), axis, forward)  76.5 us
    ppermute x14, waiting for transfers between devices, ring_scatter(): got_right = lax.ppermute(send_right.astype(jnp.bfloat16), axis, backward)  51.3 us
    psum x1, waiting for transfers between devices, shards(): qkv = lax.psum(against(tokens, w_qkv), 'tp')  34.4 us
    psum x1, waiting for transfers between devices, shards(): lax.psum(lax.psum_scatter(pair_all, 'ctx', scatter_dimension=0, tiled=Tru...  30.8 us
    all_gather x1, waiting for transfers between devices, shards(): gathered = lax.all_gather(packed, 'ctx', axis=0, tiled=False)  26 us
    ppermute x14, starting transfers between devices, ring_scatter(): got_left = lax.ppermute(send_left.astype(jnp.bfloat16), axis, forward)  22.9 us
    dot_general x4, matrix products, against(): lax.dot_general(left, right, (((1,), (1,)), ((), ())), preferred_element_...  16.8 us
    slice x2, local copies, waits for them, and re-layouts, ring_scatter(): left = blocks[:, :, :half]  14.6 us
  transfers between devices with their start and end apart: 33, of which 24 were waited for; matrix products, arithmetic and copies ran while one was open for 18% of the time, Pallas kernels for 0%

profile of v2, /device:TPU:0, one launch (start us, length us, event | category | flops | bytes accessed | tf_op | source)
XLA Modules:
  0.0 437.8 jit_solution(13091560504420638398)
XLA Ops:
  8.8 7.9 %fusion.41 = f32[256,1280]{1,0:T(8,128)} fusion(bf16[256,4096]{1,0:T(8,128)(2,1)S(1)} %copy-done, bf16[1280,4096]{1,0:T(8,128)(2,1)} %param.13), kind=kOutput, calls=%fused_computation.125 | convolution fusion | flops 2684354560 | bytes 13893632 | tf_op jit(solution)/shard_map/dot_general | solution.py:35
  16.8 7.2 %convolution_convert_fusion.2 = bf16[256,1024]{1,0:T(8,128)(2,1)} fusion(bf16[256,4096]{1,0:T(8,128)(2,1)} %param.15, bf16[1024,4096]{1,0:T(8,128)(2,1)} %param.14), kind=kOutput, calls=%fused_computation.42 | convolution fusion | flops 2147745792 | bytes 11010048 | tf_op jit(solution)/shard_map/dot_general | solution.py:35
  24.2 34.4 %all-reduce.3.cloned.1.call-done = f32[256,1280]{1,0:T(8,128)} async-done(((f32[256,1280]{1,0:T(8,128)}), f32[256,1280]{1,0:T(8,128)}) %all-reduce.3.cloned.1.call-update) | async-done | bytes 1310736 | tf_op jit(solution)/shard_map/psum | solution.py:126
  100.7 26.0 %all-gather.4.cloned.1.call-done = bf16[8,259,256]{2,1,0:T(8,128)(2,1)} async-done(((bf16[1,259,256]{2,1,0:T(8,128)(2,1)}), bf16[8,259,256]{2,1,0:T(8,128)(2,1)}) %all-gather.4.cloned.1.call-update) | async-done | bytes 1060880 | tf_op jit(solution)/shard_map/all_gather | solution.py:140
  132.8 7.3 %all_gather.14 = bf16[256,1024]{1,0:T(8,128)(2,1)S(1)} all-gather(bf16[64,1024]{1,0:T(8,128)(2,1)S(1)} %bitcast.236), channel_id=1, replica_groups=mesh['ctx'=8,'tp'=4] {'tp'}, dimensions={0}, use_global_device_ids=true | all-gather | bytes 655360 | tf_op jit(solution)/shard_map/all_gather | solution.py:175
  142.5 6.4 %fusion.37 = (f32[8,128,2048]{2,1,0:T(8,128)}, f32[8,128,2048]{2,1,0:T(8,128)}) fusion(f32[8,128,4096]{2,1,0:T(8,128)S(1)} %bitcast.223), kind=kLoop, calls=%fused_computation.121 | loop fusion | bytes 33554432 | tf_op jit(solution)/shard_map/slice | solution.py:83
  155.2 3.2 fusion.1
  162.7 2.8 collective-permute-done.14
  167.9 7.7 %convolution_convert_fusion = bf16[256,4096]{1,0:T(8,128)(2,1)} fusion(bf16[256,1024]{1,0:T(8,128)(2,1)S(1)} %all_gather.14, bf16[1024,4096]{1,0:T(8,128)(2,1)} %param.14), kind=kOutput, calls=%fused_computation.3 | convolution fusion | flops 2148532224 | bytes 11010048 | tf_op jit(solution)/shard_map/dot_general | solution.py:176
  177.8 12.7 %collective-permute-done.15 = bf16[128,2048]{1,0:T(8,128)(2,1)S(1)} collective-permute-done((bf16[128,2048]{1,0:T(8,128)(2,1)S(1)}, bf16[128,2048]{1,0:T(8,128)(2,1)S(1)}, u32[]{:S(2)}, u32[]{:S(2)}) %collective-permute-start.15) | collective-permute-done | bytes 524320 | tf_op jit(solution)/shard_map/ppermute | solution.py:94
  195.1 5.9 %collective-permute-done.22 = bf16[128,2048]{1,0:T(8,128)(2,1)S(1)} collective-permute-done((bf16[128,2048]{1,0:T(8,128)(2,1)S(1)}, bf16[128,2048]{1,0:T(8,128)(2,1)S(1)}, u32[]{:S(2)}, u32[]{:S(2)}) %collective-permute-start.22) | collective-permute-done | bytes 524320 | tf_op jit(solution)/shard_map/ppermute | solution.py:95
  201.1 5.8 %collective-permute-done.16 = bf16[128,2048]{1,0:T(8,128)(2,1)S(1)} collective-permute-done((bf16[128,2048]{1,0:T(8,128)(2,1)S(1)}, bf16[128,2048]{1,0:T(8,128)(2,1)S(1)}, u32[]{:S(2)}, u32[]{:S(2)}) %collective-permute-start.16) | collective-permute-done | bytes 524320 | tf_op jit(solution)/shard_map/ppermute | solution.py:94
  211.0 4.4 collective-permute-done.23
  218.0 4.4 %collective-permute-done.17 = bf16[128,2048]{1,0:T(8,128)(2,1)S(1)} collective-permute-done((bf16[128,2048]{1,0:T(8,128)(2,1)S(1)}, bf16[128,2048]{1,0:T(8,128)(2,1)S(1)}, u32[]{:S(2)}, u32[]{:S(2)}) %collective-permute-start.17) | collective-permute-done | bytes 524320 | tf_op jit(solution)/shard_map/ppermute | solution.py:94
  225.3 6.6 %collective-permute-done.24 = bf16[128,2048]{1,0:T(8,128)(2,1)S(1)} collective-permute-done((bf16[128,2048]{1,0:T(8,128)(2,1)S(1)}, bf16[128,2048]{1,0:T(8,128)(2,1)S(1)}, u32[]{:S(2)}, u32[]{:S(2)}) %collective-permute-start.24) | collective-permute-done | bytes 524320 | tf_op jit(solution)/shard_map/ppermute | solution.py:95
  234.8 7.4 %reduce-scatter.5.cloned.1.call-done = f32[256,256]{1,0:T(8,128)} async-done(((f32[2048,256]{1,0:T(8,128)}), f32[256,256]{1,0:T(8,128)}) %reduce-scatter.5.cloned.1.call-update) | async-done | bytes 262160 | tf_op jit(solution)/shard_map/reduce_scatter | solution.py:191
  247.1 30.8 %all-reduce.5.cloned.1.call-done = f32[256,256]{1,0:T(8,128)} async-done(((f32[256,256]{1,0:T(8,128)}), f32[256,256]{1,0:T(8,128)}) %all-reduce.5.cloned.1.call-update) | async-done | bytes 262160 | tf_op jit(solution)/shard_map/psum | solution.py:190
  279.7 7.1 %all_gather.15 = bf16[256,1280]{1,0:T(8,128)(2,1)S(1)} all-gather(bf16[64,1280]{1,0:T(8,128)(2,1)S(1)} %concatenate.39), channel_id=1, replica_groups=mesh['ctx'=8,'tp'=4] {'tp'}, dimensions={0}, use_global_device_ids=true | all-gather | bytes 819200 | tf_op jit(solution)/shard_map/all_gather | solution.py:203
  286.7 2.9 fusion.43
  289.7 8.1 %fusion.36 = (f32[8,160,2048]{2,1,0:T(8,128)}, f32[8,160,2048]{2,1,0:T(8,128)}) fusion(f32[8,160,4096]{2,1,0:T(8,128)S(1)} %bitcast.222), kind=kLoop, calls=%fused_computation.120 | loop fusion | bytes 41943040 | tf_op jit(solution)/shard_map/slice | solution.py:83
  305.9 10.4 %collective-permute-done = bf16[160,2048]{1,0:T(8,128)(2,1)S(1)} collective-permute-done((bf16[160,2048]{1,0:T(8,128)(2,1)S(1)}, bf16[160,2048]{1,0:T(8,128)(2,1)S(1)}, u32[]{:S(2)}, u32[]{:S(2)}) %collective-permute-start) | collective-permute-done | bytes 655392 | tf_op jit(solution)/shard_map/ppermute | solution.py:94
  324.7 10.7 %collective-permute-done.1 = bf16[160,2048]{1,0:T(8,128)(2,1)S(1)} collective-permute-done((bf16[160,2048]{1,0:T(8,128)(2,1)S(1)}, bf16[160,2048]{1,0:T(8,128)(2,1)S(1)}, u32[]{:S(2)}, u32[]{:S(2)}) %collective-permute-start.1) | collective-permute-done | bytes 655392 | tf_op jit(solution)/shard_map/ppermute | solution.py:94
  338.5 5.7 %collective-permute-done.8 = bf16[160,2048]{1,0:T(8,128)(2,1)S(1)} collective-permute-done((bf16[160,2048]{1,0:T(8,128)(2,1)S(1)}, bf16[160,2048]{1,0:T(8,128)(2,1)S(1)}, u32[]{:S(2)}, u32[]{:S(2)}) %collective-permute-start.8) | collective-permute-done | bytes 655392 | tf_op jit(solution)/shard_map/ppermute | solution.py:95
  348.5 10.8 %collective-permute-done.2 = bf16[160,2048]{1,0:T(8,128)(2,1)S(1)} collective-permute-done((bf16[160,2048]{1,0:T(8,128)(2,1)S(1)}, bf16[160,2048]{1,0:T(8,128)(2,1)S(1)}, u32[]{:S(2)}, u32[]{:S(2)}) %collective-permute-start.2) | collective-permute-done | bytes 655392 | tf_op jit(solution)/shard_map/ppermute | solution.py:94
  364.4 11.7 %collective-permute-done.3 = bf16[160,2048]{1,0:T(8,128)(2,1)S(1)} collective-permute-done((bf16[160,2048]{1,0:T(8,128)(2,1)S(1)}, bf16[160,2048]{1,0:T(8,128)(2,1)S(1)}, u32[]{:S(2)}, u32[]{:S(2)}) %collective-permute-start.3) | collective-permute-done | bytes 655392 | tf_op jit(solution)/shard_map/ppermute | solution.py:94
  377.8 7.8 %collective-permute-done.10 = bf16[160,2048]{1,0:T(8,128)(2,1)S(1)} collective-permute-done((bf16[160,2048]{1,0:T(8,128)(2,1)S(1)}, bf16[160,2048]{1,0:T(8,128)(2,1)S(1)}, u32[]{:S(2)}, u32[]{:S(2)}) %collective-permute-start.10) | collective-permute-done | bytes 655392 | tf_op jit(solution)/shard_map/ppermute | solution.py:95
  387.6 3.3 collective-permute-done.4
  392.6 8.0 %collective-permute-done.11 = bf16[160,2048]{1,0:T(8,128)(2,1)S(1)} collective-permute-done((bf16[160,2048]{1,0:T(8,128)(2,1)S(1)}, bf16[160,2048]{1,0:T(8,128)(2,1)S(1)}, u32[]{:S(2)}, u32[]{:S(2)}) %collective-permute-start.11) | collective-permute-done | bytes 655392 | tf_op jit(solution)/shard_map/ppermute | solution.py:95
  403.0 2.9 collective-permute-done.5
  407.5 8.0 %collective-permute-done.12 = bf16[160,2048]{1,0:T(8,128)(2,1)S(1)} collective-permute-done((bf16[160,2048]{1,0:T(8,128)(2,1)S(1)}, bf16[160,2048]{1,0:T(8,128)(2,1)S(1)}, u32[]{:S(2)}, u32[]{:S(2)}) %collective-permute-start.12) | collective-permute-done | bytes 655392 | tf_op jit(solution)/shard_map/ppermute | solution.py:95
  416.3 8.0 %convolution_convert_fusion.1 = bf16[256,4096]{1,0:T(8,128)(2,1)} fusion(bf16[256,1280]{1,0:T(8,128)(2,1)S(1)} %all_gather.15, bf16[1280,4096]{1,0:T(8,128)(2,1)} %param.13), kind=kOutput, calls=%fused_computation.4 | convolution fusion | flops 2685403136 | bytes 13238272 | tf_op jit(solution)/shard_map/dot_general | solution.py:204
  424.5 4.4 %collective-permute-done.13 = bf16[160,2048]{1,0:T(8,128)(2,1)S(1)} collective-permute-done((bf16[160,2048]{1,0:T(8,128)(2,1)S(1)}, bf16[160,2048]{1,0:T(8,128)(2,1)S(1)}, u32[]{:S(2)}, u32[]{:S(2)}) %collective-permute-start.13) | collective-permute-done | bytes 655392 | tf_op jit(solution)/shard_map/ppermute | solution.py:95
  (155 shorter events, 97.7 us)
Async XLA Ops:
  7.2 51.4 %all-reduce.3.cloned.1.call-start = ((), (), s32[]{:S(2)}) async-start(), calls=%async_computation.2 | async-start | bytes 2621440 | tf_op jit(solution)/shard_map/psum | solution.py:126
  16.8 83.0 %reduce-scatter.3.cloned.1.call-start = ((), (), s32[]{:S(2)}) async-start(), calls=%async_computation.3 | async-start | bytes 655360 | tf_op jit(solution)/shard_map/reduce_scatter | solution.py:116
  24.0 102.6 %all-gather.4.cloned.1.call-start = ((), (), s32[]{:S(2)}) async-start(), calls=%async_computation.6 | async-start | bytes 1216512 | tf_op jit(solution)/shard_map/all_gather | solution.py:140
  61.8 180.4 %reduce-scatter.5.cloned.1.call-start = ((), (), s32[]{:S(2)}) async-start(), calls=%async_computation.4 | async-start | bytes 2359296 | tf_op jit(solution)/shard_map/reduce_scatter | solution.py:191
  151.1 14.5 %collective-permute-start.14 = (bf16[128,2048]{1,0:T(8,128)(2,1)}, bf16[128,2048]{1,0:T(8,128)(2,1)}, u32[]{:S(2)}, u32[]{:S(2)}) collective-permute-start(bf16[128,2048]{1,0:T(8,128)(2,1)} %fusion.31), channel_id=1, source_target_pairs={{0,8},{8,16},{16,24},{24,28},{28,20},{20,12},{12,4},{4,0},{1,9},{9... | collective-permute-start | bytes 1572872 | tf_op jit(solution)/shard_map/ppermute | solution.py:94
  153.9 21.8 %collective-permute-start.21 = (bf16[128,2048]{1,0:T(8,128)(2,1)}, bf16[128,2048]{1,0:T(8,128)(2,1)}, u32[]{:S(2)}, u32[]{:S(2)}) collective-permute-start(bf16[128,2048]{1,0:T(8,128)(2,1)} %fusion.32), channel_id=1, source_target_pairs={{0,4},{8,0},{16,8},{24,16},{28,24},{20,28},{12,20},{4,12},{1,5},{9... | collective-permute-start | bytes 1572872 | tf_op jit(solution)/shard_map/ppermute | solution.py:95
  162.7 115.2 %all-reduce.5.cloned.1.call-start = ((), (), s32[]{:S(2)}) async-start(), calls=%async_computation.5 | async-start | bytes 524288 | tf_op jit(solution)/shard_map/psum | solution.py:190
  167.2 23.3 %collective-permute-start.15 = (bf16[128,2048]{1,0:T(8,128)(2,1)S(1)}, bf16[128,2048]{1,0:T(8,128)(2,1)S(1)}, u32[]{:S(2)}, u32[]{:S(2)}) collective-permute-start(bf16[128,2048]{1,0:T(8,128)(2,1)S(1)} %fusion.28), channel_id=1, source_target_pairs={{0,8},{8,16},{16,24},{24,28},{28,20},{20,12},{12,4},{4,0},{1,9},{9... | collective-permute-start | bytes 1572872 | tf_op jit(solution)/shard_map/ppermute | solution.py:94
  176.9 24.0 %collective-permute-start.22 = (bf16[128,2048]{1,0:T(8,128)(2,1)S(1)}, bf16[128,2048]{1,0:T(8,128)(2,1)S(1)}, u32[]{:S(2)}, u32[]{:S(2)}) collective-permute-start(bf16[128,2048]{1,0:T(8,128)(2,1)S(1)} %fusion.22), channel_id=1, source_target_pairs={{0,4},{8,0},{16,8},{24,16},{28,24},{20,28},{12,20},{4,12},{1,5},{9... | collective-permute-start | bytes 1572872 | tf_op jit(solution)/shard_map/ppermute | solution.py:95
  191.8 15.1 %collective-permute-start.16 = (bf16[128,2048]{1,0:T(8,128)(2,1)S(1)}, bf16[128,2048]{1,0:T(8,128)(2,1)S(1)}, u32[]{:S(2)}, u32[]{:S(2)}) collective-permute-start(bf16[128,2048]{1,0:T(8,128)(2,1)S(1)} %fusion.27), channel_id=1, source_target_pairs={{0,8},{8,16},{16,24},{24,28},{28,20},{20,12},{12,4},{4,0},{1,9},{9... | collective-permute-start | bytes 1572872 | tf_op jit(solution)/shard_map/ppermute | solution.py:94
  201.1 14.2 %collective-permute-start.23 = (bf16[128,2048]{1,0:T(8,128)(2,1)S(1)}, bf16[128,2048]{1,0:T(8,128)(2,1)S(1)}, u32[]{:S(2)}, u32[]{:S(2)}) collective-permute-start(bf16[128,2048]{1,0:T(8,128)(2,1)S(1)} %fusion.21), channel_id=1, source_target_pairs={{0,4},{8,0},{16,8},{24,16},{28,24},{20,28},{12,20},{4,12},{1,5},{9... | collective-permute-start | bytes 1572872 | tf_op jit(solution)/shard_map/ppermute | solution.py:95
  208.3 14.1 %collective-permute-start.17 = (bf16[128,2048]{1,0:T(8,128)(2,1)S(1)}, bf16[128,2048]{1,0:T(8,128)(2,1)S(1)}, u32[]{:S(2)}, u32[]{:S(2)}) collective-permute-start(bf16[128,2048]{1,0:T(8,128)(2,1)S(1)} %fusion.26), channel_id=1, source_target_pairs={{0,8},{8,16},{16,24},{24,28},{28,20},{20,12},{12,4},{4,0},{1,9},{9... | collective-permute-start | bytes 1572872 | tf_op jit(solution)/shard_map/ppermute | solution.py:94
  215.4 16.5 %collective-permute-start.24 = (bf16[128,2048]{1,0:T(8,128)(2,1)S(1)}, bf16[128,2048]{1,0:T(8,128)(2,1)S(1)}, u32[]{:S(2)}, u32[]{:S(2)}) collective-permute-start(bf16[128,2048]{1,0:T(8,128)(2,1)S(1)} %fusion.20), channel_id=1, source_target_pairs={{0,4},{8,0},{16,8},{24,16},{28,24},{20,28},{12,20},{4,12},{1,5},{9... | collective-permute-start | bytes 1572872 | tf_op jit(solution)/shard_map/ppermute | solution.py:95
  223.7 19.5 %collective-permute-start.18 = (bf16[128,2048]{1,0:T(8,128)(2,1)S(1)}, bf16[128,2048]{1,0:T(8,128)(2,1)S(1)}, u32[]{:S(2)}, u32[]{:S(2)}) collective-permute-start(bf16[128,2048]{1,0:T(8,128)(2,1)S(1)} %fusion.25), channel_id=1, source_target_pairs={{0,8},{8,16},{16,24},{24,28},{28,20},{20,12},{12,4},{4,0},{1,9},{9... | collective-permute-start | bytes 1572872 | tf_op jit(solution)/shard_map/ppermute | solution.py:94
  232.8 69.9 %collective-permute-start.25 = (bf16[128,2048]{1,0:T(8,128)(2,1)}, bf16[128,2048]{1,0:T(8,128)(2,1)}, u32[]{:S(2)}, u32[]{:S(2)}) collective-permute-start(bf16[128,2048]{1,0:T(8,128)(2,1)} %fusion.19), channel_id=1, source_target_pairs={{0,4},{8,0},{16,8},{24,16},{28,24},{20,28},{12,20},{4,12},{1,5},{9... | collective-permute-start | bytes 1572872 | tf_op jit(solution)/shard_map/ppermute | solution.py:95
  244.6 77.2 %collective-permute-start.19 = (bf16[128,2048]{1,0:T(8,128)(2,1)S(1)}, bf16[128,2048]{1,0:T(8,128)(2,1)S(1)}, u32[]{:S(2)}, u32[]{:S(2)}) collective-permute-start(bf16[128,2048]{1,0:T(8,128)(2,1)S(1)} %fusion.24), channel_id=1, source_target_pairs={{0,8},{8,16},{16,24},{24,28},{28,20},{20,12},{12,4},{4,0},{1,9},{9... | collective-permute-start | bytes 1572872 | tf_op jit(solution)/shard_map/ppermute | solution.py:94
  299.2 17.0 %collective-permute-start = (bf16[160,2048]{1,0:T(8,128)(2,1)S(1)}, bf16[160,2048]{1,0:T(8,128)(2,1)S(1)}, u32[]{:S(2)}, u32[]{:S(2)}) collective-permute-start(bf16[160,2048]{1,0:T(8,128)(2,1)S(1)} %fusion.29), channel_id=1, source_target_pairs={{0,8},{8,16},{16,24},{24,28},{28,20},{20,12},{12,4},{4,0},{1,9},{9... | collective-permute-start | bytes 1966088 | tf_op jit(solution)/shard_map/ppermute | solution.py:94
  302.1 17.6 %collective-permute-start.7 = (bf16[160,2048]{1,0:T(8,128)(2,1)S(1)}, bf16[160,2048]{1,0:T(8,128)(2,1)S(1)}, u32[]{:S(2)}, u32[]{:S(2)}) collective-permute-start(bf16[160,2048]{1,0:T(8,128)(2,1)S(1)} %fusion.30), channel_id=1, source_target_pairs={{0,4},{8,0},{16,8},{24,16},{28,24},{20,28},{12,20},{4,12},{1,5},{9... | collective-permute-start | bytes 1966088 | tf_op jit(solution)/shard_map/ppermute | solution.py:95
  304.3 40.6 %collective-permute-start.26 = (bf16[128,2048]{1,0:T(8,128)(2,1)S(1)}, bf16[128,2048]{1,0:T(8,128)(2,1)S(1)}, u32[]{:S(2)}, u32[]{:S(2)}) collective-permute-start(bf16[128,2048]{1,0:T(8,128)(2,1)S(1)} %fusion.18), channel_id=1, source_target_pairs={{0,4},{8,0},{16,8},{24,16},{28,24},{20,28},{12,20},{4,12},{1,5},{9... | collective-permute-start | bytes 1572872 | tf_op jit(solution)/shard_map/ppermute | solution.py:95
  317.7 17.7 %collective-permute-start.1 = (bf16[160,2048]{1,0:T(8,128)(2,1)S(1)}, bf16[160,2048]{1,0:T(8,128)(2,1)S(1)}, u32[]{:S(2)}, u32[]{:S(2)}) collective-permute-start(bf16[160,2048]{1,0:T(8,128)(2,1)S(1)} %fusion.15), channel_id=1, source_target_pairs={{0,8},{8,16},{16,24},{24,28},{28,20},{20,12},{12,4},{4,0},{1,9},{9... | collective-permute-start | bytes 1966088 | tf_op jit(solution)/shard_map/ppermute | solution.py:94
  321.2 22.9 %collective-permute-start.8 = (bf16[160,2048]{1,0:T(8,128)(2,1)S(1)}, bf16[160,2048]{1,0:T(8,128)(2,1)S(1)}, u32[]{:S(2)}, u32[]{:S(2)}) collective-permute-start(bf16[160,2048]{1,0:T(8,128)(2,1)S(1)} %fusion.9), channel_id=1, source_target_pairs={{0,4},{8,0},{16,8},{24,16},{28,24},{20,28},{12,20},{4,12},{1,5},{9... | collective-permute-start | bytes 1966088 | tf_op jit(solution)/shard_map/ppermute | solution.py:95
  323.2 39.9 %collective-permute-start.20 = (bf16[128,2048]{1,0:T(8,128)(2,1)S(1)}, bf16[128,2048]{1,0:T(8,128)(2,1)S(1)}, u32[]{:S(2)}, u32[]{:S(2)}) collective-permute-start(bf16[128,2048]{1,0:T(8,128)(2,1)S(1)} %fusion.23), channel_id=1, source_target_pairs={{0,8},{8,16},{16,24},{24,28},{28,20},{20,12},{12,4},{4,0},{1,9},{9... | collective-permute-start | bytes 1572872 | tf_op jit(solution)/shard_map/ppermute | solution.py:94
  336.9 22.3 %collective-permute-start.2 = (bf16[160,2048]{1,0:T(8,128)(2,1)S(1)}, bf16[160,2048]{1,0:T(8,128)(2,1)S(1)}, u32[]{:S(2)}, u32[]{:S(2)}) collective-permute-start(bf16[160,2048]{1,0:T(8,128)(2,1)S(1)} %fusion.14), channel_id=1, source_target_pairs={{0,8},{8,16},{16,24},{24,28},{28,20},{20,12},{12,4},{4,0},{1,9},{9... | collective-permute-start | bytes 1966088 | tf_op jit(solution)/shard_map/ppermute | solution.py:94
  344.3 17.9 %collective-permute-start.9 = (bf16[160,2048]{1,0:T(8,128)(2,1)S(1)}, bf16[160,2048]{1,0:T(8,128)(2,1)S(1)}, u32[]{:S(2)}, u32[]{:S(2)}) collective-permute-start(bf16[160,2048]{1,0:T(8,128)(2,1)S(1)} %fusion.8), channel_id=1, source_target_pairs={{0,4},{8,0},{16,8},{24,16},{28,24},{20,28},{12,20},{4,12},{1,5},{9... | collective-permute-start | bytes 1966088 | tf_op jit(solution)/shard_map/ppermute | solution.py:95
  346.6 39.7 %collective-permute-start.27 = (bf16[128,2048]{1,0:T(8,128)(2,1)S(1)}, bf16[128,2048]{1,0:T(8,128)(2,1)S(1)}, u32[]{:S(2)}, u32[]{:S(2)}) collective-permute-start(bf16[128,2048]{1,0:T(8,128)(2,1)S(1)} %fusion.17), channel_id=1, source_target_pairs={{0,4},{8,0},{16,8},{24,16},{28,24},{20,28},{12,20},{4,12},{1,5},{9... | collective-permute-start | bytes 1572872 | tf_op jit(solution)/shard_map/ppermute | solution.py:95
  360.7 15.3 %collective-permute-start.3 = (bf16[160,2048]{1,0:T(8,128)(2,1)S(1)}, bf16[160,2048]{1,0:T(8,128)(2,1)S(1)}, u32[]{:S(2)}, u32[]{:S(2)}) collective-permute-start(bf16[160,2048]{1,0:T(8,128)(2,1)S(1)} %fusion.13), channel_id=1, source_target_pairs={{0,8},{8,16},{16,24},{24,28},{28,20},{20,12},{12,4},{4,0},{1,9},{9... | collective-permute-start | bytes 1966088 | tf_op jit(solution)/shard_map/ppermute | solution.py:94
  362.4 23.1 %collective-permute-start.10 = (bf16[160,2048]{1,0:T(8,128)(2,1)S(1)}, bf16[160,2048]{1,0:T(8,128)(2,1)S(1)}, u32[]{:S(2)}, u32[]{:S(2)}) collective-permute-start(bf16[160,2048]{1,0:T(8,128)(2,1)S(1)} %fusion.7), channel_id=1, source_target_pairs={{0,4},{8,0},{16,8},{24,16},{28,24},{20,28},{12,20},{4,12},{1,5},{9... | collective-permute-start | bytes 1966088 | tf_op jit(solution)/shard_map/ppermute | solution.py:95
  376.2 14.7 %collective-permute-start.4 = (bf16[160,2048]{1,0:T(8,128)(2,1)S(1)}, bf16[160,2048]{1,0:T(8,128)(2,1)S(1)}, u32[]{:S(2)}, u32[]{:S(2)}) collective-permute-start(bf16[160,2048]{1,0:T(8,128)(2,1)S(1)} %fusion.12), channel_id=1, source_target_pairs={{0,8},{8,16},{16,24},{24,28},{28,20},{20,12},{12,4},{4,0},{1,9},{9... | collective-permute-start | bytes 1966088 | tf_op jit(solution)/shard_map/ppermute | solution.py:94
  385.7 15.0 %collective-permute-start.11 = (bf16[160,2048]{1,0:T(8,128)(2,1)S(1)}, bf16[160,2048]{1,0:T(8,128)(2,1)S(1)}, u32[]{:S(2)}, u32[]{:S(2)}) collective-permute-start(bf16[160,2048]{1,0:T(8,128)(2,1)S(1)} %fusion.6), channel_id=1, source_target_pairs={{0,4},{8,0},{16,8},{24,16},{28,24},{20,28},{12,20},{4,12},{1,5},{9... | collective-permute-start | bytes 1966088 | tf_op jit(solution)/shard_map/ppermute | solution.py:95
  391.1 14.7 %collective-permute-start.5 = (bf16[160,2048]{1,0:T(8,128)(2,1)S(1)}, bf16[160,2048]{1,0:T(8,128)(2,1)S(1)}, u32[]{:S(2)}, u32[]{:S(2)}) collective-permute-start(bf16[160,2048]{1,0:T(8,128)(2,1)S(1)} %fusion.11), channel_id=1, source_target_pairs={{0,8},{8,16},{16,24},{24,28},{28,20},{20,12},{12,4},{4,0},{1,9},{9... | collective-permute-start | bytes 1966088 | tf_op jit(solution)/shard_map/ppermute | solution.py:94
  400.9 14.7 %collective-permute-start.12 = (bf16[160,2048]{1,0:T(8,128)(2,1)S(1)}, bf16[160,2048]{1,0:T(8,128)(2,1)S(1)}, u32[]{:S(2)}, u32[]{:S(2)}) collective-permute-start(bf16[160,2048]{1,0:T(8,128)(2,1)S(1)} %fusion.5), channel_id=1, source_target_pairs={{0,4},{8,0},{16,8},{24,16},{28,24},{20,28},{12,20},{4,12},{1,5},{9... | collective-permute-start | bytes 1966088 | tf_op jit(solution)/shard_map/ppermute | solution.py:95
  406.0 18.4 %collective-permute-start.6 = (bf16[160,2048]{1,0:T(8,128)(2,1)S(1)}, bf16[160,2048]{1,0:T(8,128)(2,1)S(1)}, u32[]{:S(2)}, u32[]{:S(2)}) collective-permute-start(bf16[160,2048]{1,0:T(8,128)(2,1)S(1)} %fusion.10), channel_id=1, source_target_pairs={{0,8},{8,16},{16,24},{24,28},{28,20},{20,12},{12,4},{4,0},{1,9},{9... | collective-permute-start | bytes 1966088 | tf_op jit(solution)/shard_map/ppermute | solution.py:94
  (16 other events, 285.6 us)
Sparse Core Ops, SparseCore 0:
  16.8 41.6 all-reduce.2
  61.6 21.6 reduce-scatter.2
  86.3 40.2 all-gather.3
  162.8 79.4 reduce-scatter.4
  244.5 33.2 all-reduce.4

commit v3 on v2

--- a/solution.py
+++ b/solution.py
@@ -98,6 +98,16 @@
     return jnp.concatenate([send_left, send_right], axis=1)
 
 
+def butterfly_sum(value, axis):
+    count = lax.axis_size(axis)
+    stride = 1
+    while stride < count:
+        pairs = [(i, i ^ stride) for i in range(count)]
+        value = value + lax.ppermute(value, axis, pairs)
+        stride *= 2
+    return value
+
+
 def shards(ring, tokens, document, place, w_qkv, w_out, grad_out):
     rows_ctx, slice_width = tokens.shape
     ctx_size = lax.axis_size("ctx")
@@ -113,9 +123,7 @@
     stacked = heads * rows_mine
     total_rows = ctx_size * rows_ctx
 
-    grad_rows = lax.psum_scatter(
-        against(grad_out, w_out).astype(jnp.bfloat16), "tp", scatter_dimension=0, tiled=True
-    )
+    grad_part = against(grad_out, w_out).astype(jnp.bfloat16)
 
     cosine_all, sine_all = angles(place, head_dim)
     cosine_mine = lax.dynamic_slice_in_dim(cosine_all, first_row, rows_mine, 0)
@@ -138,6 +146,8 @@
     packed = jnp.concatenate([keys, values, ], axis=1)
     packed = jnp.concatenate([packed, info], axis=0)
     gathered = lax.all_gather(packed, "ctx", axis=0, tiled=False)
+    grad_part, gathered = lax.optimization_barrier((grad_part, gathered))
+    grad_rows = lax.psum_scatter(grad_part, "tp", scatter_dimension=0, tiled=True)
     keys_all = gathered[:, :rows_ctx, :head_dim].reshape(total_rows, head_dim)
     values_all = gathered[:, :rows_ctx, head_dim:].reshape(total_rows, head_dim)
     info_all = gathered[:, rows_ctx:, :].reshape(ctx_size, info_rows * pair_width).astype(
@@ -187,20 +197,18 @@
     key_part = across(dscore, queries) * factor
     value_part = across(prob.astype(jnp.bfloat16), grad_stack)
     pair_all = jnp.concatenate([key_part, value_part], axis=1)
-    pair_grad = lax.psum(
-        lax.psum_scatter(pair_all, "ctx", scatter_dimension=0, tiled=True), "tp"
-    )
-    pair_grad = lax.dynamic_slice_in_dim(pair_grad, first_row, rows_mine, 0)
-
-    key_raw = rotate(pair_grad[:, :head_dim], cosine_mine, -sine_mine)
+    pair_grad = butterfly_sum(ring_scatter(pair_all, ring, "ctx"), "tp")
+
+    key_raw = rotate(pair_grad[:, :head_dim], cosine_all, -sine_all)
     query_grad = jnp.transpose((query_sum * factor).reshape(heads, rows_mine, head_dim), (1, 0, 2))
     query_raw = rotate(query_grad, cosine_mine[:, None, :], -sine_mine[:, None, :]).reshape(
         rows_mine, heads_width
     )
-    d_mine = jnp.concatenate([query_raw, key_raw, pair_grad[:, head_dim:]], axis=1).astype(
-        jnp.bfloat16
-    )
-    d_qkv = lax.all_gather(d_mine, "tp", axis=0, tiled=True)
+    query_rows = lax.all_gather(query_raw.astype(jnp.bfloat16), "tp", axis=0, tiled=True)
+    d_qkv = jnp.concatenate(
+        [query_rows, key_raw.astype(jnp.bfloat16), pair_grad[:, head_dim:].astype(jnp.bfloat16)],
+        axis=1,
+    )
     grad_x = jnp.dot(d_qkv, w_qkv, preferred_element_type=jnp.float32).astype(jnp.bfloat16)
     joint_weight = across(d_qkv, tokens)
     grad_w_qkv = ring_scatter(joint_weight, ring, "ctx")

time: 440 us -> 414 us (0.941)
  waiting for transfers between devices: 226 us -> 197 us
  starting transfers between devices: 37.4 us -> 45.9 us
    ppermute x14 -> x21, waiting for transfers between devices: 76.5 us -> 125 us  [ring_scatter(): got_left = lax.ppermute(send_left.astype(jnp.bfloat16), axis, forward)]
    ppermute x14 -> x21, waiting for transfers between devices: 51.3 us -> 12.1 us  [ring_scatter(): got_right = lax.ppermute(send_right.astype(jnp.bfloat16), axis, backward)]
    psum x1 -> x0, waiting for transfers between devices: 30.8 us -> none  [shards(): lax.psum(lax.psum_scatter(pair_all, 'ctx', scatter_dimension=0, tiled=Tru...]
    all_gather x1, waiting for transfers between devices: 26 us -> 0.02 us  [shards(): gathered = lax.all_gather(packed, 'ctx', axis=0, tiled=False)]
    ppermute x14 -> x21, starting transfers between devices: 22.9 us -> 32.4 us  [ring_scatter(): got_left = lax.ppermute(send_left.astype(jnp.bfloat16), axis, forward)]
    psum x1, waiting for transfers between devices: 34.4 us -> 41.7 us  [shards(): qkv = lax.psum(against(tokens, w_qkv), 'tp')]
    reduce_scatter x2 -> x1, waiting for transfers between devices: 7.45 us -> 12.9 us  [shards(): lax.psum_scatter(grad_part, 'tp', scatter_dimension=0, tiled=True)]
    ppermute x0 -> x2, waiting for transfers between devices: none -> 4.68 us  [butterfly_sum(): value = value + lax.ppermute(value, axis, pairs)]
  transfers between devices with their start and end apart: 33 -> 47, of which waited for: 24 -> 28; matrix products, arithmetic and copies ran while one was open for 18% -> 17% of each run, Pallas kernels for 0% -> 0%
where the time goes in v3:
time: 414 us; the launch traced here: 413 us
  waiting for transfers between devices  197 us (48%)
  between operations  50.1 us (12%)
  starting transfers between devices  45.9 us (11%)
  matrix products  38.3 us (9%)
  other arithmetic  34.2 us (8%)
  local copies, waits for them, and re-layouts  33.9 us (8%)
  blocking collectives  13.7 us (3%)
    ppermute x21, waiting for transfers between devices, ring_scatter(): got_left = lax.ppermute(send_left.astype(jnp.bfloat16), axis, forward)  125 us
    psum x1, waiting for transfers between devices, shards(): qkv = lax.psum(against(tokens, w_qkv), 'tp')  41.7 us
    ppermute x21, starting transfers between devices, ring_scatter(): got_left = lax.ppermute(send_left.astype(jnp.bfloat16), axis, forward)  32.4 us
    dot_general x4, matrix products, against(): lax.dot_general(left, right, (((1,), (1,)), ((), ())), preferred_element_...  16.8 us
    slice x3, local copies, waits for them, and re-layouts, ring_scatter(): left = blocks[:, :, :half]  16.2 us
    reduce_scatter x1, waiting for transfers between devices, shards(): lax.psum_scatter(grad_part, 'tp', scatter_dimension=0, tiled=True)  12.9 us
    ppermute x21, waiting for transfers between devices, ring_scatter(): got_right = lax.ppermute(send_right.astype(jnp.bfloat16), axis, backward)  12.1 us
    ppermute x21, starting transfers between devices, ring_scatter(): got_right = lax.ppermute(send_right.astype(jnp.bfloat16), axis, backward)  12 us
  transfers between devices with their start and end apart: 47, of which 28 were waited for; matrix products, arithmetic and copies ran while one was open for 17% of the time, Pallas kernels for 0%

profile of v3, /device:TPU:0, one launch (start us, length us, event | category | flops | bytes accessed | tf_op | source)
XLA Modules:
  0.0 412.7 jit_solution(18254214603639686852)
XLA Ops:
  8.8 7.9 %fusion.74 = f32[256,1280]{1,0:T(8,128)} fusion(bf16[256,4096]{1,0:T(8,128)(2,1)S(1)} %copy-done, bf16[1280,4096]{1,0:T(8,128)(2,1)} %param.15), kind=kOutput, calls=%fused_computation.170 | convolution fusion | flops 2684354560 | bytes 13893632 | tf_op jit(solution)/shard_map/dot_general | solution.py:35
  16.9 41.7 %all-reduce.2.cloned.1.call-done = f32[256,1280]{1,0:T(8,128)} async-done(((f32[256,1280]{1,0:T(8,128)}), f32[256,1280]{1,0:T(8,128)}) %all-reduce.2.cloned.1.call-update) | async-done | bytes 1310736 | tf_op jit(solution)/shard_map/psum | solution.py:134
  99.1 7.2 %convolution_convert_fusion.2 = bf16[256,1024]{1,0:T(8,128)(2,1)} fusion(bf16[256,4096]{1,0:T(8,128)(2,1)} %param.17, bf16[1024,4096]{1,0:T(8,128)(2,1)} %param.16), kind=kOutput, calls=%fused_computation.42 | convolution fusion | flops 2147745792 | bytes 11010048 | tf_op jit(solution)/shard_map/dot_general | solution.py:35
  111.0 2.6 fusion.2
  113.6 3.9 fusion.1
  117.5 12.9 %reduce-scatter.2.cloned.1.call-done = bf16[64,1024]{1,0:T(8,128)(2,1)} async-done(((bf16[256,1024]{1,0:T(8,128)(2,1)}), bf16[64,1024]{1,0:T(8,128)(2,1)}) %reduce-scatter.2.cloned.1.call-update) | async-done | bytes 131088 | tf_op jit(solution)/shard_map/reduce_scatter | solution.py:150
  131.5 2.6 multiply_reduce_fusion
  136.2 7.1 %all_gather.14 = bf16[256,1024]{1,0:T(8,128)(2,1)S(1)} all-gather(bf16[64,1024]{1,0:T(8,128)(2,1)S(1)} %bitcast.293), channel_id=1, replica_groups=mesh['ctx'=8,'tp'=4] {'tp'}, dimensions={0}, use_global_device_ids=true | all-gather | bytes 655360 | tf_op jit(solution)/shard_map/all_gather | solution.py:185
  143.3 2.4 fusion.77
  145.8 3.7 convolution_convert_fusion
  149.5 6.4 %fusion.69 = (f32[8,128,2048]{2,1,0:T(8,128)}, f32[8,128,2048]{2,1,0:T(8,128)}) fusion(f32[8,128,4096]{2,1,0:T(8,128)S(1)} %bitcast.277), kind=kLoop, calls=%fused_computation.165 | loop fusion | bytes 33554432 | tf_op jit(solution)/shard_map/slice | solution.py:83
  155.9 2.3 fusion.31
  164.2 2.9 copy.35
  171.2 6.6 %all_gather.15 = bf16[256,1024]{1,0:T(8,128)(2,1)S(1)} all-gather(bf16[64,1024]{1,0:T(8,128)(2,1)S(1)} %copy_bitcast_fusion.1), channel_id=1, replica_groups=mesh['ctx'=8,'tp'=4] {'tp'}, dimensions={0}, use_global_device_ids=true | all-gather | bytes 655360 | tf_op jit(solution)/shard_map/all_gather | solution.py:207
  180.0 2.2 collective-permute-done.1
  206.0 2.3 fusion.28
  213.6 4.7 %collective-permute-done.15 = f32[256,256]{1,0:T(8,128)S(1)} collective-permute-done((f32[256,256]{1,0:T(8,128)S(1)}, f32[256,256]{1,0:T(8,128)S(1)}, u32[]{:S(2)}, u32[]{:S(2)}) %collective-permute-start.15) | collective-permute-done | bytes 262176 | tf_op jit(solution)/shard_map/ppermute | solution.py:106
  219.2 2.9 fusion.76
  222.1 8.1 %fusion.68 = (f32[8,160,2048]{2,1,0:T(8,128)}, f32[8,160,2048]{2,1,0:T(8,128)}) fusion(f32[8,160,4096]{2,1,0:T(8,128)S(1)} %bitcast.276), kind=kLoop, calls=%fused_computation.164 | loop fusion | bytes 41943040 | tf_op jit(solution)/shard_map/slice | solution.py:83
  230.2 8.2 %convolution_convert_fusion.1 = bf16[256,4096]{1,0:T(8,128)(2,1)} fusion(bf16[256,1280]{1,0:T(8,128)(2,1)S(1)} %concatenate.45, bf16[1280,4096]{1,0:T(8,128)(2,1)} %param.15), kind=kOutput, calls=%fused_computation.4 | convolution fusion | flops 2685403136 | bytes 13238272 | tf_op jit(solution)/shard_map/dot_general | solution.py:212
  248.1 20.0 %collective-permute-done.32 = bf16[128,2048]{1,0:T(8,128)(2,1)S(1)} collective-permute-done((bf16[128,2048]{1,0:T(8,128)(2,1)S(1)}, bf16[128,2048]{1,0:T(8,128)(2,1)S(1)}, u32[]{:S(2)}, u32[]{:S(2)}) %collective-permute-start.32) | collective-permute-done | bytes 524320 | tf_op jit(solution)/shard_map/ppermute | solution.py:94
  275.4 8.9 %collective-permute-done.33 = bf16[128,2048]{1,0:T(8,128)(2,1)S(1)} collective-permute-done((bf16[128,2048]{1,0:T(8,128)(2,1)S(1)}, bf16[128,2048]{1,0:T(8,128)(2,1)S(1)}, u32[]{:S(2)}, u32[]{:S(2)}) %collective-permute-start.33) | collective-permute-done | bytes 524320 | tf_op jit(solution)/shard_map/ppermute | solution.py:94
  287.9 10.4 %collective-permute-done.17 = bf16[160,2048]{1,0:T(8,128)(2,1)S(1)} collective-permute-done((bf16[160,2048]{1,0:T(8,128)(2,1)S(1)}, bf16[160,2048]{1,0:T(8,128)(2,1)S(1)}, u32[]{:S(2)}, u32[]{:S(2)}) %collective-permute-start.17) | collective-permute-done | bytes 655392 | tf_op jit(solution)/shard_map/ppermute | solution.py:94
  302.0 7.6 %collective-permute-done.34 = bf16[128,2048]{1,0:T(8,128)(2,1)S(1)} collective-permute-done((bf16[128,2048]{1,0:T(8,128)(2,1)S(1)}, bf16[128,2048]{1,0:T(8,128)(2,1)S(1)}, u32[]{:S(2)}, u32[]{:S(2)}) %collective-permute-start.34) | collective-permute-done | bytes 524320 | tf_op jit(solution)/shard_map/ppermute | solution.py:94
  313.2 10.4 %collective-permute-done.18 = bf16[160,2048]{1,0:T(8,128)(2,1)S(1)} collective-permute-done((bf16[160,2048]{1,0:T(8,128)(2,1)S(1)}, bf16[160,2048]{1,0:T(8,128)(2,1)S(1)}, u32[]{:S(2)}, u32[]{:S(2)}) %collective-permute-start.18) | collective-permute-done | bytes 655392 | tf_op jit(solution)/shard_map/ppermute | solution.py:94
  327.3 7.6 %collective-permute-done.35 = bf16[128,2048]{1,0:T(8,128)(2,1)S(1)} collective-permute-done((bf16[128,2048]{1,0:T(8,128)(2,1)S(1)}, bf16[128,2048]{1,0:T(8,128)(2,1)S(1)}, u32[]{:S(2)}, u32[]{:S(2)}) %collective-permute-start.35) | collective-permute-done | bytes 524320 | tf_op jit(solution)/shard_map/ppermute | solution.py:94
  338.5 10.4 %collective-permute-done.19 = bf16[160,2048]{1,0:T(8,128)(2,1)S(1)} collective-permute-done((bf16[160,2048]{1,0:T(8,128)(2,1)S(1)}, bf16[160,2048]{1,0:T(8,128)(2,1)S(1)}, u32[]{:S(2)}, u32[]{:S(2)}) %collective-permute-start.19) | collective-permute-done | bytes 655392 | tf_op jit(solution)/shard_map/ppermute | solution.py:94
  352.6 7.6 %collective-permute-done.36 = bf16[128,2048]{1,0:T(8,128)(2,1)S(1)} collective-permute-done((bf16[128,2048]{1,0:T(8,128)(2,1)S(1)}, bf16[128,2048]{1,0:T(8,128)(2,1)S(1)}, u32[]{:S(2)}, u32[]{:S(2)}) %collective-permute-start.36) | collective-permute-done | bytes 524320 | tf_op jit(solution)/shard_map/ppermute | solution.py:94
  361.5 10.2 %collective-permute-done.20 = bf16[160,2048]{1,0:T(8,128)(2,1)S(1)} collective-permute-done((bf16[160,2048]{1,0:T(8,128)(2,1)S(1)}, bf16[160,2048]{1,0:T(8,128)(2,1)S(1)}, u32[]{:S(2)}, u32[]{:S(2)}) %collective-permute-start.20) | collective-permute-done | bytes 655392 | tf_op jit(solution)/shard_map/ppermute | solution.py:94
  375.7 10.9 %collective-permute-done.21 = bf16[160,2048]{1,0:T(8,128)(2,1)S(1)} collective-permute-done((bf16[160,2048]{1,0:T(8,128)(2,1)S(1)}, bf16[160,2048]{1,0:T(8,128)(2,1)S(1)}, u32[]{:S(2)}, u32[]{:S(2)}) %collective-permute-start.21) | collective-permute-done | bytes 655392 | tf_op jit(solution)/shard_map/ppermute | solution.py:94
  391.9 8.3 %collective-permute-done.22 = bf16[160,2048]{1,0:T(8,128)(2,1)S(1)} collective-permute-done((bf16[160,2048]{1,0:T(8,128)(2,1)S(1)}, bf16[160,2048]{1,0:T(8,128)(2,1)S(1)}, u32[]{:S(2)}, u32[]{:S(2)}) %collective-permute-start.22) | collective-permute-done | bytes 655392 | tf_op jit(solution)/shard_map/ppermute | solution.py:94
  400.4 3.6 collective-permute-done.29
  (210 shorter events, 108.1 us)
Async XLA Ops:
  7.2 51.3 %all-reduce.2.cloned.1.call-start = ((), (), s32[]{:S(2)}) async-start(), calls=%async_computation.1 | async-start | bytes 2621440 | tf_op jit(solution)/shard_map/psum | solution.py:134
  16.7 91.0 %all-gather.4.cloned.1.call-start = ((), (), s32[]{:S(2)}) async-start(), calls=%async_computation.3 | async-start | bytes 1216512 | tf_op jit(solution)/shard_map/all_gather | solution.py:148
  61.8 68.6 %reduce-scatter.2.cloned.1.call-start = ((), (), s32[]{:S(2)}) async-start(), calls=%async_computation.2 | async-start | bytes 655360 | tf_op jit(solution)/shard_map/reduce_scatter | solution.py:150
  158.1 47.8 %collective-permute-start.30 = (bf16[128,2048]{1,0:T(8,128)(2,1)}, bf16[128,2048]{1,0:T(8,128)(2,1)}, u32[]{:S(2)}, u32[]{:S(2)}) collective-permute-start(bf16[128,2048]{1,0:T(8,128)(2,1)} %fusion.31), channel_id=1, source_target_pairs={{0,8},{8,16},{16,24},{24,28},{28,20},{20,12},{12,4},{4,0},{1,9},{9... | collective-permute-start | bytes 1572872 | tf_op jit(solution)/shard_map/ppermute | solution.py:94
  161.7 49.2 %collective-permute-start.37 = (bf16[128,2048]{1,0:T(8,128)(2,1)}, bf16[128,2048]{1,0:T(8,128)(2,1)S(1)}, u32[]{:S(2)}, u32[]{:S(2)}) collective-permute-start(bf16[128,2048]{1,0:T(8,128)(2,1)} %fusion.32), channel_id=1, source_target_pairs={{0,4},{8,0},{16,8},{24,16},{28,24},{20,28},{12,20},{4,12},{1,5},{9... | collective-permute-start | bytes 1572872 | tf_op jit(solution)/shard_map/ppermute | solution.py:95
  170.4 9.0 %collective-permute-start.7 = (bf16[256,128]{1,0:T(8,128)(2,1)S(1)}, bf16[256,128]{1,0:T(8,128)(2,1)S(1)}, u32[]{:S(2)}, u32[]{:S(2)}) collective-permute-start(bf16[256,128]{1,0:T(8,128)(2,1)S(1)} %fusion.63), channel_id=1, source_target_pairs={{0,4},{8,0},{16,8},{24,16},{28,24},{20,28},{12,20},{4,12},{1,5},{9... | collective-permute-start | bytes 196616 | tf_op jit(solution)/shard_map/ppermute | solution.py:95
  208.2 33.9 %collective-permute-start.31 = (bf16[128,2048]{1,0:T(8,128)(2,1)}, bf16[128,2048]{1,0:T(8,128)(2,1)}, u32[]{:S(2)}, u32[]{:S(2)}) collective-permute-start(bf16[128,2048]{1,0:T(8,128)(2,1)} %fusion.28), channel_id=1, source_target_pairs={{0,8},{8,16},{16,24},{24,28},{28,20},{20,12},{12,4},{4,0},{1,9},{9... | collective-permute-start | bytes 1572872 | tf_op jit(solution)/shard_map/ppermute | solution.py:94
  213.0 32.6 %collective-permute-start.38 = (bf16[128,2048]{1,0:T(8,128)(2,1)}, bf16[128,2048]{1,0:T(8,128)(2,1)}, u32[]{:S(2)}, u32[]{:S(2)}) collective-permute-start(bf16[128,2048]{1,0:T(8,128)(2,1)} %fusion.22), channel_id=1, source_target_pairs={{0,4},{8,0},{16,8},{24,16},{28,24},{20,28},{12,20},{4,12},{1,5},{9... | collective-permute-start | bytes 1572872 | tf_op jit(solution)/shard_map/ppermute | solution.py:95
  240.6 32.3 %collective-permute-start.16 = (bf16[160,2048]{1,0:T(8,128)(2,1)S(1)}, bf16[160,2048]{1,0:T(8,128)(2,1)S(1)}, u32[]{:S(2)}, u32[]{:S(2)}) collective-permute-start(bf16[160,2048]{1,0:T(8,128)(2,1)S(1)} %fusion.29), channel_id=1, source_target_pairs={{0,8},{8,16},{16,24},{24,28},{28,20},{20,12},{12,4},{4,0},{1,9},{9... | collective-permute-start | bytes 1966088 | tf_op jit(solution)/shard_map/ppermute | solution.py:94
  243.8 24.3 %collective-permute-start.32 = (bf16[128,2048]{1,0:T(8,128)(2,1)S(1)}, bf16[128,2048]{1,0:T(8,128)(2,1)S(1)}, u32[]{:S(2)}, u32[]{:S(2)}) collective-permute-start(bf16[128,2048]{1,0:T(8,128)(2,1)S(1)} %fusion.27), channel_id=1, source_target_pairs={{0,8},{8,16},{16,24},{24,28},{28,20},{20,12},{12,4},{4,0},{1,9},{9... | collective-permute-start | bytes 1572872 | tf_op jit(solution)/shard_map/ppermute | solution.py:94
  247.0 23.9 %collective-permute-start.39 = (bf16[128,2048]{1,0:T(8,128)(2,1)S(1)}, bf16[128,2048]{1,0:T(8,128)(2,1)S(1)}, u32[]{:S(2)}, u32[]{:S(2)}) collective-permute-start(bf16[128,2048]{1,0:T(8,128)(2,1)S(1)} %fusion.21), channel_id=1, source_target_pairs={{0,4},{8,0},{16,8},{24,16},{28,24},{20,28},{12,20},{4,12},{1,5},{9... | collective-permute-start | bytes 1572872 | tf_op jit(solution)/shard_map/ppermute | solution.py:95
  247.5 27.1 %collective-permute-start.23 = (bf16[160,2048]{1,0:T(8,128)(2,1)S(1)}, bf16[160,2048]{1,0:T(8,128)(2,1)S(1)}, u32[]{:S(2)}, u32[]{:S(2)}) collective-permute-start(bf16[160,2048]{1,0:T(8,128)(2,1)S(1)} %fusion.30), channel_id=1, source_target_pairs={{0,4},{8,0},{16,8},{24,16},{28,24},{20,28},{12,20},{4,12},{1,5},{9... | collective-permute-start | bytes 1966088 | tf_op jit(solution)/shard_map/ppermute | solution.py:95
  269.4 14.9 %collective-permute-start.33 = (bf16[128,2048]{1,0:T(8,128)(2,1)S(1)}, bf16[128,2048]{1,0:T(8,128)(2,1)S(1)}, u32[]{:S(2)}, u32[]{:S(2)}) collective-permute-start(bf16[128,2048]{1,0:T(8,128)(2,1)S(1)} %fusion.26), channel_id=1, source_target_pairs={{0,8},{8,16},{16,24},{24,28},{28,20},{20,12},{12,4},{4,0},{1,9},{9... | collective-permute-start | bytes 1572872 | tf_op jit(solution)/shard_map/ppermute | solution.py:94
  272.3 14.9 %collective-permute-start.40 = (bf16[128,2048]{1,0:T(8,128)(2,1)S(1)}, bf16[128,2048]{1,0:T(8,128)(2,1)S(1)}, u32[]{:S(2)}, u32[]{:S(2)}) collective-permute-start(bf16[128,2048]{1,0:T(8,128)(2,1)S(1)} %fusion.20), channel_id=1, source_target_pairs={{0,4},{8,0},{16,8},{24,16},{28,24},{20,28},{12,20},{4,12},{1,5},{9... | collective-permute-start | bytes 1572872 | tf_op jit(solution)/shard_map/ppermute | solution.py:95
  273.1 25.3 %collective-permute-start.17 = (bf16[160,2048]{1,0:T(8,128)(2,1)S(1)}, bf16[160,2048]{1,0:T(8,128)(2,1)S(1)}, u32[]{:S(2)}, u32[]{:S(2)}) collective-permute-start(bf16[160,2048]{1,0:T(8,128)(2,1)S(1)} %fusion.15), channel_id=1, source_target_pairs={{0,8},{8,16},{16,24},{24,28},{28,20},{20,12},{12,4},{4,0},{1,9},{9... | collective-permute-start | bytes 1966088 | tf_op jit(solution)/shard_map/ppermute | solution.py:94
  274.8 26.5 %collective-permute-start.24 = (bf16[160,2048]{1,0:T(8,128)(2,1)S(1)}, bf16[160,2048]{1,0:T(8,128)(2,1)S(1)}, u32[]{:S(2)}, u32[]{:S(2)}) collective-permute-start(bf16[160,2048]{1,0:T(8,128)(2,1)S(1)} %fusion.9), channel_id=1, source_target_pairs={{0,4},{8,0},{16,8},{24,16},{28,24},{20,28},{12,20},{4,12},{1,5},{9... | collective-permute-start | bytes 1966088 | tf_op jit(solution)/shard_map/ppermute | solution.py:95
  285.7 23.9 %collective-permute-start.34 = (bf16[128,2048]{1,0:T(8,128)(2,1)S(1)}, bf16[128,2048]{1,0:T(8,128)(2,1)S(1)}, u32[]{:S(2)}, u32[]{:S(2)}) collective-permute-start(bf16[128,2048]{1,0:T(8,128)(2,1)S(1)} %fusion.25), channel_id=1, source_target_pairs={{0,8},{8,16},{16,24},{24,28},{28,20},{20,12},{12,4},{4,0},{1,9},{9... | collective-permute-start | bytes 1572872 | tf_op jit(solution)/shard_map/ppermute | solution.py:94
  287.3 25.1 %collective-permute-start.41 = (bf16[128,2048]{1,0:T(8,128)(2,1)S(1)}, bf16[128,2048]{1,0:T(8,128)(2,1)S(1)}, u32[]{:S(2)}, u32[]{:S(2)}) collective-permute-start(bf16[128,2048]{1,0:T(8,128)(2,1)S(1)} %fusion.19), channel_id=1, source_target_pairs={{0,4},{8,0},{16,8},{24,16},{28,24},{20,28},{12,20},{4,12},{1,5},{9... | collective-permute-start | bytes 1572872 | tf_op jit(solution)/shard_map/ppermute | solution.py:95
  298.5 25.1 %collective-permute-start.18 = (bf16[160,2048]{1,0:T(8,128)(2,1)S(1)}, bf16[160,2048]{1,0:T(8,128)(2,1)S(1)}, u32[]{:S(2)}, u32[]{:S(2)}) collective-permute-start(bf16[160,2048]{1,0:T(8,128)(2,1)S(1)} %fusion.14), channel_id=1, source_target_pairs={{0,8},{8,16},{16,24},{24,28},{28,20},{20,12},{12,4},{4,0},{1,9},{9... | collective-permute-start | bytes 1966088 | tf_op jit(solution)/shard_map/ppermute | solution.py:94
  301.4 25.1 %collective-permute-start.25 = (bf16[160,2048]{1,0:T(8,128)(2,1)S(1)}, bf16[160,2048]{1,0:T(8,128)(2,1)S(1)}, u32[]{:S(2)}, u32[]{:S(2)}) collective-permute-start(bf16[160,2048]{1,0:T(8,128)(2,1)S(1)} %fusion.8), channel_id=1, source_target_pairs={{0,4},{8,0},{16,8},{24,16},{28,24},{20,28},{12,20},{4,12},{1,5},{9... | collective-permute-start | bytes 1966088 | tf_op jit(solution)/shard_map/ppermute | solution.py:95
  310.9 23.9 %collective-permute-start.35 = (bf16[128,2048]{1,0:T(8,128)(2,1)S(1)}, bf16[128,2048]{1,0:T(8,128)(2,1)S(1)}, u32[]{:S(2)}, u32[]{:S(2)}) collective-permute-start(bf16[128,2048]{1,0:T(8,128)(2,1)S(1)} %fusion.24), channel_id=1, source_target_pairs={{0,8},{8,16},{16,24},{24,28},{28,20},{20,12},{12,4},{4,0},{1,9},{9... | collective-permute-start | bytes 1572872 | tf_op jit(solution)/shard_map/ppermute | solution.py:94
  312.6 25.2 %collective-permute-start.42 = (bf16[128,2048]{1,0:T(8,128)(2,1)S(1)}, bf16[128,2048]{1,0:T(8,128)(2,1)S(1)}, u32[]{:S(2)}, u32[]{:S(2)}) collective-permute-start(bf16[128,2048]{1,0:T(8,128)(2,1)S(1)} %fusion.18), channel_id=1, source_target_pairs={{0,4},{8,0},{16,8},{24,16},{28,24},{20,28},{12,20},{4,12},{1,5},{9... | collective-permute-start | bytes 1572872 | tf_op jit(solution)/shard_map/ppermute | solution.py:95
  323.8 25.1 %collective-permute-start.19 = (bf16[160,2048]{1,0:T(8,128)(2,1)S(1)}, bf16[160,2048]{1,0:T(8,128)(2,1)S(1)}, u32[]{:S(2)}, u32[]{:S(2)}) collective-permute-start(bf16[160,2048]{1,0:T(8,128)(2,1)S(1)} %fusion.13), channel_id=1, source_target_pairs={{0,8},{8,16},{16,24},{24,28},{28,20},{20,12},{12,4},{4,0},{1,9},{9... | collective-permute-start | bytes 1966088 | tf_op jit(solution)/shard_map/ppermute | solution.py:94
  326.7 25.1 %collective-permute-start.26 = (bf16[160,2048]{1,0:T(8,128)(2,1)S(1)}, bf16[160,2048]{1,0:T(8,128)(2,1)S(1)}, u32[]{:S(2)}, u32[]{:S(2)}) collective-permute-start(bf16[160,2048]{1,0:T(8,128)(2,1)S(1)} %fusion.7), channel_id=1, source_target_pairs={{0,4},{8,0},{16,8},{24,16},{28,24},{20,28},{12,20},{4,12},{1,5},{9... | collective-permute-start | bytes 1966088 | tf_op jit(solution)/shard_map/ppermute | solution.py:95
  336.2 23.9 %collective-permute-start.36 = (bf16[128,2048]{1,0:T(8,128)(2,1)S(1)}, bf16[128,2048]{1,0:T(8,128)(2,1)S(1)}, u32[]{:S(2)}, u32[]{:S(2)}) collective-permute-start(bf16[128,2048]{1,0:T(8,128)(2,1)S(1)} %fusion.23), channel_id=1, source_target_pairs={{0,8},{8,16},{16,24},{24,28},{28,20},{20,12},{12,4},{4,0},{1,9},{9... | collective-permute-start | bytes 1572872 | tf_op jit(solution)/shard_map/ppermute | solution.py:94
  337.9 37.7 %collective-permute-start.43 = (bf16[128,2048]{1,0:T(8,128)(2,1)S(1)}, bf16[128,2048]{1,0:T(8,128)(2,1)S(1)}, u32[]{:S(2)}, u32[]{:S(2)}) collective-permute-start(bf16[128,2048]{1,0:T(8,128)(2,1)S(1)} %fusion.17), channel_id=1, source_target_pairs={{0,4},{8,0},{16,8},{24,16},{28,24},{20,28},{12,20},{4,12},{1,5},{9... | collective-permute-start | bytes 1572872 | tf_op jit(solution)/shard_map/ppermute | solution.py:95
  349.1 22.6 %collective-permute-start.20 = (bf16[160,2048]{1,0:T(8,128)(2,1)S(1)}, bf16[160,2048]{1,0:T(8,128)(2,1)S(1)}, u32[]{:S(2)}, u32[]{:S(2)}) collective-permute-start(bf16[160,2048]{1,0:T(8,128)(2,1)S(1)} %fusion.12), channel_id=1, source_target_pairs={{0,8},{8,16},{16,24},{24,28},{28,20},{20,12},{12,4},{4,0},{1,9},{9... | collective-permute-start | bytes 1966088 | tf_op jit(solution)/shard_map/ppermute | solution.py:94
  352.0 23.0 %collective-permute-start.27 = (bf16[160,2048]{1,0:T(8,128)(2,1)S(1)}, bf16[160,2048]{1,0:T(8,128)(2,1)S(1)}, u32[]{:S(2)}, u32[]{:S(2)}) collective-permute-start(bf16[160,2048]{1,0:T(8,128)(2,1)S(1)} %fusion.6), channel_id=1, source_target_pairs={{0,4},{8,0},{16,8},{24,16},{28,24},{20,28},{12,20},{4,12},{1,5},{9... | collective-permute-start | bytes 1966088 | tf_op jit(solution)/shard_map/ppermute | solution.py:95
  371.9 14.7 %collective-permute-start.21 = (bf16[160,2048]{1,0:T(8,128)(2,1)S(1)}, bf16[160,2048]{1,0:T(8,128)(2,1)S(1)}, u32[]{:S(2)}, u32[]{:S(2)}) collective-permute-start(bf16[160,2048]{1,0:T(8,128)(2,1)S(1)} %fusion.11), channel_id=1, source_target_pairs={{0,8},{8,16},{16,24},{24,28},{28,20},{20,12},{12,4},{4,0},{1,9},{9... | collective-permute-start | bytes 1966088 | tf_op jit(solution)/shard_map/ppermute | solution.py:94
  375.2 14.7 %collective-permute-start.28 = (bf16[160,2048]{1,0:T(8,128)(2,1)S(1)}, bf16[160,2048]{1,0:T(8,128)(2,1)S(1)}, u32[]{:S(2)}, u32[]{:S(2)}) collective-permute-start(bf16[160,2048]{1,0:T(8,128)(2,1)S(1)} %fusion.5), channel_id=1, source_target_pairs={{0,4},{8,0},{16,8},{24,16},{28,24},{20,28},{12,20},{4,12},{1,5},{9... | collective-permute-start | bytes 1966088 | tf_op jit(solution)/shard_map/ppermute | solution.py:95
  386.8 13.5 %collective-permute-start.22 = (bf16[160,2048]{1,0:T(8,128)(2,1)S(1)}, bf16[160,2048]{1,0:T(8,128)(2,1)S(1)}, u32[]{:S(2)}, u32[]{:S(2)}) collective-permute-start(bf16[160,2048]{1,0:T(8,128)(2,1)S(1)} %fusion.10), channel_id=1, source_target_pairs={{0,8},{8,16},{16,24},{24,28},{28,20},{20,12},{12,4},{4,0},{1,9},{9... | collective-permute-start | bytes 1966088 | tf_op jit(solution)/shard_map/ppermute | solution.py:94
  390.1 13.9 %collective-permute-start.29 = (bf16[160,2048]{1,0:T(8,128)(2,1)S(1)}, bf16[160,2048]{1,0:T(8,128)(2,1)S(1)}, u32[]{:S(2)}, u32[]{:S(2)}) collective-permute-start(bf16[160,2048]{1,0:T(8,128)(2,1)S(1)} %fusion.4), channel_id=1, source_target_pairs={{0,4},{8,0},{16,8},{24,16},{28,24},{20,28},{12,20},{4,12},{1,5},{9... | collective-permute-start | bytes 1966088 | tf_op jit(solution)/shard_map/ppermute | solution.py:95
  (32 other events, 427.8 us)
Sparse Core Ops, SparseCore 0:
  16.9 41.6 all-reduce.1
  61.9 40.3 all-gather.3
  108.7 21.6 reduce-scatter.1

commit v4 on v3

--- a/solution.py
+++ b/solution.py
@@ -70,33 +70,49 @@
     return list(range(count))
 
 
+class Ring:
+    def __init__(self, partial, ring, axis):
+        count = len(ring)
+        where = [0] * count
+        for spot, member in enumerate(ring):
+            where[member] = spot
+        self.count = count
+        self.axis = axis
+        self.spot = jnp.asarray(where, jnp.int32)[lax.axis_index(axis)]
+        self.order = jnp.asarray(ring, jnp.int32)
+        rows = partial.shape[0] // count
+        half = partial.shape[1] // 2
+        blocks = partial.reshape(count, rows, partial.shape[1])
+        self.left = blocks[:, :, :half]
+        self.right = blocks[:, :, half:]
+        self.forward = [(ring[p], ring[(p + 1) % count]) for p in range(count)]
+        self.backward = [(ring[p], ring[(p - 1) % count]) for p in range(count)]
+        self.state = (self.block(self.left, count - 1), self.block(self.right, 1))
+        self.done = 0
+
+    def block(self, side, offset):
+        index = self.order[(self.spot + offset) % self.count]
+        return lax.dynamic_index_in_dim(side, index, 0, keepdims=False)
+
+    def advance(self, upto):
+        count = self.count
+        send_left, send_right = self.state
+        for step in range(self.done, min(upto, count - 1)):
+            got_left = lax.ppermute(send_left.astype(jnp.bfloat16), self.axis, self.forward)
+            got_right = lax.ppermute(send_right.astype(jnp.bfloat16), self.axis, self.backward)
+            send_left = got_left.astype(jnp.float32) + self.block(self.left, 2 * count - step - 2)
+            send_right = got_right.astype(jnp.float32) + self.block(self.right, step + 2)
+            self.done = step + 1
+        self.state = (send_left, send_right)
+        return self
+
+    def result(self):
+        self.advance(self.count - 1)
+        return jnp.concatenate(list(self.state), axis=1)
+
+
 def ring_scatter(partial, ring, axis):
-    count = len(ring)
-    where = [0] * count
-    for spot, member in enumerate(ring):
-        where[member] = spot
-    spot = jnp.asarray(where, jnp.int32)[lax.axis_index(axis)]
-    order = jnp.asarray(ring, jnp.int32)
-    rows = partial.shape[0] // count
-    half = partial.shape[1] // 2
-    blocks = partial.reshape(count, rows, partial.shape[1])
-    left = blocks[:, :, :half]
-    right = blocks[:, :, half:]
-
-    def block(side, offset):
-        return lax.dynamic_index_in_dim(side, order[(spot + offset) % count], 0, keepdims=False)
-
-    forward = [(ring[p], ring[(p + 1) % count]) for p in range(count)]
-    backward = [(ring[p], ring[(p - 1) % count]) for p in range(count)]
-    send_left = block(left, count - 1)
-    send_right = block(right, 1)
-    for step in range(count - 1):
-        got_left = lax.ppermute(send_left.astype(jnp.bfloat16), axis, forward)
-        got_right = lax.ppermute(send_right.astype(jnp.bfloat16), axis, backward)
-        send_left = got_left.astype(jnp.float32) + block(left, 2 * count - step - 2)
-        send_right = got_right.astype(jnp.float32) + block(right, step + 2)
-    return jnp.concatenate([send_left, send_right], axis=1)
-
+    return Ring(partial, ring, axis).result()
 
 def butterfly_sum(value, axis):
     count = lax.axis_size(axis)
@@ -197,7 +213,11 @@
     key_part = across(dscore, queries) * factor
     value_part = across(prob.astype(jnp.bfloat16), grad_stack)
     pair_all = jnp.concatenate([key_part, value_part], axis=1)
+    out_ring = Ring(out_weight_grad, ring, "ctx").advance(len(ring) // 2 - 1)
+    out_ring.state, pair_all = lax.optimization_barrier((out_ring.state, pair_all))
     pair_grad = butterfly_sum(ring_scatter(pair_all, ring, "ctx"), "tp")
+    out_ring.advance(len(ring) - 1)
+    out_ring.state, pair_grad = lax.optimization_barrier((out_ring.state, pair_grad))
 
     key_raw = rotate(pair_grad[:, :head_dim], cosine_all, -sine_all)
     query_grad = jnp.transpose((query_sum * factor).reshape(heads, rows_mine, head_dim), (1, 0, 2))
@@ -212,7 +232,7 @@
     grad_x = jnp.dot(d_qkv, w_qkv, preferred_element_type=jnp.float32).astype(jnp.bfloat16)
     joint_weight = across(d_qkv, tokens)
     grad_w_qkv = ring_scatter(joint_weight, ring, "ctx")
-    grad_w_out = ring_scatter(out_weight_grad, ring, "ctx")
+    grad_w_out = out_ring.result()
     return (out, grad_x, grad_w_qkv, grad_w_out)
 
 

time: 414 us -> 423 us (1.022)
  other arithmetic: 34.2 us -> 48.4 us
  waiting for transfers between devices: 197 us -> 185 us
    convert_element_type x36 -> x34, other arithmetic: 16.6 us -> 24.7 us  [the longest x17 15.7 us: advance(): send_left.astype(jnp.bfloat16)]
    ppermute x42, waiting for transfers between devices: 137 us -> 130 us  [the longest x21 92.5 us: advance(): lax.ppermute(send_left.astype(jnp.bfloat16), self.axis, self.forward)]
    add x6 -> x8, other arithmetic: 1.82 us -> 7.99 us  [the longest x4 5.14 us: advance(): got_left.astype(jnp.float32) + self.block(self.left, 2 * count - step - 2)]
    ppermute x2, waiting for transfers between devices: 4.68 us -> 0.01 us  [butterfly_sum(): value = value + lax.ppermute(value, axis, pairs)]
  transfers between devices with their start and end apart: 47 -> 47, of which waited for: 28 -> 27; matrix products, arithmetic and copies ran while one was open for 17% -> 17% of each run, Pallas kernels for 0% -> 0%
where the time goes in v4:
time: 423 us; the launch traced here: 421 us
  waiting for transfers between devices  185 us (44%)
  between operations  50.1 us (12%)
  other arithmetic  48.4 us (11%)
  starting transfers between devices  45.9 us (11%)
  matrix products  41.5 us (10%)
  local copies, waits for them, and re-layouts  35.7 us (8%)
  blocking collectives  14.2 us (3%)
    ppermute x21, waiting for transfers between devices, advance(): lax.ppermute(send_left.astype(jnp.bfloat16), self.axis, self.forward)  92.5 us
    psum x1, waiting for transfers between devices, shards(): qkv = lax.psum(against(tokens, w_qkv), 'tp')  41.7 us
    ppermute x21, waiting for transfers between devices, advance(): lax.ppermute(send_right.astype(jnp.bfloat16), self.axis, self.backward)  37.9 us
    ppermute x21, starting transfers between devices, advance(): lax.ppermute(send_right.astype(jnp.bfloat16), self.axis, self.backward)  33.6 us
    dot_general x4, matrix products, against(): lax.dot_general(left, right, (((1,), (1,)), ((), ())), preferred_element_...  18.9 us
    convert_element_type x17, other arithmetic, advance(): send_left.astype(jnp.bfloat16)  15.7 us
    reduce_scatter x1, waiting for transfers between devices, shards(): lax.psum_scatter(grad_part, 'tp', scatter_dimension=0, tiled=True)  12.9 us
    ppermute x21, starting transfers between devices, advance(): lax.ppermute(send_left.astype(jnp.bfloat16), self.axis, self.forward)  11 us
  transfers between devices with their start and end apart: 47, of which 27 were waited for; matrix products, arithmetic and copies ran while one was open for 17% of the time, Pallas kernels for 0%

profile of v4, /device:TPU:0, one launch (start us, length us, event | category | flops | bytes accessed | tf_op | source)
XLA Modules:
  0.0 420.9 jit_solution(2220862746952966935)
XLA Ops:
  8.8 7.9 %fusion.72 = f32[256,1280]{1,0:T(8,128)} fusion(bf16[256,4096]{1,0:T(8,128)(2,1)S(1)} %copy-done, bf16[1280,4096]{1,0:T(8,128)(2,1)} %param.15), kind=kOutput, calls=%fused_computation.168 | convolution fusion | flops 2684354560 | bytes 13893632 | tf_op jit(solution)/shard_map/dot_general | solution.py:35
  16.9 41.7 %all-reduce.2.cloned.1.call-done = f32[256,1280]{1,0:T(8,128)} async-done(((f32[256,1280]{1,0:T(8,128)}), f32[256,1280]{1,0:T(8,128)}) %all-reduce.2.cloned.1.call-update) | async-done | bytes 1310736 | tf_op jit(solution)/shard_map/psum | solution.py:150
  98.9 7.2 %convolution_convert_fusion.2 = bf16[256,1024]{1,0:T(8,128)(2,1)} fusion(bf16[256,4096]{1,0:T(8,128)(2,1)} %param.17, bf16[1024,4096]{1,0:T(8,128)(2,1)} %param.16), kind=kOutput, calls=%fused_computation.42 | convolution fusion | flops 2147745792 | bytes 11010048 | tf_op jit(solution)/shard_map/dot_general | solution.py:35
  110.8 2.6 fusion.2
  113.4 3.9 fusion.1
  117.3 12.9 %reduce-scatter.2.cloned.1.call-done = bf16[64,1024]{1,0:T(8,128)(2,1)} async-done(((bf16[256,1024]{1,0:T(8,128)(2,1)}), bf16[64,1024]{1,0:T(8,128)(2,1)}) %reduce-scatter.2.cloned.1.call-update) | async-done | bytes 131088 | tf_op jit(solution)/shard_map/reduce_scatter | solution.py:166
  131.2 2.5 multiply_reduce_fusion
  133.9 7.0 %all_gather.14 = bf16[256,1024]{1,0:T(8,128)(2,1)S(1)} all-gather(bf16[64,1024]{1,0:T(8,128)(2,1)S(1)} %bitcast.285), channel_id=1, replica_groups=mesh['ctx'=8,'tp'=4] {'tp'}, dimensions={0}, use_global_device_ids=true | all-gather | bytes 655360 | tf_op jit(solution)/shard_map/all_gather | solution.py:201
  140.8 2.4 fusion.73
  143.2 6.4 %fusion.67 = (f32[8,128,2048]{2,1,0:T(8,128)}, f32[8,128,2048]{2,1,0:T(8,128)}) fusion(f32[8,128,4096]{2,1,0:T(8,128)S(1)} %bitcast.273), kind=kLoop, calls=%fused_computation.163 | loop fusion | bytes 33554432 | tf_op jit(solution)/shard_map/slice | solution.py:87
  154.3 2.9 multiply_convert_fusion
  161.5 3.6 collective-permute-done.3
  170.1 9.8 %collective-permute-done.4 = bf16[128,2048]{1,0:T(8,128)(2,1)S(1)} collective-permute-done((bf16[128,2048]{1,0:T(8,128)(2,1)S(1)}, bf16[128,2048]{1,0:T(8,128)(2,1)S(1)}, u32[]{:S(2)}, u32[]{:S(2)}) %collective-permute-start.4) | collective-permute-done | bytes 524320 | tf_op jit(solution)/shard_map/ppermute | solution.py:102
  184.8 8.9 %collective-permute-done.5 = bf16[128,2048]{1,0:T(8,128)(2,1)S(1)} collective-permute-done((bf16[128,2048]{1,0:T(8,128)(2,1)S(1)}, bf16[128,2048]{1,0:T(8,128)(2,1)S(1)}, u32[]{:S(2)}, u32[]{:S(2)}) %collective-permute-start.5) | collective-permute-done | bytes 524320 | tf_op jit(solution)/shard_map/ppermute | solution.py:102
  197.6 2.9 copy.35
  209.5 9.6 %collective-permute-done.15 = bf16[256,128]{1,0:T(8,128)(2,1)S(1)} collective-permute-done((bf16[256,128]{1,0:T(8,128)(2,1)S(1)}, bf16[256,128]{1,0:T(8,128)(2,1)S(1)}, u32[]{:S(2)}, u32[]{:S(2)}) %collective-permute-start.15) | collective-permute-done | bytes 65568 | tf_op jit(solution)/shard_map/ppermute | solution.py:101
  230.0 2.7 collective-permute-done.18
  248.4 6.8 %collective-permute-done.11 = bf16[128,2048]{1,0:T(8,128)(2,1)S(1)} collective-permute-done((bf16[128,2048]{1,0:T(8,128)(2,1)S(1)}, bf16[128,2048]{1,0:T(8,128)(2,1)S(1)}, u32[]{:S(2)}, u32[]{:S(2)}) %collective-permute-start.11) | collective-permute-done | bytes 524320 | tf_op jit(solution)/shard_map/ppermute | solution.py:102
  261.3 6.6 %collective-permute-done.12 = bf16[128,2048]{1,0:T(8,128)(2,1)S(1)} collective-permute-done((bf16[128,2048]{1,0:T(8,128)(2,1)S(1)}, bf16[128,2048]{1,0:T(8,128)(2,1)S(1)}, u32[]{:S(2)}, u32[]{:S(2)}) %collective-permute-start.12) | collective-permute-done | bytes 524320 | tf_op jit(solution)/shard_map/ppermute | solution.py:102
  273.0 7.3 %all_gather.15 = bf16[256,1024]{1,0:T(8,128)(2,1)} all-gather(bf16[64,1024]{1,0:T(8,128)(2,1)S(1)} %copy_bitcast_fusion.1), channel_id=1, replica_groups=mesh['ctx'=8,'tp'=4] {'tp'}, dimensions={0}, use_global_device_ids=true | all-gather | bytes 655360 | tf_op jit(solution)/shard_map/all_gather | solution.py:227
  281.6 2.3 bitcast_add_fusion.18
  286.5 4.0 fusion.75
  290.5 8.1 %fusion.66 = (f32[8,160,2048]{2,1,0:T(8,128)}, f32[8,160,2048]{2,1,0:T(8,128)}) fusion(f32[8,160,4096]{2,1,0:T(8,128)S(1)} %bitcast.272), kind=kLoop, calls=%fused_computation.162 | loop fusion | bytes 41943040 | tf_op jit(solution)/shard_map/slice | solution.py:86
  304.1 13.0 %collective-permute-done.30 = bf16[160,2048]{1,0:T(8,128)(2,1)S(1)} collective-permute-done((bf16[160,2048]{1,0:T(8,128)(2,1)S(1)}, bf16[160,2048]{1,0:T(8,128)(2,1)S(1)}, u32[]{:S(2)}, u32[]{:S(2)}) %collective-permute-start.30) | collective-permute-done | bytes 655392 | tf_op jit(solution)/shard_map/ppermute | solution.py:101
  322.2 12.6 %collective-permute-done.31 = bf16[160,2048]{1,0:T(8,128)(2,1)S(1)} collective-permute-done((bf16[160,2048]{1,0:T(8,128)(2,1)S(1)}, bf16[160,2048]{1,0:T(8,128)(2,1)S(1)}, u32[]{:S(2)}, u32[]{:S(2)}) %collective-permute-start.31) | collective-permute-done | bytes 655392 | tf_op jit(solution)/shard_map/ppermute | solution.py:101
  338.7 13.0 %collective-permute-done.32 = bf16[160,2048]{1,0:T(8,128)(2,1)S(1)} collective-permute-done((bf16[160,2048]{1,0:T(8,128)(2,1)S(1)}, bf16[160,2048]{1,0:T(8,128)(2,1)S(1)}, u32[]{:S(2)}, u32[]{:S(2)}) %collective-permute-start.32) | collective-permute-done | bytes 655392 | tf_op jit(solution)/shard_map/ppermute | solution.py:101
  355.5 12.1 %collective-permute-done.33 = bf16[160,2048]{1,0:T(8,128)(2,1)S(1)} collective-permute-done((bf16[160,2048]{1,0:T(8,128)(2,1)S(1)}, bf16[160,2048]{1,0:T(8,128)(2,1)S(1)}, u32[]{:S(2)}, u32[]{:S(2)}) %collective-permute-start.33) | collective-permute-done | bytes 655392 | tf_op jit(solution)/shard_map/ppermute | solution.py:101
  371.4 7.8 %convolution_convert_fusion = bf16[256,4096]{1,0:T(8,128)(2,1)} fusion(bf16[256,1024]{1,0:T(8,128)(2,1)S(1)} %copy-done.7, bf16[1024,4096]{1,0:T(8,128)(2,1)} %param.16), kind=kOutput, calls=%fused_computation.3 | convolution fusion | flops 2148532224 | bytes 11010048 | tf_op jit(solution)/shard_map/dot_general | solution.py:202
  379.2 3.3 collective-permute-done.34
  386.3 4.1 convolution_convert_fusion.1
  390.5 7.0 %collective-permute-done.35 = bf16[160,2048]{1,0:T(8,128)(2,1)S(1)} collective-permute-done((bf16[160,2048]{1,0:T(8,128)(2,1)S(1)}, bf16[160,2048]{1,0:T(8,128)(2,1)S(1)}, u32[]{:S(2)}, u32[]{:S(2)}) %collective-permute-start.35) | collective-permute-done | bytes 655392 | tf_op jit(solution)/shard_map/ppermute | solution.py:101
  402.7 7.9 %collective-permute-done.36 = bf16[160,2048]{1,0:T(8,128)(2,1)S(1)} collective-permute-done((bf16[160,2048]{1,0:T(8,128)(2,1)S(1)}, bf16[160,2048]{1,0:T(8,128)(2,1)S(1)}, u32[]{:S(2)}, u32[]{:S(2)}) %collective-permute-start.36) | collective-permute-done | bytes 655392 | tf_op jit(solution)/shard_map/ppermute | solution.py:101
  (206 shorter events, 119.9 us)
Async XLA Ops:
  7.2 51.3 %all-reduce.2.cloned.1.call-start = ((), (), s32[]{:S(2)}) async-start(), calls=%async_computation.1 | async-start | bytes 2621440 | tf_op jit(solution)/shard_map/psum | solution.py:150
  16.7 90.8 %all-gather.4.cloned.1.call-start = ((), (), s32[]{:S(2)}) async-start(), calls=%async_computation.3 | async-start | bytes 1216512 | tf_op jit(solution)/shard_map/all_gather | solution.py:164
  61.8 68.4 %reduce-scatter.2.cloned.1.call-start = ((), (), s32[]{:S(2)}) async-start(), calls=%async_computation.2 | async-start | bytes 655360 | tf_op jit(solution)/shard_map/reduce_scatter | solution.py:166
  150.9 14.2 %collective-permute-start.3 = (bf16[128,2048]{1,0:T(8,128)(2,1)S(1)}, bf16[128,2048]{1,0:T(8,128)(2,1)S(1)}, u32[]{:S(2)}, u32[]{:S(2)}) collective-permute-start(bf16[128,2048]{1,0:T(8,128)(2,1)S(1)} %fusion.30), channel_id=1, source_target_pairs={{0,4},{8,0},{16,8},{24,16},{28,24},{20,28},{12,20},{4,12},{1,5},{9... | collective-permute-start | bytes 1572872 | tf_op jit(solution)/shard_map/ppermute | solution.py:102
  153.7 14.3 %collective-permute-start = (bf16[128,2048]{1,0:T(8,128)(2,1)S(1)}, bf16[128,2048]{1,0:T(8,128)(2,1)S(1)}, u32[]{:S(2)}, u32[]{:S(2)}) collective-permute-start(bf16[128,2048]{1,0:T(8,128)(2,1)S(1)} %fusion.29), channel_id=1, source_target_pairs={{0,8},{8,16},{16,24},{24,28},{28,20},{20,12},{12,4},{4,0},{1,9},{9... | collective-permute-start | bytes 1572872 | tf_op jit(solution)/shard_map/ppermute | solution.py:101
  166.5 13.4 %collective-permute-start.4 = (bf16[128,2048]{1,0:T(8,128)(2,1)S(1)}, bf16[128,2048]{1,0:T(8,128)(2,1)S(1)}, u32[]{:S(2)}, u32[]{:S(2)}) collective-permute-start(bf16[128,2048]{1,0:T(8,128)(2,1)S(1)} %fusion.24), channel_id=1, source_target_pairs={{0,4},{8,0},{16,8},{24,16},{28,24},{20,28},{12,20},{4,12},{1,5},{9... | collective-permute-start | bytes 1572872 | tf_op jit(solution)/shard_map/ppermute | solution.py:102
  169.3 13.4 %collective-permute-start.1 = (bf16[128,2048]{1,0:T(8,128)(2,1)S(1)}, bf16[128,2048]{1,0:T(8,128)(2,1)S(1)}, u32[]{:S(2)}, u32[]{:S(2)}) collective-permute-start(bf16[128,2048]{1,0:T(8,128)(2,1)S(1)} %fusion.26), channel_id=1, source_target_pairs={{0,8},{8,16},{16,24},{24,28},{28,20},{20,12},{12,4},{4,0},{1,9},{9... | collective-permute-start | bytes 1572872 | tf_op jit(solution)/shard_map/ppermute | solution.py:101
  181.2 12.5 %collective-permute-start.5 = (bf16[128,2048]{1,0:T(8,128)(2,1)S(1)}, bf16[128,2048]{1,0:T(8,128)(2,1)S(1)}, u32[]{:S(2)}, u32[]{:S(2)}) collective-permute-start(bf16[128,2048]{1,0:T(8,128)(2,1)S(1)} %fusion.23), channel_id=1, source_target_pairs={{0,4},{8,0},{16,8},{24,16},{28,24},{20,28},{12,20},{4,12},{1,5},{9... | collective-permute-start | bytes 1572872 | tf_op jit(solution)/shard_map/ppermute | solution.py:102
  184.1 12.2 %collective-permute-start.2 = (bf16[128,2048]{1,0:T(8,128)(2,1)S(1)}, bf16[128,2048]{1,0:T(8,128)(2,1)S(1)}, u32[]{:S(2)}, u32[]{:S(2)}) collective-permute-start(bf16[128,2048]{1,0:T(8,128)(2,1)S(1)} %fusion.25), channel_id=1, source_target_pairs={{0,8},{8,16},{16,24},{24,28},{28,20},{20,12},{12,4},{4,0},{1,9},{9... | collective-permute-start | bytes 1572872 | tf_op jit(solution)/shard_map/ppermute | solution.py:101
  204.4 39.0 %collective-permute-start.10 = (bf16[128,2048]{1,0:T(8,128)(2,1)S(1)}, bf16[128,2048]{1,0:T(8,128)(2,1)S(1)}, u32[]{:S(2)}, u32[]{:S(2)}) collective-permute-start(bf16[128,2048]{1,0:T(8,128)(2,1)S(1)} %bitcast_add_fusion.22), channel_id=1, source_target_pairs={{0,4},{8,0},{16,8},{24,16},{28,24},{20,28},{12,20},{4,12},{1,5},{9... | collective-permute-start | bytes 1572872 | tf_op jit(solution)/shard_map/ppermute | solution.py:102
  205.9 40.4 %collective-permute-start.6 = (bf16[128,2048]{1,0:T(8,128)(2,1)S(1)}, bf16[128,2048]{1,0:T(8,128)(2,1)S(1)}, u32[]{:S(2)}, u32[]{:S(2)}) collective-permute-start(bf16[128,2048]{1,0:T(8,128)(2,1)S(1)} %bitcast_add_fusion.25), channel_id=1, source_target_pairs={{0,8},{8,16},{16,24},{24,28},{28,20},{20,12},{12,4},{4,0},{1,9},{9... | collective-permute-start | bytes 1572872 | tf_op jit(solution)/shard_map/ppermute | solution.py:101
  207.3 11.8 %collective-permute-start.15 = (bf16[256,128]{1,0:T(8,128)(2,1)S(1)}, bf16[256,128]{1,0:T(8,128)(2,1)S(1)}, u32[]{:S(2)}, u32[]{:S(2)}) collective-permute-start(bf16[256,128]{1,0:T(8,128)(2,1)S(1)} %fusion.59), channel_id=1, source_target_pairs={{0,8},{8,16},{16,24},{24,28},{28,20},{20,12},{12,4},{4,0},{1,9},{9... | collective-permute-start | bytes 196616 | tf_op jit(solution)/shard_map/ppermute | solution.py:101
  208.0 11.7 %collective-permute-start.22 = (bf16[256,128]{1,0:T(8,128)(2,1)S(1)}, bf16[256,128]{1,0:T(8,128)(2,1)S(1)}, u32[]{:S(2)}, u32[]{:S(2)}) collective-permute-start(bf16[256,128]{1,0:T(8,128)(2,1)S(1)} %fusion.53), channel_id=1, source_target_pairs={{0,4},{8,0},{16,8},{24,16},{28,24},{20,28},{12,20},{4,12},{1,5},{9... | collective-permute-start | bytes 196616 | tf_op jit(solution)/shard_map/ppermute | solution.py:102
  248.3 11.9 %collective-permute-start.28 = (f32[256,256]{1,0:T(8,128)S(1)}, f32[256,256]{1,0:T(8,128)S(1)}, u32[]{:S(2)}, u32[]{:S(2)}) collective-permute-start(f32[256,256]{1,0:T(8,128)S(1)} %pad_maximum_fusion.3), channel_id=1, source_target_pairs={{0,1},{1,0},{2,3},{3,2},{4,5},{5,4},{6,7},{7,6},{8,9},{9,8},{10,11... | collective-permute-start | bytes 786440 | tf_op jit(solution)/shard_map/ppermute | solution.py:122
  256.5 11.4 %collective-permute-start.12 = (bf16[128,2048]{1,0:T(8,128)(2,1)S(1)}, bf16[128,2048]{1,0:T(8,128)(2,1)S(1)}, u32[]{:S(2)}, u32[]{:S(2)}) collective-permute-start(bf16[128,2048]{1,0:T(8,128)(2,1)S(1)} %fusion.18), channel_id=1, source_target_pairs={{0,4},{8,0},{16,8},{24,16},{28,24},{20,28},{12,20},{4,12},{1,5},{9... | collective-permute-start | bytes 1572872 | tf_op jit(solution)/shard_map/ppermute | solution.py:102
  259.6 11.4 %collective-permute-start.8 = (bf16[128,2048]{1,0:T(8,128)(2,1)S(1)}, bf16[128,2048]{1,0:T(8,128)(2,1)S(1)}, u32[]{:S(2)}, u32[]{:S(2)}) collective-permute-start(bf16[128,2048]{1,0:T(8,128)(2,1)S(1)} %fusion.21), channel_id=1, source_target_pairs={{0,8},{8,16},{16,24},{24,28},{28,20},{20,12},{12,4},{4,0},{1,9},{9... | collective-permute-start | bytes 1572872 | tf_op jit(solution)/shard_map/ppermute | solution.py:101
  260.3 20.0 %collective-permute-start.29 = (f32[256,256]{1,0:T(8,128)S(1)}, f32[256,256]{1,0:T(8,128)S(1)}, u32[]{:S(2)}, u32[]{:S(2)}) collective-permute-start(f32[256,256]{1,0:T(8,128)S(1)} %fusion.64), channel_id=1, source_target_pairs={{0,2},{1,3},{2,0},{3,1},{4,6},{5,7},{6,4},{7,5},{8,10},{9,11},{10,... | collective-permute-start | bytes 786440 | tf_op jit(solution)/shard_map/ppermute | solution.py:122
  269.2 11.1 %collective-permute-start.13 = (bf16[128,2048]{1,0:T(8,128)(2,1)S(1)}, bf16[128,2048]{1,0:T(8,128)(2,1)S(1)}, u32[]{:S(2)}, u32[]{:S(2)}) collective-permute-start(bf16[128,2048]{1,0:T(8,128)(2,1)S(1)} %fusion.17), channel_id=1, source_target_pairs={{0,4},{8,0},{16,8},{24,16},{28,24},{20,28},{12,20},{4,12},{1,5},{9... | collective-permute-start | bytes 1572872 | tf_op jit(solution)/shard_map/ppermute | solution.py:102
  300.1 17.0 %collective-permute-start.30 = (bf16[160,2048]{1,0:T(8,128)(2,1)S(1)}, bf16[160,2048]{1,0:T(8,128)(2,1)S(1)}, u32[]{:S(2)}, u32[]{:S(2)}) collective-permute-start(bf16[160,2048]{1,0:T(8,128)(2,1)S(1)} %fusion.27), channel_id=1, source_target_pairs={{0,8},{8,16},{16,24},{24,28},{28,20},{20,12},{12,4},{4,0},{1,9},{9... | collective-permute-start | bytes 1966088 | tf_op jit(solution)/shard_map/ppermute | solution.py:101
  302.5 16.5 %collective-permute-start.37 = (bf16[160,2048]{1,0:T(8,128)(2,1)S(1)}, bf16[160,2048]{1,0:T(8,128)(2,1)S(1)}, u32[]{:S(2)}, u32[]{:S(2)}) collective-permute-start(bf16[160,2048]{1,0:T(8,128)(2,1)S(1)} %fusion.28), channel_id=1, source_target_pairs={{0,4},{8,0},{16,8},{24,16},{28,24},{20,28},{12,20},{4,12},{1,5},{9... | collective-permute-start | bytes 1966088 | tf_op jit(solution)/shard_map/ppermute | solution.py:102
  318.6 16.2 %collective-permute-start.31 = (bf16[160,2048]{1,0:T(8,128)(2,1)S(1)}, bf16[160,2048]{1,0:T(8,128)(2,1)S(1)}, u32[]{:S(2)}, u32[]{:S(2)}) collective-permute-start(bf16[160,2048]{1,0:T(8,128)(2,1)S(1)} %fusion.15), channel_id=1, source_target_pairs={{0,8},{8,16},{16,24},{24,28},{28,20},{20,12},{12,4},{4,0},{1,9},{9... | collective-permute-start | bytes 1966088 | tf_op jit(solution)/shard_map/ppermute | solution.py:101
  320.4 16.3 %collective-permute-start.38 = (bf16[160,2048]{1,0:T(8,128)(2,1)S(1)}, bf16[160,2048]{1,0:T(8,128)(2,1)S(1)}, u32[]{:S(2)}, u32[]{:S(2)}) collective-permute-start(bf16[160,2048]{1,0:T(8,128)(2,1)S(1)} %fusion.9), channel_id=1, source_target_pairs={{0,4},{8,0},{16,8},{24,16},{28,24},{20,28},{12,20},{4,12},{1,5},{9... | collective-permute-start | bytes 1966088 | tf_op jit(solution)/shard_map/ppermute | solution.py:102
  336.3 15.3 %collective-permute-start.32 = (bf16[160,2048]{1,0:T(8,128)(2,1)S(1)}, bf16[160,2048]{1,0:T(8,128)(2,1)S(1)}, u32[]{:S(2)}, u32[]{:S(2)}) collective-permute-start(bf16[160,2048]{1,0:T(8,128)(2,1)S(1)} %fusion.14), channel_id=1, source_target_pairs={{0,8},{8,16},{16,24},{24,28},{28,20},{20,12},{12,4},{4,0},{1,9},{9... | collective-permute-start | bytes 1966088 | tf_op jit(solution)/shard_map/ppermute | solution.py:101
  336.9 16.7 %collective-permute-start.39 = (bf16[160,2048]{1,0:T(8,128)(2,1)S(1)}, bf16[160,2048]{1,0:T(8,128)(2,1)S(1)}, u32[]{:S(2)}, u32[]{:S(2)}) collective-permute-start(bf16[160,2048]{1,0:T(8,128)(2,1)S(1)} %fusion.8), channel_id=1, source_target_pairs={{0,4},{8,0},{16,8},{24,16},{28,24},{20,28},{12,20},{4,12},{1,5},{9... | collective-permute-start | bytes 1966088 | tf_op jit(solution)/shard_map/ppermute | solution.py:102
  353.2 14.4 %collective-permute-start.33 = (bf16[160,2048]{1,0:T(8,128)(2,1)S(1)}, bf16[160,2048]{1,0:T(8,128)(2,1)S(1)}, u32[]{:S(2)}, u32[]{:S(2)}) collective-permute-start(bf16[160,2048]{1,0:T(8,128)(2,1)S(1)} %fusion.13), channel_id=1, source_target_pairs={{0,8},{8,16},{16,24},{24,28},{28,20},{20,12},{12,4},{4,0},{1,9},{9... | collective-permute-start | bytes 1966088 | tf_op jit(solution)/shard_map/ppermute | solution.py:101
  353.7 15.7 %collective-permute-start.40 = (bf16[160,2048]{1,0:T(8,128)(2,1)S(1)}, bf16[160,2048]{1,0:T(8,128)(2,1)S(1)}, u32[]{:S(2)}, u32[]{:S(2)}) collective-permute-start(bf16[160,2048]{1,0:T(8,128)(2,1)S(1)} %fusion.7), channel_id=1, source_target_pairs={{0,4},{8,0},{16,8},{24,16},{28,24},{20,28},{12,20},{4,12},{1,5},{9... | collective-permute-start | bytes 1966088 | tf_op jit(solution)/shard_map/ppermute | solution.py:102
  369.1 13.5 %collective-permute-start.34 = (bf16[160,2048]{1,0:T(8,128)(2,1)S(1)}, bf16[160,2048]{1,0:T(8,128)(2,1)S(1)}, u32[]{:S(2)}, u32[]{:S(2)}) collective-permute-start(bf16[160,2048]{1,0:T(8,128)(2,1)S(1)} %fusion.12), channel_id=1, source_target_pairs={{0,8},{8,16},{16,24},{24,28},{28,20},{20,12},{12,4},{4,0},{1,9},{9... | collective-permute-start | bytes 1966088 | tf_op jit(solution)/shard_map/ppermute | solution.py:101
  369.6 14.8 %collective-permute-start.41 = (bf16[160,2048]{1,0:T(8,128)(2,1)S(1)}, bf16[160,2048]{1,0:T(8,128)(2,1)S(1)}, u32[]{:S(2)}, u32[]{:S(2)}) collective-permute-start(bf16[160,2048]{1,0:T(8,128)(2,1)S(1)} %fusion.6), channel_id=1, source_target_pairs={{0,4},{8,0},{16,8},{24,16},{28,24},{20,28},{12,20},{4,12},{1,5},{9... | collective-permute-start | bytes 1966088 | tf_op jit(solution)/shard_map/ppermute | solution.py:102
  384.0 13.4 %collective-permute-start.35 = (bf16[160,2048]{1,0:T(8,128)(2,1)S(1)}, bf16[160,2048]{1,0:T(8,128)(2,1)S(1)}, u32[]{:S(2)}, u32[]{:S(2)}) collective-permute-start(bf16[160,2048]{1,0:T(8,128)(2,1)S(1)} %fusion.11), channel_id=1, source_target_pairs={{0,8},{8,16},{16,24},{24,28},{28,20},{20,12},{12,4},{4,0},{1,9},{9... | collective-permute-start | bytes 1966088 | tf_op jit(solution)/shard_map/ppermute | solution.py:101
  384.5 14.7 %collective-permute-start.42 = (bf16[160,2048]{1,0:T(8,128)(2,1)S(1)}, bf16[160,2048]{1,0:T(8,128)(2,1)S(1)}, u32[]{:S(2)}, u32[]{:S(2)}) collective-permute-start(bf16[160,2048]{1,0:T(8,128)(2,1)S(1)} %fusion.5), channel_id=1, source_target_pairs={{0,4},{8,0},{16,8},{24,16},{28,24},{20,28},{12,20},{4,12},{1,5},{9... | collective-permute-start | bytes 1966088 | tf_op jit(solution)/shard_map/ppermute | solution.py:102
  398.9 11.7 %collective-permute-start.36 = (bf16[160,2048]{1,0:T(8,128)(2,1)S(1)}, bf16[160,2048]{1,0:T(8,128)(2,1)S(1)}, u32[]{:S(2)}, u32[]{:S(2)}) collective-permute-start(bf16[160,2048]{1,0:T(8,128)(2,1)S(1)} %fusion.10), channel_id=1, source_target_pairs={{0,8},{8,16},{16,24},{24,28},{28,20},{20,12},{12,4},{4,0},{1,9},{9... | collective-permute-start | bytes 1966088 | tf_op jit(solution)/shard_map/ppermute | solution.py:101
  399.4 12.7 %collective-permute-start.43 = (bf16[160,2048]{1,0:T(8,128)(2,1)S(1)}, bf16[160,2048]{1,0:T(8,128)(2,1)S(1)}, u32[]{:S(2)}, u32[]{:S(2)}) collective-permute-start(bf16[160,2048]{1,0:T(8,128)(2,1)S(1)} %fusion.4), channel_id=1, source_target_pairs={{0,4},{8,0},{16,8},{24,16},{28,24},{20,28},{12,20},{4,12},{1,5},{9... | collective-permute-start | bytes 1966088 | tf_op jit(solution)/shard_map/ppermute | solution.py:102
  (31 other events, 347.8 us)
Sparse Core Ops, SparseCore 0:
  16.9 41.6 all-reduce.1
  61.9 40.3 all-gather.3
  108.5 21.6 reduce-scatter.1

commit v5 on v3

--- a/solution.py
+++ b/solution.py
@@ -98,6 +98,71 @@
     return jnp.concatenate([send_left, send_right], axis=1)
 
 
+def ring_spot(ring, axis):
+    where = [0] * len(ring)
+    for spot, member in enumerate(ring):
+        where[member] = spot
+    return jnp.asarray(where, jnp.int32)[lax.axis_index(axis)]
+
+
+def ring_gather(value, ring, axis):
+    count = len(ring)
+    forward = [(ring[p], ring[(p + 1) % count]) for p in range(count)]
+    backward = [(ring[p], ring[(p - 1) % count]) for p in range(count)]
+    ahead = count // 2
+    behind = count - 1 - ahead
+    got = [value] + [None] * (count - 1)
+    from_left = value
+    from_right = value
+    for step in range(max(ahead, behind)):
+        if step < ahead:
+            from_left = lax.ppermute(from_left, axis, forward)
+            got[count - step - 1] = from_left
+        if step < behind:
+            from_right = lax.ppermute(from_right, axis, backward)
+            got[step + 1] = from_right
+    return jnp.stack(got, axis=0)
+
+
+def ring_scatter_relative(partial, ring, axis):
+    count = len(ring)
+    rows = partial.shape[0] // count
+    half = partial.shape[1] // 2
+    blocks = partial.reshape(count, rows, partial.shape[1])
+    left = blocks[:, :, :half]
+    right = blocks[:, :, half:]
+    forward = [(ring[p], ring[(p + 1) % count]) for p in range(count)]
+    backward = [(ring[p], ring[(p - 1) % count]) for p in range(count)]
+    send_left = left[count - 1]
+    send_right = right[1 % count]
+    for step in range(count - 1):
+        got_left = lax.ppermute(send_left.astype(jnp.bfloat16), axis, forward)
+        got_right = lax.ppermute(send_right.astype(jnp.bfloat16), axis, backward)
+        send_left = got_left.astype(jnp.float32) + left[(2 * count - step - 2) % count]
+        send_right = got_right.astype(jnp.float32) + right[(step + 2) % count]
+    return jnp.concatenate([send_left, send_right], axis=1)
+
+
+def tp_project(partial, rows_mine, split, axis):
+    rank = lax.axis_index(axis)
+    core = rank % 2
+    near = [(i, i ^ 1) for i in range(4)]
+    far = [(i, i ^ 2) for i in range(4)]
+    chip = partial + lax.ppermute(partial, axis, near)
+    head = chip[:, :split]
+    tail = chip[:, split:]
+    half_rows = tail.shape[0] // 2
+    mine = lax.dynamic_slice_in_dim(head, rank * rows_mine, rows_mine, 0)
+    theirs = lax.dynamic_slice_in_dim(head, (rank ^ 2) * rows_mine, rows_mine, 0)
+    own_head = mine + lax.ppermute(theirs, axis, far)
+    tail_half = lax.dynamic_slice_in_dim(tail, core * half_rows, half_rows, 0)
+    tail_half = tail_half + lax.ppermute(tail_half, axis, far)
+    other_half = lax.ppermute(tail_half, axis, near)
+    first = jnp.where(core == 0, tail_half, other_half)
+    second = jnp.where(core == 0, other_half, tail_half)
+    return own_head, jnp.concatenate([first, second], axis=0)
+
+
 def butterfly_sum(value, axis):
     count = lax.axis_size(axis)
     stride = 1
@@ -131,11 +196,15 @@
     query_doc = lax.dynamic_slice_in_dim(document, first_row, rows_mine, 0)
     query_place = lax.dynamic_slice_in_dim(place, first_row, rows_mine, 0)
 
-    qkv = lax.psum(against(tokens, w_qkv), "tp")
-    keys = rotate(qkv[:, heads_width : heads_width + head_dim], cosine_all, sine_all).astype(
-        jnp.bfloat16
-    )
-    values = qkv[:, heads_width + head_dim :].astype(jnp.bfloat16)
+    projected = against(tokens, w_qkv)
+    if tp_size == 4 and rows_ctx % (2 * tp_size) == 0:
+        query_block, pair_rows = tp_project(projected, rows_mine, heads_width, "tp")
+    else:
+        qkv = lax.psum(projected, "tp")
+        query_block = lax.dynamic_slice_in_dim(qkv[:, :heads_width], first_row, rows_mine, 0)
+        pair_rows = qkv[:, heads_width:]
+    keys = rotate(pair_rows[:, :head_dim], cosine_all, sine_all).astype(jnp.bfloat16)
+    values = pair_rows[:, head_dim:].astype(jnp.bfloat16)
 
     info = jnp.concatenate(
         [document, place // PIECE, place % PIECE], axis=0
@@ -143,10 +212,9 @@
     info_rows = -(-info.shape[0] // pair_width)
     info = jnp.pad(info, (0, info_rows * pair_width - info.shape[0]))
     info = info.reshape(info_rows, pair_width).astype(jnp.bfloat16)
-    packed = jnp.concatenate([keys, values, ], axis=1)
+    packed = jnp.concatenate([keys, values], axis=1)
     packed = jnp.concatenate([packed, info], axis=0)
-    gathered = lax.all_gather(packed, "ctx", axis=0, tiled=False)
-    grad_part, gathered = lax.optimization_barrier((grad_part, gathered))
+    gathered = ring_gather(packed, ring, "ctx")
     grad_rows = lax.psum_scatter(grad_part, "tp", scatter_dimension=0, tiled=True)
     keys_all = gathered[:, :rows_ctx, :head_dim].reshape(total_rows, head_dim)
     values_all = gathered[:, :rows_ctx, head_dim:].reshape(total_rows, head_dim)
@@ -165,8 +233,7 @@
         stacked, total_rows
     )
 
-    mine = lax.dynamic_slice_in_dim(qkv, first_row, rows_mine, 0)
-    raw_query = mine[:, :heads_width].reshape(rows_mine, heads, head_dim)
+    raw_query = query_block.reshape(rows_mine, heads, head_dim)
     rotated = rotate(raw_query, cosine_mine[:, None, :], sine_mine[:, None, :]).astype(jnp.bfloat16)
     queries = jnp.transpose(rotated, (1, 0, 2)).reshape(stacked, head_dim)
 
@@ -197,7 +264,7 @@
     key_part = across(dscore, queries) * factor
     value_part = across(prob.astype(jnp.bfloat16), grad_stack)
     pair_all = jnp.concatenate([key_part, value_part], axis=1)
-    pair_grad = butterfly_sum(ring_scatter(pair_all, ring, "ctx"), "tp")
+    pair_grad = butterfly_sum(ring_scatter_relative(pair_all, ring, "ctx"), "tp")
 
     key_raw = rotate(pair_grad[:, :head_dim], cosine_all, -sine_all)
     query_grad = jnp.transpose((query_sum * factor).reshape(heads, rows_mine, head_dim), (1, 0, 2))

time: 414 us -> 383 us (0.925)
  waiting for transfers between devices: 197 us -> 160 us
  starting transfers between devices: 45.9 us -> 53.9 us
    psum x1 -> x0, waiting for transfers between devices: 41.7 us -> none  [shards(): qkv = lax.psum(against(tokens, w_qkv), 'tp')]
    ppermute x0 -> x25, waiting for transfers between devices: none -> 34.6 us  [the longest x7 13.1 us: ring_scatter_relative(): got_left = lax.ppermute(send_left.astype(jnp.bfloat16), axis, forward)]
    ppermute x0 -> x25, starting transfers between devices: none -> 25.1 us  [the longest x7 10.2 us: ring_scatter_relative(): got_left = lax.ppermute(send_left.astype(jnp.bfloat16), axis, forward)]
    ppermute x21 -> x14, starting transfers between devices: 32.4 us -> 13.4 us  [ring_scatter(): got_left = lax.ppermute(send_left.astype(jnp.bfloat16), axis, forward)]
    ppermute x21 -> x14, waiting for transfers between devices: 125 us -> 111 us  [ring_scatter(): got_left = lax.ppermute(send_left.astype(jnp.bfloat16), axis, forward)]
    reduce_scatter x1, waiting for transfers between devices: 12.9 us -> 0.01 us  [shards(): lax.psum_scatter(grad_part, 'tp', scatter_dimension=0, tiled=True)]
    dot_general x4, matrix products: 16.8 us -> 11.8 us  [against(): lax.dot_general(left, right, (((1,), (1,)), ((), ())), preferred_element_...]
    ppermute x21 -> x14, starting transfers between devices: 12 us -> 13.8 us  [ring_scatter(): got_right = lax.ppermute(send_right.astype(jnp.bfloat16), axis, backward)]
  transfers between devices with their start and end apart: 47 -> 56, of which waited for: 28 -> 33; matrix products, arithmetic and copies ran while one was open for 17% -> 17% of each run, Pallas kernels for 0% -> 0%
where the time goes in v5:
time: 383 us; the launch traced here: 381 us
  waiting for transfers between devices  160 us (42%)
  starting transfers between devices  53.9 us (14%)
  between operations  50.8 us (13%)
  other arithmetic  37.9 us (10%)
  matrix products  35 us (9%)
  local copies, waits for them, and re-layouts  30.3 us (8%)
  blocking collectives  13.2 us (3%)
    ppermute x14, waiting for transfers between devices, ring_scatter(): got_left = lax.ppermute(send_left.astype(jnp.bfloat16), axis, forward)  111 us
    slice x2, local copies, waits for them, and re-layouts, ring_scatter(): left = blocks[:, :, :half]  14.4 us
    ppermute x14, starting transfers between devices, ring_scatter(): got_right = lax.ppermute(send_right.astype(jnp.bfloat16), axis, backward)  13.8 us
    ppermute x14, starting transfers between devices, ring_scatter(): got_left = lax.ppermute(send_left.astype(jnp.bfloat16), axis, forward)  13.4 us
    ppermute x7, waiting for transfers between devices, ring_scatter_relative(): got_left = lax.ppermute(send_left.astype(jnp.bfloat16), axis, forward)  13.1 us
    dot_general x4, matrix products, against(): lax.dot_general(left, right, (((1,), (1,)), ((), ())), preferred_element_...  11.8 us
    ppermute x14, waiting for transfers between devices, ring_scatter(): got_right = lax.ppermute(send_right.astype(jnp.bfloat16), axis, backward)  10.9 us
    ppermute x7, starting transfers between devices, ring_scatter_relative(): got_left = lax.ppermute(send_left.astype(jnp.bfloat16), axis, forward)  10.2 us
  transfers between devices with their start and end apart: 56, of which 33 were waited for; matrix products, arithmetic and copies ran while one was open for 17% of the time, Pallas kernels for 0%

profile of v5, /device:TPU:0, one launch (start us, length us, event | category | flops | bytes accessed | tf_op | source)
XLA Modules:
  0.0 381.3 jit_solution(13528403424880526683)
XLA Ops:
  8.8 7.0 %fusion.88 = f32[256,1280]{1,0:T(8,128)S(1)} fusion(bf16[256,4096]{1,0:T(8,128)(2,1)S(1)} %copy-done, bf16[1280,4096]{1,0:T(8,128)(2,1)} %param.13), kind=kOutput, calls=%fused_computation.201 | convolution fusion | flops 2684354560 | bytes 13893632 | tf_op jit(solution)/shard_map/dot_general | solution.py:35
  16.4 3.2 convolution_convert_fusion.2
  22.3 2.6 collective-permute-start.1
  71.7 3.9 %collective-permute-done.10 = f32[64,1024]{1,0:T(8,128)S(1)} collective-permute-done((f32[64,1024]{1,0:T(8,128)S(1)}, f32[64,1024]{1,0:T(8,128)S(1)}, u32[]{:S(2)}, u32[]{:S(2)}) %collective-permute-start.10) | collective-permute-done | bytes 262176 | tf_op jit(solution)/shard_map/ppermute | solution.py:157
  78.1 3.0 collective-permute-done.4
  83.1 4.5 %collective-permute-done.8 = bf16[259,256]{1,0:T(8,128)(2,1)S(1)} collective-permute-done((bf16[259,256]{1,0:T(8,128)(2,1)S(1)}, bf16[259,256]{1,0:T(8,128)(2,1)S(1)}, u32[]{:S(2)}, u32[]{:S(2)}) %collective-permute-start.8) | collective-permute-done | bytes 132640 | tf_op jit(solution)/shard_map/ppermute | solution.py:119
  88.2 4.3 %collective-permute-done.9 = bf16[259,256]{1,0:T(8,128)(2,1)S(1)} collective-permute-done((bf16[259,256]{1,0:T(8,128)(2,1)S(1)}, bf16[259,256]{1,0:T(8,128)(2,1)S(1)}, u32[]{:S(2)}, u32[]{:S(2)}) %collective-permute-start.9) | collective-permute-done | bytes 132640 | tf_op jit(solution)/shard_map/ppermute | solution.py:119
  97.0 6.7 %all_gather.6 = bf16[256,1024]{1,0:T(8,128)(2,1)S(1)} all-gather(bf16[64,1024]{1,0:T(8,128)(2,1)S(1)} %bitcast.345), channel_id=1, replica_groups=mesh['ctx'=8,'tp'=4] {'tp'}, dimensions={0}, use_global_device_ids=true | all-gather | bytes 655360 | tf_op jit(solution)/shard_map/all_gather | solution.py:252
  103.7 2.4 fusion.91
  106.1 6.3 %fusion.84 = (f32[8,128,2048]{2,1,0:T(8,128)}, f32[8,128,2048]{2,1,0:T(8,128)}) fusion(f32[8,128,4096]{2,1,0:T(8,128)S(1)} %bitcast.322), kind=kLoop, calls=%fused_computation.197 | loop fusion | bytes 33554432 | tf_op jit(solution)/shard_map/slice | solution.py:83
  112.4 3.2 fusion.1
  119.6 2.9 copy.27
  126.3 7.1 %convolution_convert_fusion = bf16[256,4096]{1,0:T(8,128)(2,1)} fusion(bf16[256,1024]{1,0:T(8,128)(2,1)S(1)} %all_gather.6, bf16[1024,4096]{1,0:T(8,128)(2,1)} %param.14), kind=kOutput, calls=%fused_computation.3 | convolution fusion | flops 2148532224 | bytes 11010048 | tf_op jit(solution)/shard_map/dot_general | solution.py:253
  148.6 7.2 %collective-permute-done.14 = bf16[256,128]{1,0:T(8,128)(2,1)S(1)} collective-permute-done((bf16[256,128]{1,0:T(8,128)(2,1)S(1)}, bf16[256,128]{1,0:T(8,128)(2,1)S(1)}, u32[]{:S(2)}, u32[]{:S(2)}) %collective-permute-start.14) | collective-permute-done | bytes 65568 | tf_op jit(solution)/shard_map/ppermute | solution.py:139
  164.3 2.4 collective-permute-done.16
  170.7 6.5 %all_gather.7 = bf16[256,1024]{1,0:T(8,128)(2,1)S(1)} all-gather(bf16[64,1024]{1,0:T(8,128)(2,1)S(1)} %copy_bitcast_fusion.1), channel_id=1, replica_groups=mesh['ctx'=8,'tp'=4] {'tp'}, dimensions={0}, use_global_device_ids=true | all-gather | bytes 655360 | tf_op jit(solution)/shard_map/all_gather | solution.py:274
  185.3 3.9 %collective-permute-done.26 = f32[256,256]{1,0:T(8,128)S(1)} collective-permute-done((f32[256,256]{1,0:T(8,128)S(1)}, f32[256,256]{1,0:T(8,128)S(1)}, u32[]{:S(2)}, u32[]{:S(2)}) %collective-permute-start.26) | collective-permute-done | bytes 262176 | tf_op jit(solution)/shard_map/ppermute | solution.py:171
  190.1 2.9 fusion.90
  193.1 8.1 %fusion.83 = (f32[8,160,2048]{2,1,0:T(8,128)}, f32[8,160,2048]{2,1,0:T(8,128)}) fusion(f32[8,160,4096]{2,1,0:T(8,128)S(1)} %bitcast.321), kind=kLoop, calls=%fused_computation.196 | loop fusion | bytes 41943040 | tf_op jit(solution)/shard_map/slice | solution.py:83
  201.1 8.2 %convolution_convert_fusion.1 = bf16[256,4096]{1,0:T(8,128)(2,1)} fusion(bf16[256,1280]{1,0:T(8,128)(2,1)S(1)} %concatenate.49, bf16[1280,4096]{1,0:T(8,128)(2,1)} %param.13), kind=kOutput, calls=%fused_computation.4 | convolution fusion | flops 2685403136 | bytes 13238272 | tf_op jit(solution)/shard_map/dot_general | solution.py:279
  209.3 2.2 fusion.29
  219.0 19.6 %collective-permute-done.43 = bf16[128,2048]{1,0:T(8,128)(2,1)S(1)} collective-permute-done((bf16[128,2048]{1,0:T(8,128)(2,1)S(1)}, bf16[128,2048]{1,0:T(8,128)(2,1)S(1)}, u32[]{:S(2)}, u32[]{:S(2)}) %collective-permute-start.43) | collective-permute-done | bytes 524320 | tf_op jit(solution)/shard_map/ppermute | solution.py:94
  246.0 8.9 %collective-permute-done.44 = bf16[128,2048]{1,0:T(8,128)(2,1)S(1)} collective-permute-done((bf16[128,2048]{1,0:T(8,128)(2,1)S(1)}, bf16[128,2048]{1,0:T(8,128)(2,1)S(1)}, u32[]{:S(2)}, u32[]{:S(2)}) %collective-permute-start.44) | collective-permute-done | bytes 524320 | tf_op jit(solution)/shard_map/ppermute | solution.py:94
  258.5 10.4 %collective-permute-done.28 = bf16[160,2048]{1,0:T(8,128)(2,1)S(1)} collective-permute-done((bf16[160,2048]{1,0:T(8,128)(2,1)S(1)}, bf16[160,2048]{1,0:T(8,128)(2,1)S(1)}, u32[]{:S(2)}, u32[]{:S(2)}) %collective-permute-start.28) | collective-permute-done | bytes 655392 | tf_op jit(solution)/shard_map/ppermute | solution.py:94
  272.6 7.5 %collective-permute-done.45 = bf16[128,2048]{1,0:T(8,128)(2,1)S(1)} collective-permute-done((bf16[128,2048]{1,0:T(8,128)(2,1)S(1)}, bf16[128,2048]{1,0:T(8,128)(2,1)S(1)}, u32[]{:S(2)}, u32[]{:S(2)}) %collective-permute-start.45) | collective-permute-done | bytes 524320 | tf_op jit(solution)/shard_map/ppermute | solution.py:94
  284.1 10.1 %collective-permute-done.29 = bf16[160,2048]{1,0:T(8,128)(2,1)S(1)} collective-permute-done((bf16[160,2048]{1,0:T(8,128)(2,1)S(1)}, bf16[160,2048]{1,0:T(8,128)(2,1)S(1)}, u32[]{:S(2)}, u32[]{:S(2)}) %collective-permute-start.29) | collective-permute-done | bytes 655392 | tf_op jit(solution)/shard_map/ppermute | solution.py:94
  297.9 7.5 %collective-permute-done.46 = bf16[128,2048]{1,0:T(8,128)(2,1)S(1)} collective-permute-done((bf16[128,2048]{1,0:T(8,128)(2,1)S(1)}, bf16[128,2048]{1,0:T(8,128)(2,1)S(1)}, u32[]{:S(2)}, u32[]{:S(2)}) %collective-permute-start.46) | collective-permute-done | bytes 524320 | tf_op jit(solution)/shard_map/ppermute | solution.py:94
  309.1 10.4 %collective-permute-done.30 = bf16[160,2048]{1,0:T(8,128)(2,1)S(1)} collective-permute-done((bf16[160,2048]{1,0:T(8,128)(2,1)S(1)}, bf16[160,2048]{1,0:T(8,128)(2,1)S(1)}, u32[]{:S(2)}, u32[]{:S(2)}) %collective-permute-start.30) | collective-permute-done | bytes 655392 | tf_op jit(solution)/shard_map/ppermute | solution.py:94
  323.2 7.5 %collective-permute-done.47 = bf16[128,2048]{1,0:T(8,128)(2,1)S(1)} collective-permute-done((bf16[128,2048]{1,0:T(8,128)(2,1)S(1)}, bf16[128,2048]{1,0:T(8,128)(2,1)S(1)}, u32[]{:S(2)}, u32[]{:S(2)}) %collective-permute-start.47) | collective-permute-done | bytes 524320 | tf_op jit(solution)/shard_map/ppermute | solution.py:94
  332.1 9.8 %collective-permute-done.31 = bf16[160,2048]{1,0:T(8,128)(2,1)S(1)} collective-permute-done((bf16[160,2048]{1,0:T(8,128)(2,1)S(1)}, bf16[160,2048]{1,0:T(8,128)(2,1)S(1)}, u32[]{:S(2)}, u32[]{:S(2)}) %collective-permute-start.31) | collective-permute-done | bytes 655392 | tf_op jit(solution)/shard_map/ppermute | solution.py:94
  345.8 11.1 %collective-permute-done.32 = bf16[160,2048]{1,0:T(8,128)(2,1)S(1)} collective-permute-done((bf16[160,2048]{1,0:T(8,128)(2,1)S(1)}, bf16[160,2048]{1,0:T(8,128)(2,1)S(1)}, u32[]{:S(2)}, u32[]{:S(2)}) %collective-permute-start.32) | collective-permute-done | bytes 655392 | tf_op jit(solution)/shard_map/ppermute | solution.py:94
  362.0 8.1 %collective-permute-done.33 = bf16[160,2048]{1,0:T(8,128)(2,1)S(1)} collective-permute-done((bf16[160,2048]{1,0:T(8,128)(2,1)S(1)}, bf16[160,2048]{1,0:T(8,128)(2,1)S(1)}, u32[]{:S(2)}, u32[]{:S(2)}) %collective-permute-start.33) | collective-permute-done | bytes 655392 | tf_op jit(solution)/shard_map/ppermute | solution.py:94
  (239 shorter events, 121.1 us)
Async XLA Ops:
  7.2 58.6 %reduce-scatter.2.cloned.1.call-start = ((), (), s32[]{:S(2)}) async-start(), calls=%async_computation.1 | async-start | bytes 655360 | tf_op jit(solution)/shard_map/reduce_scatter | solution.py:218
  22.3 42.3 %collective-permute-start.1 = (f32[128,256]{1,0:T(8,128)S(1)}, f32[128,256]{1,0:T(8,128)}, u32[]{:S(2)}, u32[]{:S(2)}) collective-permute-start(f32[128,256]{1,0:T(8,128)S(1)} %constant_dynamic-slice_fusion.3), channel_id=1, source_target_pairs={{0,2},{1,3},{2,0},{3,1},{4,6},{5,7},{6,4},{7,5},{8,10},{9,11},{10,... | collective-permute-start | bytes 393224 | tf_op jit(solution)/shard_map/ppermute | solution.py:159
  124.2 9.2 %collective-permute-start.11 = (bf16[256,128]{1,0:T(8,128)(2,1)S(1)}, bf16[256,128]{1,0:T(8,128)(2,1)S(1)}, u32[]{:S(2)}, u32[]{:S(2)}) collective-permute-start(bf16[256,128]{1,0:T(8,128)(2,1)S(1)} %get-tuple-element.32), channel_id=1, source_target_pairs={{0,8},{8,16},{16,24},{24,28},{28,20},{20,12},{12,4},{4,0},{1,9},{9... | collective-permute-start | bytes 196616 | tf_op jit(solution)/shard_map/ppermute | solution.py:139
  142.1 35.6 %collective-permute-start.41 = (bf16[128,2048]{1,0:T(8,128)(2,1)S(1)}, bf16[128,2048]{1,0:T(8,128)(2,1)S(1)}, u32[]{:S(2)}, u32[]{:S(2)}) collective-permute-start(bf16[128,2048]{1,0:T(8,128)(2,1)S(1)} %fusion.31), channel_id=1, source_target_pairs={{0,8},{8,16},{16,24},{24,28},{28,20},{20,12},{12,4},{4,0},{1,9},{9... | collective-permute-start | bytes 1572872 | tf_op jit(solution)/shard_map/ppermute | solution.py:94
  145.1 10.6 %collective-permute-start.14 = (bf16[256,128]{1,0:T(8,128)(2,1)S(1)}, bf16[256,128]{1,0:T(8,128)(2,1)S(1)}, u32[]{:S(2)}, u32[]{:S(2)}) collective-permute-start(bf16[256,128]{1,0:T(8,128)(2,1)S(1)} %get-tuple-element.24), channel_id=1, source_target_pairs={{0,8},{8,16},{16,24},{24,28},{28,20},{20,12},{12,4},{4,0},{1,9},{9... | collective-permute-start | bytes 196616 | tf_op jit(solution)/shard_map/ppermute | solution.py:139
  148.5 33.6 %collective-permute-start.48 = (bf16[128,2048]{1,0:T(8,128)(2,1)S(1)}, bf16[128,2048]{1,0:T(8,128)(2,1)S(1)}, u32[]{:S(2)}, u32[]{:S(2)}) collective-permute-start(bf16[128,2048]{1,0:T(8,128)(2,1)S(1)} %fusion.32), channel_id=1, source_target_pairs={{0,4},{8,0},{16,8},{24,16},{28,24},{20,28},{12,20},{4,12},{1,5},{9... | collective-permute-start | bytes 1572872 | tf_op jit(solution)/shard_map/ppermute | solution.py:95
  179.8 32.6 %collective-permute-start.42 = (bf16[128,2048]{1,0:T(8,128)(2,1)}, bf16[128,2048]{1,0:T(8,128)(2,1)}, u32[]{:S(2)}, u32[]{:S(2)}) collective-permute-start(bf16[128,2048]{1,0:T(8,128)(2,1)} %fusion.28), channel_id=1, source_target_pairs={{0,8},{8,16},{16,24},{24,28},{28,20},{20,12},{12,4},{4,0},{1,9},{9... | collective-permute-start | bytes 1572872 | tf_op jit(solution)/shard_map/ppermute | solution.py:94
  184.2 30.3 %collective-permute-start.49 = (bf16[128,2048]{1,0:T(8,128)(2,1)}, bf16[128,2048]{1,0:T(8,128)(2,1)}, u32[]{:S(2)}, u32[]{:S(2)}) collective-permute-start(bf16[128,2048]{1,0:T(8,128)(2,1)} %fusion.22), channel_id=1, source_target_pairs={{0,4},{8,0},{16,8},{24,16},{28,24},{20,28},{12,20},{4,12},{1,5},{9... | collective-permute-start | bytes 1572872 | tf_op jit(solution)/shard_map/ppermute | solution.py:95
  211.6 31.9 %collective-permute-start.27 = (bf16[160,2048]{1,0:T(8,128)(2,1)S(1)}, bf16[160,2048]{1,0:T(8,128)(2,1)S(1)}, u32[]{:S(2)}, u32[]{:S(2)}) collective-permute-start(bf16[160,2048]{1,0:T(8,128)(2,1)S(1)} %fusion.29), channel_id=1, source_target_pairs={{0,8},{8,16},{16,24},{24,28},{28,20},{20,12},{12,4},{4,0},{1,9},{9... | collective-permute-start | bytes 1966088 | tf_op jit(solution)/shard_map/ppermute | solution.py:94
  214.0 24.6 %collective-permute-start.43 = (bf16[128,2048]{1,0:T(8,128)(2,1)S(1)}, bf16[128,2048]{1,0:T(8,128)(2,1)S(1)}, u32[]{:S(2)}, u32[]{:S(2)}) collective-permute-start(bf16[128,2048]{1,0:T(8,128)(2,1)S(1)} %fusion.27), channel_id=1, source_target_pairs={{0,8},{8,16},{16,24},{24,28},{28,20},{20,12},{12,4},{4,0},{1,9},{9... | collective-permute-start | bytes 1572872 | tf_op jit(solution)/shard_map/ppermute | solution.py:94
  216.0 24.8 %collective-permute-start.50 = (bf16[128,2048]{1,0:T(8,128)(2,1)S(1)}, bf16[128,2048]{1,0:T(8,128)(2,1)S(1)}, u32[]{:S(2)}, u32[]{:S(2)}) collective-permute-start(bf16[128,2048]{1,0:T(8,128)(2,1)S(1)} %fusion.21), channel_id=1, source_target_pairs={{0,4},{8,0},{16,8},{24,16},{28,24},{20,28},{12,20},{4,12},{1,5},{9... | collective-permute-start | bytes 1572872 | tf_op jit(solution)/shard_map/ppermute | solution.py:95
  217.7 27.2 %collective-permute-start.34 = (bf16[160,2048]{1,0:T(8,128)(2,1)S(1)}, bf16[160,2048]{1,0:T(8,128)(2,1)S(1)}, u32[]{:S(2)}, u32[]{:S(2)}) collective-permute-start(bf16[160,2048]{1,0:T(8,128)(2,1)S(1)} %fusion.30), channel_id=1, source_target_pairs={{0,4},{8,0},{16,8},{24,16},{28,24},{20,28},{12,20},{4,12},{1,5},{9... | collective-permute-start | bytes 1966088 | tf_op jit(solution)/shard_map/ppermute | solution.py:95
  240.0 14.9 %collective-permute-start.44 = (bf16[128,2048]{1,0:T(8,128)(2,1)S(1)}, bf16[128,2048]{1,0:T(8,128)(2,1)S(1)}, u32[]{:S(2)}, u32[]{:S(2)}) collective-permute-start(bf16[128,2048]{1,0:T(8,128)(2,1)S(1)} %fusion.26), channel_id=1, source_target_pairs={{0,8},{8,16},{16,24},{24,28},{28,20},{20,12},{12,4},{4,0},{1,9},{9... | collective-permute-start | bytes 1572872 | tf_op jit(solution)/shard_map/ppermute | solution.py:94
  242.6 14.9 %collective-permute-start.51 = (bf16[128,2048]{1,0:T(8,128)(2,1)S(1)}, bf16[128,2048]{1,0:T(8,128)(2,1)S(1)}, u32[]{:S(2)}, u32[]{:S(2)}) collective-permute-start(bf16[128,2048]{1,0:T(8,128)(2,1)S(1)} %fusion.20), channel_id=1, source_target_pairs={{0,4},{8,0},{16,8},{24,16},{28,24},{20,28},{12,20},{4,12},{1,5},{9... | collective-permute-start | bytes 1572872 | tf_op jit(solution)/shard_map/ppermute | solution.py:95
  243.7 25.2 %collective-permute-start.28 = (bf16[160,2048]{1,0:T(8,128)(2,1)S(1)}, bf16[160,2048]{1,0:T(8,128)(2,1)S(1)}, u32[]{:S(2)}, u32[]{:S(2)}) collective-permute-start(bf16[160,2048]{1,0:T(8,128)(2,1)S(1)} %fusion.15), channel_id=1, source_target_pairs={{0,8},{8,16},{16,24},{24,28},{28,20},{20,12},{12,4},{4,0},{1,9},{9... | collective-permute-start | bytes 1966088 | tf_op jit(solution)/shard_map/ppermute | solution.py:94
  245.1 26.5 %collective-permute-start.35 = (bf16[160,2048]{1,0:T(8,128)(2,1)S(1)}, bf16[160,2048]{1,0:T(8,128)(2,1)S(1)}, u32[]{:S(2)}, u32[]{:S(2)}) collective-permute-start(bf16[160,2048]{1,0:T(8,128)(2,1)S(1)} %fusion.9), channel_id=1, source_target_pairs={{0,4},{8,0},{16,8},{24,16},{28,24},{20,28},{12,20},{4,12},{1,5},{9... | collective-permute-start | bytes 1966088 | tf_op jit(solution)/shard_map/ppermute | solution.py:95
  256.2 23.9 %collective-permute-start.45 = (bf16[128,2048]{1,0:T(8,128)(2,1)S(1)}, bf16[128,2048]{1,0:T(8,128)(2,1)S(1)}, u32[]{:S(2)}, u32[]{:S(2)}) collective-permute-start(bf16[128,2048]{1,0:T(8,128)(2,1)S(1)} %fusion.25), channel_id=1, source_target_pairs={{0,8},{8,16},{16,24},{24,28},{28,20},{20,12},{12,4},{4,0},{1,9},{9... | collective-permute-start | bytes 1572872 | tf_op jit(solution)/shard_map/ppermute | solution.py:94
  257.6 25.2 %collective-permute-start.52 = (bf16[128,2048]{1,0:T(8,128)(2,1)S(1)}, bf16[128,2048]{1,0:T(8,128)(2,1)S(1)}, u32[]{:S(2)}, u32[]{:S(2)}) collective-permute-start(bf16[128,2048]{1,0:T(8,128)(2,1)S(1)} %fusion.19), channel_id=1, source_target_pairs={{0,4},{8,0},{16,8},{24,16},{28,24},{20,28},{12,20},{4,12},{1,5},{9... | collective-permute-start | bytes 1572872 | tf_op jit(solution)/shard_map/ppermute | solution.py:95
  269.1 25.1 %collective-permute-start.29 = (bf16[160,2048]{1,0:T(8,128)(2,1)S(1)}, bf16[160,2048]{1,0:T(8,128)(2,1)S(1)}, u32[]{:S(2)}, u32[]{:S(2)}) collective-permute-start(bf16[160,2048]{1,0:T(8,128)(2,1)S(1)} %fusion.14), channel_id=1, source_target_pairs={{0,8},{8,16},{16,24},{24,28},{28,20},{20,12},{12,4},{4,0},{1,9},{9... | collective-permute-start | bytes 1966088 | tf_op jit(solution)/shard_map/ppermute | solution.py:94
  271.7 25.1 %collective-permute-start.36 = (bf16[160,2048]{1,0:T(8,128)(2,1)S(1)}, bf16[160,2048]{1,0:T(8,128)(2,1)S(1)}, u32[]{:S(2)}, u32[]{:S(2)}) collective-permute-start(bf16[160,2048]{1,0:T(8,128)(2,1)S(1)} %fusion.8), channel_id=1, source_target_pairs={{0,4},{8,0},{16,8},{24,16},{28,24},{20,28},{12,20},{4,12},{1,5},{9... | collective-permute-start | bytes 1966088 | tf_op jit(solution)/shard_map/ppermute | solution.py:95
  281.5 23.9 %collective-permute-start.46 = (bf16[128,2048]{1,0:T(8,128)(2,1)S(1)}, bf16[128,2048]{1,0:T(8,128)(2,1)S(1)}, u32[]{:S(2)}, u32[]{:S(2)}) collective-permute-start(bf16[128,2048]{1,0:T(8,128)(2,1)S(1)} %fusion.24), channel_id=1, source_target_pairs={{0,8},{8,16},{16,24},{24,28},{28,20},{20,12},{12,4},{4,0},{1,9},{9... | collective-permute-start | bytes 1572872 | tf_op jit(solution)/shard_map/ppermute | solution.py:94
  282.9 25.2 %collective-permute-start.53 = (bf16[128,2048]{1,0:T(8,128)(2,1)S(1)}, bf16[128,2048]{1,0:T(8,128)(2,1)S(1)}, u32[]{:S(2)}, u32[]{:S(2)}) collective-permute-start(bf16[128,2048]{1,0:T(8,128)(2,1)S(1)} %fusion.18), channel_id=1, source_target_pairs={{0,4},{8,0},{16,8},{24,16},{28,24},{20,28},{12,20},{4,12},{1,5},{9... | collective-permute-start | bytes 1572872 | tf_op jit(solution)/shard_map/ppermute | solution.py:95
  294.4 25.1 %collective-permute-start.30 = (bf16[160,2048]{1,0:T(8,128)(2,1)S(1)}, bf16[160,2048]{1,0:T(8,128)(2,1)S(1)}, u32[]{:S(2)}, u32[]{:S(2)}) collective-permute-start(bf16[160,2048]{1,0:T(8,128)(2,1)S(1)} %fusion.13), channel_id=1, source_target_pairs={{0,8},{8,16},{16,24},{24,28},{28,20},{20,12},{12,4},{4,0},{1,9},{9... | collective-permute-start | bytes 1966088 | tf_op jit(solution)/shard_map/ppermute | solution.py:94
  297.0 25.1 %collective-permute-start.37 = (bf16[160,2048]{1,0:T(8,128)(2,1)S(1)}, bf16[160,2048]{1,0:T(8,128)(2,1)S(1)}, u32[]{:S(2)}, u32[]{:S(2)}) collective-permute-start(bf16[160,2048]{1,0:T(8,128)(2,1)S(1)} %fusion.7), channel_id=1, source_target_pairs={{0,4},{8,0},{16,8},{24,16},{28,24},{20,28},{12,20},{4,12},{1,5},{9... | collective-permute-start | bytes 1966088 | tf_op jit(solution)/shard_map/ppermute | solution.py:95
  306.8 23.9 %collective-permute-start.47 = (bf16[128,2048]{1,0:T(8,128)(2,1)S(1)}, bf16[128,2048]{1,0:T(8,128)(2,1)S(1)}, u32[]{:S(2)}, u32[]{:S(2)}) collective-permute-start(bf16[128,2048]{1,0:T(8,128)(2,1)S(1)} %fusion.23), channel_id=1, source_target_pairs={{0,8},{8,16},{16,24},{24,28},{28,20},{20,12},{12,4},{4,0},{1,9},{9... | collective-permute-start | bytes 1572872 | tf_op jit(solution)/shard_map/ppermute | solution.py:94
  308.2 37.5 %collective-permute-start.54 = (bf16[128,2048]{1,0:T(8,128)(2,1)S(1)}, bf16[128,2048]{1,0:T(8,128)(2,1)S(1)}, u32[]{:S(2)}, u32[]{:S(2)}) collective-permute-start(bf16[128,2048]{1,0:T(8,128)(2,1)S(1)} %fusion.17), channel_id=1, source_target_pairs={{0,4},{8,0},{16,8},{24,16},{28,24},{20,28},{12,20},{4,12},{1,5},{9... | collective-permute-start | bytes 1572872 | tf_op jit(solution)/shard_map/ppermute | solution.py:95
  319.7 22.3 %collective-permute-start.31 = (bf16[160,2048]{1,0:T(8,128)(2,1)S(1)}, bf16[160,2048]{1,0:T(8,128)(2,1)S(1)}, u32[]{:S(2)}, u32[]{:S(2)}) collective-permute-start(bf16[160,2048]{1,0:T(8,128)(2,1)S(1)} %fusion.12), channel_id=1, source_target_pairs={{0,8},{8,16},{16,24},{24,28},{28,20},{20,12},{12,4},{4,0},{1,9},{9... | collective-permute-start | bytes 1966088 | tf_op jit(solution)/shard_map/ppermute | solution.py:94
  322.3 22.1 %collective-permute-start.38 = (bf16[160,2048]{1,0:T(8,128)(2,1)S(1)}, bf16[160,2048]{1,0:T(8,128)(2,1)S(1)}, u32[]{:S(2)}, u32[]{:S(2)}) collective-permute-start(bf16[160,2048]{1,0:T(8,128)(2,1)S(1)} %fusion.6), channel_id=1, source_target_pairs={{0,4},{8,0},{16,8},{24,16},{28,24},{20,28},{12,20},{4,12},{1,5},{9... | collective-permute-start | bytes 1966088 | tf_op jit(solution)/shard_map/ppermute | solution.py:95
  342.1 14.7 %collective-permute-start.32 = (bf16[160,2048]{1,0:T(8,128)(2,1)S(1)}, bf16[160,2048]{1,0:T(8,128)(2,1)S(1)}, u32[]{:S(2)}, u32[]{:S(2)}) collective-permute-start(bf16[160,2048]{1,0:T(8,128)(2,1)S(1)} %fusion.11), channel_id=1, source_target_pairs={{0,8},{8,16},{16,24},{24,28},{28,20},{20,12},{12,4},{4,0},{1,9},{9... | collective-permute-start | bytes 1966088 | tf_op jit(solution)/shard_map/ppermute | solution.py:94
  344.5 14.7 %collective-permute-start.39 = (bf16[160,2048]{1,0:T(8,128)(2,1)S(1)}, bf16[160,2048]{1,0:T(8,128)(2,1)S(1)}, u32[]{:S(2)}, u32[]{:S(2)}) collective-permute-start(bf16[160,2048]{1,0:T(8,128)(2,1)S(1)} %fusion.5), channel_id=1, source_target_pairs={{0,4},{8,0},{16,8},{24,16},{28,24},{20,28},{12,20},{4,12},{1,5},{9... | collective-permute-start | bytes 1966088 | tf_op jit(solution)/shard_map/ppermute | solution.py:95
  357.0 13.1 %collective-permute-start.33 = (bf16[160,2048]{1,0:T(8,128)(2,1)S(1)}, bf16[160,2048]{1,0:T(8,128)(2,1)S(1)}, u32[]{:S(2)}, u32[]{:S(2)}) collective-permute-start(bf16[160,2048]{1,0:T(8,128)(2,1)S(1)} %fusion.10), channel_id=1, source_target_pairs={{0,8},{8,16},{16,24},{24,28},{28,20},{20,12},{12,4},{4,0},{1,9},{9... | collective-permute-start | bytes 1966088 | tf_op jit(solution)/shard_map/ppermute | solution.py:94
  359.4 12.8 %collective-permute-start.40 = (bf16[160,2048]{1,0:T(8,128)(2,1)S(1)}, bf16[160,2048]{1,0:T(8,128)(2,1)S(1)}, u32[]{:S(2)}, u32[]{:S(2)}) collective-permute-start(bf16[160,2048]{1,0:T(8,128)(2,1)S(1)} %fusion.4), channel_id=1, source_target_pairs={{0,4},{8,0},{16,8},{24,16},{28,24},{20,28},{12,20},{4,12},{1,5},{9... | collective-permute-start | bytes 1966088 | tf_op jit(solution)/shard_map/ppermute | solution.py:95
  (46 other events, 437.0 us)
Sparse Core Ops, SparseCore 0:
  19.7 24.0 reduce-scatter.1

commit v6 on v5

--- a/solution.py
+++ b/solution.py
@@ -163,6 +163,23 @@
     return own_head, jnp.concatenate([first, second], axis=0)
 
 
+def tp_scatter(partial, rows_mine, axis):
+    rank = lax.axis_index(axis)
+    far = [(i, i ^ 2) for i in range(4)]
+    near = [(i, i ^ 1) for i in range(4)]
+    pair_rows = 2 * rows_mine
+    chip = rank // 2
+    kept = lax.dynamic_slice_in_dim(partial, chip * pair_rows, pair_rows, 0)
+    sent = lax.dynamic_slice_in_dim(partial, (1 - chip) * pair_rows, pair_rows, 0)
+    kept = kept.astype(jnp.float32) + lax.ppermute(
+        sent.astype(jnp.bfloat16), axis, far
+    ).astype(jnp.float32)
+    core = rank % 2
+    mine = lax.dynamic_slice_in_dim(kept, core * rows_mine, rows_mine, 0)
+    other = lax.dynamic_slice_in_dim(kept, (1 - core) * rows_mine, rows_mine, 0)
+    return mine + lax.ppermute(other.astype(jnp.bfloat16), axis, near).astype(jnp.float32)
+
+
 def butterfly_sum(value, axis):
     count = lax.axis_size(axis)
     stride = 1
@@ -215,7 +232,10 @@
     packed = jnp.concatenate([keys, values], axis=1)
     packed = jnp.concatenate([packed, info], axis=0)
     gathered = ring_gather(packed, ring, "ctx")
-    grad_rows = lax.psum_scatter(grad_part, "tp", scatter_dimension=0, tiled=True)
+    if tp_size == 4 and rows_ctx % (2 * tp_size) == 0:
+        grad_rows = tp_scatter(grad_part, rows_mine, "tp").astype(jnp.bfloat16)
+    else:
+        grad_rows = lax.psum_scatter(grad_part, "tp", scatter_dimension=0, tiled=True)
     keys_all = gathered[:, :rows_ctx, :head_dim].reshape(total_rows, head_dim)
     values_all = gathered[:, :rows_ctx, head_dim:].reshape(total_rows, head_dim)
     info_all = gathered[:, rows_ctx:, :].reshape(ctx_size, info_rows * pair_width).astype(

time: 383 us -> 374 us (0.977)
  between operations: 50.8 us -> 36.8 us
  waiting for transfers between devices: 160 us -> 168 us
    ppermute x1, waiting for transfers between devices: 0.01 us -> 4.25 us  [tp_project(): tail_half = tail_half + lax.ppermute(tail_half, axis, far)]
  transfers between devices with their start and end apart: 56 -> 57, of which waited for: 33 -> 35; matrix products, arithmetic and copies ran while one was open for 17% -> 18% of each run, Pallas kernels for 0% -> 0%
where the time goes in v6:
time: 374 us; the launch traced here: 372 us
  waiting for transfers between devices  168 us (45%)
  starting transfers between devices  52.4 us (14%)
  matrix products  38 us (10%)
  between operations  36.8 us (10%)
  other arithmetic  34.4 us (9%)
  local copies, waits for them, and re-layouts  29.5 us (8%)
  blocking collectives  13.4 us (4%)
    ppermute x14, waiting for transfers between devices, ring_scatter(): got_left = lax.ppermute(send_left.astype(jnp.bfloat16), axis, forward)  112 us
    dot_general x4, matrix products, against(): lax.dot_general(left, right, (((1,), (1,)), ((), ())), preferred_element_...  14.9 us
    slice x2, local copies, waits for them, and re-layouts, ring_scatter(): left = blocks[:, :, :half]  14.4 us
    ppermute x14, starting transfers between devices, ring_scatter(): got_left = lax.ppermute(send_left.astype(jnp.bfloat16), axis, forward)  14 us
    ppermute x7, waiting for transfers between devices, ring_scatter_relative(): got_left = lax.ppermute(send_left.astype(jnp.bfloat16), axis, forward)  13.1 us
    ppermute x14, starting transfers between devices, ring_scatter(): got_right = lax.ppermute(send_right.astype(jnp.bfloat16), axis, backward)  12 us
    ppermute x14, waiting for transfers between devices, ring_scatter(): got_right = lax.ppermute(send_right.astype(jnp.bfloat16), axis, backward)  10.7 us
    convert_element_type x12, other arithmetic, ring_scatter(): got_left = lax.ppermute(send_left.astype(jnp.bfloat16), axis, forward)  10.1 us
  transfers between devices with their start and end apart: 57, of which 35 were waited for; matrix products, arithmetic and copies ran while one was open for 18% of the time, Pallas kernels for 0%

profile of v6, /device:TPU:0, one launch (start us, length us, event | category | flops | bytes accessed | tf_op | source)
XLA Modules:
  0.0 372.4 jit_solution(6639238716454775481)
XLA Ops:
  2.2 6.9 %fusion.89 = f32[256,1280]{1,0:T(8,128)S(1)} fusion(bf16[256,4096]{1,0:T(8,128)(2,1)S(1)} %copy-done, bf16[1280,4096]{1,0:T(8,128)(2,1)} %param.13), kind=kOutput, calls=%fused_computation.206 | convolution fusion | flops 2684354560 | bytes 13893632 | tf_op jit(solution)/shard_map/dot_general | solution.py:35
  9.6 6.4 %convolution_convert_fusion.2 = bf16[256,1024]{1,0:T(8,128)(2,1)S(1)} fusion(bf16[256,4096]{1,0:T(8,128)(2,1)} %param.15, bf16[1024,4096]{1,0:T(8,128)(2,1)} %param.14), kind=kOutput, calls=%fused_computation.42 | convolution fusion | flops 2147745792 | bytes 11010048 | tf_op jit(solution)/shard_map/dot_general | solution.py:35
  17.6 2.6 collective-permute-start.11
  59.9 4.2 %collective-permute-done.1 = f32[128,256]{1,0:T(8,128)S(1)} collective-permute-done((f32[128,256]{1,0:T(8,128)S(1)}, f32[128,256]{1,0:T(8,128)S(1)}, u32[]{:S(2)}, u32[]{:S(2)}) %collective-permute-start.1) | collective-permute-done | bytes 131104 | tf_op jit(solution)/shard_map/ppermute | solution.py:159
  68.4 4.8 %collective-permute-done.10 = f32[64,1024]{1,0:T(8,128)S(1)} collective-permute-done((f32[64,1024]{1,0:T(8,128)S(1)}, f32[64,1024]{1,0:T(8,128)S(1)}, u32[]{:S(2)}, u32[]{:S(2)}) %collective-permute-start.10) | collective-permute-done | bytes 262176 | tf_op jit(solution)/shard_map/ppermute | solution.py:157
  75.8 3.1 collective-permute-done.4
  81.0 4.5 %collective-permute-done.8 = bf16[259,256]{1,0:T(8,128)(2,1)S(1)} collective-permute-done((bf16[259,256]{1,0:T(8,128)(2,1)S(1)}, bf16[259,256]{1,0:T(8,128)(2,1)S(1)}, u32[]{:S(2)}, u32[]{:S(2)}) %collective-permute-start.8) | collective-permute-done | bytes 132640 | tf_op jit(solution)/shard_map/ppermute | solution.py:119
  86.0 4.5 %collective-permute-done.9 = bf16[259,256]{1,0:T(8,128)(2,1)S(1)} collective-permute-done((bf16[259,256]{1,0:T(8,128)(2,1)S(1)}, bf16[259,256]{1,0:T(8,128)(2,1)S(1)}, u32[]{:S(2)}, u32[]{:S(2)}) %collective-permute-start.9) | collective-permute-done | bytes 132640 | tf_op jit(solution)/shard_map/ppermute | solution.py:119
  94.9 6.5 %all_gather.6 = bf16[256,1024]{1,0:T(8,128)(2,1)S(1)} all-gather(bf16[64,1024]{1,0:T(8,128)(2,1)S(1)} %bitcast.345), channel_id=1, replica_groups=mesh['ctx'=8,'tp'=4] {'tp'}, dimensions={0}, use_global_device_ids=true | all-gather | bytes 655360 | tf_op jit(solution)/shard_map/all_gather | solution.py:272
  101.4 2.4 fusion.92
  103.8 6.3 %fusion.85 = (f32[8,128,2048]{2,1,0:T(8,128)}, f32[8,128,2048]{2,1,0:T(8,128)}) fusion(f32[8,128,4096]{2,1,0:T(8,128)S(1)} %bitcast.322), kind=kLoop, calls=%fused_computation.202 | loop fusion | bytes 33554432 | tf_op jit(solution)/shard_map/slice | solution.py:83
  110.1 3.2 fusion.1
  117.4 2.9 copy.27
  124.0 7.0 %convolution_convert_fusion = bf16[256,4096]{1,0:T(8,128)(2,1)} fusion(bf16[256,1024]{1,0:T(8,128)(2,1)S(1)} %all_gather.6, bf16[1024,4096]{1,0:T(8,128)(2,1)} %param.14), kind=kOutput, calls=%fused_computation.3 | convolution fusion | flops 2148532224 | bytes 11010048 | tf_op jit(solution)/shard_map/dot_general | solution.py:273
  146.0 7.2 %collective-permute-done.16 = bf16[256,128]{1,0:T(8,128)(2,1)S(1)} collective-permute-done((bf16[256,128]{1,0:T(8,128)(2,1)S(1)}, bf16[256,128]{1,0:T(8,128)(2,1)S(1)}, u32[]{:S(2)}, u32[]{:S(2)}) %collective-permute-start.16) | collective-permute-done | bytes 65568 | tf_op jit(solution)/shard_map/ppermute | solution.py:139
  161.4 2.4 collective-permute-done.18
  167.6 6.8 %all_gather.7 = bf16[256,1024]{1,0:T(8,128)(2,1)S(1)} all-gather(bf16[64,1024]{1,0:T(8,128)(2,1)S(1)} %copy_bitcast_fusion.1), channel_id=1, replica_groups=mesh['ctx'=8,'tp'=4] {'tp'}, dimensions={0}, use_global_device_ids=true | all-gather | bytes 655360 | tf_op jit(solution)/shard_map/all_gather | solution.py:294
  182.1 5.0 %collective-permute-done.28 = f32[256,256]{1,0:T(8,128)S(1)} collective-permute-done((f32[256,256]{1,0:T(8,128)S(1)}, f32[256,256]{1,0:T(8,128)S(1)}, u32[]{:S(2)}, u32[]{:S(2)}) %collective-permute-start.28) | collective-permute-done | bytes 262176 | tf_op jit(solution)/shard_map/ppermute | solution.py:188
  188.0 2.9 fusion.91
  190.9 8.0 %fusion.84 = (f32[8,160,2048]{2,1,0:T(8,128)}, f32[8,160,2048]{2,1,0:T(8,128)}) fusion(f32[8,160,4096]{2,1,0:T(8,128)S(1)} %bitcast.321), kind=kLoop, calls=%fused_computation.201 | loop fusion | bytes 41943040 | tf_op jit(solution)/shard_map/slice | solution.py:83
  199.0 8.2 %convolution_convert_fusion.1 = bf16[256,4096]{1,0:T(8,128)(2,1)} fusion(bf16[256,1280]{1,0:T(8,128)(2,1)S(1)} %concatenate.49, bf16[1280,4096]{1,0:T(8,128)(2,1)} %param.13), kind=kOutput, calls=%fused_computation.4 | convolution fusion | flops 2685403136 | bytes 13238272 | tf_op jit(solution)/shard_map/dot_general | solution.py:299
  216.9 19.6 %collective-permute-done.45 = bf16[128,2048]{1,0:T(8,128)(2,1)S(1)} collective-permute-done((bf16[128,2048]{1,0:T(8,128)(2,1)S(1)}, bf16[128,2048]{1,0:T(8,128)(2,1)S(1)}, u32[]{:S(2)}, u32[]{:S(2)}) %collective-permute-start.45) | collective-permute-done | bytes 524320 | tf_op jit(solution)/shard_map/ppermute | solution.py:94
  243.8 8.9 %collective-permute-done.46 = bf16[128,2048]{1,0:T(8,128)(2,1)S(1)} collective-permute-done((bf16[128,2048]{1,0:T(8,128)(2,1)S(1)}, bf16[128,2048]{1,0:T(8,128)(2,1)S(1)}, u32[]{:S(2)}, u32[]{:S(2)}) %collective-permute-start.46) | collective-permute-done | bytes 524320 | tf_op jit(solution)/shard_map/ppermute | solution.py:94
  256.4 10.4 %collective-permute-done.30 = bf16[160,2048]{1,0:T(8,128)(2,1)S(1)} collective-permute-done((bf16[160,2048]{1,0:T(8,128)(2,1)S(1)}, bf16[160,2048]{1,0:T(8,128)(2,1)S(1)}, u32[]{:S(2)}, u32[]{:S(2)}) %collective-permute-start.30) | collective-permute-done | bytes 655392 | tf_op jit(solution)/shard_map/ppermute | solution.py:94
  270.4 7.6 %collective-permute-done.47 = bf16[128,2048]{1,0:T(8,128)(2,1)S(1)} collective-permute-done((bf16[128,2048]{1,0:T(8,128)(2,1)S(1)}, bf16[128,2048]{1,0:T(8,128)(2,1)S(1)}, u32[]{:S(2)}, u32[]{:S(2)}) %collective-permute-start.47) | collective-permute-done | bytes 524320 | tf_op jit(solution)/shard_map/ppermute | solution.py:94
  281.9 10.2 %collective-permute-done.31 = bf16[160,2048]{1,0:T(8,128)(2,1)S(1)} collective-permute-done((bf16[160,2048]{1,0:T(8,128)(2,1)S(1)}, bf16[160,2048]{1,0:T(8,128)(2,1)S(1)}, u32[]{:S(2)}, u32[]{:S(2)}) %collective-permute-start.31) | collective-permute-done | bytes 655392 | tf_op jit(solution)/shard_map/ppermute | solution.py:94
  295.7 7.6 %collective-permute-done.48 = bf16[128,2048]{1,0:T(8,128)(2,1)S(1)} collective-permute-done((bf16[128,2048]{1,0:T(8,128)(2,1)S(1)}, bf16[128,2048]{1,0:T(8,128)(2,1)S(1)}, u32[]{:S(2)}, u32[]{:S(2)}) %collective-permute-start.48) | collective-permute-done | bytes 524320 | tf_op jit(solution)/shard_map/ppermute | solution.py:94
  306.9 10.4 %collective-permute-done.32 = bf16[160,2048]{1,0:T(8,128)(2,1)S(1)} collective-permute-done((bf16[160,2048]{1,0:T(8,128)(2,1)S(1)}, bf16[160,2048]{1,0:T(8,128)(2,1)S(1)}, u32[]{:S(2)}, u32[]{:S(2)}) %collective-permute-start.32) | collective-permute-done | bytes 655392 | tf_op jit(solution)/shard_map/ppermute | solution.py:94
  321.0 7.6 %collective-permute-done.49 = bf16[128,2048]{1,0:T(8,128)(2,1)S(1)} collective-permute-done((bf16[128,2048]{1,0:T(8,128)(2,1)S(1)}, bf16[128,2048]{1,0:T(8,128)(2,1)S(1)}, u32[]{:S(2)}, u32[]{:S(2)}) %collective-permute-start.49) | collective-permute-done | bytes 524320 | tf_op jit(solution)/shard_map/ppermute | solution.py:94
  329.9 9.9 %collective-permute-done.33 = bf16[160,2048]{1,0:T(8,128)(2,1)S(1)} collective-permute-done((bf16[160,2048]{1,0:T(8,128)(2,1)S(1)}, bf16[160,2048]{1,0:T(8,128)(2,1)S(1)}, u32[]{:S(2)}, u32[]{:S(2)}) %collective-permute-start.33) | collective-permute-done | bytes 655392 | tf_op jit(solution)/shard_map/ppermute | solution.py:94
  343.4 11.2 %collective-permute-done.34 = bf16[160,2048]{1,0:T(8,128)(2,1)S(1)} collective-permute-done((bf16[160,2048]{1,0:T(8,128)(2,1)S(1)}, bf16[160,2048]{1,0:T(8,128)(2,1)S(1)}, u32[]{:S(2)}, u32[]{:S(2)}) %collective-permute-start.34) | collective-permute-done | bytes 655392 | tf_op jit(solution)/shard_map/ppermute | solution.py:94
  359.0 8.9 %collective-permute-done.35 = bf16[160,2048]{1,0:T(8,128)(2,1)S(1)} collective-permute-done((bf16[160,2048]{1,0:T(8,128)(2,1)S(1)}, bf16[160,2048]{1,0:T(8,128)(2,1)S(1)}, u32[]{:S(2)}, u32[]{:S(2)}) %collective-permute-start.35) | collective-permute-done | bytes 655392 | tf_op jit(solution)/shard_map/ppermute | solution.py:94
  (237 shorter events, 117.4 us)
Async XLA Ops:
  9.1 47.8 %collective-permute-start = (f32[256,1280]{1,0:T(8,128)S(1)}, f32[256,1280]{1,0:T(8,128)}, u32[]{:S(2)}, u32[]{:S(2)}) collective-permute-start(f32[256,1280]{1,0:T(8,128)S(1)} %fusion.89), channel_id=1, source_target_pairs={{0,1},{1,0},{2,3},{3,2},{4,5},{5,4},{6,7},{7,6},{8,9},{9,8},{10,11... | collective-permute-start | bytes 3932168 | tf_op jit(solution)/shard_map/ppermute | solution.py:151
  17.6 41.0 %collective-permute-start.11 = (bf16[128,1024]{1,0:T(8,128)(2,1)}, bf16[128,1024]{1,0:T(8,128)(2,1)}, u32[]{:S(2)}, u32[]{:S(2)}) collective-permute-start(bf16[128,1024]{1,0:T(8,128)(2,1)} %constant_dynamic-slice_fusion), channel_id=1, source_target_pairs={{0,2},{1,3},{2,0},{3,1},{4,6},{5,7},{6,4},{7,5},{8,10},{9,11},{10,... | collective-permute-start | bytes 786440 | tf_op jit(solution)/shard_map/ppermute | solution.py:174
  139.6 35.3 %collective-permute-start.43 = (bf16[128,2048]{1,0:T(8,128)(2,1)S(1)}, bf16[128,2048]{1,0:T(8,128)(2,1)S(1)}, u32[]{:S(2)}, u32[]{:S(2)}) collective-permute-start(bf16[128,2048]{1,0:T(8,128)(2,1)S(1)} %fusion.31), channel_id=1, source_target_pairs={{0,8},{8,16},{16,24},{24,28},{28,20},{20,12},{12,4},{4,0},{1,9},{9... | collective-permute-start | bytes 1572872 | tf_op jit(solution)/shard_map/ppermute | solution.py:94
  142.2 11.0 %collective-permute-start.16 = (bf16[256,128]{1,0:T(8,128)(2,1)S(1)}, bf16[256,128]{1,0:T(8,128)(2,1)S(1)}, u32[]{:S(2)}, u32[]{:S(2)}) collective-permute-start(bf16[256,128]{1,0:T(8,128)(2,1)S(1)} %get-tuple-element.24), channel_id=1, source_target_pairs={{0,8},{8,16},{16,24},{24,28},{28,20},{20,12},{12,4},{4,0},{1,9},{9... | collective-permute-start | bytes 196616 | tf_op jit(solution)/shard_map/ppermute | solution.py:139
  143.8 9.4 %collective-permute-start.23 = (bf16[256,128]{1,0:T(8,128)(2,1)S(1)}, bf16[256,128]{1,0:T(8,128)(2,1)S(1)}, u32[]{:S(2)}, u32[]{:S(2)}) collective-permute-start(bf16[256,128]{1,0:T(8,128)(2,1)S(1)} %get-tuple-element.25), channel_id=1, source_target_pairs={{0,4},{8,0},{16,8},{24,16},{28,24},{20,28},{12,20},{4,12},{1,5},{9... | collective-permute-start | bytes 196616 | tf_op jit(solution)/shard_map/ppermute | solution.py:140
  145.6 34.3 %collective-permute-start.50 = (bf16[128,2048]{1,0:T(8,128)(2,1)S(1)}, bf16[128,2048]{1,0:T(8,128)(2,1)S(1)}, u32[]{:S(2)}, u32[]{:S(2)}) collective-permute-start(bf16[128,2048]{1,0:T(8,128)(2,1)S(1)} %fusion.32), channel_id=1, source_target_pairs={{0,4},{8,0},{16,8},{24,16},{28,24},{20,28},{12,20},{4,12},{1,5},{9... | collective-permute-start | bytes 1572872 | tf_op jit(solution)/shard_map/ppermute | solution.py:95
  177.0 33.3 %collective-permute-start.44 = (bf16[128,2048]{1,0:T(8,128)(2,1)}, bf16[128,2048]{1,0:T(8,128)(2,1)}, u32[]{:S(2)}, u32[]{:S(2)}) collective-permute-start(bf16[128,2048]{1,0:T(8,128)(2,1)} %fusion.28), channel_id=1, source_target_pairs={{0,8},{8,16},{16,24},{24,28},{28,20},{20,12},{12,4},{4,0},{1,9},{9... | collective-permute-start | bytes 1572872 | tf_op jit(solution)/shard_map/ppermute | solution.py:94
  181.9 30.5 %collective-permute-start.51 = (bf16[128,2048]{1,0:T(8,128)(2,1)}, bf16[128,2048]{1,0:T(8,128)(2,1)}, u32[]{:S(2)}, u32[]{:S(2)}) collective-permute-start(bf16[128,2048]{1,0:T(8,128)(2,1)} %fusion.22), channel_id=1, source_target_pairs={{0,4},{8,0},{16,8},{24,16},{28,24},{20,28},{12,20},{4,12},{1,5},{9... | collective-permute-start | bytes 1572872 | tf_op jit(solution)/shard_map/ppermute | solution.py:95
  209.4 31.9 %collective-permute-start.29 = (bf16[160,2048]{1,0:T(8,128)(2,1)S(1)}, bf16[160,2048]{1,0:T(8,128)(2,1)S(1)}, u32[]{:S(2)}, u32[]{:S(2)}) collective-permute-start(bf16[160,2048]{1,0:T(8,128)(2,1)S(1)} %fusion.29), channel_id=1, source_target_pairs={{0,8},{8,16},{16,24},{24,28},{28,20},{20,12},{12,4},{4,0},{1,9},{9... | collective-permute-start | bytes 1966088 | tf_op jit(solution)/shard_map/ppermute | solution.py:94
  211.9 24.5 %collective-permute-start.45 = (bf16[128,2048]{1,0:T(8,128)(2,1)S(1)}, bf16[128,2048]{1,0:T(8,128)(2,1)S(1)}, u32[]{:S(2)}, u32[]{:S(2)}) collective-permute-start(bf16[128,2048]{1,0:T(8,128)(2,1)S(1)} %fusion.27), channel_id=1, source_target_pairs={{0,8},{8,16},{16,24},{24,28},{28,20},{20,12},{12,4},{4,0},{1,9},{9... | collective-permute-start | bytes 1572872 | tf_op jit(solution)/shard_map/ppermute | solution.py:94
  213.9 24.8 %collective-permute-start.52 = (bf16[128,2048]{1,0:T(8,128)(2,1)S(1)}, bf16[128,2048]{1,0:T(8,128)(2,1)S(1)}, u32[]{:S(2)}, u32[]{:S(2)}) collective-permute-start(bf16[128,2048]{1,0:T(8,128)(2,1)S(1)} %fusion.21), channel_id=1, source_target_pairs={{0,4},{8,0},{16,8},{24,16},{28,24},{20,28},{12,20},{4,12},{1,5},{9... | collective-permute-start | bytes 1572872 | tf_op jit(solution)/shard_map/ppermute | solution.py:95
  215.6 27.2 %collective-permute-start.36 = (bf16[160,2048]{1,0:T(8,128)(2,1)S(1)}, bf16[160,2048]{1,0:T(8,128)(2,1)S(1)}, u32[]{:S(2)}, u32[]{:S(2)}) collective-permute-start(bf16[160,2048]{1,0:T(8,128)(2,1)S(1)} %fusion.30), channel_id=1, source_target_pairs={{0,4},{8,0},{16,8},{24,16},{28,24},{20,28},{12,20},{4,12},{1,5},{9... | collective-permute-start | bytes 1966088 | tf_op jit(solution)/shard_map/ppermute | solution.py:95
  237.8 14.9 %collective-permute-start.46 = (bf16[128,2048]{1,0:T(8,128)(2,1)S(1)}, bf16[128,2048]{1,0:T(8,128)(2,1)S(1)}, u32[]{:S(2)}, u32[]{:S(2)}) collective-permute-start(bf16[128,2048]{1,0:T(8,128)(2,1)S(1)} %fusion.26), channel_id=1, source_target_pairs={{0,8},{8,16},{16,24},{24,28},{28,20},{20,12},{12,4},{4,0},{1,9},{9... | collective-permute-start | bytes 1572872 | tf_op jit(solution)/shard_map/ppermute | solution.py:94
  240.4 14.9 %collective-permute-start.53 = (bf16[128,2048]{1,0:T(8,128)(2,1)S(1)}, bf16[128,2048]{1,0:T(8,128)(2,1)S(1)}, u32[]{:S(2)}, u32[]{:S(2)}) collective-permute-start(bf16[128,2048]{1,0:T(8,128)(2,1)S(1)} %fusion.20), channel_id=1, source_target_pairs={{0,4},{8,0},{16,8},{24,16},{28,24},{20,28},{12,20},{4,12},{1,5},{9... | collective-permute-start | bytes 1572872 | tf_op jit(solution)/shard_map/ppermute | solution.py:95
  241.5 25.3 %collective-permute-start.30 = (bf16[160,2048]{1,0:T(8,128)(2,1)S(1)}, bf16[160,2048]{1,0:T(8,128)(2,1)S(1)}, u32[]{:S(2)}, u32[]{:S(2)}) collective-permute-start(bf16[160,2048]{1,0:T(8,128)(2,1)S(1)} %fusion.15), channel_id=1, source_target_pairs={{0,8},{8,16},{16,24},{24,28},{28,20},{20,12},{12,4},{4,0},{1,9},{9... | collective-permute-start | bytes 1966088 | tf_op jit(solution)/shard_map/ppermute | solution.py:94
  242.9 26.5 %collective-permute-start.37 = (bf16[160,2048]{1,0:T(8,128)(2,1)S(1)}, bf16[160,2048]{1,0:T(8,128)(2,1)S(1)}, u32[]{:S(2)}, u32[]{:S(2)}) collective-permute-start(bf16[160,2048]{1,0:T(8,128)(2,1)S(1)} %fusion.9), channel_id=1, source_target_pairs={{0,4},{8,0},{16,8},{24,16},{28,24},{20,28},{12,20},{4,12},{1,5},{9... | collective-permute-start | bytes 1966088 | tf_op jit(solution)/shard_map/ppermute | solution.py:95
  254.1 23.9 %collective-permute-start.47 = (bf16[128,2048]{1,0:T(8,128)(2,1)S(1)}, bf16[128,2048]{1,0:T(8,128)(2,1)S(1)}, u32[]{:S(2)}, u32[]{:S(2)}) collective-permute-start(bf16[128,2048]{1,0:T(8,128)(2,1)S(1)} %fusion.25), channel_id=1, source_target_pairs={{0,8},{8,16},{16,24},{24,28},{28,20},{20,12},{12,4},{4,0},{1,9},{9... | collective-permute-start | bytes 1572872 | tf_op jit(solution)/shard_map/ppermute | solution.py:94
  255.5 25.2 %collective-permute-start.54 = (bf16[128,2048]{1,0:T(8,128)(2,1)S(1)}, bf16[128,2048]{1,0:T(8,128)(2,1)S(1)}, u32[]{:S(2)}, u32[]{:S(2)}) collective-permute-start(bf16[128,2048]{1,0:T(8,128)(2,1)S(1)} %fusion.19), channel_id=1, source_target_pairs={{0,4},{8,0},{16,8},{24,16},{28,24},{20,28},{12,20},{4,12},{1,5},{9... | collective-permute-start | bytes 1572872 | tf_op jit(solution)/shard_map/ppermute | solution.py:95
  267.0 25.1 %collective-permute-start.31 = (bf16[160,2048]{1,0:T(8,128)(2,1)S(1)}, bf16[160,2048]{1,0:T(8,128)(2,1)S(1)}, u32[]{:S(2)}, u32[]{:S(2)}) collective-permute-start(bf16[160,2048]{1,0:T(8,128)(2,1)S(1)} %fusion.14), channel_id=1, source_target_pairs={{0,8},{8,16},{16,24},{24,28},{28,20},{20,12},{12,4},{4,0},{1,9},{9... | collective-permute-start | bytes 1966088 | tf_op jit(solution)/shard_map/ppermute | solution.py:94
  269.6 25.1 %collective-permute-start.38 = (bf16[160,2048]{1,0:T(8,128)(2,1)S(1)}, bf16[160,2048]{1,0:T(8,128)(2,1)S(1)}, u32[]{:S(2)}, u32[]{:S(2)}) collective-permute-start(bf16[160,2048]{1,0:T(8,128)(2,1)S(1)} %fusion.8), channel_id=1, source_target_pairs={{0,4},{8,0},{16,8},{24,16},{28,24},{20,28},{12,20},{4,12},{1,5},{9... | collective-permute-start | bytes 1966088 | tf_op jit(solution)/shard_map/ppermute | solution.py:95
  279.4 23.9 %collective-permute-start.48 = (bf16[128,2048]{1,0:T(8,128)(2,1)S(1)}, bf16[128,2048]{1,0:T(8,128)(2,1)S(1)}, u32[]{:S(2)}, u32[]{:S(2)}) collective-permute-start(bf16[128,2048]{1,0:T(8,128)(2,1)S(1)} %fusion.24), channel_id=1, source_target_pairs={{0,8},{8,16},{16,24},{24,28},{28,20},{20,12},{12,4},{4,0},{1,9},{9... | collective-permute-start | bytes 1572872 | tf_op jit(solution)/shard_map/ppermute | solution.py:94
  280.7 25.2 %collective-permute-start.55 = (bf16[128,2048]{1,0:T(8,128)(2,1)S(1)}, bf16[128,2048]{1,0:T(8,128)(2,1)S(1)}, u32[]{:S(2)}, u32[]{:S(2)}) collective-permute-start(bf16[128,2048]{1,0:T(8,128)(2,1)S(1)} %fusion.18), channel_id=1, source_target_pairs={{0,4},{8,0},{16,8},{24,16},{28,24},{20,28},{12,20},{4,12},{1,5},{9... | collective-permute-start | bytes 1572872 | tf_op jit(solution)/shard_map/ppermute | solution.py:95
  292.2 25.1 %collective-permute-start.32 = (bf16[160,2048]{1,0:T(8,128)(2,1)S(1)}, bf16[160,2048]{1,0:T(8,128)(2,1)S(1)}, u32[]{:S(2)}, u32[]{:S(2)}) collective-permute-start(bf16[160,2048]{1,0:T(8,128)(2,1)S(1)} %fusion.13), channel_id=1, source_target_pairs={{0,8},{8,16},{16,24},{24,28},{28,20},{20,12},{12,4},{4,0},{1,9},{9... | collective-permute-start | bytes 1966088 | tf_op jit(solution)/shard_map/ppermute | solution.py:94
  294.8 25.1 %collective-permute-start.39 = (bf16[160,2048]{1,0:T(8,128)(2,1)S(1)}, bf16[160,2048]{1,0:T(8,128)(2,1)S(1)}, u32[]{:S(2)}, u32[]{:S(2)}) collective-permute-start(bf16[160,2048]{1,0:T(8,128)(2,1)S(1)} %fusion.7), channel_id=1, source_target_pairs={{0,4},{8,0},{16,8},{24,16},{28,24},{20,28},{12,20},{4,12},{1,5},{9... | collective-permute-start | bytes 1966088 | tf_op jit(solution)/shard_map/ppermute | solution.py:95
  304.7 23.9 %collective-permute-start.49 = (bf16[128,2048]{1,0:T(8,128)(2,1)S(1)}, bf16[128,2048]{1,0:T(8,128)(2,1)S(1)}, u32[]{:S(2)}, u32[]{:S(2)}) collective-permute-start(bf16[128,2048]{1,0:T(8,128)(2,1)S(1)} %fusion.23), channel_id=1, source_target_pairs={{0,8},{8,16},{16,24},{24,28},{28,20},{20,12},{12,4},{4,0},{1,9},{9... | collective-permute-start | bytes 1572872 | tf_op jit(solution)/shard_map/ppermute | solution.py:94
  306.0 37.3 %collective-permute-start.56 = (bf16[128,2048]{1,0:T(8,128)(2,1)S(1)}, bf16[128,2048]{1,0:T(8,128)(2,1)S(1)}, u32[]{:S(2)}, u32[]{:S(2)}) collective-permute-start(bf16[128,2048]{1,0:T(8,128)(2,1)S(1)} %fusion.17), channel_id=1, source_target_pairs={{0,4},{8,0},{16,8},{24,16},{28,24},{20,28},{12,20},{4,12},{1,5},{9... | collective-permute-start | bytes 1572872 | tf_op jit(solution)/shard_map/ppermute | solution.py:95
  317.5 22.3 %collective-permute-start.33 = (bf16[160,2048]{1,0:T(8,128)(2,1)S(1)}, bf16[160,2048]{1,0:T(8,128)(2,1)S(1)}, u32[]{:S(2)}, u32[]{:S(2)}) collective-permute-start(bf16[160,2048]{1,0:T(8,128)(2,1)S(1)} %fusion.12), channel_id=1, source_target_pairs={{0,8},{8,16},{16,24},{24,28},{28,20},{20,12},{12,4},{4,0},{1,9},{9... | collective-permute-start | bytes 1966088 | tf_op jit(solution)/shard_map/ppermute | solution.py:94
  320.1 22.1 %collective-permute-start.40 = (bf16[160,2048]{1,0:T(8,128)(2,1)S(1)}, bf16[160,2048]{1,0:T(8,128)(2,1)S(1)}, u32[]{:S(2)}, u32[]{:S(2)}) collective-permute-start(bf16[160,2048]{1,0:T(8,128)(2,1)S(1)} %fusion.6), channel_id=1, source_target_pairs={{0,4},{8,0},{16,8},{24,16},{28,24},{20,28},{12,20},{4,12},{1,5},{9... | collective-permute-start | bytes 1966088 | tf_op jit(solution)/shard_map/ppermute | solution.py:95
  339.9 14.7 %collective-permute-start.34 = (bf16[160,2048]{1,0:T(8,128)(2,1)S(1)}, bf16[160,2048]{1,0:T(8,128)(2,1)S(1)}, u32[]{:S(2)}, u32[]{:S(2)}) collective-permute-start(bf16[160,2048]{1,0:T(8,128)(2,1)S(1)} %fusion.11), channel_id=1, source_target_pairs={{0,8},{8,16},{16,24},{24,28},{28,20},{20,12},{12,4},{4,0},{1,9},{9... | collective-permute-start | bytes 1966088 | tf_op jit(solution)/shard_map/ppermute | solution.py:94
  342.4 14.7 %collective-permute-start.41 = (bf16[160,2048]{1,0:T(8,128)(2,1)S(1)}, bf16[160,2048]{1,0:T(8,128)(2,1)S(1)}, u32[]{:S(2)}, u32[]{:S(2)}) collective-permute-start(bf16[160,2048]{1,0:T(8,128)(2,1)S(1)} %fusion.5), channel_id=1, source_target_pairs={{0,4},{8,0},{16,8},{24,16},{28,24},{20,28},{12,20},{4,12},{1,5},{9... | collective-permute-start | bytes 1966088 | tf_op jit(solution)/shard_map/ppermute | solution.py:95
  354.8 13.1 %collective-permute-start.35 = (bf16[160,2048]{1,0:T(8,128)(2,1)S(1)}, bf16[160,2048]{1,0:T(8,128)(2,1)S(1)}, u32[]{:S(2)}, u32[]{:S(2)}) collective-permute-start(bf16[160,2048]{1,0:T(8,128)(2,1)S(1)} %fusion.10), channel_id=1, source_target_pairs={{0,8},{8,16},{16,24},{24,28},{28,20},{20,12},{12,4},{4,0},{1,9},{9... | collective-permute-start | bytes 1966088 | tf_op jit(solution)/shard_map/ppermute | solution.py:94
  357.3 12.8 %collective-permute-start.42 = (bf16[160,2048]{1,0:T(8,128)(2,1)S(1)}, bf16[160,2048]{1,0:T(8,128)(2,1)S(1)}, u32[]{:S(2)}, u32[]{:S(2)}) collective-permute-start(bf16[160,2048]{1,0:T(8,128)(2,1)S(1)} %fusion.4), channel_id=1, source_target_pairs={{0,4},{8,0},{16,8},{24,16},{28,24},{20,28},{12,20},{4,12},{1,5},{9... | collective-permute-start | bytes 1966088 | tf_op jit(solution)/shard_map/ppermute | solution.py:95
  (44 other events, 430.9 us)

commit v7 on v6

--- a/solution.py
+++ b/solution.py
@@ -143,6 +143,44 @@
     return jnp.concatenate([send_left, send_right], axis=1)
 
 
+class Ring:
+    def __init__(self, partial, ring, axis):
+        count = len(ring)
+        self.count = count
+        self.axis = axis
+        self.spot = ring_spot(ring, axis)
+        self.order = jnp.asarray(ring, jnp.int32)
+        rows = partial.shape[0] // count
+        half = partial.shape[1] // 2
+        blocks = partial.reshape(count, rows, partial.shape[1])
+        self.left = blocks[:, :, :half]
+        self.right = blocks[:, :, half:]
+        self.forward = [(ring[p], ring[(p + 1) % count]) for p in range(count)]
+        self.backward = [(ring[p], ring[(p - 1) % count]) for p in range(count)]
+        self.state = (self.block(self.left, count - 1), self.block(self.right, 1))
+        self.done = 0
+
+    def block(self, side, offset):
+        index = self.order[(self.spot + offset) % self.count]
+        return lax.dynamic_index_in_dim(side, index, 0, keepdims=False)
+
+    def advance(self, upto):
+        count = self.count
+        send_left, send_right = self.state
+        for step in range(self.done, min(upto, count - 1)):
+            got_left = lax.ppermute(send_left.astype(jnp.bfloat16), self.axis, self.forward)
+            got_right = lax.ppermute(send_right.astype(jnp.bfloat16), self.axis, self.backward)
+            send_left = got_left.astype(jnp.float32) + self.block(self.left, 2 * count - step - 2)
+            send_right = got_right.astype(jnp.float32) + self.block(self.right, step + 2)
+            self.done = step + 1
+        self.state = (send_left, send_right)
+        return self
+
+    def result(self):
+        self.advance(self.count - 1)
+        return jnp.concatenate(list(self.state), axis=1)
+
+
 def tp_project(partial, rows_mine, split, axis):
     rank = lax.axis_index(axis)
     core = rank % 2
@@ -284,7 +322,9 @@
     key_part = across(dscore, queries) * factor
     value_part = across(prob.astype(jnp.bfloat16), grad_stack)
     pair_all = jnp.concatenate([key_part, value_part], axis=1)
+    out_ring = Ring(out_weight_grad, ring, "ctx").advance(len(ring) // 2)
     pair_grad = butterfly_sum(ring_scatter_relative(pair_all, ring, "ctx"), "tp")
+    out_ring.state, pair_grad = lax.optimization_barrier((out_ring.state, pair_grad))
 
     key_raw = rotate(pair_grad[:, :head_dim], cosine_all, -sine_all)
     query_grad = jnp.transpose((query_sum * factor).reshape(heads, rows_mine, head_dim), (1, 0, 2))
@@ -298,8 +338,10 @@
     )
     grad_x = jnp.dot(d_qkv, w_qkv, preferred_element_type=jnp.float32).astype(jnp.bfloat16)
     joint_weight = across(d_qkv, tokens)
+    out_ring.advance(len(ring) - 1)
+    out_ring.state, joint_weight = lax.optimization_barrier((out_ring.state, joint_weight))
     grad_w_qkv = ring_scatter(joint_weight, ring, "ctx")
-    grad_w_out = ring_scatter(out_weight_grad, ring, "ctx")
+    grad_w_out = out_ring.result()
     return (out, grad_x, grad_w_qkv, grad_w_out)
 
 

time: 374 us -> 359 us (0.960)
  waiting for transfers between devices: 168 us -> 137 us
  other arithmetic: 34.4 us -> 45.3 us
  starting transfers between devices: 52.4 us -> 57.9 us
    ppermute x14 -> x7, waiting for transfers between devices: 112 us -> 60.6 us  [ring_scatter(): got_left = lax.ppermute(send_left.astype(jnp.bfloat16), axis, forward)]
    ppermute x0 -> x14, waiting for transfers between devices: none -> 40.1 us  [the longest x7 37.4 us: advance(): lax.ppermute(send_right.astype(jnp.bfloat16), self.axis, self.backward)]
    ppermute x0 -> x14, starting transfers between devices: none -> 15.6 us  [the longest x7 8.55 us: advance(): lax.ppermute(send_right.astype(jnp.bfloat16), self.axis, self.backward)]
    convert_element_type x0 -> x10, other arithmetic: none -> 11.5 us  [the longest x5 7.58 us: advance(): send_right.astype(jnp.bfloat16)]
    ppermute x14 -> x7, waiting for transfers between devices: 10.7 us -> 0.68 us  [ring_scatter(): got_right = lax.ppermute(send_right.astype(jnp.bfloat16), axis, backward)]
    ppermute x7, waiting for transfers between devices: 13.1 us -> 3.21 us  [ring_scatter_relative(): got_left = lax.ppermute(send_left.astype(jnp.bfloat16), axis, forward)]
    ppermute x14 -> x7, starting transfers between devices: 14 us -> 5.64 us  [ring_scatter(): got_left = lax.ppermute(send_left.astype(jnp.bfloat16), axis, forward)]
    slice x2 -> x1, local copies, waits for them, and re-layouts: 14.4 us -> 8.09 us  [ring_scatter(): left = blocks[:, :, :half]]
  transfers between devices with their start and end apart: 57 -> 57, of which waited for: 35 -> 29; matrix products, arithmetic and copies ran while one was open for 18% -> 20% of each run, Pallas kernels for 0% -> 0%
where the time goes in v7:
time: 359 us; the launch traced here: 358 us
  waiting for transfers between devices  137 us (38%)
  starting transfers between devices  57.9 us (16%)
  other arithmetic  45.3 us (13%)
  between operations  37.4 us (10%)
  matrix products  34.6 us (10%)
  local copies, waits for them, and re-layouts  31 us (9%)
  blocking collectives  14.5 us (4%)
    ppermute x7, waiting for transfers between devices, ring_scatter(): got_left = lax.ppermute(send_left.astype(jnp.bfloat16), axis, forward)  60.6 us
    ppermute x7, waiting for transfers between devices, advance(): lax.ppermute(send_right.astype(jnp.bfloat16), self.axis, self.backward)  37.4 us
    dot_general x4, matrix products, against(): lax.dot_general(left, right, (((1,), (1,)), ((), ())), preferred_element_...  14.9 us
    ppermute x7, starting transfers between devices, ring_scatter_relative(): got_left = lax.ppermute(send_left.astype(jnp.bfloat16), axis, forward)  11.2 us
    ppermute x4, waiting for transfers between devices, ring_gather(): from_left = lax.ppermute(from_left, axis, forward)  9.24 us
    ppermute x7, starting transfers between devices, ring_scatter(): got_right = lax.ppermute(send_right.astype(jnp.bfloat16), axis, backward)  9.13 us
    ppermute x7, waiting for transfers between devices, ring_scatter_relative(): got_right = lax.ppermute(send_right.astype(jnp.bfloat16), axis, backward)  9.07 us
    convert_element_type x6, other arithmetic, ring_scatter(): got_left = lax.ppermute(send_left.astype(jnp.bfloat16), axis, forward)  8.84 us
  transfers between devices with their start and end apart: 57, of which 29 were waited for; matrix products, arithmetic and copies ran while one was open for 20% of the time, Pallas kernels for 0%

profile of v7, /device:TPU:0, one launch (start us, length us, event | category | flops | bytes accessed | tf_op | source)
XLA Modules:
  0.0 357.7 jit_solution(12365563404311751912)
XLA Ops:
  2.2 6.9 %fusion.87 = f32[256,1280]{1,0:T(8,128)S(1)} fusion(bf16[256,4096]{1,0:T(8,128)(2,1)S(1)} %copy-done, bf16[1280,4096]{1,0:T(8,128)(2,1)} %param.13), kind=kOutput, calls=%fused_computation.204 | convolution fusion | flops 2684354560 | bytes 13893632 | tf_op jit(solution)/shard_map/dot_general | solution.py:35
  9.6 6.4 %convolution_convert_fusion.2 = bf16[256,1024]{1,0:T(8,128)(2,1)S(1)} fusion(bf16[256,4096]{1,0:T(8,128)(2,1)} %param.15, bf16[1024,4096]{1,0:T(8,128)(2,1)} %param.14), kind=kOutput, calls=%fused_computation.42 | convolution fusion | flops 2147745792 | bytes 11010048 | tf_op jit(solution)/shard_map/dot_general | solution.py:35
  17.6 2.6 collective-permute-start.11
  22.0 5.6 %collective-permute-done.11 = bf16[128,1024]{1,0:T(8,128)(2,1)} collective-permute-done((bf16[128,1024]{1,0:T(8,128)(2,1)}, bf16[128,1024]{1,0:T(8,128)(2,1)}, u32[]{:S(2)}, u32[]{:S(2)}) %collective-permute-start.11) | collective-permute-done | bytes 262176 | tf_op jit(solution)/shard_map/ppermute | solution.py:212
  35.1 4.0 %collective-permute-done.10 = f32[64,1024]{1,0:T(8,128)S(1)} collective-permute-done((f32[64,1024]{1,0:T(8,128)S(1)}, f32[64,1024]{1,0:T(8,128)S(1)}, u32[]{:S(2)}, u32[]{:S(2)}) %collective-permute-start.10) | collective-permute-done | bytes 262176 | tf_op jit(solution)/shard_map/ppermute | solution.py:195
  41.7 3.2 collective-permute-done.4
  46.9 4.6 %collective-permute-done.8 = bf16[259,256]{1,0:T(8,128)(2,1)S(1)} collective-permute-done((bf16[259,256]{1,0:T(8,128)(2,1)S(1)}, bf16[259,256]{1,0:T(8,128)(2,1)S(1)}, u32[]{:S(2)}, u32[]{:S(2)}) %collective-permute-start.8) | collective-permute-done | bytes 132640 | tf_op jit(solution)/shard_map/ppermute | solution.py:119
  51.9 4.6 %collective-permute-done.9 = bf16[259,256]{1,0:T(8,128)(2,1)S(1)} collective-permute-done((bf16[259,256]{1,0:T(8,128)(2,1)S(1)}, bf16[259,256]{1,0:T(8,128)(2,1)S(1)}, u32[]{:S(2)}, u32[]{:S(2)}) %collective-permute-start.9) | collective-permute-done | bytes 132640 | tf_op jit(solution)/shard_map/ppermute | solution.py:119
  65.4 2.9 copy.27
  72.1 2.7 collective-permute-done.21
  118.4 7.5 %all_gather.6 = bf16[256,1024]{1,0:T(8,128)(2,1)S(1)} all-gather(bf16[64,1024]{1,0:T(8,128)(2,1)S(1)} %bitcast.337), channel_id=1, replica_groups=mesh['ctx'=8,'tp'=4] {'tp'}, dimensions={0}, use_global_device_ids=true | all-gather | bytes 655360 | tf_op jit(solution)/shard_map/all_gather | solution.py:310
  129.0 2.4 fusion.88
  135.0 6.3 %fusion.83 = (f32[8,128,2048]{2,1,0:T(8,128)}, f32[8,128,2048]{2,1,0:T(8,128)}) fusion(f32[8,128,4096]{2,1,0:T(8,128)S(1)} %bitcast.318), kind=kLoop, calls=%fused_computation.200 | loop fusion | bytes 33554432 | tf_op jit(solution)/shard_map/slice | solution.py:157
  145.7 2.3 collective-permute-done.33
  153.3 5.2 %collective-permute-done.34 = bf16[256,128]{1,0:T(8,128)(2,1)S(1)} collective-permute-done((bf16[256,128]{1,0:T(8,128)(2,1)S(1)}, bf16[256,128]{1,0:T(8,128)(2,1)S(1)}, u32[]{:S(2)}, u32[]{:S(2)}) %collective-permute-start.34) | collective-permute-done | bytes 65568 | tf_op jit(solution)/shard_map/ppermute | solution.py:140
  165.1 6.3 %collective-permute-done.18 = bf16[128,2048]{1,0:T(8,128)(2,1)S(1)} collective-permute-done((bf16[128,2048]{1,0:T(8,128)(2,1)S(1)}, bf16[128,2048]{1,0:T(8,128)(2,1)S(1)}, u32[]{:S(2)}, u32[]{:S(2)}) %collective-permute-start.18) | collective-permute-done | bytes 524320 | tf_op jit(solution)/shard_map/ppermute | solution.py:172
  176.5 7.0 %collective-permute-done.19 = bf16[128,2048]{1,0:T(8,128)(2,1)S(1)} collective-permute-done((bf16[128,2048]{1,0:T(8,128)(2,1)S(1)}, bf16[128,2048]{1,0:T(8,128)(2,1)S(1)}, u32[]{:S(2)}, u32[]{:S(2)}) %collective-permute-start.19) | collective-permute-done | bytes 524320 | tf_op jit(solution)/shard_map/ppermute | solution.py:172
  187.9 7.3 %collective-permute-done.20 = bf16[128,2048]{1,0:T(8,128)(2,1)S(1)} collective-permute-done((bf16[128,2048]{1,0:T(8,128)(2,1)S(1)}, bf16[128,2048]{1,0:T(8,128)(2,1)S(1)}, u32[]{:S(2)}, u32[]{:S(2)}) %collective-permute-start.20) | collective-permute-done | bytes 524320 | tf_op jit(solution)/shard_map/ppermute | solution.py:172
  199.1 6.9 %all_gather.7 = bf16[256,1024]{1,0:T(8,128)(2,1)} all-gather(bf16[64,1024]{1,0:T(8,128)(2,1)S(1)} %copy_bitcast_fusion.1), channel_id=1, replica_groups=mesh['ctx'=8,'tp'=4] {'tp'}, dimensions={0}, use_global_device_ids=true | all-gather | bytes 655360 | tf_op jit(solution)/shard_map/all_gather | solution.py:334
  212.9 9.9 %collective-permute-done.41 = bf16[128,2048]{1,0:T(8,128)(2,1)} collective-permute-done((bf16[128,2048]{1,0:T(8,128)(2,1)}, bf16[128,2048]{1,0:T(8,128)(2,1)}, u32[]{:S(2)}, u32[]{:S(2)}) %collective-permute-start.41) | collective-permute-done | bytes 524320 | tf_op jit(solution)/shard_map/ppermute | solution.py:172
  227.8 2.9 fusion.90
  230.7 7.0 %collective-permute-done.42 = bf16[128,2048]{1,0:T(8,128)(2,1)S(1)} collective-permute-done((bf16[128,2048]{1,0:T(8,128)(2,1)S(1)}, bf16[128,2048]{1,0:T(8,128)(2,1)S(1)}, u32[]{:S(2)}, u32[]{:S(2)}) %collective-permute-start.42) | collective-permute-done | bytes 524320 | tf_op jit(solution)/shard_map/ppermute | solution.py:172
  241.7 8.1 %fusion.82 = (f32[8,160,2048]{2,1,0:T(8,128)}, f32[8,160,2048]{2,1,0:T(8,128)}) fusion(f32[8,160,4096]{2,1,0:T(8,128)S(1)} %bitcast.317), kind=kLoop, calls=%fused_computation.199 | loop fusion | bytes 41943040 | tf_op jit(solution)/shard_map/slice | solution.py:83
  255.3 11.0 %collective-permute-done.43 = bf16[160,2048]{1,0:T(8,128)(2,1)S(1)} collective-permute-done((bf16[160,2048]{1,0:T(8,128)(2,1)S(1)}, bf16[160,2048]{1,0:T(8,128)(2,1)S(1)}, u32[]{:S(2)}, u32[]{:S(2)}) %collective-permute-start.43) | collective-permute-done | bytes 655392 | tf_op jit(solution)/shard_map/ppermute | solution.py:94
  271.5 10.5 %collective-permute-done.44 = bf16[160,2048]{1,0:T(8,128)(2,1)S(1)} collective-permute-done((bf16[160,2048]{1,0:T(8,128)(2,1)S(1)}, bf16[160,2048]{1,0:T(8,128)(2,1)S(1)}, u32[]{:S(2)}, u32[]{:S(2)}) %collective-permute-start.44) | collective-permute-done | bytes 655392 | tf_op jit(solution)/shard_map/ppermute | solution.py:94
  286.1 10.8 %collective-permute-done.45 = bf16[160,2048]{1,0:T(8,128)(2,1)S(1)} collective-permute-done((bf16[160,2048]{1,0:T(8,128)(2,1)S(1)}, bf16[160,2048]{1,0:T(8,128)(2,1)S(1)}, u32[]{:S(2)}, u32[]{:S(2)}) %collective-permute-start.45) | collective-permute-done | bytes 655392 | tf_op jit(solution)/shard_map/ppermute | solution.py:94
  300.7 11.1 %collective-permute-done.46 = bf16[160,2048]{1,0:T(8,128)(2,1)S(1)} collective-permute-done((bf16[160,2048]{1,0:T(8,128)(2,1)S(1)}, bf16[160,2048]{1,0:T(8,128)(2,1)S(1)}, u32[]{:S(2)}, u32[]{:S(2)}) %collective-permute-start.46) | collective-permute-done | bytes 655392 | tf_op jit(solution)/shard_map/ppermute | solution.py:94
  315.8 7.8 %convolution_convert_fusion = bf16[256,4096]{1,0:T(8,128)(2,1)} fusion(bf16[256,1024]{1,0:T(8,128)(2,1)S(1)} %all_gather.6, bf16[1024,4096]{1,0:T(8,128)(2,1)} %param.14), kind=kOutput, calls=%fused_computation.3 | convolution fusion | flops 2148532224 | bytes 11010048 | tf_op jit(solution)/shard_map/dot_general | solution.py:311
  323.6 3.1 collective-permute-done.47
  330.5 4.1 %convolution_convert_fusion.1 = bf16[256,4096]{1,0:T(8,128)(2,1)} fusion(bf16[256,1280]{1,0:T(8,128)(2,1)S(1)} %concatenate.49, bf16[1280,4096]{1,0:T(8,128)(2,1)S(1)} %bitcast.344), kind=kOutput, calls=%fused_computation.4 | convolution fusion | flops 2685403136 | bytes 13238272 | tf_op jit(solution)/shard_map/dot_general | solution.py:339
  334.6 7.2 %collective-permute-done.48 = bf16[160,2048]{1,0:T(8,128)(2,1)S(1)} collective-permute-done((bf16[160,2048]{1,0:T(8,128)(2,1)S(1)}, bf16[160,2048]{1,0:T(8,128)(2,1)S(1)}, u32[]{:S(2)}, u32[]{:S(2)}) %collective-permute-start.48) | collective-permute-done | bytes 655392 | tf_op jit(solution)/shard_map/ppermute | solution.py:94
  347.1 6.8 %collective-permute-done.49 = bf16[160,2048]{1,0:T(8,128)(2,1)S(1)} collective-permute-done((bf16[160,2048]{1,0:T(8,128)(2,1)S(1)}, bf16[160,2048]{1,0:T(8,128)(2,1)S(1)}, u32[]{:S(2)}, u32[]{:S(2)}) %collective-permute-start.49) | collective-permute-done | bytes 655392 | tf_op jit(solution)/shard_map/ppermute | solution.py:94
  (232 shorter events, 125.3 us)
Async XLA Ops:
  9.1 11.2 %collective-permute-start = (f32[256,1280]{1,0:T(8,128)S(1)}, f32[256,1280]{1,0:T(8,128)}, u32[]{:S(2)}, u32[]{:S(2)}) collective-permute-start(f32[256,1280]{1,0:T(8,128)S(1)} %fusion.87), channel_id=1, source_target_pairs={{0,1},{1,0},{2,3},{3,2},{4,5},{5,4},{6,7},{7,6},{8,9},{9,8},{10,11... | collective-permute-start | bytes 3932168 | tf_op jit(solution)/shard_map/ppermute | solution.py:189
  75.8 39.3 %collective-permute-start.22 = (bf16[256,128]{1,0:T(8,128)(2,1)S(1)}, bf16[256,128]{1,0:T(8,128)(2,1)S(1)}, u32[]{:S(2)}, u32[]{:S(2)}) collective-permute-start(bf16[256,128]{1,0:T(8,128)(2,1)S(1)} %get-tuple-element.40), channel_id=1, source_target_pairs={{0,8},{8,16},{16,24},{24,28},{28,20},{20,12},{12,4},{4,0},{1,9},{9... | collective-permute-start | bytes 196616 | tf_op jit(solution)/shard_map/ppermute | solution.py:139
  77.9 37.3 %collective-permute-start.29 = (bf16[256,128]{1,0:T(8,128)(2,1)S(1)}, bf16[256,128]{1,0:T(8,128)(2,1)S(1)}, u32[]{:S(2)}, u32[]{:S(2)}) collective-permute-start(bf16[256,128]{1,0:T(8,128)(2,1)S(1)} %get-tuple-element.41), channel_id=1, source_target_pairs={{0,4},{8,0},{16,8},{24,16},{28,24},{20,28},{12,20},{4,12},{1,5},{9... | collective-permute-start | bytes 196616 | tf_op jit(solution)/shard_map/ppermute | solution.py:140
  144.7 13.8 %collective-permute-start.17 = (bf16[128,2048]{1,0:T(8,128)(2,1)S(1)}, bf16[128,2048]{1,0:T(8,128)(2,1)S(1)}, u32[]{:S(2)}, u32[]{:S(2)}) collective-permute-start(bf16[128,2048]{1,0:T(8,128)(2,1)S(1)} %fusion.30), channel_id=1, source_target_pairs={{0,4},{8,0},{16,8},{24,16},{28,24},{20,28},{12,20},{4,12},{1,5},{9... | collective-permute-start | bytes 1572872 | tf_op jit(solution)/shard_map/ppermute | solution.py:172
  151.8 10.2 %collective-permute-start.13 = (bf16[128,2048]{1,0:T(8,128)(2,1)S(1)}, bf16[128,2048]{1,0:T(8,128)(2,1)S(1)}, u32[]{:S(2)}, u32[]{:S(2)}) collective-permute-start(bf16[128,2048]{1,0:T(8,128)(2,1)S(1)} %fusion.29), channel_id=1, source_target_pairs={{0,8},{8,16},{16,24},{24,28},{28,20},{20,12},{12,4},{4,0},{1,9},{9... | collective-permute-start | bytes 1572872 | tf_op jit(solution)/shard_map/ppermute | solution.py:171
  159.9 11.5 %collective-permute-start.18 = (bf16[128,2048]{1,0:T(8,128)(2,1)S(1)}, bf16[128,2048]{1,0:T(8,128)(2,1)S(1)}, u32[]{:S(2)}, u32[]{:S(2)}) collective-permute-start(bf16[128,2048]{1,0:T(8,128)(2,1)S(1)} %fusion.23), channel_id=1, source_target_pairs={{0,4},{8,0},{16,8},{24,16},{28,24},{20,28},{12,20},{4,12},{1,5},{9... | collective-permute-start | bytes 1572872 | tf_op jit(solution)/shard_map/ppermute | solution.py:172
  163.3 10.6 %collective-permute-start.14 = (bf16[128,2048]{1,0:T(8,128)(2,1)S(1)}, bf16[128,2048]{1,0:T(8,128)(2,1)S(1)}, u32[]{:S(2)}, u32[]{:S(2)}) collective-permute-start(bf16[128,2048]{1,0:T(8,128)(2,1)S(1)} %fusion.26), channel_id=1, source_target_pairs={{0,8},{8,16},{16,24},{24,28},{28,20},{20,12},{12,4},{4,0},{1,9},{9... | collective-permute-start | bytes 1572872 | tf_op jit(solution)/shard_map/ppermute | solution.py:171
  165.0 10.6 %collective-permute-start.35 = (f32[256,256]{1,0:T(8,128)S(1)}, f32[256,256]{1,0:T(8,128)S(1)}, u32[]{:S(2)}, u32[]{:S(2)}) collective-permute-start(f32[256,256]{1,0:T(8,128)S(1)} %pad_maximum_fusion.3), channel_id=1, source_target_pairs={{0,1},{1,0},{2,3},{3,2},{4,5},{5,4},{6,7},{7,6},{8,9},{9,8},{10,11... | collective-permute-start | bytes 786440 | tf_op jit(solution)/shard_map/ppermute | solution.py:226
  172.7 10.8 %collective-permute-start.19 = (bf16[128,2048]{1,0:T(8,128)(2,1)S(1)}, bf16[128,2048]{1,0:T(8,128)(2,1)S(1)}, u32[]{:S(2)}, u32[]{:S(2)}) collective-permute-start(bf16[128,2048]{1,0:T(8,128)(2,1)S(1)} %fusion.22), channel_id=1, source_target_pairs={{0,4},{8,0},{16,8},{24,16},{28,24},{20,28},{12,20},{4,12},{1,5},{9... | collective-permute-start | bytes 1572872 | tf_op jit(solution)/shard_map/ppermute | solution.py:172
  174.1 12.2 %collective-permute-start.15 = (bf16[128,2048]{1,0:T(8,128)(2,1)S(1)}, bf16[128,2048]{1,0:T(8,128)(2,1)S(1)}, u32[]{:S(2)}, u32[]{:S(2)}) collective-permute-start(bf16[128,2048]{1,0:T(8,128)(2,1)S(1)} %fusion.25), channel_id=1, source_target_pairs={{0,8},{8,16},{16,24},{24,28},{28,20},{20,12},{12,4},{4,0},{1,9},{9... | collective-permute-start | bytes 1572872 | tf_op jit(solution)/shard_map/ppermute | solution.py:171
  175.7 12.2 %collective-permute-start.36 = (f32[256,256]{1,0:T(8,128)S(1)}, f32[256,256]{1,0:T(8,128)S(1)}, u32[]{:S(2)}, u32[]{:S(2)}) collective-permute-start(f32[256,256]{1,0:T(8,128)S(1)} %fusion.80), channel_id=1, source_target_pairs={{0,2},{1,3},{2,0},{3,1},{4,6},{5,7},{6,4},{7,5},{8,10},{9,11},{10,... | collective-permute-start | bytes 786440 | tf_op jit(solution)/shard_map/ppermute | solution.py:226
  184.8 10.3 %collective-permute-start.20 = (bf16[128,2048]{1,0:T(8,128)(2,1)S(1)}, bf16[128,2048]{1,0:T(8,128)(2,1)S(1)}, u32[]{:S(2)}, u32[]{:S(2)}) collective-permute-start(bf16[128,2048]{1,0:T(8,128)(2,1)S(1)} %fusion.21), channel_id=1, source_target_pairs={{0,4},{8,0},{16,8},{24,16},{28,24},{20,28},{12,20},{4,12},{1,5},{9... | collective-permute-start | bytes 1572872 | tf_op jit(solution)/shard_map/ppermute | solution.py:172
  186.3 10.2 %collective-permute-start.16 = (bf16[128,2048]{1,0:T(8,128)(2,1)S(1)}, bf16[128,2048]{1,0:T(8,128)(2,1)S(1)}, u32[]{:S(2)}, u32[]{:S(2)}) collective-permute-start(bf16[128,2048]{1,0:T(8,128)(2,1)S(1)} %fusion.24), channel_id=1, source_target_pairs={{0,8},{8,16},{16,24},{24,28},{28,20},{20,12},{12,4},{4,0},{1,9},{9... | collective-permute-start | bytes 1572872 | tf_op jit(solution)/shard_map/ppermute | solution.py:171
  198.6 11.2 %collective-permute-start.37 = (bf16[128,2048]{1,0:T(8,128)(2,1)S(1)}, bf16[128,2048]{1,0:T(8,128)(2,1)S(1)}, u32[]{:S(2)}, u32[]{:S(2)}) collective-permute-start(bf16[128,2048]{1,0:T(8,128)(2,1)S(1)} %bitcast_add_fusion.24), channel_id=1, source_target_pairs={{0,8},{8,16},{16,24},{24,28},{28,20},{20,12},{12,4},{4,0},{1,9},{9... | collective-permute-start | bytes 1572872 | tf_op jit(solution)/shard_map/ppermute | solution.py:171
  208.2 14.6 %collective-permute-start.41 = (bf16[128,2048]{1,0:T(8,128)(2,1)}, bf16[128,2048]{1,0:T(8,128)(2,1)}, u32[]{:S(2)}, u32[]{:S(2)}) collective-permute-start(bf16[128,2048]{1,0:T(8,128)(2,1)} %fusion.18), channel_id=1, source_target_pairs={{0,4},{8,0},{16,8},{24,16},{28,24},{20,28},{12,20},{4,12},{1,5},{9... | collective-permute-start | bytes 1572872 | tf_op jit(solution)/shard_map/ppermute | solution.py:172
  210.6 15.1 %collective-permute-start.38 = (bf16[128,2048]{1,0:T(8,128)(2,1)}, bf16[128,2048]{1,0:T(8,128)(2,1)}, u32[]{:S(2)}, u32[]{:S(2)}) collective-permute-start(bf16[128,2048]{1,0:T(8,128)(2,1)} %fusion.20), channel_id=1, source_target_pairs={{0,8},{8,16},{16,24},{24,28},{28,20},{20,12},{12,4},{4,0},{1,9},{9... | collective-permute-start | bytes 1572872 | tf_op jit(solution)/shard_map/ppermute | solution.py:171
  224.2 13.5 %collective-permute-start.42 = (bf16[128,2048]{1,0:T(8,128)(2,1)S(1)}, bf16[128,2048]{1,0:T(8,128)(2,1)S(1)}, u32[]{:S(2)}, u32[]{:S(2)}) collective-permute-start(bf16[128,2048]{1,0:T(8,128)(2,1)S(1)} %fusion.17), channel_id=1, source_target_pairs={{0,4},{8,0},{16,8},{24,16},{28,24},{20,28},{12,20},{4,12},{1,5},{9... | collective-permute-start | bytes 1572872 | tf_op jit(solution)/shard_map/ppermute | solution.py:172
  227.2 13.1 %collective-permute-start.39 = (bf16[128,2048]{1,0:T(8,128)(2,1)S(1)}, bf16[128,2048]{1,0:T(8,128)(2,1)S(1)}, u32[]{:S(2)}, u32[]{:S(2)}) collective-permute-start(bf16[128,2048]{1,0:T(8,128)(2,1)S(1)} %fusion.19), channel_id=1, source_target_pairs={{0,8},{8,16},{16,24},{24,28},{28,20},{20,12},{12,4},{4,0},{1,9},{9... | collective-permute-start | bytes 1572872 | tf_op jit(solution)/shard_map/ppermute | solution.py:171
  251.4 15.0 %collective-permute-start.43 = (bf16[160,2048]{1,0:T(8,128)(2,1)S(1)}, bf16[160,2048]{1,0:T(8,128)(2,1)S(1)}, u32[]{:S(2)}, u32[]{:S(2)}) collective-permute-start(bf16[160,2048]{1,0:T(8,128)(2,1)S(1)} %fusion.27), channel_id=1, source_target_pairs={{0,8},{8,16},{16,24},{24,28},{28,20},{20,12},{12,4},{4,0},{1,9},{9... | collective-permute-start | bytes 1966088 | tf_op jit(solution)/shard_map/ppermute | solution.py:94
  254.0 14.8 %collective-permute-start.50 = (bf16[160,2048]{1,0:T(8,128)(2,1)S(1)}, bf16[160,2048]{1,0:T(8,128)(2,1)S(1)}, u32[]{:S(2)}, u32[]{:S(2)}) collective-permute-start(bf16[160,2048]{1,0:T(8,128)(2,1)S(1)} %fusion.28), channel_id=1, source_target_pairs={{0,4},{8,0},{16,8},{24,16},{28,24},{20,28},{12,20},{4,12},{1,5},{9... | collective-permute-start | bytes 1966088 | tf_op jit(solution)/shard_map/ppermute | solution.py:95
  267.9 14.1 %collective-permute-start.44 = (bf16[160,2048]{1,0:T(8,128)(2,1)S(1)}, bf16[160,2048]{1,0:T(8,128)(2,1)S(1)}, u32[]{:S(2)}, u32[]{:S(2)}) collective-permute-start(bf16[160,2048]{1,0:T(8,128)(2,1)S(1)} %fusion.15), channel_id=1, source_target_pairs={{0,8},{8,16},{16,24},{24,28},{28,20},{20,12},{12,4},{4,0},{1,9},{9... | collective-permute-start | bytes 1966088 | tf_op jit(solution)/shard_map/ppermute | solution.py:94
  270.2 14.6 %collective-permute-start.51 = (bf16[160,2048]{1,0:T(8,128)(2,1)S(1)}, bf16[160,2048]{1,0:T(8,128)(2,1)S(1)}, u32[]{:S(2)}, u32[]{:S(2)}) collective-permute-start(bf16[160,2048]{1,0:T(8,128)(2,1)S(1)} %fusion.9), channel_id=1, source_target_pairs={{0,4},{8,0},{16,8},{24,16},{28,24},{20,28},{12,20},{4,12},{1,5},{9... | collective-permute-start | bytes 1966088 | tf_op jit(solution)/shard_map/ppermute | solution.py:95
  283.5 13.4 %collective-permute-start.45 = (bf16[160,2048]{1,0:T(8,128)(2,1)S(1)}, bf16[160,2048]{1,0:T(8,128)(2,1)S(1)}, u32[]{:S(2)}, u32[]{:S(2)}) collective-permute-start(bf16[160,2048]{1,0:T(8,128)(2,1)S(1)} %fusion.14), channel_id=1, source_target_pairs={{0,8},{8,16},{16,24},{24,28},{28,20},{20,12},{12,4},{4,0},{1,9},{9... | collective-permute-start | bytes 1966088 | tf_op jit(solution)/shard_map/ppermute | solution.py:94
  285.0 14.3 %collective-permute-start.52 = (bf16[160,2048]{1,0:T(8,128)(2,1)S(1)}, bf16[160,2048]{1,0:T(8,128)(2,1)S(1)}, u32[]{:S(2)}, u32[]{:S(2)}) collective-permute-start(bf16[160,2048]{1,0:T(8,128)(2,1)S(1)} %fusion.8), channel_id=1, source_target_pairs={{0,4},{8,0},{16,8},{24,16},{28,24},{20,28},{12,20},{4,12},{1,5},{9... | collective-permute-start | bytes 1966088 | tf_op jit(solution)/shard_map/ppermute | solution.py:95
  298.4 13.4 %collective-permute-start.46 = (bf16[160,2048]{1,0:T(8,128)(2,1)S(1)}, bf16[160,2048]{1,0:T(8,128)(2,1)S(1)}, u32[]{:S(2)}, u32[]{:S(2)}) collective-permute-start(bf16[160,2048]{1,0:T(8,128)(2,1)S(1)} %fusion.13), channel_id=1, source_target_pairs={{0,8},{8,16},{16,24},{24,28},{28,20},{20,12},{12,4},{4,0},{1,9},{9... | collective-permute-start | bytes 1966088 | tf_op jit(solution)/shard_map/ppermute | solution.py:94
  299.4 14.7 %collective-permute-start.53 = (bf16[160,2048]{1,0:T(8,128)(2,1)S(1)}, bf16[160,2048]{1,0:T(8,128)(2,1)S(1)}, u32[]{:S(2)}, u32[]{:S(2)}) collective-permute-start(bf16[160,2048]{1,0:T(8,128)(2,1)S(1)} %fusion.7), channel_id=1, source_target_pairs={{0,4},{8,0},{16,8},{24,16},{28,24},{20,28},{12,20},{4,12},{1,5},{9... | collective-permute-start | bytes 1966088 | tf_op jit(solution)/shard_map/ppermute | solution.py:95
  313.3 13.4 %collective-permute-start.47 = (bf16[160,2048]{1,0:T(8,128)(2,1)S(1)}, bf16[160,2048]{1,0:T(8,128)(2,1)S(1)}, u32[]{:S(2)}, u32[]{:S(2)}) collective-permute-start(bf16[160,2048]{1,0:T(8,128)(2,1)S(1)} %fusion.12), channel_id=1, source_target_pairs={{0,8},{8,16},{16,24},{24,28},{28,20},{20,12},{12,4},{4,0},{1,9},{9... | collective-permute-start | bytes 1966088 | tf_op jit(solution)/shard_map/ppermute | solution.py:94
  314.3 14.8 %collective-permute-start.54 = (bf16[160,2048]{1,0:T(8,128)(2,1)S(1)}, bf16[160,2048]{1,0:T(8,128)(2,1)S(1)}, u32[]{:S(2)}, u32[]{:S(2)}) collective-permute-start(bf16[160,2048]{1,0:T(8,128)(2,1)S(1)} %fusion.6), channel_id=1, source_target_pairs={{0,4},{8,0},{16,8},{24,16},{28,24},{20,28},{12,20},{4,12},{1,5},{9... | collective-permute-start | bytes 1966088 | tf_op jit(solution)/shard_map/ppermute | solution.py:95
  328.2 13.6 %collective-permute-start.48 = (bf16[160,2048]{1,0:T(8,128)(2,1)S(1)}, bf16[160,2048]{1,0:T(8,128)(2,1)S(1)}, u32[]{:S(2)}, u32[]{:S(2)}) collective-permute-start(bf16[160,2048]{1,0:T(8,128)(2,1)S(1)} %fusion.11), channel_id=1, source_target_pairs={{0,8},{8,16},{16,24},{24,28},{28,20},{20,12},{12,4},{4,0},{1,9},{9... | collective-permute-start | bytes 1966088 | tf_op jit(solution)/shard_map/ppermute | solution.py:94
  329.3 14.7 %collective-permute-start.55 = (bf16[160,2048]{1,0:T(8,128)(2,1)S(1)}, bf16[160,2048]{1,0:T(8,128)(2,1)S(1)}, u32[]{:S(2)}, u32[]{:S(2)}) collective-permute-start(bf16[160,2048]{1,0:T(8,128)(2,1)S(1)} %fusion.5), channel_id=1, source_target_pairs={{0,4},{8,0},{16,8},{24,16},{28,24},{20,28},{12,20},{4,12},{1,5},{9... | collective-permute-start | bytes 1966088 | tf_op jit(solution)/shard_map/ppermute | solution.py:95
  343.3 10.6 %collective-permute-start.49 = (bf16[160,2048]{1,0:T(8,128)(2,1)S(1)}, bf16[160,2048]{1,0:T(8,128)(2,1)S(1)}, u32[]{:S(2)}, u32[]{:S(2)}) collective-permute-start(bf16[160,2048]{1,0:T(8,128)(2,1)S(1)} %fusion.10), channel_id=1, source_target_pairs={{0,8},{8,16},{16,24},{24,28},{28,20},{20,12},{12,4},{4,0},{1,9},{9... | collective-permute-start | bytes 1966088 | tf_op jit(solution)/shard_map/ppermute | solution.py:94
  344.1 11.3 %collective-permute-start.56 = (bf16[160,2048]{1,0:T(8,128)(2,1)S(1)}, bf16[160,2048]{1,0:T(8,128)(2,1)S(1)}, u32[]{:S(2)}, u32[]{:S(2)}) collective-permute-start(bf16[160,2048]{1,0:T(8,128)(2,1)S(1)} %fusion.4), channel_id=1, source_target_pairs={{0,4},{8,0},{16,8},{24,16},{28,24},{20,28},{12,20},{4,12},{1,5},{9... | collective-permute-start | bytes 1966088 | tf_op jit(solution)/shard_map/ppermute | solution.py:95
  (42 other events, 354.9 us)

commit v8 on v7

--- a/solution.py
+++ b/solution.py
@@ -218,6 +218,28 @@
     return mine + lax.ppermute(other.astype(jnp.bfloat16), axis, near).astype(jnp.float32)
 
 
+def direct_gather(value, axis):
+    count = lax.axis_size(axis)
+    got = [value] + [None] * (count - 1)
+    for shift in range(1, count):
+        pairs = [(i, (i + shift) % count) for i in range(count)]
+        got[count - shift] = lax.ppermute(value, axis, pairs)
+    return jnp.stack(got, axis=0)
+
+
+def direct_scatter(partial, axis):
+    count = lax.axis_size(axis)
+    rows = partial.shape[0] // count
+    blocks = partial.reshape(count, rows, partial.shape[1])
+    total = blocks[0]
+    for shift in range(1, count):
+        pairs = [(i, (i + shift) % count) for i in range(count)]
+        total = total + lax.ppermute(blocks[shift].astype(jnp.bfloat16), axis, pairs).astype(
+            jnp.float32
+        )
+    return total
+
+
 def butterfly_sum(value, axis):
     count = lax.axis_size(axis)
     stride = 1
@@ -269,7 +291,7 @@
     info = info.reshape(info_rows, pair_width).astype(jnp.bfloat16)
     packed = jnp.concatenate([keys, values], axis=1)
     packed = jnp.concatenate([packed, info], axis=0)
-    gathered = ring_gather(packed, ring, "ctx")
+    gathered = direct_gather(packed, "ctx")
     if tp_size == 4 and rows_ctx % (2 * tp_size) == 0:
         grad_rows = tp_scatter(grad_part, rows_mine, "tp").astype(jnp.bfloat16)
     else:
@@ -323,7 +345,7 @@
     value_part = across(prob.astype(jnp.bfloat16), grad_stack)
     pair_all = jnp.concatenate([key_part, value_part], axis=1)
     out_ring = Ring(out_weight_grad, ring, "ctx").advance(len(ring) // 2)
-    pair_grad = butterfly_sum(ring_scatter_relative(pair_all, ring, "ctx"), "tp")
+    pair_grad = butterfly_sum(direct_scatter(pair_all, "ctx"), "tp")
     out_ring.state, pair_grad = lax.optimization_barrier((out_ring.state, pair_grad))
 
     key_raw = rotate(pair_grad[:, :head_dim], cosine_all, -sine_all)

time: 359 us -> 359 us (level)
  starting transfers between devices: 57.9 us -> 64.3 us
  waiting for transfers between devices: 137 us -> 132 us
    ppermute x7, waiting for transfers between devices: 0.68 us -> 16.5 us  [ring_scatter(): got_right = lax.ppermute(send_right.astype(jnp.bfloat16), axis, backward)]
    ppermute x7, waiting for transfers between devices: 60.6 us -> 47.3 us  [ring_scatter(): got_left = lax.ppermute(send_left.astype(jnp.bfloat16), axis, forward)]
    ppermute x7, starting transfers between devices: 5.64 us -> 14.9 us  [ring_scatter(): got_left = lax.ppermute(send_left.astype(jnp.bfloat16), axis, forward)]
    ppermute x7, starting transfers between devices: 7.06 us -> 15.5 us  [advance(): lax.ppermute(send_left.astype(jnp.bfloat16), self.axis, self.forward)]
    ppermute x7, starting transfers between devices: 9.13 us -> 1.44 us  [ring_scatter(): got_right = lax.ppermute(send_right.astype(jnp.bfloat16), axis, backward)]
    ppermute x1, waiting for transfers between devices: 5.6 us -> 0.01 us  [tp_scatter(): lax.ppermute(sent.astype(jnp.bfloat16), axis, far).astype(jnp.float32)]
    convert_element_type x5, other arithmetic: 3.91 us -> 8.54 us  [advance(): send_left.astype(jnp.bfloat16)]
    ppermute x1, waiting for transfers between devices: 4.03 us -> 0.01 us  [tp_project(): own_head = mine + lax.ppermute(theirs, axis, far)]
  transfers between devices with their start and end apart: 57 -> 50, of which waited for: 29 -> 33; matrix products, arithmetic and copies ran while one was open for 20% -> 19% of each run, Pallas kernels for 0% -> 0%
where the time goes in v8:
time: 359 us; the launch traced here: 357 us
  waiting for transfers between devices  132 us (37%)
  starting transfers between devices  64.3 us (18%)
  other arithmetic  47.4 us (13%)
  between operations  37.4 us (10%)
  matrix products  34.6 us (10%)
  local copies, waits for them, and re-layouts  28.1 us (8%)
  blocking collectives  13.9 us (4%)
    ppermute x7, waiting for transfers between devices, ring_scatter(): got_left = lax.ppermute(send_left.astype(jnp.bfloat16), axis, forward)  47.3 us
    ppermute x7, waiting for transfers between devices, advance(): lax.ppermute(send_right.astype(jnp.bfloat16), self.axis, self.backward)  35 us
    ppermute x7, waiting for transfers between devices, ring_scatter(): got_right = lax.ppermute(send_right.astype(jnp.bfloat16), axis, backward)  16.5 us
    ppermute x7, waiting for transfers between devices, direct_gather(): got[count - shift] = lax.ppermute(value, axis, pairs)  16.1 us
    ppermute x7, starting transfers between devices, advance(): lax.ppermute(send_left.astype(jnp.bfloat16), self.axis, self.forward)  15.5 us
    dot_general x4, matrix products, against(): lax.dot_general(left, right, (((1,), (1,)), ((), ())), preferred_element_...  14.9 us
    ppermute x7, starting transfers between devices, ring_scatter(): got_left = lax.ppermute(send_left.astype(jnp.bfloat16), axis, forward)  14.9 us
    ppermute x7, starting transfers between devices, direct_gather(): got[count - shift] = lax.ppermute(value, axis, pairs)  12.2 us
  transfers between devices with their start and end apart: 50, of which 33 were waited for; matrix products, arithmetic and copies ran while one was open for 19% of the time, Pallas kernels for 0%

profile of v8, /device:TPU:0, one launch (start us, length us, event | category | flops | bytes accessed | tf_op | source)
XLA Modules:
  0.0 357.2 jit_solution(18087477965783857097)
XLA Ops:
  2.2 6.9 %fusion.70 = f32[256,1280]{1,0:T(8,128)S(1)} fusion(bf16[256,4096]{1,0:T(8,128)(2,1)S(1)} %copy-done, bf16[1280,4096]{1,0:T(8,128)(2,1)} %param.13), kind=kOutput, calls=%fused_computation.172 | convolution fusion | flops 2684354560 | bytes 13893632 | tf_op jit(solution)/shard_map/dot_general | solution.py:35
  9.6 6.4 %convolution_convert_fusion.2 = bf16[256,1024]{1,0:T(8,128)(2,1)S(1)} fusion(bf16[256,4096]{1,0:T(8,128)(2,1)} %param.15, bf16[1024,4096]{1,0:T(8,128)(2,1)} %param.14), kind=kOutput, calls=%fused_computation.45 | convolution fusion | flops 2147745792 | bytes 11010048 | tf_op jit(solution)/shard_map/dot_general | solution.py:35
  45.1 4.2 %collective-permute-done.1 = f32[128,256]{1,0:T(8,128)S(1)} collective-permute-done((f32[128,256]{1,0:T(8,128)S(1)}, f32[128,256]{1,0:T(8,128)S(1)}, u32[]{:S(2)}, u32[]{:S(2)}) %collective-permute-start.1) | collective-permute-done | bytes 131104 | tf_op jit(solution)/shard_map/ppermute | solution.py:197
  51.5 4.6 %collective-permute-start.3 = (bf16[259,256]{1,0:T(8,128)(2,1)S(1)}, bf16[259,256]{1,0:T(8,128)(2,1)S(1)}, u32[]{:S(2)}, u32[]{:S(2)}) collective-permute-start(bf16[259,256]{1,0:T(8,128)(2,1)S(1)} %get-tuple-element.19), channel_id=1, source_target_pairs={{0,28},{4,0},{8,4},{12,8},{16,12},{20,16},{24,20},{28,24},{1,29},{... | collective-permute-start | bytes 397832 | tf_op jit(solution)/shard_map/ppermute | solution.py:226
  56.5 3.0 collective-permute-start.6
  65.9 13.5 %collective-permute-done.6 = bf16[259,256]{1,0:T(8,128)(2,1)S(1)} collective-permute-done((bf16[259,256]{1,0:T(8,128)(2,1)S(1)}, bf16[259,256]{1,0:T(8,128)(2,1)S(1)}, u32[]{:S(2)}, u32[]{:S(2)}) %collective-permute-start.6) | collective-permute-done | bytes 132640 | tf_op jit(solution)/shard_map/ppermute | solution.py:226
  88.6 6.7 %all_gather.6 = bf16[256,1024]{1,0:T(8,128)(2,1)S(1)} all-gather(bf16[64,1024]{1,0:T(8,128)(2,1)S(1)} %bitcast.244), channel_id=1, replica_groups=mesh['ctx'=8,'tp'=4] {'tp'}, dimensions={0}, use_global_device_ids=true | all-gather | bytes 655360 | tf_op jit(solution)/shard_map/all_gather | solution.py:332
  97.7 6.3 %fusion.65 = (f32[8,128,2048]{2,1,0:T(8,128)}, f32[8,128,2048]{2,1,0:T(8,128)}) fusion(f32[8,128,4096]{2,1,0:T(8,128)S(1)} %bitcast.233), kind=kLoop, calls=%fused_computation.167 | loop fusion | bytes 33554432 | tf_op jit(solution)/shard_map/slice | solution.py:157
  113.0 6.6 %collective-permute-done.17 = bf16[128,2048]{1,0:T(8,128)(2,1)S(1)} collective-permute-done((bf16[128,2048]{1,0:T(8,128)(2,1)S(1)}, bf16[128,2048]{1,0:T(8,128)(2,1)S(1)}, u32[]{:S(2)}, u32[]{:S(2)}) %collective-permute-start.17) | collective-permute-done | bytes 524320 | tf_op jit(solution)/shard_map/ppermute | solution.py:172
  119.6 3.1 collective-permute-start.24
  125.0 3.3 collective-permute-start.26
  128.3 7.6 %collective-permute-done.23 = bf16[256,256]{1,0:T(8,128)(2,1)S(1)} collective-permute-done((bf16[256,256]{1,0:T(8,128)(2,1)S(1)}, bf16[256,256]{1,0:T(8,128)(2,1)S(1)}, u32[]{:S(2)}, u32[]{:S(2)}) %collective-permute-start.23) | collective-permute-done | bytes 131104 | tf_op jit(solution)/shard_map/ppermute | solution.py:237
  142.3 8.2 %collective-permute-done.18 = bf16[128,2048]{1,0:T(8,128)(2,1)S(1)} collective-permute-done((bf16[128,2048]{1,0:T(8,128)(2,1)S(1)}, bf16[128,2048]{1,0:T(8,128)(2,1)S(1)}, u32[]{:S(2)}, u32[]{:S(2)}) %collective-permute-start.18) | collective-permute-done | bytes 524320 | tf_op jit(solution)/shard_map/ppermute | solution.py:172
  156.1 4.0 %collective-permute-start.15 = (bf16[128,2048]{1,0:T(8,128)(2,1)}, bf16[128,2048]{1,0:T(8,128)(2,1)}, u32[]{:S(2)}, u32[]{:S(2)}) collective-permute-start(bf16[128,2048]{1,0:T(8,128)(2,1)} %fusion.26), channel_id=1, source_target_pairs={{0,8},{8,16},{16,24},{24,28},{28,20},{20,12},{12,4},{4,0},{1,9},{9... | collective-permute-start | bytes 1572872 | tf_op jit(solution)/shard_map/ppermute | solution.py:171
  184.6 7.8 %collective-permute-done.20 = bf16[128,2048]{1,0:T(8,128)(2,1)S(1)} collective-permute-done((bf16[128,2048]{1,0:T(8,128)(2,1)S(1)}, bf16[128,2048]{1,0:T(8,128)(2,1)S(1)}, u32[]{:S(2)}, u32[]{:S(2)}) %collective-permute-start.20) | collective-permute-done | bytes 524320 | tf_op jit(solution)/shard_map/ppermute | solution.py:172
  197.7 7.2 %all_gather.7 = bf16[256,1024]{1,0:T(8,128)(2,1)} all-gather(bf16[64,1024]{1,0:T(8,128)(2,1)S(1)} %copy_bitcast_fusion.1), channel_id=1, replica_groups=mesh['ctx'=8,'tp'=4] {'tp'}, dimensions={0}, use_global_device_ids=true | all-gather | bytes 655360 | tf_op jit(solution)/shard_map/all_gather | solution.py:356
  204.8 2.8 collective-permute-done.33
  215.7 5.8 %collective-permute-done.34 = bf16[128,2048]{1,0:T(8,128)(2,1)} collective-permute-done((bf16[128,2048]{1,0:T(8,128)(2,1)}, bf16[128,2048]{1,0:T(8,128)(2,1)}, u32[]{:S(2)}, u32[]{:S(2)}) %collective-permute-start.34) | collective-permute-done | bytes 524320 | tf_op jit(solution)/shard_map/ppermute | solution.py:172
  227.0 2.9 fusion.73
  229.9 3.8 %collective-permute-done.35 = bf16[128,2048]{1,0:T(8,128)(2,1)S(1)} collective-permute-done((bf16[128,2048]{1,0:T(8,128)(2,1)S(1)}, bf16[128,2048]{1,0:T(8,128)(2,1)S(1)}, u32[]{:S(2)}, u32[]{:S(2)}) %collective-permute-start.35) | collective-permute-done | bytes 524320 | tf_op jit(solution)/shard_map/ppermute | solution.py:172
  237.5 8.1 %fusion.64 = (f32[8,160,2048]{2,1,0:T(8,128)}, f32[8,160,2048]{2,1,0:T(8,128)}) fusion(f32[8,160,4096]{2,1,0:T(8,128)S(1)} %bitcast.232), kind=kLoop, calls=%fused_computation.166 | loop fusion | bytes 41943040 | tf_op jit(solution)/shard_map/slice | solution.py:83
  251.4 8.3 %collective-permute-done.36 = bf16[160,2048]{1,0:T(8,128)(2,1)S(1)} collective-permute-done((bf16[160,2048]{1,0:T(8,128)(2,1)S(1)}, bf16[160,2048]{1,0:T(8,128)(2,1)S(1)}, u32[]{:S(2)}, u32[]{:S(2)}) %collective-permute-start.36) | collective-permute-done | bytes 655392 | tf_op jit(solution)/shard_map/ppermute | solution.py:94
  265.3 9.3 %collective-permute-done.37 = bf16[160,2048]{1,0:T(8,128)(2,1)S(1)} collective-permute-done((bf16[160,2048]{1,0:T(8,128)(2,1)S(1)}, bf16[160,2048]{1,0:T(8,128)(2,1)S(1)}, u32[]{:S(2)}, u32[]{:S(2)}) %collective-permute-start.37) | collective-permute-done | bytes 655392 | tf_op jit(solution)/shard_map/ppermute | solution.py:94
  280.2 9.3 %collective-permute-done.38 = bf16[160,2048]{1,0:T(8,128)(2,1)S(1)} collective-permute-done((bf16[160,2048]{1,0:T(8,128)(2,1)S(1)}, bf16[160,2048]{1,0:T(8,128)(2,1)S(1)}, u32[]{:S(2)}, u32[]{:S(2)}) %collective-permute-start.38) | collective-permute-done | bytes 655392 | tf_op jit(solution)/shard_map/ppermute | solution.py:94
  295.1 9.3 %collective-permute-done.39 = bf16[160,2048]{1,0:T(8,128)(2,1)S(1)} collective-permute-done((bf16[160,2048]{1,0:T(8,128)(2,1)S(1)}, bf16[160,2048]{1,0:T(8,128)(2,1)S(1)}, u32[]{:S(2)}, u32[]{:S(2)}) %collective-permute-start.39) | collective-permute-done | bytes 655392 | tf_op jit(solution)/shard_map/ppermute | solution.py:94
  310.7 7.2 %convolution_convert_fusion = bf16[256,4096]{1,0:T(8,128)(2,1)} fusion(bf16[256,1024]{1,0:T(8,128)(2,1)S(1)} %all_gather.6, bf16[1024,4096]{1,0:T(8,128)(2,1)} %param.14), kind=kOutput, calls=%fused_computation.3 | convolution fusion | flops 2148532224 | bytes 11010048 | tf_op jit(solution)/shard_map/dot_general | solution.py:333
  323.9 3.0 collective-permute-done.47
  327.2 4.1 %convolution_convert_fusion.1 = bf16[256,4096]{1,0:T(8,128)(2,1)} fusion(bf16[256,1280]{1,0:T(8,128)(2,1)S(1)} %concatenate.45, bf16[1280,4096]{1,0:T(8,128)(2,1)S(1)} %bitcast.251), kind=kOutput, calls=%fused_computation.4 | convolution fusion | flops 2685403136 | bytes 13238272 | tf_op jit(solution)/shard_map/dot_general | solution.py:361
  331.3 5.3 %collective-permute-done.41 = bf16[160,2048]{1,0:T(8,128)(2,1)S(1)} collective-permute-done((bf16[160,2048]{1,0:T(8,128)(2,1)S(1)}, bf16[160,2048]{1,0:T(8,128)(2,1)S(1)}, u32[]{:S(2)}, u32[]{:S(2)}) %collective-permute-start.41) | collective-permute-done | bytes 655392 | tf_op jit(solution)/shard_map/ppermute | solution.py:94
  338.1 3.6 %collective-permute-start.42 = (bf16[160,2048]{1,0:T(8,128)(2,1)S(1)}, bf16[160,2048]{1,0:T(8,128)(2,1)S(1)}, u32[]{:S(2)}, u32[]{:S(2)}) collective-permute-start(bf16[160,2048]{1,0:T(8,128)(2,1)S(1)} %fusion.11), channel_id=1, source_target_pairs={{0,8},{8,16},{16,24},{24,28},{28,20},{20,12},{12,4},{4,0},{1,9},{9... | collective-permute-start | bytes 1966088 | tf_op jit(solution)/shard_map/ppermute | solution.py:94
  346.0 3.8 %collective-permute-done.42 = bf16[160,2048]{1,0:T(8,128)(2,1)S(1)} collective-permute-done((bf16[160,2048]{1,0:T(8,128)(2,1)S(1)}, bf16[160,2048]{1,0:T(8,128)(2,1)S(1)}, u32[]{:S(2)}, u32[]{:S(2)}) %collective-permute-start.42) | collective-permute-done | bytes 655392 | tf_op jit(solution)/shard_map/ppermute | solution.py:94
  351.3 3.7 %collective-permute-done.49 = bf16[160,2048]{1,0:T(8,128)(2,1)S(1)} collective-permute-done((bf16[160,2048]{1,0:T(8,128)(2,1)S(1)}, bf16[160,2048]{1,0:T(8,128)(2,1)S(1)}, u32[]{:S(2)}, u32[]{:S(2)}) %collective-permute-start.49) | collective-permute-done | bytes 655392 | tf_op jit(solution)/shard_map/ppermute | solution.py:95
  (211 shorter events, 130.2 us)
Async XLA Ops:
  9.1 33.0 %collective-permute-start = (f32[256,1280]{1,0:T(8,128)S(1)}, f32[256,1280]{1,0:T(8,128)}, u32[]{:S(2)}, u32[]{:S(2)}) collective-permute-start(f32[256,1280]{1,0:T(8,128)S(1)} %fusion.70), channel_id=1, source_target_pairs={{0,1},{1,0},{2,3},{3,2},{4,5},{5,4},{6,7},{7,6},{8,9},{9,8},{10,11... | collective-permute-start | bytes 3932168 | tf_op jit(solution)/shard_map/ppermute | solution.py:189
  17.6 26.1 %collective-permute-start.11 = (bf16[128,1024]{1,0:T(8,128)(2,1)}, bf16[128,1024]{1,0:T(8,128)(2,1)}, u32[]{:S(2)}, u32[]{:S(2)}) collective-permute-start(bf16[128,1024]{1,0:T(8,128)(2,1)} %constant_dynamic-slice_fusion), channel_id=1, source_target_pairs={{0,2},{1,3},{2,0},{3,1},{4,6},{5,7},{6,4},{7,5},{8,10},{9,11},{10,... | collective-permute-start | bytes 786440 | tf_op jit(solution)/shard_map/ppermute | solution.py:212
  56.5 22.9 %collective-permute-start.6 = (bf16[259,256]{1,0:T(8,128)(2,1)S(1)}, bf16[259,256]{1,0:T(8,128)(2,1)S(1)}, u32[]{:S(2)}, u32[]{:S(2)}) collective-permute-start(bf16[259,256]{1,0:T(8,128)(2,1)S(1)} %get-tuple-element.19), channel_id=1, source_target_pairs={{0,16},{4,20},{8,24},{12,28},{16,0},{20,4},{24,8},{28,12},{1,17},{... | collective-permute-start | bytes 397832 | tf_op jit(solution)/shard_map/ppermute | solution.py:226
  60.2 20.7 %collective-permute-start.7 = (bf16[259,256]{1,0:T(8,128)(2,1)S(1)}, bf16[259,256]{1,0:T(8,128)(2,1)S(1)}, u32[]{:S(2)}, u32[]{:S(2)}) collective-permute-start(bf16[259,256]{1,0:T(8,128)(2,1)S(1)} %get-tuple-element.19), channel_id=1, source_target_pairs={{0,12},{4,16},{8,20},{12,24},{16,28},{20,0},{24,4},{28,8},{1,13},{... | collective-permute-start | bytes 397832 | tf_op jit(solution)/shard_map/ppermute | solution.py:226
  61.3 19.6 %collective-permute-start.8 = (bf16[259,256]{1,0:T(8,128)(2,1)S(1)}, bf16[259,256]{1,0:T(8,128)(2,1)S(1)}, u32[]{:S(2)}, u32[]{:S(2)}) collective-permute-start(bf16[259,256]{1,0:T(8,128)(2,1)S(1)} %get-tuple-element.19), channel_id=1, source_target_pairs={{0,8},{4,12},{8,16},{12,20},{16,24},{20,28},{24,0},{28,4},{1,9},{5... | collective-permute-start | bytes 397832 | tf_op jit(solution)/shard_map/ppermute | solution.py:226
  63.0 17.9 %collective-permute-start.9 = (bf16[259,256]{1,0:T(8,128)(2,1)S(1)}, bf16[259,256]{1,0:T(8,128)(2,1)S(1)}, u32[]{:S(2)}, u32[]{:S(2)}) collective-permute-start(bf16[259,256]{1,0:T(8,128)(2,1)S(1)} %get-tuple-element.19), channel_id=1, source_target_pairs={{0,4},{4,8},{8,12},{12,16},{16,20},{20,24},{24,28},{28,0},{1,5},{5... | collective-permute-start | bytes 397832 | tf_op jit(solution)/shard_map/ppermute | solution.py:226
  105.3 14.2 %collective-permute-start.17 = (bf16[128,2048]{1,0:T(8,128)(2,1)S(1)}, bf16[128,2048]{1,0:T(8,128)(2,1)S(1)}, u32[]{:S(2)}, u32[]{:S(2)}) collective-permute-start(bf16[128,2048]{1,0:T(8,128)(2,1)S(1)} %fusion.31), channel_id=1, source_target_pairs={{0,4},{8,0},{16,8},{24,16},{28,24},{20,28},{12,20},{4,12},{1,5},{9... | collective-permute-start | bytes 1572872 | tf_op jit(solution)/shard_map/ppermute | solution.py:172
  106.7 29.2 %collective-permute-start.13 = (bf16[128,2048]{1,0:T(8,128)(2,1)S(1)}, bf16[128,2048]{1,0:T(8,128)(2,1)S(1)}, u32[]{:S(2)}, u32[]{:S(2)}) collective-permute-start(bf16[128,2048]{1,0:T(8,128)(2,1)S(1)} %fusion.30), channel_id=1, source_target_pairs={{0,8},{8,16},{16,24},{24,28},{28,20},{20,12},{12,4},{4,0},{1,9},{9... | collective-permute-start | bytes 1572872 | tf_op jit(solution)/shard_map/ppermute | solution.py:171
  108.9 15.2 %collective-permute-start.21 = (bf16[256,256]{1,0:T(8,128)(2,1)S(1)}, bf16[256,256]{1,0:T(8,128)(2,1)S(1)}, u32[]{:S(2)}, u32[]{:S(2)}) collective-permute-start(bf16[256,256]{1,0:T(8,128)(2,1)S(1)} %get-tuple-element.30), channel_id=1, source_target_pairs={{0,4},{4,8},{8,12},{12,16},{16,20},{20,24},{24,28},{28,0},{1,5},{5... | collective-permute-start | bytes 393224 | tf_op jit(solution)/shard_map/ppermute | solution.py:237
  109.0 16.0 %collective-permute-start.22 = (bf16[256,256]{1,0:T(8,128)(2,1)S(1)}, bf16[256,256]{1,0:T(8,128)(2,1)S(1)}, u32[]{:S(2)}, u32[]{:S(2)}) collective-permute-start(bf16[256,256]{1,0:T(8,128)(2,1)S(1)} %get-tuple-element.36), channel_id=1, source_target_pairs={{0,8},{4,12},{8,16},{12,20},{16,24},{20,28},{24,0},{28,4},{1,9},{5... | collective-permute-start | bytes 393224 | tf_op jit(solution)/shard_map/ppermute | solution.py:237
  110.1 25.8 %collective-permute-start.23 = (bf16[256,256]{1,0:T(8,128)(2,1)S(1)}, bf16[256,256]{1,0:T(8,128)(2,1)S(1)}, u32[]{:S(2)}, u32[]{:S(2)}) collective-permute-start(bf16[256,256]{1,0:T(8,128)(2,1)S(1)} %get-tuple-element.35), channel_id=1, source_target_pairs={{0,12},{4,16},{8,20},{12,24},{16,28},{20,0},{24,4},{28,8},{1,13},{... | collective-permute-start | bytes 393224 | tf_op jit(solution)/shard_map/ppermute | solution.py:237
  119.6 19.7 %collective-permute-start.24 = (bf16[256,256]{1,0:T(8,128)(2,1)S(1)}, bf16[256,256]{1,0:T(8,128)(2,1)S(1)}, u32[]{:S(2)}, u32[]{:S(2)}) collective-permute-start(bf16[256,256]{1,0:T(8,128)(2,1)S(1)} %get-tuple-element.34), channel_id=1, source_target_pairs={{0,16},{4,20},{8,24},{12,28},{16,0},{20,4},{24,8},{28,12},{1,17},{... | collective-permute-start | bytes 393224 | tf_op jit(solution)/shard_map/ppermute | solution.py:237
  124.2 17.6 %collective-permute-start.25 = (bf16[256,256]{1,0:T(8,128)(2,1)S(1)}, bf16[256,256]{1,0:T(8,128)(2,1)S(1)}, u32[]{:S(2)}, u32[]{:S(2)}) collective-permute-start(bf16[256,256]{1,0:T(8,128)(2,1)S(1)} %get-tuple-element.33), channel_id=1, source_target_pairs={{0,20},{4,24},{8,28},{12,0},{16,4},{20,8},{24,12},{28,16},{1,21},{... | collective-permute-start | bytes 393224 | tf_op jit(solution)/shard_map/ppermute | solution.py:237
  125.0 16.8 %collective-permute-start.26 = (bf16[256,256]{1,0:T(8,128)(2,1)S(1)}, bf16[256,256]{1,0:T(8,128)(2,1)S(1)}, u32[]{:S(2)}, u32[]{:S(2)}) collective-permute-start(bf16[256,256]{1,0:T(8,128)(2,1)S(1)} %get-tuple-element.32), channel_id=1, source_target_pairs={{0,24},{4,28},{8,0},{12,4},{16,8},{20,12},{24,16},{28,20},{1,25},{... | collective-permute-start | bytes 393224 | tf_op jit(solution)/shard_map/ppermute | solution.py:237
  135.9 14.5 %collective-permute-start.18 = (bf16[128,2048]{1,0:T(8,128)(2,1)S(1)}, bf16[128,2048]{1,0:T(8,128)(2,1)S(1)}, u32[]{:S(2)}, u32[]{:S(2)}) collective-permute-start(bf16[128,2048]{1,0:T(8,128)(2,1)S(1)} %fusion.24), channel_id=1, source_target_pairs={{0,4},{8,0},{16,8},{24,16},{28,24},{20,28},{12,20},{4,12},{1,5},{9... | collective-permute-start | bytes 1572872 | tf_op jit(solution)/shard_map/ppermute | solution.py:172
  139.3 14.7 %collective-permute-start.14 = (bf16[128,2048]{1,0:T(8,128)(2,1)S(1)}, bf16[128,2048]{1,0:T(8,128)(2,1)S(1)}, u32[]{:S(2)}, u32[]{:S(2)}) collective-permute-start(bf16[128,2048]{1,0:T(8,128)(2,1)S(1)} %fusion.27), channel_id=1, source_target_pairs={{0,8},{8,16},{16,24},{24,28},{28,20},{20,12},{12,4},{4,0},{1,9},{9... | collective-permute-start | bytes 1572872 | tf_op jit(solution)/shard_map/ppermute | solution.py:171
  142.2 33.3 %collective-permute-start.28 = (f32[256,256]{1,0:T(8,128)S(1)}, f32[256,256]{1,0:T(8,128)}, u32[]{:S(2)}, u32[]{:S(2)}) collective-permute-start(f32[256,256]{1,0:T(8,128)S(1)} %fusion.39), channel_id=1, source_target_pairs={{0,1},{1,0},{2,3},{3,2},{4,5},{5,4},{6,7},{7,6},{8,9},{9,8},{10,11... | collective-permute-start | bytes 786440 | tf_op jit(solution)/shard_map/ppermute | solution.py:248
  152.5 25.0 %collective-permute-start.19 = (bf16[128,2048]{1,0:T(8,128)(2,1)}, bf16[128,2048]{1,0:T(8,128)(2,1)}, u32[]{:S(2)}, u32[]{:S(2)}) collective-permute-start(bf16[128,2048]{1,0:T(8,128)(2,1)} %fusion.23), channel_id=1, source_target_pairs={{0,4},{8,0},{16,8},{24,16},{28,24},{20,28},{12,20},{4,12},{1,5},{9... | collective-permute-start | bytes 1572872 | tf_op jit(solution)/shard_map/ppermute | solution.py:172
  156.1 23.0 %collective-permute-start.15 = (bf16[128,2048]{1,0:T(8,128)(2,1)}, bf16[128,2048]{1,0:T(8,128)(2,1)}, u32[]{:S(2)}, u32[]{:S(2)}) collective-permute-start(bf16[128,2048]{1,0:T(8,128)(2,1)} %fusion.26), channel_id=1, source_target_pairs={{0,8},{8,16},{16,24},{24,28},{28,20},{20,12},{12,4},{4,0},{1,9},{9... | collective-permute-start | bytes 1572872 | tf_op jit(solution)/shard_map/ppermute | solution.py:171
  179.0 13.3 %collective-permute-start.20 = (bf16[128,2048]{1,0:T(8,128)(2,1)S(1)}, bf16[128,2048]{1,0:T(8,128)(2,1)S(1)}, u32[]{:S(2)}, u32[]{:S(2)}) collective-permute-start(bf16[128,2048]{1,0:T(8,128)(2,1)S(1)} %fusion.22), channel_id=1, source_target_pairs={{0,4},{8,0},{16,8},{24,16},{28,24},{20,28},{12,20},{4,12},{1,5},{9... | collective-permute-start | bytes 1572872 | tf_op jit(solution)/shard_map/ppermute | solution.py:172
  195.7 14.5 %collective-permute-start.30 = (bf16[128,2048]{1,0:T(8,128)(2,1)S(1)}, bf16[128,2048]{1,0:T(8,128)(2,1)S(1)}, u32[]{:S(2)}, u32[]{:S(2)}) collective-permute-start(bf16[128,2048]{1,0:T(8,128)(2,1)S(1)} %bitcast_add_fusion.24), channel_id=1, source_target_pairs={{0,8},{8,16},{16,24},{24,28},{28,20},{20,12},{12,4},{4,0},{1,9},{9... | collective-permute-start | bytes 1572872 | tf_op jit(solution)/shard_map/ppermute | solution.py:171
  250.3 13.4 %collective-permute-start.43 = (bf16[160,2048]{1,0:T(8,128)(2,1)S(1)}, bf16[160,2048]{1,0:T(8,128)(2,1)S(1)}, u32[]{:S(2)}, u32[]{:S(2)}) collective-permute-start(bf16[160,2048]{1,0:T(8,128)(2,1)S(1)} %fusion.29), channel_id=1, source_target_pairs={{0,4},{8,0},{16,8},{24,16},{28,24},{20,28},{12,20},{4,12},{1,5},{9... | collective-permute-start | bytes 1966088 | tf_op jit(solution)/shard_map/ppermute | solution.py:95
  261.2 13.4 %collective-permute-start.37 = (bf16[160,2048]{1,0:T(8,128)(2,1)S(1)}, bf16[160,2048]{1,0:T(8,128)(2,1)S(1)}, u32[]{:S(2)}, u32[]{:S(2)}) collective-permute-start(bf16[160,2048]{1,0:T(8,128)(2,1)S(1)} %fusion.16), channel_id=1, source_target_pairs={{0,8},{8,16},{16,24},{24,28},{28,20},{20,12},{12,4},{4,0},{1,9},{9... | collective-permute-start | bytes 1966088 | tf_op jit(solution)/shard_map/ppermute | solution.py:94
  265.2 14.7 %collective-permute-start.44 = (bf16[160,2048]{1,0:T(8,128)(2,1)S(1)}, bf16[160,2048]{1,0:T(8,128)(2,1)S(1)}, u32[]{:S(2)}, u32[]{:S(2)}) collective-permute-start(bf16[160,2048]{1,0:T(8,128)(2,1)S(1)} %fusion.10), channel_id=1, source_target_pairs={{0,4},{8,0},{16,8},{24,16},{28,24},{20,28},{12,20},{4,12},{1,5},{9... | collective-permute-start | bytes 1966088 | tf_op jit(solution)/shard_map/ppermute | solution.py:95
  276.1 13.4 %collective-permute-start.38 = (bf16[160,2048]{1,0:T(8,128)(2,1)S(1)}, bf16[160,2048]{1,0:T(8,128)(2,1)S(1)}, u32[]{:S(2)}, u32[]{:S(2)}) collective-permute-start(bf16[160,2048]{1,0:T(8,128)(2,1)S(1)} %fusion.15), channel_id=1, source_target_pairs={{0,8},{8,16},{16,24},{24,28},{28,20},{20,12},{12,4},{4,0},{1,9},{9... | collective-permute-start | bytes 1966088 | tf_op jit(solution)/shard_map/ppermute | solution.py:94
  280.1 14.7 %collective-permute-start.45 = (bf16[160,2048]{1,0:T(8,128)(2,1)S(1)}, bf16[160,2048]{1,0:T(8,128)(2,1)S(1)}, u32[]{:S(2)}, u32[]{:S(2)}) collective-permute-start(bf16[160,2048]{1,0:T(8,128)(2,1)S(1)} %fusion.9), channel_id=1, source_target_pairs={{0,4},{8,0},{16,8},{24,16},{28,24},{20,28},{12,20},{4,12},{1,5},{9... | collective-permute-start | bytes 1966088 | tf_op jit(solution)/shard_map/ppermute | solution.py:95
  291.0 13.4 %collective-permute-start.39 = (bf16[160,2048]{1,0:T(8,128)(2,1)S(1)}, bf16[160,2048]{1,0:T(8,128)(2,1)S(1)}, u32[]{:S(2)}, u32[]{:S(2)}) collective-permute-start(bf16[160,2048]{1,0:T(8,128)(2,1)S(1)} %fusion.14), channel_id=1, source_target_pairs={{0,8},{8,16},{16,24},{24,28},{28,20},{20,12},{12,4},{4,0},{1,9},{9... | collective-permute-start | bytes 1966088 | tf_op jit(solution)/shard_map/ppermute | solution.py:94
  295.0 15.4 %collective-permute-start.46 = (bf16[160,2048]{1,0:T(8,128)(2,1)S(1)}, bf16[160,2048]{1,0:T(8,128)(2,1)S(1)}, u32[]{:S(2)}, u32[]{:S(2)}) collective-permute-start(bf16[160,2048]{1,0:T(8,128)(2,1)S(1)} %fusion.8), channel_id=1, source_target_pairs={{0,4},{8,0},{16,8},{24,16},{28,24},{20,28},{12,20},{4,12},{1,5},{9... | collective-permute-start | bytes 1966088 | tf_op jit(solution)/shard_map/ppermute | solution.py:95
  305.9 14.0 %collective-permute-start.40 = (bf16[160,2048]{1,0:T(8,128)(2,1)S(1)}, bf16[160,2048]{1,0:T(8,128)(2,1)S(1)}, u32[]{:S(2)}, u32[]{:S(2)}) collective-permute-start(bf16[160,2048]{1,0:T(8,128)(2,1)S(1)} %fusion.13), channel_id=1, source_target_pairs={{0,8},{8,16},{16,24},{24,28},{28,20},{20,12},{12,4},{4,0},{1,9},{9... | collective-permute-start | bytes 1966088 | tf_op jit(solution)/shard_map/ppermute | solution.py:94
  310.6 16.2 %collective-permute-start.47 = (bf16[160,2048]{1,0:T(8,128)(2,1)S(1)}, bf16[160,2048]{1,0:T(8,128)(2,1)S(1)}, u32[]{:S(2)}, u32[]{:S(2)}) collective-permute-start(bf16[160,2048]{1,0:T(8,128)(2,1)S(1)} %fusion.7), channel_id=1, source_target_pairs={{0,4},{8,0},{16,8},{24,16},{28,24},{20,28},{12,20},{4,12},{1,5},{9... | collective-permute-start | bytes 1966088 | tf_op jit(solution)/shard_map/ppermute | solution.py:95
  321.4 15.2 %collective-permute-start.41 = (bf16[160,2048]{1,0:T(8,128)(2,1)S(1)}, bf16[160,2048]{1,0:T(8,128)(2,1)S(1)}, u32[]{:S(2)}, u32[]{:S(2)}) collective-permute-start(bf16[160,2048]{1,0:T(8,128)(2,1)S(1)} %fusion.12), channel_id=1, source_target_pairs={{0,8},{8,16},{16,24},{24,28},{28,20},{20,12},{12,4},{4,0},{1,9},{9... | collective-permute-start | bytes 1966088 | tf_op jit(solution)/shard_map/ppermute | solution.py:94
  327.1 17.2 %collective-permute-start.48 = (bf16[160,2048]{1,0:T(8,128)(2,1)S(1)}, bf16[160,2048]{1,0:T(8,128)(2,1)S(1)}, u32[]{:S(2)}, u32[]{:S(2)}) collective-permute-start(bf16[160,2048]{1,0:T(8,128)(2,1)S(1)} %fusion.6), channel_id=1, source_target_pairs={{0,4},{8,0},{16,8},{24,16},{28,24},{20,28},{12,20},{4,12},{1,5},{9... | collective-permute-start | bytes 1966088 | tf_op jit(solution)/shard_map/ppermute | solution.py:95
  (36 other events, 352.9 us)

commit v9 on v8

--- a/solution.py
+++ b/solution.py
@@ -333,6 +333,7 @@
     out = jnp.dot(piece, w_out, preferred_element_type=jnp.float32).astype(jnp.bfloat16)
     out_weight_grad = across(piece, grad_out)
 
+    out, grad_rows = lax.optimization_barrier((out, grad_rows))
     grad_stack = jnp.transpose(grad_rows.reshape(rows_mine, heads, head_dim), (1, 0, 2)).reshape(
         stacked, head_dim
     )
@@ -361,7 +362,9 @@
     grad_x = jnp.dot(d_qkv, w_qkv, preferred_element_type=jnp.float32).astype(jnp.bfloat16)
     joint_weight = across(d_qkv, tokens)
     out_ring.advance(len(ring) - 1)
-    out_ring.state, joint_weight = lax.optimization_barrier((out_ring.state, joint_weight))
+    out_ring.state, joint_weight, grad_x = lax.optimization_barrier(
+        (out_ring.state, joint_weight, grad_x)
+    )
     grad_w_qkv = ring_scatter(joint_weight, ring, "ctx")
     grad_w_out = out_ring.result()
     return (out, grad_x, grad_w_qkv, grad_w_out)

time: 359 us -> 379 us (1.056)
  starting transfers between devices: 64.3 us -> 93.4 us
  other arithmetic: 47.4 us -> 41.3 us
    ppermute x7, waiting for transfers between devices: 1.74 us -> 22.7 us  [advance(): lax.ppermute(send_left.astype(jnp.bfloat16), self.axis, self.forward)]
    ppermute x7, waiting for transfers between devices: 47.3 us -> 65.8 us  [ring_scatter(): got_left = lax.ppermute(send_left.astype(jnp.bfloat16), axis, forward)]
    ppermute x7, starting transfers between devices: 10.5 us -> 27.5 us  [direct_scatter(): lax.ppermute(blocks[shift].astype(jnp.bfloat16), axis, pairs)]
    ppermute x7, waiting for transfers between devices: 35 us -> 18.9 us  [advance(): lax.ppermute(send_right.astype(jnp.bfloat16), self.axis, self.backward)]
    ppermute x7, waiting for transfers between devices: 16.5 us -> 3.27 us  [ring_scatter(): got_right = lax.ppermute(send_right.astype(jnp.bfloat16), axis, backward)]
    ppermute x7, waiting for transfers between devices: 8.87 us -> 1.31 us  [direct_scatter(): lax.ppermute(blocks[shift].astype(jnp.bfloat16), axis, pairs)]
    ppermute x7, starting transfers between devices: 12.2 us -> 18 us  [direct_gather(): got[count - shift] = lax.ppermute(value, axis, pairs)]
    ppermute x7, starting transfers between devices: 4.9 us -> 10.3 us  [advance(): lax.ppermute(send_right.astype(jnp.bfloat16), self.axis, self.backward)]
  transfers between devices with their start and end apart: 50 -> 50, of which waited for: 33 -> 27; matrix products, arithmetic and copies ran while one was open for 19% -> 15% of each run, Pallas kernels for 0% -> 0%
where the time goes in v9:
time: 379 us; the launch traced here: 377 us
  waiting for transfers between devices  131 us (35%)
  starting transfers between devices  93.4 us (25%)
  other arithmetic  41.3 us (11%)
  between operations  36.4 us (10%)
  matrix products  35.8 us (9%)
  local copies, waits for them, and re-layouts  25.8 us (7%)
  blocking collectives  13.4 us (4%)
    ppermute x7, waiting for transfers between devices, ring_scatter(): got_left = lax.ppermute(send_left.astype(jnp.bfloat16), axis, forward)  65.8 us
    ppermute x7, starting transfers between devices, direct_scatter(): lax.ppermute(blocks[shift].astype(jnp.bfloat16), axis, pairs)  27.5 us
    ppermute x7, waiting for transfers between devices, advance(): lax.ppermute(send_left.astype(jnp.bfloat16), self.axis, self.forward)  22.7 us
    ppermute x7, waiting for transfers between devices, advance(): lax.ppermute(send_right.astype(jnp.bfloat16), self.axis, self.backward)  18.9 us
    ppermute x7, starting transfers between devices, direct_gather(): got[count - shift] = lax.ppermute(value, axis, pairs)  18 us
    ppermute x7, starting transfers between devices, ring_scatter(): got_left = lax.ppermute(send_left.astype(jnp.bfloat16), axis, forward)  16.1 us
    dot_general x4, matrix products, against(): lax.dot_general(left, right, (((1,), (1,)), ((), ())), preferred_element_...  14.9 us
    ppermute x7, waiting for transfers between devices, direct_gather(): got[count - shift] = lax.ppermute(value, axis, pairs)  14.1 us
  transfers between devices with their start and end apart: 50, of which 27 were waited for; matrix products, arithmetic and copies ran while one was open for 15% of the time, Pallas kernels for 0%

profile of v9, /device:TPU:0, one launch (start us, length us, event | category | flops | bytes accessed | tf_op | source)
XLA Modules:
  0.0 377.3 jit_solution(17219259767724098018)
XLA Ops:
  2.2 6.9 %fusion.69 = f32[256,1280]{1,0:T(8,128)S(1)} fusion(bf16[256,4096]{1,0:T(8,128)(2,1)S(1)} %copy-done, bf16[1280,4096]{1,0:T(8,128)(2,1)} %param.13), kind=kOutput, calls=%fused_computation.171 | convolution fusion | flops 2684354560 | bytes 13893632 | tf_op jit(solution)/shard_map/dot_general | solution.py:35
  9.6 6.4 %convolution_convert_fusion.2 = bf16[256,1024]{1,0:T(8,128)(2,1)S(1)} fusion(bf16[256,4096]{1,0:T(8,128)(2,1)} %param.15, bf16[1024,4096]{1,0:T(8,128)(2,1)} %param.14), kind=kOutput, calls=%fused_computation.45 | convolution fusion | flops 2147745792 | bytes 11010048 | tf_op jit(solution)/shard_map/dot_general | solution.py:35
  59.5 4.2 %collective-permute-done.1 = f32[128,256]{1,0:T(8,128)S(1)} collective-permute-done((f32[128,256]{1,0:T(8,128)S(1)}, f32[128,256]{1,0:T(8,128)S(1)}, u32[]{:S(2)}, u32[]{:S(2)}) %collective-permute-start.1) | collective-permute-done | bytes 131104 | tf_op jit(solution)/shard_map/ppermute | solution.py:197
  77.8 5.5 %collective-permute-done.3 = bf16[259,256]{1,0:T(8,128)(2,1)S(1)} collective-permute-done((bf16[259,256]{1,0:T(8,128)(2,1)S(1)}, bf16[259,256]{1,0:T(8,128)(2,1)S(1)}, u32[]{:S(2)}, u32[]{:S(2)}) %collective-permute-start.3) | collective-permute-done | bytes 132640 | tf_op jit(solution)/shard_map/ppermute | solution.py:226
  84.7 6.1 %collective-permute-done.4 = bf16[259,256]{1,0:T(8,128)(2,1)S(1)} collective-permute-done((bf16[259,256]{1,0:T(8,128)(2,1)S(1)}, bf16[259,256]{1,0:T(8,128)(2,1)S(1)}, u32[]{:S(2)}, u32[]{:S(2)}) %collective-permute-start.4) | collective-permute-done | bytes 132640 | tf_op jit(solution)/shard_map/ppermute | solution.py:226
  90.9 5.8 %collective-permute-start.9 = (bf16[259,256]{1,0:T(8,128)(2,1)S(1)}, bf16[259,256]{1,0:T(8,128)(2,1)S(1)}, u32[]{:S(2)}, u32[]{:S(2)}) collective-permute-start(bf16[259,256]{1,0:T(8,128)(2,1)S(1)} %get-tuple-element.25), channel_id=1, source_target_pairs={{0,4},{4,8},{8,12},{12,16},{16,20},{20,24},{24,28},{28,0},{1,5},{5... | collective-permute-start | bytes 397832 | tf_op jit(solution)/shard_map/ppermute | solution.py:226
  103.0 6.7 %all_gather.6 = bf16[256,1024]{1,0:T(8,128)(2,1)S(1)} all-gather(bf16[64,1024]{1,0:T(8,128)(2,1)S(1)} %bitcast.244), channel_id=1, replica_groups=mesh['ctx'=8,'tp'=4] {'tp'}, dimensions={0}, use_global_device_ids=true | all-gather | bytes 655360 | tf_op jit(solution)/shard_map/all_gather | solution.py:332
  109.7 3.7 convolution_convert_fusion
  120.3 6.3 %fusion.64 = (f32[8,128,2048]{2,1,0:T(8,128)}, f32[8,128,2048]{2,1,0:T(8,128)}) fusion(f32[8,128,4096]{2,1,0:T(8,128)S(1)} %bitcast.233), kind=kLoop, calls=%fused_computation.166 | loop fusion | bytes 33554432 | tf_op jit(solution)/shard_map/slice | solution.py:157
  128.1 4.7 %collective-permute-start.13 = (bf16[128,2048]{1,0:T(8,128)(2,1)S(1)}, bf16[128,2048]{1,0:T(8,128)(2,1)S(1)}, u32[]{:S(2)}, u32[]{:S(2)}) collective-permute-start(bf16[128,2048]{1,0:T(8,128)(2,1)S(1)} %fusion.30), channel_id=1, source_target_pairs={{0,8},{8,16},{16,24},{24,28},{28,20},{20,12},{12,4},{4,0},{1,9},{9... | collective-permute-start | bytes 1572872 | tf_op jit(solution)/shard_map/ppermute | solution.py:171
  141.8 3.2 collective-permute-done.13
  145.0 6.2 %collective-permute-start.25 = (bf16[256,256]{1,0:T(8,128)(2,1)S(1)}, bf16[256,256]{1,0:T(8,128)(2,1)S(1)}, u32[]{:S(2)}, u32[]{:S(2)}) collective-permute-start(bf16[256,256]{1,0:T(8,128)(2,1)S(1)} %get-tuple-element.39), channel_id=1, source_target_pairs={{0,20},{4,24},{8,28},{12,0},{16,4},{20,8},{24,12},{28,16},{1,21},{... | collective-permute-start | bytes 393224 | tf_op jit(solution)/shard_map/ppermute | solution.py:237
  152.6 4.5 %collective-permute-start.24 = (bf16[256,256]{1,0:T(8,128)(2,1)S(1)}, bf16[256,256]{1,0:T(8,128)(2,1)S(1)}, u32[]{:S(2)}, u32[]{:S(2)}) collective-permute-start(bf16[256,256]{1,0:T(8,128)(2,1)S(1)} %get-tuple-element.40), channel_id=1, source_target_pairs={{0,16},{4,20},{8,24},{12,28},{16,0},{20,4},{24,8},{28,12},{1,17},{... | collective-permute-start | bytes 393224 | tf_op jit(solution)/shard_map/ppermute | solution.py:237
  157.1 2.8 collective-permute-start.23
  160.0 8.0 %collective-permute-start.22 = (bf16[256,256]{1,0:T(8,128)(2,1)S(1)}, bf16[256,256]{1,0:T(8,128)(2,1)S(1)}, u32[]{:S(2)}, u32[]{:S(2)}) collective-permute-start(bf16[256,256]{1,0:T(8,128)(2,1)S(1)} %get-tuple-element.42), channel_id=1, source_target_pairs={{0,8},{4,12},{8,16},{12,20},{16,24},{20,28},{24,0},{28,4},{1,9},{5... | collective-permute-start | bytes 393224 | tf_op jit(solution)/shard_map/ppermute | solution.py:237
  168.1 3.6 collective-permute-start.18
  173.2 4.6 %collective-permute-done.14 = bf16[128,2048]{1,0:T(8,128)(2,1)S(1)} collective-permute-done((bf16[128,2048]{1,0:T(8,128)(2,1)S(1)}, bf16[128,2048]{1,0:T(8,128)(2,1)S(1)}, u32[]{:S(2)}, u32[]{:S(2)}) %collective-permute-start.14) | collective-permute-done | bytes 524320 | tf_op jit(solution)/shard_map/ppermute | solution.py:171
  185.8 4.3 %collective-permute-done.15 = bf16[128,2048]{1,0:T(8,128)(2,1)S(1)} collective-permute-done((bf16[128,2048]{1,0:T(8,128)(2,1)S(1)}, bf16[128,2048]{1,0:T(8,128)(2,1)S(1)}, u32[]{:S(2)}, u32[]{:S(2)}) %collective-permute-start.15) | collective-permute-done | bytes 524320 | tf_op jit(solution)/shard_map/ppermute | solution.py:171
  196.7 9.2 %collective-permute-done.16 = bf16[128,2048]{1,0:T(8,128)(2,1)S(1)} collective-permute-done((bf16[128,2048]{1,0:T(8,128)(2,1)S(1)}, bf16[128,2048]{1,0:T(8,128)(2,1)S(1)}, u32[]{:S(2)}, u32[]{:S(2)}) %collective-permute-start.16) | collective-permute-done | bytes 524320 | tf_op jit(solution)/shard_map/ppermute | solution.py:171
  210.3 6.7 %all_gather.7 = bf16[256,1024]{1,0:T(8,128)(2,1)S(1)} all-gather(bf16[64,1024]{1,0:T(8,128)(2,1)S(1)} %copy_bitcast_fusion.1), channel_id=1, replica_groups=mesh['ctx'=8,'tp'=4] {'tp'}, dimensions={0}, use_global_device_ids=true | all-gather | bytes 655360 | tf_op jit(solution)/shard_map/all_gather | solution.py:357
  223.0 8.4 %collective-permute-done.33 = bf16[128,2048]{1,0:T(8,128)(2,1)} collective-permute-done((bf16[128,2048]{1,0:T(8,128)(2,1)}, bf16[128,2048]{1,0:T(8,128)(2,1)}, u32[]{:S(2)}, u32[]{:S(2)}) %collective-permute-start.33) | collective-permute-done | bytes 524320 | tf_op jit(solution)/shard_map/ppermute | solution.py:172
  234.0 2.9 fusion.72
  239.3 7.0 %collective-permute-done.34 = bf16[128,2048]{1,0:T(8,128)(2,1)S(1)} collective-permute-done((bf16[128,2048]{1,0:T(8,128)(2,1)S(1)}, bf16[128,2048]{1,0:T(8,128)(2,1)S(1)}, u32[]{:S(2)}, u32[]{:S(2)}) %collective-permute-start.34) | collective-permute-done | bytes 524320 | tf_op jit(solution)/shard_map/ppermute | solution.py:172
  248.8 8.0 %convolution_convert_fusion.1 = bf16[256,4096]{1,0:T(8,128)(2,1)} fusion(bf16[256,1280]{1,0:T(8,128)(2,1)S(1)} %concatenate.45, bf16[1280,4096]{1,0:T(8,128)(2,1)} %param.13), kind=kOutput, calls=%fused_computation.4 | convolution fusion | flops 2685403136 | bytes 13238272 | tf_op jit(solution)/shard_map/dot_general | solution.py:362
  261.6 8.1 %fusion.63 = (f32[8,160,2048]{2,1,0:T(8,128)}, f32[8,160,2048]{2,1,0:T(8,128)}) fusion(f32[8,160,4096]{2,1,0:T(8,128)S(1)} %bitcast.232), kind=kLoop, calls=%fused_computation.165 | loop fusion | bytes 41943040 | tf_op jit(solution)/shard_map/slice | solution.py:83
  275.5 10.2 %collective-permute-done.36 = bf16[160,2048]{1,0:T(8,128)(2,1)S(1)} collective-permute-done((bf16[160,2048]{1,0:T(8,128)(2,1)S(1)}, bf16[160,2048]{1,0:T(8,128)(2,1)S(1)}, u32[]{:S(2)}, u32[]{:S(2)}) %collective-permute-start.36) | collective-permute-done | bytes 655392 | tf_op jit(solution)/shard_map/ppermute | solution.py:94
  291.0 9.7 %collective-permute-done.37 = bf16[160,2048]{1,0:T(8,128)(2,1)S(1)} collective-permute-done((bf16[160,2048]{1,0:T(8,128)(2,1)S(1)}, bf16[160,2048]{1,0:T(8,128)(2,1)S(1)}, u32[]{:S(2)}, u32[]{:S(2)}) %collective-permute-start.37) | collective-permute-done | bytes 655392 | tf_op jit(solution)/shard_map/ppermute | solution.py:94
  305.6 9.7 %collective-permute-done.38 = bf16[160,2048]{1,0:T(8,128)(2,1)S(1)} collective-permute-done((bf16[160,2048]{1,0:T(8,128)(2,1)S(1)}, bf16[160,2048]{1,0:T(8,128)(2,1)S(1)}, u32[]{:S(2)}, u32[]{:S(2)}) %collective-permute-start.38) | collective-permute-done | bytes 655392 | tf_op jit(solution)/shard_map/ppermute | solution.py:94
  320.3 9.9 %collective-permute-done.39 = bf16[160,2048]{1,0:T(8,128)(2,1)S(1)} collective-permute-done((bf16[160,2048]{1,0:T(8,128)(2,1)S(1)}, bf16[160,2048]{1,0:T(8,128)(2,1)S(1)}, u32[]{:S(2)}, u32[]{:S(2)}) %collective-permute-start.39) | collective-permute-done | bytes 655392 | tf_op jit(solution)/shard_map/ppermute | solution.py:94
  335.2 9.9 %collective-permute-done.40 = bf16[160,2048]{1,0:T(8,128)(2,1)S(1)} collective-permute-done((bf16[160,2048]{1,0:T(8,128)(2,1)S(1)}, bf16[160,2048]{1,0:T(8,128)(2,1)S(1)}, u32[]{:S(2)}, u32[]{:S(2)}) %collective-permute-start.40) | collective-permute-done | bytes 655392 | tf_op jit(solution)/shard_map/ppermute | solution.py:94
  350.1 10.5 %collective-permute-done.41 = bf16[160,2048]{1,0:T(8,128)(2,1)S(1)} collective-permute-done((bf16[160,2048]{1,0:T(8,128)(2,1)S(1)}, bf16[160,2048]{1,0:T(8,128)(2,1)S(1)}, u32[]{:S(2)}, u32[]{:S(2)}) %collective-permute-start.41) | collective-permute-done | bytes 655392 | tf_op jit(solution)/shard_map/ppermute | solution.py:94
  366.6 6.1 %collective-permute-done.42 = bf16[160,2048]{1,0:T(8,128)(2,1)S(1)} collective-permute-done((bf16[160,2048]{1,0:T(8,128)(2,1)S(1)}, bf16[160,2048]{1,0:T(8,128)(2,1)S(1)}, u32[]{:S(2)}, u32[]{:S(2)}) %collective-permute-start.42) | collective-permute-done | bytes 655392 | tf_op jit(solution)/shard_map/ppermute | solution.py:94
  (205 shorter events, 131.1 us)
Async XLA Ops:
  9.1 47.4 %collective-permute-start = (f32[256,1280]{1,0:T(8,128)S(1)}, f32[256,1280]{1,0:T(8,128)}, u32[]{:S(2)}, u32[]{:S(2)}) collective-permute-start(f32[256,1280]{1,0:T(8,128)S(1)} %fusion.69), channel_id=1, source_target_pairs={{0,1},{1,0},{2,3},{3,2},{4,5},{5,4},{6,7},{7,6},{8,9},{9,8},{10,11... | collective-permute-start | bytes 3932168 | tf_op jit(solution)/shard_map/ppermute | solution.py:189
  17.6 40.6 %collective-permute-start.11 = (bf16[128,1024]{1,0:T(8,128)(2,1)}, bf16[128,1024]{1,0:T(8,128)(2,1)}, u32[]{:S(2)}, u32[]{:S(2)}) collective-permute-start(bf16[128,1024]{1,0:T(8,128)(2,1)} %constant_dynamic-slice_fusion), channel_id=1, source_target_pairs={{0,2},{1,3},{2,0},{3,1},{4,6},{5,7},{6,4},{7,5},{8,10},{9,11},{10,... | collective-permute-start | bytes 786440 | tf_op jit(solution)/shard_map/ppermute | solution.py:212
  65.9 30.9 %collective-permute-start.8 = (bf16[259,256]{1,0:T(8,128)(2,1)S(1)}, bf16[259,256]{1,0:T(8,128)(2,1)S(1)}, u32[]{:S(2)}, u32[]{:S(2)}) collective-permute-start(bf16[259,256]{1,0:T(8,128)(2,1)S(1)} %get-tuple-element.25), channel_id=1, source_target_pairs={{0,8},{4,12},{8,16},{12,20},{16,24},{20,28},{24,0},{28,4},{1,9},{5... | collective-permute-start | bytes 397832 | tf_op jit(solution)/shard_map/ppermute | solution.py:226
  67.6 29.2 %collective-permute-start.7 = (bf16[259,256]{1,0:T(8,128)(2,1)S(1)}, bf16[259,256]{1,0:T(8,128)(2,1)S(1)}, u32[]{:S(2)}, u32[]{:S(2)}) collective-permute-start(bf16[259,256]{1,0:T(8,128)(2,1)S(1)} %get-tuple-element.25), channel_id=1, source_target_pairs={{0,12},{4,16},{8,20},{12,24},{16,28},{20,0},{24,4},{28,8},{1,13},{... | collective-permute-start | bytes 397832 | tf_op jit(solution)/shard_map/ppermute | solution.py:226
  70.1 26.7 %collective-permute-start.6 = (bf16[259,256]{1,0:T(8,128)(2,1)S(1)}, bf16[259,256]{1,0:T(8,128)(2,1)S(1)}, u32[]{:S(2)}, u32[]{:S(2)}) collective-permute-start(bf16[259,256]{1,0:T(8,128)(2,1)S(1)} %get-tuple-element.25), channel_id=1, source_target_pairs={{0,16},{4,20},{8,24},{12,28},{16,0},{20,4},{24,8},{28,12},{1,17},{... | collective-permute-start | bytes 397832 | tf_op jit(solution)/shard_map/ppermute | solution.py:226
  71.3 25.4 %collective-permute-start.5 = (bf16[259,256]{1,0:T(8,128)(2,1)S(1)}, bf16[259,256]{1,0:T(8,128)(2,1)S(1)}, u32[]{:S(2)}, u32[]{:S(2)}) collective-permute-start(bf16[259,256]{1,0:T(8,128)(2,1)S(1)} %get-tuple-element.25), channel_id=1, source_target_pairs={{0,20},{4,24},{8,28},{12,0},{16,4},{20,8},{24,12},{28,16},{1,21},{... | collective-permute-start | bytes 397832 | tf_op jit(solution)/shard_map/ppermute | solution.py:226
  128.1 17.0 %collective-permute-start.13 = (bf16[128,2048]{1,0:T(8,128)(2,1)S(1)}, bf16[128,2048]{1,0:T(8,128)(2,1)S(1)}, u32[]{:S(2)}, u32[]{:S(2)}) collective-permute-start(bf16[128,2048]{1,0:T(8,128)(2,1)S(1)} %fusion.30), channel_id=1, source_target_pairs={{0,8},{8,16},{16,24},{24,28},{28,20},{20,12},{12,4},{4,0},{1,9},{9... | collective-permute-start | bytes 1572872 | tf_op jit(solution)/shard_map/ppermute | solution.py:171
  134.1 33.8 %collective-permute-start.17 = (bf16[128,2048]{1,0:T(8,128)(2,1)S(1)}, bf16[128,2048]{1,0:T(8,128)(2,1)S(1)}, u32[]{:S(2)}, u32[]{:S(2)}) collective-permute-start(bf16[128,2048]{1,0:T(8,128)(2,1)S(1)} %fusion.31), channel_id=1, source_target_pairs={{0,4},{8,0},{16,8},{24,16},{28,24},{20,28},{12,20},{4,12},{1,5},{9... | collective-permute-start | bytes 1572872 | tf_op jit(solution)/shard_map/ppermute | solution.py:172
  135.8 16.8 %collective-permute-start.21 = (bf16[256,256]{1,0:T(8,128)(2,1)S(1)}, bf16[256,256]{1,0:T(8,128)(2,1)S(1)}, u32[]{:S(2)}, u32[]{:S(2)}) collective-permute-start(bf16[256,256]{1,0:T(8,128)(2,1)S(1)} %get-tuple-element.36), channel_id=1, source_target_pairs={{0,4},{4,8},{8,12},{12,16},{16,20},{20,24},{24,28},{28,0},{1,5},{5... | collective-permute-start | bytes 393224 | tf_op jit(solution)/shard_map/ppermute | solution.py:237
  138.5 18.6 %collective-permute-start.27 = (bf16[256,256]{1,0:T(8,128)(2,1)S(1)}, bf16[256,256]{1,0:T(8,128)(2,1)S(1)}, u32[]{:S(2)}, u32[]{:S(2)}) collective-permute-start(bf16[256,256]{1,0:T(8,128)(2,1)S(1)} %get-tuple-element.37), channel_id=1, source_target_pairs={{0,28},{4,0},{8,4},{12,8},{16,12},{20,16},{24,20},{28,24},{1,29},{... | collective-permute-start | bytes 393224 | tf_op jit(solution)/shard_map/ppermute | solution.py:237
  140.5 19.4 %collective-permute-start.26 = (bf16[256,256]{1,0:T(8,128)(2,1)S(1)}, bf16[256,256]{1,0:T(8,128)(2,1)S(1)}, u32[]{:S(2)}, u32[]{:S(2)}) collective-permute-start(bf16[256,256]{1,0:T(8,128)(2,1)S(1)} %get-tuple-element.38), channel_id=1, source_target_pairs={{0,24},{4,28},{8,0},{12,4},{16,8},{20,12},{24,16},{28,20},{1,25},{... | collective-permute-start | bytes 393224 | tf_op jit(solution)/shard_map/ppermute | solution.py:237
  145.0 23.0 %collective-permute-start.25 = (bf16[256,256]{1,0:T(8,128)(2,1)S(1)}, bf16[256,256]{1,0:T(8,128)(2,1)S(1)}, u32[]{:S(2)}, u32[]{:S(2)}) collective-permute-start(bf16[256,256]{1,0:T(8,128)(2,1)S(1)} %get-tuple-element.39), channel_id=1, source_target_pairs={{0,20},{4,24},{8,28},{12,0},{16,4},{20,8},{24,12},{28,16},{1,21},{... | collective-permute-start | bytes 393224 | tf_op jit(solution)/shard_map/ppermute | solution.py:237
  152.6 20.4 %collective-permute-start.24 = (bf16[256,256]{1,0:T(8,128)(2,1)S(1)}, bf16[256,256]{1,0:T(8,128)(2,1)S(1)}, u32[]{:S(2)}, u32[]{:S(2)}) collective-permute-start(bf16[256,256]{1,0:T(8,128)(2,1)S(1)} %get-tuple-element.40), channel_id=1, source_target_pairs={{0,16},{4,20},{8,24},{12,28},{16,0},{20,4},{24,8},{28,12},{1,17},{... | collective-permute-start | bytes 393224 | tf_op jit(solution)/shard_map/ppermute | solution.py:237
  157.1 15.8 %collective-permute-start.23 = (bf16[256,256]{1,0:T(8,128)(2,1)S(1)}, bf16[256,256]{1,0:T(8,128)(2,1)S(1)}, u32[]{:S(2)}, u32[]{:S(2)}) collective-permute-start(bf16[256,256]{1,0:T(8,128)(2,1)S(1)} %get-tuple-element.41), channel_id=1, source_target_pairs={{0,12},{4,16},{8,20},{12,24},{16,28},{20,0},{24,4},{28,8},{1,13},{... | collective-permute-start | bytes 393224 | tf_op jit(solution)/shard_map/ppermute | solution.py:237
  168.1 13.5 %collective-permute-start.18 = (bf16[128,2048]{1,0:T(8,128)(2,1)S(1)}, bf16[128,2048]{1,0:T(8,128)(2,1)S(1)}, u32[]{:S(2)}, u32[]{:S(2)}) collective-permute-start(bf16[128,2048]{1,0:T(8,128)(2,1)S(1)} %fusion.24), channel_id=1, source_target_pairs={{0,4},{8,0},{16,8},{24,16},{28,24},{20,28},{12,20},{4,12},{1,5},{9... | collective-permute-start | bytes 1572872 | tf_op jit(solution)/shard_map/ppermute | solution.py:172
  181.7 13.7 %collective-permute-start.19 = (bf16[128,2048]{1,0:T(8,128)(2,1)S(1)}, bf16[128,2048]{1,0:T(8,128)(2,1)S(1)}, u32[]{:S(2)}, u32[]{:S(2)}) collective-permute-start(bf16[128,2048]{1,0:T(8,128)(2,1)S(1)} %fusion.23), channel_id=1, source_target_pairs={{0,4},{8,0},{16,8},{24,16},{28,24},{20,28},{12,20},{4,12},{1,5},{9... | collective-permute-start | bytes 1572872 | tf_op jit(solution)/shard_map/ppermute | solution.py:172
  191.5 14.5 %collective-permute-start.16 = (bf16[128,2048]{1,0:T(8,128)(2,1)S(1)}, bf16[128,2048]{1,0:T(8,128)(2,1)S(1)}, u32[]{:S(2)}, u32[]{:S(2)}) collective-permute-start(bf16[128,2048]{1,0:T(8,128)(2,1)S(1)} %fusion.25), channel_id=1, source_target_pairs={{0,8},{8,16},{16,24},{24,28},{28,20},{20,12},{12,4},{4,0},{1,9},{9... | collective-permute-start | bytes 1572872 | tf_op jit(solution)/shard_map/ppermute | solution.py:171
  217.0 14.5 %collective-permute-start.33 = (bf16[128,2048]{1,0:T(8,128)(2,1)}, bf16[128,2048]{1,0:T(8,128)(2,1)}, u32[]{:S(2)}, u32[]{:S(2)}) collective-permute-start(bf16[128,2048]{1,0:T(8,128)(2,1)} %bitcast_add_fusion.20), channel_id=1, source_target_pairs={{0,4},{8,0},{16,8},{24,16},{28,24},{20,28},{12,20},{4,12},{1,5},{9... | collective-permute-start | bytes 1572872 | tf_op jit(solution)/shard_map/ppermute | solution.py:172
  221.8 15.1 %collective-permute-start.31 = (bf16[128,2048]{1,0:T(8,128)(2,1)S(1)}, bf16[128,2048]{1,0:T(8,128)(2,1)S(1)}, u32[]{:S(2)}, u32[]{:S(2)}) collective-permute-start(bf16[128,2048]{1,0:T(8,128)(2,1)S(1)} %fusion.21), channel_id=1, source_target_pairs={{0,8},{8,16},{16,24},{24,28},{28,20},{20,12},{12,4},{4,0},{1,9},{9... | collective-permute-start | bytes 1572872 | tf_op jit(solution)/shard_map/ppermute | solution.py:171
  232.9 13.4 %collective-permute-start.34 = (bf16[128,2048]{1,0:T(8,128)(2,1)S(1)}, bf16[128,2048]{1,0:T(8,128)(2,1)S(1)}, u32[]{:S(2)}, u32[]{:S(2)}) collective-permute-start(bf16[128,2048]{1,0:T(8,128)(2,1)S(1)} %fusion.19), channel_id=1, source_target_pairs={{0,4},{8,0},{16,8},{24,16},{28,24},{20,28},{12,20},{4,12},{1,5},{9... | collective-permute-start | bytes 1572872 | tf_op jit(solution)/shard_map/ppermute | solution.py:172
  238.3 18.5 %collective-permute-start.32 = (bf16[128,2048]{1,0:T(8,128)(2,1)S(1)}, bf16[128,2048]{1,0:T(8,128)(2,1)S(1)}, u32[]{:S(2)}, u32[]{:S(2)}) collective-permute-start(bf16[128,2048]{1,0:T(8,128)(2,1)S(1)} %fusion.20), channel_id=1, source_target_pairs={{0,8},{8,16},{16,24},{24,28},{28,20},{20,12},{12,4},{4,0},{1,9},{9... | collective-permute-start | bytes 1572872 | tf_op jit(solution)/shard_map/ppermute | solution.py:171
  271.2 14.4 %collective-permute-start.36 = (bf16[160,2048]{1,0:T(8,128)(2,1)S(1)}, bf16[160,2048]{1,0:T(8,128)(2,1)S(1)}, u32[]{:S(2)}, u32[]{:S(2)}) collective-permute-start(bf16[160,2048]{1,0:T(8,128)(2,1)S(1)} %fusion.28), channel_id=1, source_target_pairs={{0,8},{8,16},{16,24},{24,28},{28,20},{20,12},{12,4},{4,0},{1,9},{9... | collective-permute-start | bytes 1966088 | tf_op jit(solution)/shard_map/ppermute | solution.py:94
  274.5 14.7 %collective-permute-start.43 = (bf16[160,2048]{1,0:T(8,128)(2,1)S(1)}, bf16[160,2048]{1,0:T(8,128)(2,1)S(1)}, u32[]{:S(2)}, u32[]{:S(2)}) collective-permute-start(bf16[160,2048]{1,0:T(8,128)(2,1)S(1)} %fusion.29), channel_id=1, source_target_pairs={{0,4},{8,0},{16,8},{24,16},{28,24},{20,28},{12,20},{4,12},{1,5},{9... | collective-permute-start | bytes 1966088 | tf_op jit(solution)/shard_map/ppermute | solution.py:95
  287.1 13.5 %collective-permute-start.37 = (bf16[160,2048]{1,0:T(8,128)(2,1)S(1)}, bf16[160,2048]{1,0:T(8,128)(2,1)S(1)}, u32[]{:S(2)}, u32[]{:S(2)}) collective-permute-start(bf16[160,2048]{1,0:T(8,128)(2,1)S(1)} %fusion.16), channel_id=1, source_target_pairs={{0,8},{8,16},{16,24},{24,28},{28,20},{20,12},{12,4},{4,0},{1,9},{9... | collective-permute-start | bytes 1966088 | tf_op jit(solution)/shard_map/ppermute | solution.py:94
  290.7 14.2 %collective-permute-start.44 = (bf16[160,2048]{1,0:T(8,128)(2,1)S(1)}, bf16[160,2048]{1,0:T(8,128)(2,1)S(1)}, u32[]{:S(2)}, u32[]{:S(2)}) collective-permute-start(bf16[160,2048]{1,0:T(8,128)(2,1)S(1)} %fusion.10), channel_id=1, source_target_pairs={{0,4},{8,0},{16,8},{24,16},{28,24},{20,28},{12,20},{4,12},{1,5},{9... | collective-permute-start | bytes 1966088 | tf_op jit(solution)/shard_map/ppermute | solution.py:95
  305.0 14.8 %collective-permute-start.45 = (bf16[160,2048]{1,0:T(8,128)(2,1)S(1)}, bf16[160,2048]{1,0:T(8,128)(2,1)S(1)}, u32[]{:S(2)}, u32[]{:S(2)}) collective-permute-start(bf16[160,2048]{1,0:T(8,128)(2,1)S(1)} %fusion.9), channel_id=1, source_target_pairs={{0,4},{8,0},{16,8},{24,16},{28,24},{20,28},{12,20},{4,12},{1,5},{9... | collective-permute-start | bytes 1966088 | tf_op jit(solution)/shard_map/ppermute | solution.py:95
  316.8 13.4 %collective-permute-start.39 = (bf16[160,2048]{1,0:T(8,128)(2,1)S(1)}, bf16[160,2048]{1,0:T(8,128)(2,1)S(1)}, u32[]{:S(2)}, u32[]{:S(2)}) collective-permute-start(bf16[160,2048]{1,0:T(8,128)(2,1)S(1)} %fusion.14), channel_id=1, source_target_pairs={{0,8},{8,16},{16,24},{24,28},{28,20},{20,12},{12,4},{4,0},{1,9},{9... | collective-permute-start | bytes 1966088 | tf_op jit(solution)/shard_map/ppermute | solution.py:94
  320.0 14.7 %collective-permute-start.46 = (bf16[160,2048]{1,0:T(8,128)(2,1)S(1)}, bf16[160,2048]{1,0:T(8,128)(2,1)S(1)}, u32[]{:S(2)}, u32[]{:S(2)}) collective-permute-start(bf16[160,2048]{1,0:T(8,128)(2,1)S(1)} %fusion.8), channel_id=1, source_target_pairs={{0,4},{8,0},{16,8},{24,16},{28,24},{20,28},{12,20},{4,12},{1,5},{9... | collective-permute-start | bytes 1966088 | tf_op jit(solution)/shard_map/ppermute | solution.py:95
  331.7 13.4 %collective-permute-start.40 = (bf16[160,2048]{1,0:T(8,128)(2,1)S(1)}, bf16[160,2048]{1,0:T(8,128)(2,1)S(1)}, u32[]{:S(2)}, u32[]{:S(2)}) collective-permute-start(bf16[160,2048]{1,0:T(8,128)(2,1)S(1)} %fusion.13), channel_id=1, source_target_pairs={{0,8},{8,16},{16,24},{24,28},{28,20},{20,12},{12,4},{4,0},{1,9},{9... | collective-permute-start | bytes 1966088 | tf_op jit(solution)/shard_map/ppermute | solution.py:94
  334.9 14.7 %collective-permute-start.47 = (bf16[160,2048]{1,0:T(8,128)(2,1)S(1)}, bf16[160,2048]{1,0:T(8,128)(2,1)S(1)}, u32[]{:S(2)}, u32[]{:S(2)}) collective-permute-start(bf16[160,2048]{1,0:T(8,128)(2,1)S(1)} %fusion.7), channel_id=1, source_target_pairs={{0,4},{8,0},{16,8},{24,16},{28,24},{20,28},{12,20},{4,12},{1,5},{9... | collective-permute-start | bytes 1966088 | tf_op jit(solution)/shard_map/ppermute | solution.py:95
  346.6 14.0 %collective-permute-start.41 = (bf16[160,2048]{1,0:T(8,128)(2,1)S(1)}, bf16[160,2048]{1,0:T(8,128)(2,1)S(1)}, u32[]{:S(2)}, u32[]{:S(2)}) collective-permute-start(bf16[160,2048]{1,0:T(8,128)(2,1)S(1)} %fusion.12), channel_id=1, source_target_pairs={{0,8},{8,16},{16,24},{24,28},{28,20},{20,12},{12,4},{4,0},{1,9},{9... | collective-permute-start | bytes 1966088 | tf_op jit(solution)/shard_map/ppermute | solution.py:94
  349.8 14.8 %collective-permute-start.48 = (bf16[160,2048]{1,0:T(8,128)(2,1)S(1)}, bf16[160,2048]{1,0:T(8,128)(2,1)S(1)}, u32[]{:S(2)}, u32[]{:S(2)}) collective-permute-start(bf16[160,2048]{1,0:T(8,128)(2,1)S(1)} %fusion.6), channel_id=1, source_target_pairs={{0,4},{8,0},{16,8},{24,16},{28,24},{20,28},{12,20},{4,12},{1,5},{9... | collective-permute-start | bytes 1966088 | tf_op jit(solution)/shard_map/ppermute | solution.py:95
  (32 other events, 370.2 us)

commit v10 on v8

--- a/solution.py
+++ b/solution.py
@@ -344,7 +344,7 @@
     key_part = across(dscore, queries) * factor
     value_part = across(prob.astype(jnp.bfloat16), grad_stack)
     pair_all = jnp.concatenate([key_part, value_part], axis=1)
-    out_ring = Ring(out_weight_grad, ring, "ctx").advance(len(ring) // 2)
+    out_ring = Ring(out_weight_grad, ring, "ctx").advance(len(ring) // 4)
     pair_grad = butterfly_sum(direct_scatter(pair_all, "ctx"), "tp")
     out_ring.state, pair_grad = lax.optimization_barrier((out_ring.state, pair_grad))
 

time: 359 us -> 348 us (0.969)
  waiting for transfers between devices: 132 us -> 122 us
  starting transfers between devices: 64.3 us -> 57.5 us
    ppermute x7, waiting for transfers between devices: 16.5 us -> 4.23 us  [ring_scatter(): got_right = lax.ppermute(send_right.astype(jnp.bfloat16), axis, backward)]
    ppermute x7, starting transfers between devices: 14.9 us -> 5.27 us  [ring_scatter(): got_left = lax.ppermute(send_left.astype(jnp.bfloat16), axis, forward)]
    ppermute x7, starting transfers between devices: 15.5 us -> 6.64 us  [advance(): lax.ppermute(send_left.astype(jnp.bfloat16), self.axis, self.forward)]
    ppermute x7, waiting for transfers between devices: 47.3 us -> 55.9 us  [ring_scatter(): got_left = lax.ppermute(send_left.astype(jnp.bfloat16), axis, forward)]
    ppermute x7, starting transfers between devices: 1.44 us -> 9.87 us  [ring_scatter(): got_right = lax.ppermute(send_right.astype(jnp.bfloat16), axis, backward)]
    ppermute x7, waiting for transfers between devices: 8.87 us -> 1.05 us  [direct_scatter(): lax.ppermute(blocks[shift].astype(jnp.bfloat16), axis, pairs)]
  transfers between devices with their start and end apart: 50 -> 50, of which waited for: 33 -> 28; matrix products, arithmetic and copies ran while one was open for 19% -> 24% of each run, Pallas kernels for 0% -> 0%
where the time goes in v10:
time: 348 us; the launch traced here: 346 us
  waiting for transfers between devices  122 us (35%)
  starting transfers between devices  57.5 us (17%)
  other arithmetic  50 us (14%)
  between operations  37.1 us (11%)
  matrix products  35.2 us (10%)
  local copies, waits for them, and re-layouts  30.3 us (9%)
  blocking collectives  13.8 us (4%)
    ppermute x7, waiting for transfers between devices, ring_scatter(): got_left = lax.ppermute(send_left.astype(jnp.bfloat16), axis, forward)  55.9 us
    ppermute x7, waiting for transfers between devices, advance(): lax.ppermute(send_right.astype(jnp.bfloat16), self.axis, self.backward)  35.6 us
    ppermute x7, waiting for transfers between devices, direct_gather(): got[count - shift] = lax.ppermute(value, axis, pairs)  16.1 us
    dot_general x4, matrix products, against(): lax.dot_general(left, right, (((1,), (1,)), ((), ())), preferred_element_...  14.9 us
    ppermute x7, starting transfers between devices, direct_gather(): got[count - shift] = lax.ppermute(value, axis, pairs)  12.2 us
    ppermute x7, starting transfers between devices, direct_scatter(): lax.ppermute(blocks[shift].astype(jnp.bfloat16), axis, pairs)  11.9 us
    ppermute x7, starting transfers between devices, ring_scatter(): got_right = lax.ppermute(send_right.astype(jnp.bfloat16), axis, backward)  9.87 us
    convert_element_type x6, other arithmetic, ring_scatter(): got_left = lax.ppermute(send_left.astype(jnp.bfloat16), axis, forward)  8.84 us
  transfers between devices with their start and end apart: 50, of which 28 were waited for; matrix products, arithmetic and copies ran while one was open for 24% of the time, Pallas kernels for 0%

profile of v10, /device:TPU:0, one launch (start us, length us, event | category | flops | bytes accessed | tf_op | source)
XLA Modules:
  0.0 346.1 jit_solution(10542800763910754592)
XLA Ops:
  2.2 6.9 %fusion.70 = f32[256,1280]{1,0:T(8,128)S(1)} fusion(bf16[256,4096]{1,0:T(8,128)(2,1)S(1)} %copy-done, bf16[1280,4096]{1,0:T(8,128)(2,1)} %param.13), kind=kOutput, calls=%fused_computation.172 | convolution fusion | flops 2684354560 | bytes 13893632 | tf_op jit(solution)/shard_map/dot_general | solution.py:35
  9.6 6.4 %convolution_convert_fusion.2 = bf16[256,1024]{1,0:T(8,128)(2,1)S(1)} fusion(bf16[256,4096]{1,0:T(8,128)(2,1)} %param.15, bf16[1024,4096]{1,0:T(8,128)(2,1)} %param.14), kind=kOutput, calls=%fused_computation.45 | convolution fusion | flops 2147745792 | bytes 11010048 | tf_op jit(solution)/shard_map/dot_general | solution.py:35
  17.6 2.6 collective-permute-start.11
  37.9 4.2 %collective-permute-done.1 = f32[128,256]{1,0:T(8,128)S(1)} collective-permute-done((f32[128,256]{1,0:T(8,128)S(1)}, f32[128,256]{1,0:T(8,128)S(1)}, u32[]{:S(2)}, u32[]{:S(2)}) %collective-permute-start.1) | collective-permute-done | bytes 131104 | tf_op jit(solution)/shard_map/ppermute | solution.py:197
  44.3 4.6 %collective-permute-start.3 = (bf16[259,256]{1,0:T(8,128)(2,1)S(1)}, bf16[259,256]{1,0:T(8,128)(2,1)S(1)}, u32[]{:S(2)}, u32[]{:S(2)}) collective-permute-start(bf16[259,256]{1,0:T(8,128)(2,1)S(1)} %get-tuple-element.19), channel_id=1, source_target_pairs={{0,28},{4,0},{8,4},{12,8},{16,12},{20,16},{24,20},{28,24},{1,29},{... | collective-permute-start | bytes 397832 | tf_op jit(solution)/shard_map/ppermute | solution.py:226
  49.4 3.0 collective-permute-start.6
  58.8 13.5 %collective-permute-done.6 = bf16[259,256]{1,0:T(8,128)(2,1)S(1)} collective-permute-done((bf16[259,256]{1,0:T(8,128)(2,1)S(1)}, bf16[259,256]{1,0:T(8,128)(2,1)S(1)}, u32[]{:S(2)}, u32[]{:S(2)}) %collective-permute-start.6) | collective-permute-done | bytes 132640 | tf_op jit(solution)/shard_map/ppermute | solution.py:226
  83.2 2.8 collective-permute-start.19
  89.0 6.7 %all_gather.6 = bf16[256,1024]{1,0:T(8,128)(2,1)S(1)} all-gather(bf16[64,1024]{1,0:T(8,128)(2,1)S(1)} %bitcast.244), channel_id=1, replica_groups=mesh['ctx'=8,'tp'=4] {'tp'}, dimensions={0}, use_global_device_ids=true | all-gather | bytes 655360 | tf_op jit(solution)/shard_map/all_gather | solution.py:332
  95.7 2.4 fusion.71
  98.2 6.3 %fusion.65 = (f32[8,128,2048]{2,1,0:T(8,128)}, f32[8,128,2048]{2,1,0:T(8,128)}) fusion(f32[8,128,4096]{2,1,0:T(8,128)S(1)} %bitcast.233), kind=kLoop, calls=%fused_computation.167 | loop fusion | bytes 33554432 | tf_op jit(solution)/shard_map/slice | solution.py:157
  104.5 2.4 collective-permute-start.22
  106.9 2.9 collective-permute-start.23
  123.3 2.5 collective-permute-done.15
  125.8 2.3 fusion.26
  128.4 2.7 collective-permute-done.13
  131.1 2.3 fusion.27
  160.0 10.3 %collective-permute-done.31 = bf16[128,2048]{1,0:T(8,128)(2,1)S(1)} collective-permute-done((bf16[128,2048]{1,0:T(8,128)(2,1)S(1)}, bf16[128,2048]{1,0:T(8,128)(2,1)S(1)}, u32[]{:S(2)}, u32[]{:S(2)}) %collective-permute-start.31) | collective-permute-done | bytes 524320 | tf_op jit(solution)/shard_map/ppermute | solution.py:172
  175.2 9.0 %collective-permute-done.32 = bf16[128,2048]{1,0:T(8,128)(2,1)S(1)} collective-permute-done((bf16[128,2048]{1,0:T(8,128)(2,1)S(1)}, bf16[128,2048]{1,0:T(8,128)(2,1)S(1)}, u32[]{:S(2)}, u32[]{:S(2)}) %collective-permute-start.32) | collective-permute-done | bytes 524320 | tf_op jit(solution)/shard_map/ppermute | solution.py:172
  189.5 7.1 %all_gather.7 = bf16[256,1024]{1,0:T(8,128)(2,1)} all-gather(bf16[64,1024]{1,0:T(8,128)(2,1)S(1)} %copy_bitcast_fusion.1), channel_id=1, replica_groups=mesh['ctx'=8,'tp'=4] {'tp'}, dimensions={0}, use_global_device_ids=true | all-gather | bytes 655360 | tf_op jit(solution)/shard_map/all_gather | solution.py:356
  206.4 7.1 %collective-permute-done.34 = bf16[128,2048]{1,0:T(8,128)(2,1)} collective-permute-done((bf16[128,2048]{1,0:T(8,128)(2,1)}, bf16[128,2048]{1,0:T(8,128)(2,1)}, u32[]{:S(2)}, u32[]{:S(2)}) %collective-permute-start.34) | collective-permute-done | bytes 524320 | tf_op jit(solution)/shard_map/ppermute | solution.py:172
  218.9 2.9 fusion.73
  221.8 5.0 %collective-permute-done.35 = bf16[128,2048]{1,0:T(8,128)(2,1)S(1)} collective-permute-done((bf16[128,2048]{1,0:T(8,128)(2,1)S(1)}, bf16[128,2048]{1,0:T(8,128)(2,1)S(1)}, u32[]{:S(2)}, u32[]{:S(2)}) %collective-permute-start.35) | collective-permute-done | bytes 524320 | tf_op jit(solution)/shard_map/ppermute | solution.py:172
  230.9 8.1 %fusion.64 = (f32[8,160,2048]{2,1,0:T(8,128)}, f32[8,160,2048]{2,1,0:T(8,128)}) fusion(f32[8,160,4096]{2,1,0:T(8,128)S(1)} %bitcast.232), kind=kLoop, calls=%fused_computation.166 | loop fusion | bytes 41943040 | tf_op jit(solution)/shard_map/slice | solution.py:83
  244.4 9.9 %collective-permute-done.36 = bf16[160,2048]{1,0:T(8,128)(2,1)S(1)} collective-permute-done((bf16[160,2048]{1,0:T(8,128)(2,1)S(1)}, bf16[160,2048]{1,0:T(8,128)(2,1)S(1)}, u32[]{:S(2)}, u32[]{:S(2)}) %collective-permute-start.36) | collective-permute-done | bytes 655392 | tf_op jit(solution)/shard_map/ppermute | solution.py:94
  259.4 9.8 %collective-permute-done.37 = bf16[160,2048]{1,0:T(8,128)(2,1)S(1)} collective-permute-done((bf16[160,2048]{1,0:T(8,128)(2,1)S(1)}, bf16[160,2048]{1,0:T(8,128)(2,1)S(1)}, u32[]{:S(2)}, u32[]{:S(2)}) %collective-permute-start.37) | collective-permute-done | bytes 655392 | tf_op jit(solution)/shard_map/ppermute | solution.py:94
  274.1 10.0 %collective-permute-done.38 = bf16[160,2048]{1,0:T(8,128)(2,1)S(1)} collective-permute-done((bf16[160,2048]{1,0:T(8,128)(2,1)S(1)}, bf16[160,2048]{1,0:T(8,128)(2,1)S(1)}, u32[]{:S(2)}, u32[]{:S(2)}) %collective-permute-start.38) | collective-permute-done | bytes 655392 | tf_op jit(solution)/shard_map/ppermute | solution.py:94
  289.0 10.0 %collective-permute-done.39 = bf16[160,2048]{1,0:T(8,128)(2,1)S(1)} collective-permute-done((bf16[160,2048]{1,0:T(8,128)(2,1)S(1)}, bf16[160,2048]{1,0:T(8,128)(2,1)S(1)}, u32[]{:S(2)}, u32[]{:S(2)}) %collective-permute-start.39) | collective-permute-done | bytes 655392 | tf_op jit(solution)/shard_map/ppermute | solution.py:94
  303.9 7.8 %convolution_convert_fusion = bf16[256,4096]{1,0:T(8,128)(2,1)} fusion(bf16[256,1024]{1,0:T(8,128)(2,1)S(1)} %all_gather.6, bf16[1024,4096]{1,0:T(8,128)(2,1)} %param.14), kind=kOutput, calls=%fused_computation.3 | convolution fusion | flops 2148532224 | bytes 11010048 | tf_op jit(solution)/shard_map/dot_general | solution.py:333
  318.5 4.1 %convolution_convert_fusion.1 = bf16[256,4096]{1,0:T(8,128)(2,1)} fusion(bf16[256,1280]{1,0:T(8,128)(2,1)S(1)} %concatenate.45, bf16[1280,4096]{1,0:T(8,128)(2,1)S(1)} %bitcast.251), kind=kOutput, calls=%fused_computation.4 | convolution fusion | flops 2685403136 | bytes 13238272 | tf_op jit(solution)/shard_map/dot_general | solution.py:361
  322.7 7.4 %collective-permute-done.41 = bf16[160,2048]{1,0:T(8,128)(2,1)S(1)} collective-permute-done((bf16[160,2048]{1,0:T(8,128)(2,1)S(1)}, bf16[160,2048]{1,0:T(8,128)(2,1)S(1)}, u32[]{:S(2)}, u32[]{:S(2)}) %collective-permute-start.41) | collective-permute-done | bytes 655392 | tf_op jit(solution)/shard_map/ppermute | solution.py:94
  335.6 6.8 %collective-permute-done.42 = bf16[160,2048]{1,0:T(8,128)(2,1)S(1)} collective-permute-done((bf16[160,2048]{1,0:T(8,128)(2,1)S(1)}, bf16[160,2048]{1,0:T(8,128)(2,1)S(1)}, u32[]{:S(2)}, u32[]{:S(2)}) %collective-permute-start.42) | collective-permute-done | bytes 655392 | tf_op jit(solution)/shard_map/ppermute | solution.py:94
  (213 shorter events, 119.3 us)
Async XLA Ops:
  9.1 25.8 %collective-permute-start = (f32[256,1280]{1,0:T(8,128)S(1)}, f32[256,1280]{1,0:T(8,128)}, u32[]{:S(2)}, u32[]{:S(2)}) collective-permute-start(f32[256,1280]{1,0:T(8,128)S(1)} %fusion.70), channel_id=1, source_target_pairs={{0,1},{1,0},{2,3},{3,2},{4,5},{5,4},{6,7},{7,6},{8,9},{9,8},{10,11... | collective-permute-start | bytes 3932168 | tf_op jit(solution)/shard_map/ppermute | solution.py:189
  17.6 19.0 %collective-permute-start.11 = (bf16[128,1024]{1,0:T(8,128)(2,1)}, bf16[128,1024]{1,0:T(8,128)(2,1)}, u32[]{:S(2)}, u32[]{:S(2)}) collective-permute-start(bf16[128,1024]{1,0:T(8,128)(2,1)} %constant_dynamic-slice_fusion), channel_id=1, source_target_pairs={{0,2},{1,3},{2,0},{3,1},{4,6},{5,7},{6,4},{7,5},{8,10},{9,11},{10,... | collective-permute-start | bytes 786440 | tf_op jit(solution)/shard_map/ppermute | solution.py:212
  49.4 22.9 %collective-permute-start.6 = (bf16[259,256]{1,0:T(8,128)(2,1)S(1)}, bf16[259,256]{1,0:T(8,128)(2,1)S(1)}, u32[]{:S(2)}, u32[]{:S(2)}) collective-permute-start(bf16[259,256]{1,0:T(8,128)(2,1)S(1)} %get-tuple-element.19), channel_id=1, source_target_pairs={{0,16},{4,20},{8,24},{12,28},{16,0},{20,4},{24,8},{28,12},{1,17},{... | collective-permute-start | bytes 397832 | tf_op jit(solution)/shard_map/ppermute | solution.py:226
  53.0 20.7 %collective-permute-start.7 = (bf16[259,256]{1,0:T(8,128)(2,1)S(1)}, bf16[259,256]{1,0:T(8,128)(2,1)S(1)}, u32[]{:S(2)}, u32[]{:S(2)}) collective-permute-start(bf16[259,256]{1,0:T(8,128)(2,1)S(1)} %get-tuple-element.19), channel_id=1, source_target_pairs={{0,12},{4,16},{8,20},{12,24},{16,28},{20,0},{24,4},{28,8},{1,13},{... | collective-permute-start | bytes 397832 | tf_op jit(solution)/shard_map/ppermute | solution.py:226
  54.2 19.6 %collective-permute-start.8 = (bf16[259,256]{1,0:T(8,128)(2,1)S(1)}, bf16[259,256]{1,0:T(8,128)(2,1)S(1)}, u32[]{:S(2)}, u32[]{:S(2)}) collective-permute-start(bf16[259,256]{1,0:T(8,128)(2,1)S(1)} %get-tuple-element.19), channel_id=1, source_target_pairs={{0,8},{4,12},{8,16},{12,20},{16,24},{20,28},{24,0},{28,4},{1,9},{5... | collective-permute-start | bytes 397832 | tf_op jit(solution)/shard_map/ppermute | solution.py:226
  55.8 17.9 %collective-permute-start.9 = (bf16[259,256]{1,0:T(8,128)(2,1)S(1)}, bf16[259,256]{1,0:T(8,128)(2,1)S(1)}, u32[]{:S(2)}, u32[]{:S(2)}) collective-permute-start(bf16[259,256]{1,0:T(8,128)(2,1)S(1)} %get-tuple-element.19), channel_id=1, source_target_pairs={{0,4},{4,8},{8,12},{12,16},{16,20},{20,24},{24,28},{28,0},{1,5},{5... | collective-permute-start | bytes 397832 | tf_op jit(solution)/shard_map/ppermute | solution.py:226
  82.3 22.2 %collective-permute-start.17 = (bf16[256,256]{1,0:T(8,128)(2,1)}, bf16[256,256]{1,0:T(8,128)(2,1)}, u32[]{:S(2)}, u32[]{:S(2)}) collective-permute-start(bf16[256,256]{1,0:T(8,128)(2,1)} %get-tuple-element.30), channel_id=1, source_target_pairs={{0,4},{4,8},{8,12},{12,16},{16,20},{20,24},{24,28},{28,0},{1,5},{5... | collective-permute-start | bytes 393224 | tf_op jit(solution)/shard_map/ppermute | solution.py:237
  82.3 24.6 %collective-permute-start.18 = (bf16[256,256]{1,0:T(8,128)(2,1)}, bf16[256,256]{1,0:T(8,128)(2,1)}, u32[]{:S(2)}, u32[]{:S(2)}) collective-permute-start(bf16[256,256]{1,0:T(8,128)(2,1)} %get-tuple-element.36), channel_id=1, source_target_pairs={{0,8},{4,12},{8,16},{12,20},{16,24},{20,28},{24,0},{28,4},{1,9},{5... | collective-permute-start | bytes 393224 | tf_op jit(solution)/shard_map/ppermute | solution.py:237
  83.2 28.7 %collective-permute-start.19 = (bf16[256,256]{1,0:T(8,128)(2,1)}, bf16[256,256]{1,0:T(8,128)(2,1)}, u32[]{:S(2)}, u32[]{:S(2)}) collective-permute-start(bf16[256,256]{1,0:T(8,128)(2,1)} %get-tuple-element.35), channel_id=1, source_target_pairs={{0,12},{4,16},{8,20},{12,24},{16,28},{20,0},{24,4},{28,8},{1,13},{... | collective-permute-start | bytes 393224 | tf_op jit(solution)/shard_map/ppermute | solution.py:237
  86.0 25.9 %collective-permute-start.20 = (bf16[256,256]{1,0:T(8,128)(2,1)}, bf16[256,256]{1,0:T(8,128)(2,1)}, u32[]{:S(2)}, u32[]{:S(2)}) collective-permute-start(bf16[256,256]{1,0:T(8,128)(2,1)} %get-tuple-element.34), channel_id=1, source_target_pairs={{0,16},{4,20},{8,24},{12,28},{16,0},{20,4},{24,8},{28,12},{1,17},{... | collective-permute-start | bytes 393224 | tf_op jit(solution)/shard_map/ppermute | solution.py:237
  87.6 24.3 %collective-permute-start.21 = (bf16[256,256]{1,0:T(8,128)(2,1)}, bf16[256,256]{1,0:T(8,128)(2,1)}, u32[]{:S(2)}, u32[]{:S(2)}) collective-permute-start(bf16[256,256]{1,0:T(8,128)(2,1)} %get-tuple-element.33), channel_id=1, source_target_pairs={{0,20},{4,24},{8,28},{12,0},{16,4},{20,8},{24,12},{28,16},{1,21},{... | collective-permute-start | bytes 393224 | tf_op jit(solution)/shard_map/ppermute | solution.py:237
  111.9 13.9 %collective-permute-start.15 = (bf16[128,2048]{1,0:T(8,128)(2,1)}, bf16[128,2048]{1,0:T(8,128)(2,1)}, u32[]{:S(2)}, u32[]{:S(2)}) collective-permute-start(bf16[128,2048]{1,0:T(8,128)(2,1)} %fusion.31), channel_id=1, source_target_pairs={{0,4},{8,0},{16,8},{24,16},{28,24},{20,28},{12,20},{4,12},{1,5},{9... | collective-permute-start | bytes 1572872 | tf_op jit(solution)/shard_map/ppermute | solution.py:172
  116.4 14.6 %collective-permute-start.13 = (bf16[128,2048]{1,0:T(8,128)(2,1)}, bf16[128,2048]{1,0:T(8,128)(2,1)}, u32[]{:S(2)}, u32[]{:S(2)}) collective-permute-start(bf16[128,2048]{1,0:T(8,128)(2,1)} %fusion.30), channel_id=1, source_target_pairs={{0,8},{8,16},{16,24},{24,28},{28,20},{20,12},{12,4},{4,0},{1,9},{9... | collective-permute-start | bytes 1572872 | tf_op jit(solution)/shard_map/ppermute | solution.py:171
  122.3 30.6 %collective-permute-start.25 = (f32[256,256]{1,0:T(8,128)S(1)}, f32[256,256]{1,0:T(8,128)}, u32[]{:S(2)}, u32[]{:S(2)}) collective-permute-start(f32[256,256]{1,0:T(8,128)S(1)} %add.689), channel_id=1, source_target_pairs={{0,2},{1,3},{2,0},{3,1},{4,6},{5,7},{6,4},{7,5},{8,10},{9,11},{10,... | collective-permute-start | bytes 786440 | tf_op jit(solution)/shard_map/ppermute | solution.py:248
  128.1 25.8 %collective-permute-start.16 = (bf16[128,2048]{1,0:T(8,128)(2,1)}, bf16[128,2048]{1,0:T(8,128)(2,1)}, u32[]{:S(2)}, u32[]{:S(2)}) collective-permute-start(bf16[128,2048]{1,0:T(8,128)(2,1)} %fusion.26), channel_id=1, source_target_pairs={{0,4},{8,0},{16,8},{24,16},{28,24},{20,28},{12,20},{4,12},{1,5},{9... | collective-permute-start | bytes 1572872 | tf_op jit(solution)/shard_map/ppermute | solution.py:172
  133.3 22.2 %collective-permute-start.14 = (bf16[128,2048]{1,0:T(8,128)(2,1)}, bf16[128,2048]{1,0:T(8,128)(2,1)}, u32[]{:S(2)}, u32[]{:S(2)}) collective-permute-start(bf16[128,2048]{1,0:T(8,128)(2,1)} %fusion.27), channel_id=1, source_target_pairs={{0,8},{8,16},{16,24},{24,28},{28,20},{20,12},{12,4},{4,0},{1,9},{9... | collective-permute-start | bytes 1572872 | tf_op jit(solution)/shard_map/ppermute | solution.py:171
  157.0 13.3 %collective-permute-start.31 = (bf16[128,2048]{1,0:T(8,128)(2,1)S(1)}, bf16[128,2048]{1,0:T(8,128)(2,1)S(1)}, u32[]{:S(2)}, u32[]{:S(2)}) collective-permute-start(bf16[128,2048]{1,0:T(8,128)(2,1)S(1)} %bitcast_add_fusion.24), channel_id=1, source_target_pairs={{0,4},{8,0},{16,8},{24,16},{28,24},{20,28},{12,20},{4,12},{1,5},{9... | collective-permute-start | bytes 1572872 | tf_op jit(solution)/shard_map/ppermute | solution.py:172
  158.8 14.4 %collective-permute-start.26 = (bf16[128,2048]{1,0:T(8,128)(2,1)S(1)}, bf16[128,2048]{1,0:T(8,128)(2,1)S(1)}, u32[]{:S(2)}, u32[]{:S(2)}) collective-permute-start(bf16[128,2048]{1,0:T(8,128)(2,1)S(1)} %bitcast_add_fusion.26), channel_id=1, source_target_pairs={{0,8},{8,16},{16,24},{24,28},{28,20},{20,12},{12,4},{4,0},{1,9},{9... | collective-permute-start | bytes 1572872 | tf_op jit(solution)/shard_map/ppermute | solution.py:171
  200.5 13.0 %collective-permute-start.34 = (bf16[128,2048]{1,0:T(8,128)(2,1)}, bf16[128,2048]{1,0:T(8,128)(2,1)}, u32[]{:S(2)}, u32[]{:S(2)}) collective-permute-start(bf16[128,2048]{1,0:T(8,128)(2,1)} %fusion.19), channel_id=1, source_target_pairs={{0,4},{8,0},{16,8},{24,16},{28,24},{20,28},{12,20},{4,12},{1,5},{9... | collective-permute-start | bytes 1572872 | tf_op jit(solution)/shard_map/ppermute | solution.py:172
  203.5 12.9 %collective-permute-start.29 = (bf16[128,2048]{1,0:T(8,128)(2,1)}, bf16[128,2048]{1,0:T(8,128)(2,1)}, u32[]{:S(2)}, u32[]{:S(2)}) collective-permute-start(bf16[128,2048]{1,0:T(8,128)(2,1)} %fusion.23), channel_id=1, source_target_pairs={{0,8},{8,16},{16,24},{24,28},{28,20},{20,12},{12,4},{4,0},{1,9},{9... | collective-permute-start | bytes 1572872 | tf_op jit(solution)/shard_map/ppermute | solution.py:171
  240.5 13.8 %collective-permute-start.36 = (bf16[160,2048]{1,0:T(8,128)(2,1)S(1)}, bf16[160,2048]{1,0:T(8,128)(2,1)S(1)}, u32[]{:S(2)}, u32[]{:S(2)}) collective-permute-start(bf16[160,2048]{1,0:T(8,128)(2,1)S(1)} %fusion.28), channel_id=1, source_target_pairs={{0,8},{8,16},{16,24},{24,28},{28,20},{20,12},{12,4},{4,0},{1,9},{9... | collective-permute-start | bytes 1966088 | tf_op jit(solution)/shard_map/ppermute | solution.py:94
  243.5 13.5 %collective-permute-start.43 = (bf16[160,2048]{1,0:T(8,128)(2,1)S(1)}, bf16[160,2048]{1,0:T(8,128)(2,1)S(1)}, u32[]{:S(2)}, u32[]{:S(2)}) collective-permute-start(bf16[160,2048]{1,0:T(8,128)(2,1)S(1)} %fusion.29), channel_id=1, source_target_pairs={{0,4},{8,0},{16,8},{24,16},{28,24},{20,28},{12,20},{4,12},{1,5},{9... | collective-permute-start | bytes 1966088 | tf_op jit(solution)/shard_map/ppermute | solution.py:95
  255.8 13.4 %collective-permute-start.37 = (bf16[160,2048]{1,0:T(8,128)(2,1)S(1)}, bf16[160,2048]{1,0:T(8,128)(2,1)S(1)}, u32[]{:S(2)}, u32[]{:S(2)}) collective-permute-start(bf16[160,2048]{1,0:T(8,128)(2,1)S(1)} %fusion.16), channel_id=1, source_target_pairs={{0,8},{8,16},{16,24},{24,28},{28,20},{20,12},{12,4},{4,0},{1,9},{9... | collective-permute-start | bytes 1966088 | tf_op jit(solution)/shard_map/ppermute | solution.py:94
  258.5 13.8 %collective-permute-start.44 = (bf16[160,2048]{1,0:T(8,128)(2,1)S(1)}, bf16[160,2048]{1,0:T(8,128)(2,1)S(1)}, u32[]{:S(2)}, u32[]{:S(2)}) collective-permute-start(bf16[160,2048]{1,0:T(8,128)(2,1)S(1)} %fusion.10), channel_id=1, source_target_pairs={{0,4},{8,0},{16,8},{24,16},{28,24},{20,28},{12,20},{4,12},{1,5},{9... | collective-permute-start | bytes 1966088 | tf_op jit(solution)/shard_map/ppermute | solution.py:95
  270.7 13.4 %collective-permute-start.38 = (bf16[160,2048]{1,0:T(8,128)(2,1)S(1)}, bf16[160,2048]{1,0:T(8,128)(2,1)S(1)}, u32[]{:S(2)}, u32[]{:S(2)}) collective-permute-start(bf16[160,2048]{1,0:T(8,128)(2,1)S(1)} %fusion.15), channel_id=1, source_target_pairs={{0,8},{8,16},{16,24},{24,28},{28,20},{20,12},{12,4},{4,0},{1,9},{9... | collective-permute-start | bytes 1966088 | tf_op jit(solution)/shard_map/ppermute | solution.py:94
  272.5 14.7 %collective-permute-start.45 = (bf16[160,2048]{1,0:T(8,128)(2,1)S(1)}, bf16[160,2048]{1,0:T(8,128)(2,1)S(1)}, u32[]{:S(2)}, u32[]{:S(2)}) collective-permute-start(bf16[160,2048]{1,0:T(8,128)(2,1)S(1)} %fusion.9), channel_id=1, source_target_pairs={{0,4},{8,0},{16,8},{24,16},{28,24},{20,28},{12,20},{4,12},{1,5},{9... | collective-permute-start | bytes 1966088 | tf_op jit(solution)/shard_map/ppermute | solution.py:95
  285.6 13.4 %collective-permute-start.39 = (bf16[160,2048]{1,0:T(8,128)(2,1)S(1)}, bf16[160,2048]{1,0:T(8,128)(2,1)S(1)}, u32[]{:S(2)}, u32[]{:S(2)}) collective-permute-start(bf16[160,2048]{1,0:T(8,128)(2,1)S(1)} %fusion.14), channel_id=1, source_target_pairs={{0,8},{8,16},{16,24},{24,28},{28,20},{20,12},{12,4},{4,0},{1,9},{9... | collective-permute-start | bytes 1966088 | tf_op jit(solution)/shard_map/ppermute | solution.py:94
  287.3 14.7 %collective-permute-start.46 = (bf16[160,2048]{1,0:T(8,128)(2,1)S(1)}, bf16[160,2048]{1,0:T(8,128)(2,1)S(1)}, u32[]{:S(2)}, u32[]{:S(2)}) collective-permute-start(bf16[160,2048]{1,0:T(8,128)(2,1)S(1)} %fusion.8), channel_id=1, source_target_pairs={{0,4},{8,0},{16,8},{24,16},{28,24},{20,28},{12,20},{4,12},{1,5},{9... | collective-permute-start | bytes 1966088 | tf_op jit(solution)/shard_map/ppermute | solution.py:95
  300.5 13.2 %collective-permute-start.40 = (bf16[160,2048]{1,0:T(8,128)(2,1)S(1)}, bf16[160,2048]{1,0:T(8,128)(2,1)S(1)}, u32[]{:S(2)}, u32[]{:S(2)}) collective-permute-start(bf16[160,2048]{1,0:T(8,128)(2,1)S(1)} %fusion.13), channel_id=1, source_target_pairs={{0,8},{8,16},{16,24},{24,28},{28,20},{20,12},{12,4},{4,0},{1,9},{9... | collective-permute-start | bytes 1966088 | tf_op jit(solution)/shard_map/ppermute | solution.py:94
  302.2 14.7 %collective-permute-start.47 = (bf16[160,2048]{1,0:T(8,128)(2,1)S(1)}, bf16[160,2048]{1,0:T(8,128)(2,1)S(1)}, u32[]{:S(2)}, u32[]{:S(2)}) collective-permute-start(bf16[160,2048]{1,0:T(8,128)(2,1)S(1)} %fusion.7), channel_id=1, source_target_pairs={{0,4},{8,0},{16,8},{24,16},{28,24},{20,28},{12,20},{4,12},{1,5},{9... | collective-permute-start | bytes 1966088 | tf_op jit(solution)/shard_map/ppermute | solution.py:95
  315.1 14.9 %collective-permute-start.41 = (bf16[160,2048]{1,0:T(8,128)(2,1)S(1)}, bf16[160,2048]{1,0:T(8,128)(2,1)S(1)}, u32[]{:S(2)}, u32[]{:S(2)}) collective-permute-start(bf16[160,2048]{1,0:T(8,128)(2,1)S(1)} %fusion.12), channel_id=1, source_target_pairs={{0,8},{8,16},{16,24},{24,28},{28,20},{20,12},{12,4},{4,0},{1,9},{9... | collective-permute-start | bytes 1966088 | tf_op jit(solution)/shard_map/ppermute | solution.py:94
  317.1 15.2 %collective-permute-start.48 = (bf16[160,2048]{1,0:T(8,128)(2,1)S(1)}, bf16[160,2048]{1,0:T(8,128)(2,1)S(1)}, u32[]{:S(2)}, u32[]{:S(2)}) collective-permute-start(bf16[160,2048]{1,0:T(8,128)(2,1)S(1)} %fusion.6), channel_id=1, source_target_pairs={{0,4},{8,0},{16,8},{24,16},{28,24},{20,28},{12,20},{4,12},{1,5},{9... | collective-permute-start | bytes 1966088 | tf_op jit(solution)/shard_map/ppermute | solution.py:95
  (37 other events, 348.0 us)

commit v11 on v10

--- a/solution.py
+++ b/solution.py
@@ -344,7 +344,7 @@
     key_part = across(dscore, queries) * factor
     value_part = across(prob.astype(jnp.bfloat16), grad_stack)
     pair_all = jnp.concatenate([key_part, value_part], axis=1)
-    out_ring = Ring(out_weight_grad, ring, "ctx").advance(len(ring) // 4)
+    out_ring = Ring(out_weight_grad, ring, "ctx").advance(len(ring) // 8)
     pair_grad = butterfly_sum(direct_scatter(pair_all, "ctx"), "tp")
     out_ring.state, pair_grad = lax.optimization_barrier((out_ring.state, pair_grad))
 

time: 348 us -> 358 us (1.029)
  waiting for transfers between devices: 122 us -> 129 us
    ppermute x7, waiting for transfers between devices: 4.4 us -> 26.2 us  [advance(): lax.ppermute(send_left.astype(jnp.bfloat16), self.axis, self.forward)]
    ppermute x7, waiting for transfers between devices: 35.6 us -> 19.9 us  [advance(): lax.ppermute(send_right.astype(jnp.bfloat16), self.axis, self.backward)]
    ppermute x7, waiting for transfers between devices: 55.9 us -> 60.3 us  [ring_scatter(): got_left = lax.ppermute(send_left.astype(jnp.bfloat16), axis, forward)]
  transfers between devices with their start and end apart: 50 -> 50, of which waited for: 28 -> 26; matrix products, arithmetic and copies ran while one was open for 24% -> 24% of each run, Pallas kernels for 0% -> 0%
where the time goes in v11:
time: 358 us; the launch traced here: 356 us
  waiting for transfers between devices  129 us (36%)
  starting transfers between devices  58.5 us (16%)
  other arithmetic  49.3 us (14%)
  between operations  37.2 us (10%)
  matrix products  36.8 us (10%)
  local copies, waits for them, and re-layouts  31 us (9%)
  blocking collectives  13.9 us (4%)
    ppermute x7, waiting for transfers between devices, ring_scatter(): got_left = lax.ppermute(send_left.astype(jnp.bfloat16), axis, forward)  60.3 us
    ppermute x7, waiting for transfers between devices, advance(): lax.ppermute(send_left.astype(jnp.bfloat16), self.axis, self.forward)  26.2 us
    ppermute x7, waiting for transfers between devices, advance(): lax.ppermute(send_right.astype(jnp.bfloat16), self.axis, self.backward)  19.9 us
    ppermute x7, waiting for transfers between devices, direct_gather(): got[count - shift] = lax.ppermute(value, axis, pairs)  16.1 us
    dot_general x4, matrix products, against(): lax.dot_general(left, right, (((1,), (1,)), ((), ())), preferred_element_...  14.9 us
    ppermute x7, starting transfers between devices, direct_gather(): got[count - shift] = lax.ppermute(value, axis, pairs)  12.2 us
    ppermute x7, starting transfers between devices, direct_scatter(): lax.ppermute(blocks[shift].astype(jnp.bfloat16), axis, pairs)  11.9 us
    ppermute x7, starting transfers between devices, ring_scatter(): got_right = lax.ppermute(send_right.astype(jnp.bfloat16), axis, backward)  10.3 us
  transfers between devices with their start and end apart: 50, of which 26 were waited for; matrix products, arithmetic and copies ran while one was open for 24% of the time, Pallas kernels for 0%

profile of v11, /device:TPU:0, one launch (start us, length us, event | category | flops | bytes accessed | tf_op | source)
XLA Modules:
  0.0 355.9 jit_solution(16965689534788065610)
XLA Ops:
  2.2 6.9 %fusion.70 = f32[256,1280]{1,0:T(8,128)S(1)} fusion(bf16[256,4096]{1,0:T(8,128)(2,1)S(1)} %copy-done, bf16[1280,4096]{1,0:T(8,128)(2,1)} %param.13), kind=kOutput, calls=%fused_computation.172 | convolution fusion | flops 2684354560 | bytes 13893632 | tf_op jit(solution)/shard_map/dot_general | solution.py:35
  9.6 6.4 %convolution_convert_fusion.2 = bf16[256,1024]{1,0:T(8,128)(2,1)S(1)} fusion(bf16[256,4096]{1,0:T(8,128)(2,1)} %param.15, bf16[1024,4096]{1,0:T(8,128)(2,1)} %param.14), kind=kOutput, calls=%fused_computation.45 | convolution fusion | flops 2147745792 | bytes 11010048 | tf_op jit(solution)/shard_map/dot_general | solution.py:35
  17.6 2.6 collective-permute-start.11
  37.9 4.2 %collective-permute-done.1 = f32[128,256]{1,0:T(8,128)S(1)} collective-permute-done((f32[128,256]{1,0:T(8,128)S(1)}, f32[128,256]{1,0:T(8,128)S(1)}, u32[]{:S(2)}, u32[]{:S(2)}) %collective-permute-start.1) | collective-permute-done | bytes 131104 | tf_op jit(solution)/shard_map/ppermute | solution.py:197
  44.3 4.6 %collective-permute-start.3 = (bf16[259,256]{1,0:T(8,128)(2,1)S(1)}, bf16[259,256]{1,0:T(8,128)(2,1)S(1)}, u32[]{:S(2)}, u32[]{:S(2)}) collective-permute-start(bf16[259,256]{1,0:T(8,128)(2,1)S(1)} %get-tuple-element.19), channel_id=1, source_target_pairs={{0,28},{4,0},{8,4},{12,8},{16,12},{20,16},{24,20},{28,24},{1,29},{... | collective-permute-start | bytes 397832 | tf_op jit(solution)/shard_map/ppermute | solution.py:226
  49.4 3.0 collective-permute-start.6
  58.8 13.5 %collective-permute-done.6 = bf16[259,256]{1,0:T(8,128)(2,1)S(1)} collective-permute-done((bf16[259,256]{1,0:T(8,128)(2,1)S(1)}, bf16[259,256]{1,0:T(8,128)(2,1)S(1)}, u32[]{:S(2)}, u32[]{:S(2)}) %collective-permute-start.6) | collective-permute-done | bytes 132640 | tf_op jit(solution)/shard_map/ppermute | solution.py:226
  83.2 2.8 collective-permute-start.17
  89.0 6.7 %all_gather.6 = bf16[256,1024]{1,0:T(8,128)(2,1)S(1)} all-gather(bf16[64,1024]{1,0:T(8,128)(2,1)S(1)} %bitcast.244), channel_id=1, replica_groups=mesh['ctx'=8,'tp'=4] {'tp'}, dimensions={0}, use_global_device_ids=true | all-gather | bytes 655360 | tf_op jit(solution)/shard_map/all_gather | solution.py:332
  95.7 2.4 fusion.71
  98.2 6.3 %fusion.65 = (f32[8,128,2048]{2,1,0:T(8,128)}, f32[8,128,2048]{2,1,0:T(8,128)}) fusion(f32[8,128,4096]{2,1,0:T(8,128)S(1)} %bitcast.233), kind=kLoop, calls=%fused_computation.167 | loop fusion | bytes 33554432 | tf_op jit(solution)/shard_map/slice | solution.py:157
  104.5 2.4 collective-permute-start.20
  106.9 2.9 collective-permute-start.21
  123.1 2.7 collective-permute-done.14
  128.1 3.0 collective-permute-done.13
  160.3 7.8 %collective-permute-done.24 = bf16[128,2048]{1,0:T(8,128)(2,1)S(1)} collective-permute-done((bf16[128,2048]{1,0:T(8,128)(2,1)}, bf16[128,2048]{1,0:T(8,128)(2,1)S(1)}, u32[]{:S(2)}, u32[]{:S(2)}) %collective-permute-start.24) | collective-permute-done | bytes 524320 | tf_op jit(solution)/shard_map/ppermute | solution.py:171
  174.9 7.2 %collective-permute-done.25 = bf16[128,2048]{1,0:T(8,128)(2,1)S(1)} collective-permute-done((bf16[128,2048]{1,0:T(8,128)(2,1)S(1)}, bf16[128,2048]{1,0:T(8,128)(2,1)S(1)}, u32[]{:S(2)}, u32[]{:S(2)}) %collective-permute-start.25) | collective-permute-done | bytes 524320 | tf_op jit(solution)/shard_map/ppermute | solution.py:171
  188.5 6.6 %collective-permute-done.26 = bf16[128,2048]{1,0:T(8,128)(2,1)S(1)} collective-permute-done((bf16[128,2048]{1,0:T(8,128)(2,1)S(1)}, bf16[128,2048]{1,0:T(8,128)(2,1)S(1)}, u32[]{:S(2)}, u32[]{:S(2)}) %collective-permute-start.26) | collective-permute-done | bytes 524320 | tf_op jit(solution)/shard_map/ppermute | solution.py:171
  197.3 7.1 %all_gather.7 = bf16[256,1024]{1,0:T(8,128)(2,1)} all-gather(bf16[64,1024]{1,0:T(8,128)(2,1)S(1)} %copy_bitcast_fusion.1), channel_id=1, replica_groups=mesh['ctx'=8,'tp'=4] {'tp'}, dimensions={0}, use_global_device_ids=true | all-gather | bytes 655360 | tf_op jit(solution)/shard_map/all_gather | solution.py:356
  213.8 7.2 %collective-permute-done.34 = bf16[128,2048]{1,0:T(8,128)(2,1)} collective-permute-done((bf16[128,2048]{1,0:T(8,128)(2,1)}, bf16[128,2048]{1,0:T(8,128)(2,1)}, u32[]{:S(2)}, u32[]{:S(2)}) %collective-permute-start.34) | collective-permute-done | bytes 524320 | tf_op jit(solution)/shard_map/ppermute | solution.py:172
  226.4 2.9 fusion.73
  229.4 6.6 %collective-permute-done.35 = bf16[128,2048]{1,0:T(8,128)(2,1)S(1)} collective-permute-done((bf16[128,2048]{1,0:T(8,128)(2,1)S(1)}, bf16[128,2048]{1,0:T(8,128)(2,1)S(1)}, u32[]{:S(2)}, u32[]{:S(2)}) %collective-permute-start.35) | collective-permute-done | bytes 524320 | tf_op jit(solution)/shard_map/ppermute | solution.py:172
  240.0 8.1 %fusion.64 = (f32[8,160,2048]{2,1,0:T(8,128)}, f32[8,160,2048]{2,1,0:T(8,128)}) fusion(f32[8,160,4096]{2,1,0:T(8,128)S(1)} %bitcast.232), kind=kLoop, calls=%fused_computation.166 | loop fusion | bytes 41943040 | tf_op jit(solution)/shard_map/slice | solution.py:83
  253.7 10.9 %collective-permute-done.36 = bf16[160,2048]{1,0:T(8,128)(2,1)S(1)} collective-permute-done((bf16[160,2048]{1,0:T(8,128)(2,1)S(1)}, bf16[160,2048]{1,0:T(8,128)(2,1)S(1)}, u32[]{:S(2)}, u32[]{:S(2)}) %collective-permute-start.36) | collective-permute-done | bytes 655392 | tf_op jit(solution)/shard_map/ppermute | solution.py:94
  269.8 10.4 %collective-permute-done.37 = bf16[160,2048]{1,0:T(8,128)(2,1)S(1)} collective-permute-done((bf16[160,2048]{1,0:T(8,128)(2,1)S(1)}, bf16[160,2048]{1,0:T(8,128)(2,1)S(1)}, u32[]{:S(2)}, u32[]{:S(2)}) %collective-permute-start.37) | collective-permute-done | bytes 655392 | tf_op jit(solution)/shard_map/ppermute | solution.py:94
  284.3 10.7 %collective-permute-done.38 = bf16[160,2048]{1,0:T(8,128)(2,1)S(1)} collective-permute-done((bf16[160,2048]{1,0:T(8,128)(2,1)S(1)}, bf16[160,2048]{1,0:T(8,128)(2,1)S(1)}, u32[]{:S(2)}, u32[]{:S(2)}) %collective-permute-start.38) | collective-permute-done | bytes 655392 | tf_op jit(solution)/shard_map/ppermute | solution.py:94
  298.8 11.1 %collective-permute-done.39 = bf16[160,2048]{1,0:T(8,128)(2,1)S(1)} collective-permute-done((bf16[160,2048]{1,0:T(8,128)(2,1)S(1)}, bf16[160,2048]{1,0:T(8,128)(2,1)S(1)}, u32[]{:S(2)}, u32[]{:S(2)}) %collective-permute-start.39) | collective-permute-done | bytes 655392 | tf_op jit(solution)/shard_map/ppermute | solution.py:94
  313.8 7.8 %convolution_convert_fusion = bf16[256,4096]{1,0:T(8,128)(2,1)} fusion(bf16[256,1024]{1,0:T(8,128)(2,1)S(1)} %all_gather.6, bf16[1024,4096]{1,0:T(8,128)(2,1)} %param.14), kind=kOutput, calls=%fused_computation.3 | convolution fusion | flops 2148532224 | bytes 11010048 | tf_op jit(solution)/shard_map/dot_general | solution.py:333
  321.6 3.3 collective-permute-done.40
  328.9 4.1 %convolution_convert_fusion.1 = bf16[256,4096]{1,0:T(8,128)(2,1)} fusion(bf16[256,1280]{1,0:T(8,128)(2,1)S(1)} %concatenate.45, bf16[1280,4096]{1,0:T(8,128)(2,1)S(1)} %bitcast.251), kind=kOutput, calls=%fused_computation.4 | convolution fusion | flops 2685403136 | bytes 13238272 | tf_op jit(solution)/shard_map/dot_general | solution.py:361
  333.0 7.0 %collective-permute-done.41 = bf16[160,2048]{1,0:T(8,128)(2,1)S(1)} collective-permute-done((bf16[160,2048]{1,0:T(8,128)(2,1)S(1)}, bf16[160,2048]{1,0:T(8,128)(2,1)S(1)}, u32[]{:S(2)}, u32[]{:S(2)}) %collective-permute-start.41) | collective-permute-done | bytes 655392 | tf_op jit(solution)/shard_map/ppermute | solution.py:94
  345.3 6.8 %collective-permute-done.42 = bf16[160,2048]{1,0:T(8,128)(2,1)S(1)} collective-permute-done((bf16[160,2048]{1,0:T(8,128)(2,1)S(1)}, bf16[160,2048]{1,0:T(8,128)(2,1)S(1)}, u32[]{:S(2)}, u32[]{:S(2)}) %collective-permute-start.42) | collective-permute-done | bytes 655392 | tf_op jit(solution)/shard_map/ppermute | solution.py:94
  (209 shorter events, 122.6 us)
Async XLA Ops:
  9.1 25.8 %collective-permute-start = (f32[256,1280]{1,0:T(8,128)S(1)}, f32[256,1280]{1,0:T(8,128)}, u32[]{:S(2)}, u32[]{:S(2)}) collective-permute-start(f32[256,1280]{1,0:T(8,128)S(1)} %fusion.70), channel_id=1, source_target_pairs={{0,1},{1,0},{2,3},{3,2},{4,5},{5,4},{6,7},{7,6},{8,9},{9,8},{10,11... | collective-permute-start | bytes 3932168 | tf_op jit(solution)/shard_map/ppermute | solution.py:189
  17.6 19.0 %collective-permute-start.11 = (bf16[128,1024]{1,0:T(8,128)(2,1)}, bf16[128,1024]{1,0:T(8,128)(2,1)}, u32[]{:S(2)}, u32[]{:S(2)}) collective-permute-start(bf16[128,1024]{1,0:T(8,128)(2,1)} %constant_dynamic-slice_fusion), channel_id=1, source_target_pairs={{0,2},{1,3},{2,0},{3,1},{4,6},{5,7},{6,4},{7,5},{8,10},{9,11},{10,... | collective-permute-start | bytes 786440 | tf_op jit(solution)/shard_map/ppermute | solution.py:212
  49.4 22.9 %collective-permute-start.6 = (bf16[259,256]{1,0:T(8,128)(2,1)S(1)}, bf16[259,256]{1,0:T(8,128)(2,1)S(1)}, u32[]{:S(2)}, u32[]{:S(2)}) collective-permute-start(bf16[259,256]{1,0:T(8,128)(2,1)S(1)} %get-tuple-element.19), channel_id=1, source_target_pairs={{0,16},{4,20},{8,24},{12,28},{16,0},{20,4},{24,8},{28,12},{1,17},{... | collective-permute-start | bytes 397832 | tf_op jit(solution)/shard_map/ppermute | solution.py:226
  53.0 20.7 %collective-permute-start.7 = (bf16[259,256]{1,0:T(8,128)(2,1)S(1)}, bf16[259,256]{1,0:T(8,128)(2,1)S(1)}, u32[]{:S(2)}, u32[]{:S(2)}) collective-permute-start(bf16[259,256]{1,0:T(8,128)(2,1)S(1)} %get-tuple-element.19), channel_id=1, source_target_pairs={{0,12},{4,16},{8,20},{12,24},{16,28},{20,0},{24,4},{28,8},{1,13},{... | collective-permute-start | bytes 397832 | tf_op jit(solution)/shard_map/ppermute | solution.py:226
  54.2 19.6 %collective-permute-start.8 = (bf16[259,256]{1,0:T(8,128)(2,1)S(1)}, bf16[259,256]{1,0:T(8,128)(2,1)S(1)}, u32[]{:S(2)}, u32[]{:S(2)}) collective-permute-start(bf16[259,256]{1,0:T(8,128)(2,1)S(1)} %get-tuple-element.19), channel_id=1, source_target_pairs={{0,8},{4,12},{8,16},{12,20},{16,24},{20,28},{24,0},{28,4},{1,9},{5... | collective-permute-start | bytes 397832 | tf_op jit(solution)/shard_map/ppermute | solution.py:226
  55.8 17.9 %collective-permute-start.9 = (bf16[259,256]{1,0:T(8,128)(2,1)S(1)}, bf16[259,256]{1,0:T(8,128)(2,1)S(1)}, u32[]{:S(2)}, u32[]{:S(2)}) collective-permute-start(bf16[259,256]{1,0:T(8,128)(2,1)S(1)} %get-tuple-element.19), channel_id=1, source_target_pairs={{0,4},{4,8},{8,12},{12,16},{16,20},{20,24},{24,28},{28,0},{1,5},{5... | collective-permute-start | bytes 397832 | tf_op jit(solution)/shard_map/ppermute | solution.py:226
  82.3 22.2 %collective-permute-start.15 = (bf16[256,256]{1,0:T(8,128)(2,1)}, bf16[256,256]{1,0:T(8,128)(2,1)}, u32[]{:S(2)}, u32[]{:S(2)}) collective-permute-start(bf16[256,256]{1,0:T(8,128)(2,1)} %get-tuple-element.30), channel_id=1, source_target_pairs={{0,4},{4,8},{8,12},{12,16},{16,20},{20,24},{24,28},{28,0},{1,5},{5... | collective-permute-start | bytes 393224 | tf_op jit(solution)/shard_map/ppermute | solution.py:237
  82.3 24.6 %collective-permute-start.16 = (bf16[256,256]{1,0:T(8,128)(2,1)}, bf16[256,256]{1,0:T(8,128)(2,1)}, u32[]{:S(2)}, u32[]{:S(2)}) collective-permute-start(bf16[256,256]{1,0:T(8,128)(2,1)} %get-tuple-element.36), channel_id=1, source_target_pairs={{0,8},{4,12},{8,16},{12,20},{16,24},{20,28},{24,0},{28,4},{1,9},{5... | collective-permute-start | bytes 393224 | tf_op jit(solution)/shard_map/ppermute | solution.py:237
  83.2 28.7 %collective-permute-start.17 = (bf16[256,256]{1,0:T(8,128)(2,1)}, bf16[256,256]{1,0:T(8,128)(2,1)}, u32[]{:S(2)}, u32[]{:S(2)}) collective-permute-start(bf16[256,256]{1,0:T(8,128)(2,1)} %get-tuple-element.35), channel_id=1, source_target_pairs={{0,12},{4,16},{8,20},{12,24},{16,28},{20,0},{24,4},{28,8},{1,13},{... | collective-permute-start | bytes 393224 | tf_op jit(solution)/shard_map/ppermute | solution.py:237
  86.0 25.9 %collective-permute-start.18 = (bf16[256,256]{1,0:T(8,128)(2,1)}, bf16[256,256]{1,0:T(8,128)(2,1)}, u32[]{:S(2)}, u32[]{:S(2)}) collective-permute-start(bf16[256,256]{1,0:T(8,128)(2,1)} %get-tuple-element.34), channel_id=1, source_target_pairs={{0,16},{4,20},{8,24},{12,28},{16,0},{20,4},{24,8},{28,12},{1,17},{... | collective-permute-start | bytes 393224 | tf_op jit(solution)/shard_map/ppermute | solution.py:237
  87.6 24.3 %collective-permute-start.19 = (bf16[256,256]{1,0:T(8,128)(2,1)}, bf16[256,256]{1,0:T(8,128)(2,1)}, u32[]{:S(2)}, u32[]{:S(2)}) collective-permute-start(bf16[256,256]{1,0:T(8,128)(2,1)} %get-tuple-element.33), channel_id=1, source_target_pairs={{0,20},{4,24},{8,28},{12,0},{16,4},{20,8},{24,12},{28,16},{1,21},{... | collective-permute-start | bytes 393224 | tf_op jit(solution)/shard_map/ppermute | solution.py:237
  111.9 13.9 %collective-permute-start.14 = (bf16[128,2048]{1,0:T(8,128)(2,1)}, bf16[128,2048]{1,0:T(8,128)(2,1)}, u32[]{:S(2)}, u32[]{:S(2)}) collective-permute-start(bf16[128,2048]{1,0:T(8,128)(2,1)} %fusion.31), channel_id=1, source_target_pairs={{0,4},{8,0},{16,8},{24,16},{28,24},{20,28},{12,20},{4,12},{1,5},{9... | collective-permute-start | bytes 1572872 | tf_op jit(solution)/shard_map/ppermute | solution.py:172
  116.4 14.6 %collective-permute-start.13 = (bf16[128,2048]{1,0:T(8,128)(2,1)}, bf16[128,2048]{1,0:T(8,128)(2,1)}, u32[]{:S(2)}, u32[]{:S(2)}) collective-permute-start(bf16[128,2048]{1,0:T(8,128)(2,1)} %fusion.30), channel_id=1, source_target_pairs={{0,8},{8,16},{16,24},{24,28},{28,20},{20,12},{12,4},{4,0},{1,9},{9... | collective-permute-start | bytes 1572872 | tf_op jit(solution)/shard_map/ppermute | solution.py:171
  133.3 23.5 %collective-permute-start.30 = (bf16[128,2048]{1,0:T(8,128)(2,1)}, bf16[128,2048]{1,0:T(8,128)(2,1)}, u32[]{:S(2)}, u32[]{:S(2)}) collective-permute-start(bf16[128,2048]{1,0:T(8,128)(2,1)} %bitcast_add_fusion.26), channel_id=1, source_target_pairs={{0,4},{8,0},{16,8},{24,16},{28,24},{20,28},{12,20},{4,12},{1,5},{9... | collective-permute-start | bytes 1572872 | tf_op jit(solution)/shard_map/ppermute | solution.py:172
  154.1 13.9 %collective-permute-start.24 = (bf16[128,2048]{1,0:T(8,128)(2,1)}, bf16[128,2048]{1,0:T(8,128)(2,1)S(1)}, u32[]{:S(2)}, u32[]{:S(2)}) collective-permute-start(bf16[128,2048]{1,0:T(8,128)(2,1)} %bitcast_add_fusion.27), channel_id=1, source_target_pairs={{0,8},{8,16},{16,24},{24,28},{28,20},{20,12},{12,4},{4,0},{1,9},{9... | collective-permute-start | bytes 1572872 | tf_op jit(solution)/shard_map/ppermute | solution.py:171
  158.3 13.5 %collective-permute-start.31 = (bf16[128,2048]{1,0:T(8,128)(2,1)S(1)}, bf16[128,2048]{1,0:T(8,128)(2,1)S(1)}, u32[]{:S(2)}, u32[]{:S(2)}) collective-permute-start(bf16[128,2048]{1,0:T(8,128)(2,1)S(1)} %fusion.22), channel_id=1, source_target_pairs={{0,4},{8,0},{16,8},{24,16},{28,24},{20,28},{12,20},{4,12},{1,5},{9... | collective-permute-start | bytes 1572872 | tf_op jit(solution)/shard_map/ppermute | solution.py:172
  187.0 17.4 %collective-permute-start.33 = (bf16[128,2048]{1,0:T(8,128)(2,1)S(1)}, bf16[128,2048]{1,0:T(8,128)(2,1)S(1)}, u32[]{:S(2)}, u32[]{:S(2)}) collective-permute-start(bf16[128,2048]{1,0:T(8,128)(2,1)S(1)} %fusion.20), channel_id=1, source_target_pairs={{0,4},{8,0},{16,8},{24,16},{28,24},{20,28},{12,20},{4,12},{1,5},{9... | collective-permute-start | bytes 1572872 | tf_op jit(solution)/shard_map/ppermute | solution.py:172
  206.6 14.5 %collective-permute-start.34 = (bf16[128,2048]{1,0:T(8,128)(2,1)}, bf16[128,2048]{1,0:T(8,128)(2,1)}, u32[]{:S(2)}, u32[]{:S(2)}) collective-permute-start(bf16[128,2048]{1,0:T(8,128)(2,1)} %fusion.19), channel_id=1, source_target_pairs={{0,4},{8,0},{16,8},{24,16},{28,24},{20,28},{12,20},{4,12},{1,5},{9... | collective-permute-start | bytes 1572872 | tf_op jit(solution)/shard_map/ppermute | solution.py:172
  209.9 14.2 %collective-permute-start.28 = (bf16[128,2048]{1,0:T(8,128)(2,1)}, bf16[128,2048]{1,0:T(8,128)(2,1)}, u32[]{:S(2)}, u32[]{:S(2)}) collective-permute-start(bf16[128,2048]{1,0:T(8,128)(2,1)} %fusion.24), channel_id=1, source_target_pairs={{0,8},{8,16},{16,24},{24,28},{28,20},{20,12},{12,4},{4,0},{1,9},{9... | collective-permute-start | bytes 1572872 | tf_op jit(solution)/shard_map/ppermute | solution.py:171
  222.5 13.4 %collective-permute-start.35 = (bf16[128,2048]{1,0:T(8,128)(2,1)S(1)}, bf16[128,2048]{1,0:T(8,128)(2,1)S(1)}, u32[]{:S(2)}, u32[]{:S(2)}) collective-permute-start(bf16[128,2048]{1,0:T(8,128)(2,1)S(1)} %fusion.18), channel_id=1, source_target_pairs={{0,4},{8,0},{16,8},{24,16},{28,24},{20,28},{12,20},{4,12},{1,5},{9... | collective-permute-start | bytes 1572872 | tf_op jit(solution)/shard_map/ppermute | solution.py:172
  249.6 15.0 %collective-permute-start.36 = (bf16[160,2048]{1,0:T(8,128)(2,1)S(1)}, bf16[160,2048]{1,0:T(8,128)(2,1)S(1)}, u32[]{:S(2)}, u32[]{:S(2)}) collective-permute-start(bf16[160,2048]{1,0:T(8,128)(2,1)S(1)} %fusion.28), channel_id=1, source_target_pairs={{0,8},{8,16},{16,24},{24,28},{28,20},{20,12},{12,4},{4,0},{1,9},{9... | collective-permute-start | bytes 1966088 | tf_op jit(solution)/shard_map/ppermute | solution.py:94
  252.5 14.6 %collective-permute-start.43 = (bf16[160,2048]{1,0:T(8,128)(2,1)S(1)}, bf16[160,2048]{1,0:T(8,128)(2,1)S(1)}, u32[]{:S(2)}, u32[]{:S(2)}) collective-permute-start(bf16[160,2048]{1,0:T(8,128)(2,1)S(1)} %fusion.29), channel_id=1, source_target_pairs={{0,4},{8,0},{16,8},{24,16},{28,24},{20,28},{12,20},{4,12},{1,5},{9... | collective-permute-start | bytes 1966088 | tf_op jit(solution)/shard_map/ppermute | solution.py:95
  266.1 14.1 %collective-permute-start.37 = (bf16[160,2048]{1,0:T(8,128)(2,1)S(1)}, bf16[160,2048]{1,0:T(8,128)(2,1)S(1)}, u32[]{:S(2)}, u32[]{:S(2)}) collective-permute-start(bf16[160,2048]{1,0:T(8,128)(2,1)S(1)} %fusion.16), channel_id=1, source_target_pairs={{0,8},{8,16},{16,24},{24,28},{28,20},{20,12},{12,4},{4,0},{1,9},{9... | collective-permute-start | bytes 1966088 | tf_op jit(solution)/shard_map/ppermute | solution.py:94
  268.6 14.5 %collective-permute-start.44 = (bf16[160,2048]{1,0:T(8,128)(2,1)S(1)}, bf16[160,2048]{1,0:T(8,128)(2,1)S(1)}, u32[]{:S(2)}, u32[]{:S(2)}) collective-permute-start(bf16[160,2048]{1,0:T(8,128)(2,1)S(1)} %fusion.10), channel_id=1, source_target_pairs={{0,4},{8,0},{16,8},{24,16},{28,24},{20,28},{12,20},{4,12},{1,5},{9... | collective-permute-start | bytes 1966088 | tf_op jit(solution)/shard_map/ppermute | solution.py:95
  281.7 13.4 %collective-permute-start.38 = (bf16[160,2048]{1,0:T(8,128)(2,1)S(1)}, bf16[160,2048]{1,0:T(8,128)(2,1)S(1)}, u32[]{:S(2)}, u32[]{:S(2)}) collective-permute-start(bf16[160,2048]{1,0:T(8,128)(2,1)S(1)} %fusion.15), channel_id=1, source_target_pairs={{0,8},{8,16},{16,24},{24,28},{28,20},{20,12},{12,4},{4,0},{1,9},{9... | collective-permute-start | bytes 1966088 | tf_op jit(solution)/shard_map/ppermute | solution.py:94
  283.3 13.9 %collective-permute-start.45 = (bf16[160,2048]{1,0:T(8,128)(2,1)S(1)}, bf16[160,2048]{1,0:T(8,128)(2,1)S(1)}, u32[]{:S(2)}, u32[]{:S(2)}) collective-permute-start(bf16[160,2048]{1,0:T(8,128)(2,1)S(1)} %fusion.9), channel_id=1, source_target_pairs={{0,4},{8,0},{16,8},{24,16},{28,24},{20,28},{12,20},{4,12},{1,5},{9... | collective-permute-start | bytes 1966088 | tf_op jit(solution)/shard_map/ppermute | solution.py:95
  296.6 13.4 %collective-permute-start.39 = (bf16[160,2048]{1,0:T(8,128)(2,1)S(1)}, bf16[160,2048]{1,0:T(8,128)(2,1)S(1)}, u32[]{:S(2)}, u32[]{:S(2)}) collective-permute-start(bf16[160,2048]{1,0:T(8,128)(2,1)S(1)} %fusion.14), channel_id=1, source_target_pairs={{0,8},{8,16},{16,24},{24,28},{28,20},{20,12},{12,4},{4,0},{1,9},{9... | collective-permute-start | bytes 1966088 | tf_op jit(solution)/shard_map/ppermute | solution.py:94
  297.4 14.6 %collective-permute-start.46 = (bf16[160,2048]{1,0:T(8,128)(2,1)S(1)}, bf16[160,2048]{1,0:T(8,128)(2,1)S(1)}, u32[]{:S(2)}, u32[]{:S(2)}) collective-permute-start(bf16[160,2048]{1,0:T(8,128)(2,1)S(1)} %fusion.8), channel_id=1, source_target_pairs={{0,4},{8,0},{16,8},{24,16},{28,24},{20,28},{12,20},{4,12},{1,5},{9... | collective-permute-start | bytes 1966088 | tf_op jit(solution)/shard_map/ppermute | solution.py:95
  311.5 13.4 %collective-permute-start.40 = (bf16[160,2048]{1,0:T(8,128)(2,1)S(1)}, bf16[160,2048]{1,0:T(8,128)(2,1)S(1)}, u32[]{:S(2)}, u32[]{:S(2)}) collective-permute-start(bf16[160,2048]{1,0:T(8,128)(2,1)S(1)} %fusion.13), channel_id=1, source_target_pairs={{0,8},{8,16},{16,24},{24,28},{28,20},{20,12},{12,4},{4,0},{1,9},{9... | collective-permute-start | bytes 1966088 | tf_op jit(solution)/shard_map/ppermute | solution.py:94
  312.1 14.7 %collective-permute-start.47 = (bf16[160,2048]{1,0:T(8,128)(2,1)S(1)}, bf16[160,2048]{1,0:T(8,128)(2,1)S(1)}, u32[]{:S(2)}, u32[]{:S(2)}) collective-permute-start(bf16[160,2048]{1,0:T(8,128)(2,1)S(1)} %fusion.7), channel_id=1, source_target_pairs={{0,4},{8,0},{16,8},{24,16},{28,24},{20,28},{12,20},{4,12},{1,5},{9... | collective-permute-start | bytes 1966088 | tf_op jit(solution)/shard_map/ppermute | solution.py:95
  326.4 13.7 %collective-permute-start.41 = (bf16[160,2048]{1,0:T(8,128)(2,1)S(1)}, bf16[160,2048]{1,0:T(8,128)(2,1)S(1)}, u32[]{:S(2)}, u32[]{:S(2)}) collective-permute-start(bf16[160,2048]{1,0:T(8,128)(2,1)S(1)} %fusion.12), channel_id=1, source_target_pairs={{0,8},{8,16},{16,24},{24,28},{28,20},{20,12},{12,4},{4,0},{1,9},{9... | collective-permute-start | bytes 1966088 | tf_op jit(solution)/shard_map/ppermute | solution.py:94
  327.0 14.7 %collective-permute-start.48 = (bf16[160,2048]{1,0:T(8,128)(2,1)S(1)}, bf16[160,2048]{1,0:T(8,128)(2,1)S(1)}, u32[]{:S(2)}, u32[]{:S(2)}) collective-permute-start(bf16[160,2048]{1,0:T(8,128)(2,1)S(1)} %fusion.6), channel_id=1, source_target_pairs={{0,4},{8,0},{16,8},{24,16},{28,24},{20,28},{12,20},{4,12},{1,5},{9... | collective-permute-start | bytes 1966088 | tf_op jit(solution)/shard_map/ppermute | solution.py:95
  (35 other events, 355.1 us)

commit v12 on v11

--- a/solution.py
+++ b/solution.py
@@ -344,7 +344,7 @@
     key_part = across(dscore, queries) * factor
     value_part = across(prob.astype(jnp.bfloat16), grad_stack)
     pair_all = jnp.concatenate([key_part, value_part], axis=1)
-    out_ring = Ring(out_weight_grad, ring, "ctx").advance(len(ring) // 8)
+    out_ring = Ring(out_weight_grad, ring, "ctx").advance(3 * len(ring) // 8)
     pair_grad = butterfly_sum(direct_scatter(pair_all, "ctx"), "tp")
     out_ring.state, pair_grad = lax.optimization_barrier((out_ring.state, pair_grad))
 

time: 358 us -> 354 us (0.989)
  starting transfers between devices: 58.5 us -> 68.2 us
  waiting for transfers between devices: 129 us -> 123 us
    ppermute x7, waiting for transfers between devices: 26.2 us -> 7.43 us  [advance(): lax.ppermute(send_left.astype(jnp.bfloat16), self.axis, self.forward)]
    ppermute x7, waiting for transfers between devices: 60.3 us -> 50.6 us  [ring_scatter(): got_left = lax.ppermute(send_left.astype(jnp.bfloat16), axis, forward)]
    ppermute x7, waiting for transfers between devices: 1.05 us -> 9.93 us  [direct_scatter(): lax.ppermute(blocks[shift].astype(jnp.bfloat16), axis, pairs)]
    ppermute x7, starting transfers between devices: 4.55 us -> 13 us  [ring_scatter(): got_left = lax.ppermute(send_left.astype(jnp.bfloat16), axis, forward)]
    ppermute x7, waiting for transfers between devices: 0.7 us -> 8.52 us  [ring_scatter(): got_right = lax.ppermute(send_right.astype(jnp.bfloat16), axis, backward)]
    ppermute x7, starting transfers between devices: 4.87 us -> 11.5 us  [advance(): lax.ppermute(send_left.astype(jnp.bfloat16), self.axis, self.forward)]
    ppermute x7, waiting for transfers between devices: 19.9 us -> 25 us  [advance(): lax.ppermute(send_right.astype(jnp.bfloat16), self.axis, self.backward)]
    ppermute x7, starting transfers between devices: 10.3 us -> 5.89 us  [ring_scatter(): got_right = lax.ppermute(send_right.astype(jnp.bfloat16), axis, backward)]
  transfers between devices with their start and end apart: 50 -> 50, of which waited for: 26 -> 28; matrix products, arithmetic and copies ran while one was open for 24% -> 22% of each run, Pallas kernels for 0% -> 0%
where the time goes in v12:
time: 354 us; the launch traced here: 352 us
  waiting for transfers between devices  123 us (35%)
  starting transfers between devices  68.2 us (19%)
  other arithmetic  48.3 us (14%)
  between operations  36.8 us (10%)
  matrix products  34.8 us (10%)
  local copies, waits for them, and re-layouts  28.4 us (8%)
  blocking collectives  13.4 us (4%)
    ppermute x7, waiting for transfers between devices, ring_scatter(): got_left = lax.ppermute(send_left.astype(jnp.bfloat16), axis, forward)  50.6 us
    ppermute x7, waiting for transfers between devices, advance(): lax.ppermute(send_right.astype(jnp.bfloat16), self.axis, self.backward)  25 us
    ppermute x7, waiting for transfers between devices, direct_gather(): got[count - shift] = lax.ppermute(value, axis, pairs)  16.1 us
    dot_general x4, matrix products, against(): lax.dot_general(left, right, (((1,), (1,)), ((), ())), preferred_element_...  14.9 us
    ppermute x7, starting transfers between devices, ring_scatter(): got_left = lax.ppermute(send_left.astype(jnp.bfloat16), axis, forward)  13 us
    ppermute x7, starting transfers between devices, direct_gather(): got[count - shift] = lax.ppermute(value, axis, pairs)  12.8 us
    ppermute x7, starting transfers between devices, advance(): lax.ppermute(send_left.astype(jnp.bfloat16), self.axis, self.forward)  11.5 us
    ppermute x7, starting transfers between devices, direct_scatter(): lax.ppermute(blocks[shift].astype(jnp.bfloat16), axis, pairs)  11.4 us
  transfers between devices with their start and end apart: 50, of which 28 were waited for; matrix products, arithmetic and copies ran while one was open for 22% of the time, Pallas kernels for 0%

profile of v12, /device:TPU:0, one launch (start us, length us, event | category | flops | bytes accessed | tf_op | source)
XLA Modules:
  0.0 352.4 jit_solution(1362450559447962073)
XLA Ops:
  2.2 6.9 %fusion.70 = f32[256,1280]{1,0:T(8,128)S(1)} fusion(bf16[256,4096]{1,0:T(8,128)(2,1)S(1)} %copy-done, bf16[1280,4096]{1,0:T(8,128)(2,1)} %param.13), kind=kOutput, calls=%fused_computation.172 | convolution fusion | flops 2684354560 | bytes 13893632 | tf_op jit(solution)/shard_map/dot_general | solution.py:35
  9.6 6.4 %convolution_convert_fusion.2 = bf16[256,1024]{1,0:T(8,128)(2,1)S(1)} fusion(bf16[256,4096]{1,0:T(8,128)(2,1)} %param.15, bf16[1024,4096]{1,0:T(8,128)(2,1)} %param.14), kind=kOutput, calls=%fused_computation.45 | convolution fusion | flops 2147745792 | bytes 11010048 | tf_op jit(solution)/shard_map/dot_general | solution.py:35
  17.6 2.6 collective-permute-start.11
  36.0 4.2 %collective-permute-done.1 = f32[128,256]{1,0:T(8,128)S(1)} collective-permute-done((f32[128,256]{1,0:T(8,128)S(1)}, f32[128,256]{1,0:T(8,128)S(1)}, u32[]{:S(2)}, u32[]{:S(2)}) %collective-permute-start.1) | collective-permute-done | bytes 131104 | tf_op jit(solution)/shard_map/ppermute | solution.py:197
  42.4 4.6 %collective-permute-start.3 = (bf16[259,256]{1,0:T(8,128)(2,1)S(1)}, bf16[259,256]{1,0:T(8,128)(2,1)S(1)}, u32[]{:S(2)}, u32[]{:S(2)}) collective-permute-start(bf16[259,256]{1,0:T(8,128)(2,1)S(1)} %get-tuple-element.19), channel_id=1, source_target_pairs={{0,28},{4,0},{8,4},{12,8},{16,12},{20,16},{24,20},{28,24},{1,29},{... | collective-permute-start | bytes 397832 | tf_op jit(solution)/shard_map/ppermute | solution.py:226
  47.4 3.0 collective-permute-start.6
  56.8 13.5 %collective-permute-done.6 = bf16[259,256]{1,0:T(8,128)(2,1)S(1)} collective-permute-done((bf16[259,256]{1,0:T(8,128)(2,1)S(1)}, bf16[259,256]{1,0:T(8,128)(2,1)S(1)}, u32[]{:S(2)}, u32[]{:S(2)}) %collective-permute-start.6) | collective-permute-done | bytes 132640 | tf_op jit(solution)/shard_map/ppermute | solution.py:226
  81.5 2.8 collective-permute-start.21
  84.5 6.7 %all_gather.6 = bf16[256,1024]{1,0:T(8,128)(2,1)S(1)} all-gather(bf16[64,1024]{1,0:T(8,128)(2,1)S(1)} %bitcast.244), channel_id=1, replica_groups=mesh['ctx'=8,'tp'=4] {'tp'}, dimensions={0}, use_global_device_ids=true | all-gather | bytes 655360 | tf_op jit(solution)/shard_map/all_gather | solution.py:332
  91.2 2.4 fusion.71
  93.6 6.4 %fusion.65 = (f32[8,128,2048]{2,1,0:T(8,128)}, f32[8,128,2048]{2,1,0:T(8,128)}) fusion(f32[8,128,4096]{2,1,0:T(8,128)S(1)} %bitcast.233), kind=kLoop, calls=%fused_computation.167 | loop fusion | bytes 33554432 | tf_op jit(solution)/shard_map/slice | solution.py:157
  108.1 3.1 collective-permute-start.22
  112.1 3.7 %collective-permute-start.24 = (bf16[256,256]{1,0:T(8,128)(2,1)S(1)}, bf16[256,256]{1,0:T(8,128)(2,1)S(1)}, u32[]{:S(2)}, u32[]{:S(2)}) collective-permute-start(bf16[256,256]{1,0:T(8,128)(2,1)S(1)} %get-tuple-element.32), channel_id=1, source_target_pairs={{0,24},{4,28},{8,0},{12,4},{16,8},{20,12},{24,16},{28,20},{1,25},{... | collective-permute-start | bytes 393224 | tf_op jit(solution)/shard_map/ppermute | solution.py:237
  117.1 9.9 %collective-permute-done.22 = bf16[256,256]{1,0:T(8,128)(2,1)S(1)} collective-permute-done((bf16[256,256]{1,0:T(8,128)(2,1)}, bf16[256,256]{1,0:T(8,128)(2,1)S(1)}, u32[]{:S(2)}, u32[]{:S(2)}) %collective-permute-start.22) | collective-permute-done | bytes 131104 | tf_op jit(solution)/shard_map/ppermute | solution.py:237
  130.0 4.1 %collective-permute-start.17 = (bf16[128,2048]{1,0:T(8,128)(2,1)S(1)}, bf16[128,2048]{1,0:T(8,128)(2,1)}, u32[]{:S(2)}, u32[]{:S(2)}) collective-permute-start(bf16[128,2048]{1,0:T(8,128)(2,1)S(1)} %fusion.25), channel_id=1, source_target_pairs={{0,4},{8,0},{16,8},{24,16},{28,24},{20,28},{12,20},{4,12},{1,5},{9... | collective-permute-start | bytes 1572872 | tf_op jit(solution)/shard_map/ppermute | solution.py:172
  134.1 5.7 %collective-permute-done.13 = bf16[128,2048]{1,0:T(8,128)(2,1)S(1)} collective-permute-done((bf16[128,2048]{1,0:T(8,128)(2,1)S(1)}, bf16[128,2048]{1,0:T(8,128)(2,1)S(1)}, u32[]{:S(2)}, u32[]{:S(2)}) %collective-permute-start.13) | collective-permute-done | bytes 524320 | tf_op jit(solution)/shard_map/ppermute | solution.py:171
  150.2 3.1 collective-permute-start.18
  178.5 2.5 collective-permute-start.28
  181.2 9.6 %collective-permute-done.32 = bf16[128,2048]{1,0:T(8,128)(2,1)S(1)} collective-permute-done((bf16[128,2048]{1,0:T(8,128)(2,1)S(1)}, bf16[128,2048]{1,0:T(8,128)(2,1)S(1)}, u32[]{:S(2)}, u32[]{:S(2)}) %collective-permute-start.32) | collective-permute-done | bytes 524320 | tf_op jit(solution)/shard_map/ppermute | solution.py:172
  195.6 6.7 %all_gather.7 = bf16[256,1024]{1,0:T(8,128)(2,1)S(1)} all-gather(bf16[64,1024]{1,0:T(8,128)(2,1)S(1)} %copy_bitcast_fusion.1), channel_id=1, replica_groups=mesh['ctx'=8,'tp'=4] {'tp'}, dimensions={0}, use_global_device_ids=true | all-gather | bytes 655360 | tf_op jit(solution)/shard_map/all_gather | solution.py:356
  211.2 7.8 %collective-permute-done.34 = bf16[128,2048]{1,0:T(8,128)(2,1)} collective-permute-done((bf16[128,2048]{1,0:T(8,128)(2,1)}, bf16[128,2048]{1,0:T(8,128)(2,1)}, u32[]{:S(2)}, u32[]{:S(2)}) %collective-permute-start.34) | collective-permute-done | bytes 524320 | tf_op jit(solution)/shard_map/ppermute | solution.py:172
  224.3 2.9 fusion.73
  227.3 5.1 %collective-permute-done.35 = bf16[128,2048]{1,0:T(8,128)(2,1)S(1)} collective-permute-done((bf16[128,2048]{1,0:T(8,128)(2,1)S(1)}, bf16[128,2048]{1,0:T(8,128)(2,1)S(1)}, u32[]{:S(2)}, u32[]{:S(2)}) %collective-permute-start.35) | collective-permute-done | bytes 524320 | tf_op jit(solution)/shard_map/ppermute | solution.py:172
  235.2 8.1 %fusion.64 = (f32[8,160,2048]{2,1,0:T(8,128)}, f32[8,160,2048]{2,1,0:T(8,128)}) fusion(f32[8,160,4096]{2,1,0:T(8,128)S(1)} %bitcast.232), kind=kLoop, calls=%fused_computation.166 | loop fusion | bytes 41943040 | tf_op jit(solution)/shard_map/slice | solution.py:83
  249.1 9.4 %collective-permute-done.36 = bf16[160,2048]{1,0:T(8,128)(2,1)S(1)} collective-permute-done((bf16[160,2048]{1,0:T(8,128)(2,1)S(1)}, bf16[160,2048]{1,0:T(8,128)(2,1)S(1)}, u32[]{:S(2)}, u32[]{:S(2)}) %collective-permute-start.36) | collective-permute-done | bytes 655392 | tf_op jit(solution)/shard_map/ppermute | solution.py:94
  264.0 9.4 %collective-permute-done.37 = bf16[160,2048]{1,0:T(8,128)(2,1)S(1)} collective-permute-done((bf16[160,2048]{1,0:T(8,128)(2,1)S(1)}, bf16[160,2048]{1,0:T(8,128)(2,1)S(1)}, u32[]{:S(2)}, u32[]{:S(2)}) %collective-permute-start.37) | collective-permute-done | bytes 655392 | tf_op jit(solution)/shard_map/ppermute | solution.py:94
  278.9 9.4 %collective-permute-done.38 = bf16[160,2048]{1,0:T(8,128)(2,1)S(1)} collective-permute-done((bf16[160,2048]{1,0:T(8,128)(2,1)S(1)}, bf16[160,2048]{1,0:T(8,128)(2,1)S(1)}, u32[]{:S(2)}, u32[]{:S(2)}) %collective-permute-start.38) | collective-permute-done | bytes 655392 | tf_op jit(solution)/shard_map/ppermute | solution.py:94
  293.8 9.4 %collective-permute-done.39 = bf16[160,2048]{1,0:T(8,128)(2,1)S(1)} collective-permute-done((bf16[160,2048]{1,0:T(8,128)(2,1)S(1)}, bf16[160,2048]{1,0:T(8,128)(2,1)S(1)}, u32[]{:S(2)}, u32[]{:S(2)}) %collective-permute-start.39) | collective-permute-done | bytes 655392 | tf_op jit(solution)/shard_map/ppermute | solution.py:94
  308.7 7.5 %convolution_convert_fusion = bf16[256,4096]{1,0:T(8,128)(2,1)} fusion(bf16[256,1024]{1,0:T(8,128)(2,1)S(1)} %copy-done.9, bf16[1024,4096]{1,0:T(8,128)(2,1)} %param.14), kind=kOutput, calls=%fused_computation.3 | convolution fusion | flops 2148532224 | bytes 11010048 | tf_op jit(solution)/shard_map/dot_general | solution.py:333
  324.2 4.1 %convolution_convert_fusion.1 = bf16[256,4096]{1,0:T(8,128)(2,1)} fusion(bf16[256,1280]{1,0:T(8,128)(2,1)S(1)} %concatenate.45, bf16[1280,4096]{1,0:T(8,128)(2,1)S(1)} %bitcast.251), kind=kOutput, calls=%fused_computation.4 | convolution fusion | flops 2685403136 | bytes 13238272 | tf_op jit(solution)/shard_map/dot_general | solution.py:361
  328.4 6.3 %collective-permute-done.41 = bf16[160,2048]{1,0:T(8,128)(2,1)S(1)} collective-permute-done((bf16[160,2048]{1,0:T(8,128)(2,1)S(1)}, bf16[160,2048]{1,0:T(8,128)(2,1)S(1)}, u32[]{:S(2)}, u32[]{:S(2)}) %collective-permute-start.41) | collective-permute-done | bytes 655392 | tf_op jit(solution)/shard_map/ppermute | solution.py:94
  342.1 4.7 %collective-permute-done.42 = bf16[160,2048]{1,0:T(8,128)(2,1)S(1)} collective-permute-done((bf16[160,2048]{1,0:T(8,128)(2,1)S(1)}, bf16[160,2048]{1,0:T(8,128)(2,1)S(1)}, u32[]{:S(2)}, u32[]{:S(2)}) %collective-permute-start.42) | collective-permute-done | bytes 655392 | tf_op jit(solution)/shard_map/ppermute | solution.py:94
  (215 shorter events, 123.7 us)
Async XLA Ops:
  9.1 23.9 %collective-permute-start = (f32[256,1280]{1,0:T(8,128)S(1)}, f32[256,1280]{1,0:T(8,128)}, u32[]{:S(2)}, u32[]{:S(2)}) collective-permute-start(f32[256,1280]{1,0:T(8,128)S(1)} %fusion.70), channel_id=1, source_target_pairs={{0,1},{1,0},{2,3},{3,2},{4,5},{5,4},{6,7},{7,6},{8,9},{9,8},{10,11... | collective-permute-start | bytes 3932168 | tf_op jit(solution)/shard_map/ppermute | solution.py:189
  17.6 17.1 %collective-permute-start.11 = (bf16[128,1024]{1,0:T(8,128)(2,1)}, bf16[128,1024]{1,0:T(8,128)(2,1)}, u32[]{:S(2)}, u32[]{:S(2)}) collective-permute-start(bf16[128,1024]{1,0:T(8,128)(2,1)} %constant_dynamic-slice_fusion), channel_id=1, source_target_pairs={{0,2},{1,3},{2,0},{3,1},{4,6},{5,7},{6,4},{7,5},{8,10},{9,11},{10,... | collective-permute-start | bytes 786440 | tf_op jit(solution)/shard_map/ppermute | solution.py:212
  47.4 22.9 %collective-permute-start.6 = (bf16[259,256]{1,0:T(8,128)(2,1)S(1)}, bf16[259,256]{1,0:T(8,128)(2,1)S(1)}, u32[]{:S(2)}, u32[]{:S(2)}) collective-permute-start(bf16[259,256]{1,0:T(8,128)(2,1)S(1)} %get-tuple-element.19), channel_id=1, source_target_pairs={{0,16},{4,20},{8,24},{12,28},{16,0},{20,4},{24,8},{28,12},{1,17},{... | collective-permute-start | bytes 397832 | tf_op jit(solution)/shard_map/ppermute | solution.py:226
  50.5 21.3 %collective-permute-start.7 = (bf16[259,256]{1,0:T(8,128)(2,1)S(1)}, bf16[259,256]{1,0:T(8,128)(2,1)S(1)}, u32[]{:S(2)}, u32[]{:S(2)}) collective-permute-start(bf16[259,256]{1,0:T(8,128)(2,1)S(1)} %get-tuple-element.19), channel_id=1, source_target_pairs={{0,12},{4,16},{8,20},{12,24},{16,28},{20,0},{24,4},{28,8},{1,13},{... | collective-permute-start | bytes 397832 | tf_op jit(solution)/shard_map/ppermute | solution.py:226
  52.2 19.6 %collective-permute-start.8 = (bf16[259,256]{1,0:T(8,128)(2,1)S(1)}, bf16[259,256]{1,0:T(8,128)(2,1)S(1)}, u32[]{:S(2)}, u32[]{:S(2)}) collective-permute-start(bf16[259,256]{1,0:T(8,128)(2,1)S(1)} %get-tuple-element.19), channel_id=1, source_target_pairs={{0,8},{4,12},{8,16},{12,20},{16,24},{20,28},{24,0},{28,4},{1,9},{5... | collective-permute-start | bytes 397832 | tf_op jit(solution)/shard_map/ppermute | solution.py:226
  53.9 17.9 %collective-permute-start.9 = (bf16[259,256]{1,0:T(8,128)(2,1)S(1)}, bf16[259,256]{1,0:T(8,128)(2,1)S(1)}, u32[]{:S(2)}, u32[]{:S(2)}) collective-permute-start(bf16[259,256]{1,0:T(8,128)(2,1)S(1)} %get-tuple-element.19), channel_id=1, source_target_pairs={{0,4},{4,8},{8,12},{12,16},{16,20},{20,24},{24,28},{28,0},{1,5},{5... | collective-permute-start | bytes 397832 | tf_op jit(solution)/shard_map/ppermute | solution.py:226
  80.7 30.5 %collective-permute-start.19 = (bf16[256,256]{1,0:T(8,128)(2,1)}, bf16[256,256]{1,0:T(8,128)(2,1)}, u32[]{:S(2)}, u32[]{:S(2)}) collective-permute-start(bf16[256,256]{1,0:T(8,128)(2,1)} %get-tuple-element.30), channel_id=1, source_target_pairs={{0,4},{4,8},{8,12},{12,16},{16,20},{20,24},{24,28},{28,0},{1,5},{5... | collective-permute-start | bytes 393224 | tf_op jit(solution)/shard_map/ppermute | solution.py:237
  80.7 31.4 %collective-permute-start.20 = (bf16[256,256]{1,0:T(8,128)(2,1)}, bf16[256,256]{1,0:T(8,128)(2,1)}, u32[]{:S(2)}, u32[]{:S(2)}) collective-permute-start(bf16[256,256]{1,0:T(8,128)(2,1)} %get-tuple-element.36), channel_id=1, source_target_pairs={{0,8},{4,12},{8,16},{12,20},{16,24},{20,28},{24,0},{28,4},{1,9},{5... | collective-permute-start | bytes 393224 | tf_op jit(solution)/shard_map/ppermute | solution.py:237
  81.5 34.3 %collective-permute-start.21 = (bf16[256,256]{1,0:T(8,128)(2,1)}, bf16[256,256]{1,0:T(8,128)(2,1)}, u32[]{:S(2)}, u32[]{:S(2)}) collective-permute-start(bf16[256,256]{1,0:T(8,128)(2,1)} %get-tuple-element.35), channel_id=1, source_target_pairs={{0,12},{4,16},{8,20},{12,24},{16,28},{20,0},{24,4},{28,8},{1,13},{... | collective-permute-start | bytes 393224 | tf_op jit(solution)/shard_map/ppermute | solution.py:237
  102.1 26.5 %collective-permute-start.16 = (bf16[128,2048]{1,0:T(8,128)(2,1)}, bf16[128,2048]{1,0:T(8,128)(2,1)}, u32[]{:S(2)}, u32[]{:S(2)}) collective-permute-start(bf16[128,2048]{1,0:T(8,128)(2,1)} %fusion.31), channel_id=1, source_target_pairs={{0,4},{8,0},{16,8},{24,16},{28,24},{20,28},{12,20},{4,12},{1,5},{9... | collective-permute-start | bytes 1572872 | tf_op jit(solution)/shard_map/ppermute | solution.py:172
  108.1 18.9 %collective-permute-start.22 = (bf16[256,256]{1,0:T(8,128)(2,1)}, bf16[256,256]{1,0:T(8,128)(2,1)S(1)}, u32[]{:S(2)}, u32[]{:S(2)}) collective-permute-start(bf16[256,256]{1,0:T(8,128)(2,1)} %get-tuple-element.34), channel_id=1, source_target_pairs={{0,16},{4,20},{8,24},{12,28},{16,0},{20,4},{24,8},{28,12},{1,17},{... | collective-permute-start | bytes 393224 | tf_op jit(solution)/shard_map/ppermute | solution.py:237
  111.2 16.0 %collective-permute-start.23 = (bf16[256,256]{1,0:T(8,128)(2,1)}, bf16[256,256]{1,0:T(8,128)(2,1)S(1)}, u32[]{:S(2)}, u32[]{:S(2)}) collective-permute-start(bf16[256,256]{1,0:T(8,128)(2,1)} %get-tuple-element.33), channel_id=1, source_target_pairs={{0,20},{4,24},{8,28},{12,0},{16,4},{20,8},{24,12},{28,16},{1,21},{... | collective-permute-start | bytes 393224 | tf_op jit(solution)/shard_map/ppermute | solution.py:237
  112.1 15.1 %collective-permute-start.24 = (bf16[256,256]{1,0:T(8,128)(2,1)S(1)}, bf16[256,256]{1,0:T(8,128)(2,1)S(1)}, u32[]{:S(2)}, u32[]{:S(2)}) collective-permute-start(bf16[256,256]{1,0:T(8,128)(2,1)S(1)} %get-tuple-element.32), channel_id=1, source_target_pairs={{0,24},{4,28},{8,0},{12,4},{16,8},{20,12},{24,16},{28,20},{1,25},{... | collective-permute-start | bytes 393224 | tf_op jit(solution)/shard_map/ppermute | solution.py:237
  128.5 18.3 %collective-permute-start.26 = (f32[256,256]{1,0:T(8,128)S(1)}, f32[256,256]{1,0:T(8,128)S(1)}, u32[]{:S(2)}, u32[]{:S(2)}) collective-permute-start(f32[256,256]{1,0:T(8,128)S(1)} %fusion.39), channel_id=1, source_target_pairs={{0,1},{1,0},{2,3},{3,2},{4,5},{5,4},{6,7},{7,6},{8,9},{9,8},{10,11... | collective-permute-start | bytes 786440 | tf_op jit(solution)/shard_map/ppermute | solution.py:248
  130.0 18.7 %collective-permute-start.17 = (bf16[128,2048]{1,0:T(8,128)(2,1)S(1)}, bf16[128,2048]{1,0:T(8,128)(2,1)}, u32[]{:S(2)}, u32[]{:S(2)}) collective-permute-start(bf16[128,2048]{1,0:T(8,128)(2,1)S(1)} %fusion.25), channel_id=1, source_target_pairs={{0,4},{8,0},{16,8},{24,16},{28,24},{20,28},{12,20},{4,12},{1,5},{9... | collective-permute-start | bytes 1572872 | tf_op jit(solution)/shard_map/ppermute | solution.py:172
  146.8 26.7 %collective-permute-start.27 = (f32[256,256]{1,0:T(8,128)S(1)}, f32[256,256]{1,0:T(8,128)}, u32[]{:S(2)}, u32[]{:S(2)}) collective-permute-start(f32[256,256]{1,0:T(8,128)S(1)} %add.701), channel_id=1, source_target_pairs={{0,2},{1,3},{2,0},{3,1},{4,6},{5,7},{6,4},{7,5},{8,10},{9,11},{10,... | collective-permute-start | bytes 786440 | tf_op jit(solution)/shard_map/ppermute | solution.py:248
  150.2 24.4 %collective-permute-start.18 = (bf16[128,2048]{1,0:T(8,128)(2,1)S(1)}, bf16[128,2048]{1,0:T(8,128)(2,1)S(1)}, u32[]{:S(2)}, u32[]{:S(2)}) collective-permute-start(bf16[128,2048]{1,0:T(8,128)(2,1)S(1)} %fusion.24), channel_id=1, source_target_pairs={{0,4},{8,0},{16,8},{24,16},{28,24},{20,28},{12,20},{4,12},{1,5},{9... | collective-permute-start | bytes 1572872 | tf_op jit(solution)/shard_map/ppermute | solution.py:172
  156.7 19.4 %collective-permute-start.15 = (bf16[128,2048]{1,0:T(8,128)(2,1)}, bf16[128,2048]{1,0:T(8,128)(2,1)}, u32[]{:S(2)}, u32[]{:S(2)}) collective-permute-start(bf16[128,2048]{1,0:T(8,128)(2,1)} %fusion.26), channel_id=1, source_target_pairs={{0,8},{8,16},{16,24},{24,28},{28,20},{20,12},{12,4},{4,0},{1,9},{9... | collective-permute-start | bytes 1572872 | tf_op jit(solution)/shard_map/ppermute | solution.py:171
  177.6 13.2 %collective-permute-start.32 = (bf16[128,2048]{1,0:T(8,128)(2,1)S(1)}, bf16[128,2048]{1,0:T(8,128)(2,1)S(1)}, u32[]{:S(2)}, u32[]{:S(2)}) collective-permute-start(bf16[128,2048]{1,0:T(8,128)(2,1)S(1)} %bitcast_add_fusion.22), channel_id=1, source_target_pairs={{0,4},{8,0},{16,8},{24,16},{28,24},{20,28},{12,20},{4,12},{1,5},{9... | collective-permute-start | bytes 1572872 | tf_op jit(solution)/shard_map/ppermute | solution.py:172
  178.5 13.7 %collective-permute-start.28 = (bf16[128,2048]{1,0:T(8,128)(2,1)S(1)}, bf16[128,2048]{1,0:T(8,128)(2,1)S(1)}, u32[]{:S(2)}, u32[]{:S(2)}) collective-permute-start(bf16[128,2048]{1,0:T(8,128)(2,1)S(1)} %bitcast_add_fusion.25), channel_id=1, source_target_pairs={{0,8},{8,16},{16,24},{24,28},{28,20},{20,12},{12,4},{4,0},{1,9},{9... | collective-permute-start | bytes 1572872 | tf_op jit(solution)/shard_map/ppermute | solution.py:171
  244.9 13.6 %collective-permute-start.36 = (bf16[160,2048]{1,0:T(8,128)(2,1)S(1)}, bf16[160,2048]{1,0:T(8,128)(2,1)S(1)}, u32[]{:S(2)}, u32[]{:S(2)}) collective-permute-start(bf16[160,2048]{1,0:T(8,128)(2,1)S(1)} %fusion.28), channel_id=1, source_target_pairs={{0,8},{8,16},{16,24},{24,28},{28,20},{20,12},{12,4},{4,0},{1,9},{9... | collective-permute-start | bytes 1966088 | tf_op jit(solution)/shard_map/ppermute | solution.py:94
  248.1 13.6 %collective-permute-start.43 = (bf16[160,2048]{1,0:T(8,128)(2,1)S(1)}, bf16[160,2048]{1,0:T(8,128)(2,1)S(1)}, u32[]{:S(2)}, u32[]{:S(2)}) collective-permute-start(bf16[160,2048]{1,0:T(8,128)(2,1)S(1)} %fusion.29), channel_id=1, source_target_pairs={{0,4},{8,0},{16,8},{24,16},{28,24},{20,28},{12,20},{4,12},{1,5},{9... | collective-permute-start | bytes 1966088 | tf_op jit(solution)/shard_map/ppermute | solution.py:95
  259.9 13.4 %collective-permute-start.37 = (bf16[160,2048]{1,0:T(8,128)(2,1)S(1)}, bf16[160,2048]{1,0:T(8,128)(2,1)S(1)}, u32[]{:S(2)}, u32[]{:S(2)}) collective-permute-start(bf16[160,2048]{1,0:T(8,128)(2,1)S(1)} %fusion.16), channel_id=1, source_target_pairs={{0,8},{8,16},{16,24},{24,28},{28,20},{20,12},{12,4},{4,0},{1,9},{9... | collective-permute-start | bytes 1966088 | tf_op jit(solution)/shard_map/ppermute | solution.py:94
  263.2 14.7 %collective-permute-start.44 = (bf16[160,2048]{1,0:T(8,128)(2,1)S(1)}, bf16[160,2048]{1,0:T(8,128)(2,1)S(1)}, u32[]{:S(2)}, u32[]{:S(2)}) collective-permute-start(bf16[160,2048]{1,0:T(8,128)(2,1)S(1)} %fusion.10), channel_id=1, source_target_pairs={{0,4},{8,0},{16,8},{24,16},{28,24},{20,28},{12,20},{4,12},{1,5},{9... | collective-permute-start | bytes 1966088 | tf_op jit(solution)/shard_map/ppermute | solution.py:95
  274.8 13.4 %collective-permute-start.38 = (bf16[160,2048]{1,0:T(8,128)(2,1)S(1)}, bf16[160,2048]{1,0:T(8,128)(2,1)S(1)}, u32[]{:S(2)}, u32[]{:S(2)}) collective-permute-start(bf16[160,2048]{1,0:T(8,128)(2,1)S(1)} %fusion.15), channel_id=1, source_target_pairs={{0,8},{8,16},{16,24},{24,28},{28,20},{20,12},{12,4},{4,0},{1,9},{9... | collective-permute-start | bytes 1966088 | tf_op jit(solution)/shard_map/ppermute | solution.py:94
  278.1 14.7 %collective-permute-start.45 = (bf16[160,2048]{1,0:T(8,128)(2,1)S(1)}, bf16[160,2048]{1,0:T(8,128)(2,1)S(1)}, u32[]{:S(2)}, u32[]{:S(2)}) collective-permute-start(bf16[160,2048]{1,0:T(8,128)(2,1)S(1)} %fusion.9), channel_id=1, source_target_pairs={{0,4},{8,0},{16,8},{24,16},{28,24},{20,28},{12,20},{4,12},{1,5},{9... | collective-permute-start | bytes 1966088 | tf_op jit(solution)/shard_map/ppermute | solution.py:95
  289.7 13.4 %collective-permute-start.39 = (bf16[160,2048]{1,0:T(8,128)(2,1)S(1)}, bf16[160,2048]{1,0:T(8,128)(2,1)S(1)}, u32[]{:S(2)}, u32[]{:S(2)}) collective-permute-start(bf16[160,2048]{1,0:T(8,128)(2,1)S(1)} %fusion.14), channel_id=1, source_target_pairs={{0,8},{8,16},{16,24},{24,28},{28,20},{20,12},{12,4},{4,0},{1,9},{9... | collective-permute-start | bytes 1966088 | tf_op jit(solution)/shard_map/ppermute | solution.py:94
  293.0 14.7 %collective-permute-start.46 = (bf16[160,2048]{1,0:T(8,128)(2,1)S(1)}, bf16[160,2048]{1,0:T(8,128)(2,1)S(1)}, u32[]{:S(2)}, u32[]{:S(2)}) collective-permute-start(bf16[160,2048]{1,0:T(8,128)(2,1)S(1)} %fusion.8), channel_id=1, source_target_pairs={{0,4},{8,0},{16,8},{24,16},{28,24},{20,28},{12,20},{4,12},{1,5},{9... | collective-permute-start | bytes 1966088 | tf_op jit(solution)/shard_map/ppermute | solution.py:95
  304.6 13.6 %collective-permute-start.40 = (bf16[160,2048]{1,0:T(8,128)(2,1)S(1)}, bf16[160,2048]{1,0:T(8,128)(2,1)S(1)}, u32[]{:S(2)}, u32[]{:S(2)}) collective-permute-start(bf16[160,2048]{1,0:T(8,128)(2,1)S(1)} %fusion.13), channel_id=1, source_target_pairs={{0,8},{8,16},{16,24},{24,28},{28,20},{20,12},{12,4},{4,0},{1,9},{9... | collective-permute-start | bytes 1966088 | tf_op jit(solution)/shard_map/ppermute | solution.py:94
  307.9 15.3 %collective-permute-start.47 = (bf16[160,2048]{1,0:T(8,128)(2,1)S(1)}, bf16[160,2048]{1,0:T(8,128)(2,1)S(1)}, u32[]{:S(2)}, u32[]{:S(2)}) collective-permute-start(bf16[160,2048]{1,0:T(8,128)(2,1)S(1)} %fusion.7), channel_id=1, source_target_pairs={{0,4},{8,0},{16,8},{24,16},{28,24},{20,28},{12,20},{4,12},{1,5},{9... | collective-permute-start | bytes 1966088 | tf_op jit(solution)/shard_map/ppermute | solution.py:95
  319.7 14.9 %collective-permute-start.41 = (bf16[160,2048]{1,0:T(8,128)(2,1)S(1)}, bf16[160,2048]{1,0:T(8,128)(2,1)S(1)}, u32[]{:S(2)}, u32[]{:S(2)}) collective-permute-start(bf16[160,2048]{1,0:T(8,128)(2,1)S(1)} %fusion.12), channel_id=1, source_target_pairs={{0,8},{8,16},{16,24},{24,28},{28,20},{20,12},{12,4},{4,0},{1,9},{9... | collective-permute-start | bytes 1966088 | tf_op jit(solution)/shard_map/ppermute | solution.py:94
  323.4 16.1 %collective-permute-start.48 = (bf16[160,2048]{1,0:T(8,128)(2,1)S(1)}, bf16[160,2048]{1,0:T(8,128)(2,1)S(1)}, u32[]{:S(2)}, u32[]{:S(2)}) collective-permute-start(bf16[160,2048]{1,0:T(8,128)(2,1)S(1)} %fusion.6), channel_id=1, source_target_pairs={{0,4},{8,0},{16,8},{24,16},{28,24},{20,28},{12,20},{4,12},{1,5},{9... | collective-permute-start | bytes 1966088 | tf_op jit(solution)/shard_map/ppermute | solution.py:95
  (38 other events, 361.0 us)

commit v13 on v10

--- a/solution.py
+++ b/solution.py
@@ -360,8 +360,6 @@
     )
     grad_x = jnp.dot(d_qkv, w_qkv, preferred_element_type=jnp.float32).astype(jnp.bfloat16)
     joint_weight = across(d_qkv, tokens)
-    out_ring.advance(len(ring) - 1)
-    out_ring.state, joint_weight = lax.optimization_barrier((out_ring.state, joint_weight))
     grad_w_qkv = ring_scatter(joint_weight, ring, "ctx")
     grad_w_out = out_ring.result()
     return (out, grad_x, grad_w_qkv, grad_w_out)

time: 348 us -> 351 us (level)
  waiting for transfers between devices: 122 us -> 136 us
  other arithmetic: 50 us -> 41.1 us
  local copies, waits for them, and re-layouts: 30.3 us -> 26.2 us
    ppermute x7, waiting for transfers between devices: 4.4 us -> 28.2 us  [advance(): lax.ppermute(send_left.astype(jnp.bfloat16), self.axis, self.forward)]
    ppermute x7, waiting for transfers between devices: 35.6 us -> 13.7 us  [advance(): lax.ppermute(send_right.astype(jnp.bfloat16), self.axis, self.backward)]
    ppermute x7, waiting for transfers between devices: 55.9 us -> 65.7 us  [ring_scatter(): got_left = lax.ppermute(send_left.astype(jnp.bfloat16), axis, forward)]
    dot_general x1, matrix products: 4.12 us -> 8.13 us  [shards(): jnp.dot(d_qkv, w_qkv, preferred_element_type=jnp.float32)]
    convert_element_type x6, other arithmetic: 8.84 us -> 5.1 us  [ring_scatter(): got_left = lax.ppermute(send_left.astype(jnp.bfloat16), axis, forward)]
  transfers between devices with their start and end apart: 50 -> 50, of which waited for: 28 -> 24; matrix products, arithmetic and copies ran while one was open for 24% -> 18% of each run, Pallas kernels for 0% -> 0%
where the time goes in v13:
time: 351 us; the launch traced here: 350 us
  waiting for transfers between devices  136 us (39%)
  starting transfers between devices  58.2 us (17%)
  other arithmetic  41.1 us (12%)
  matrix products  38.4 us (11%)
  between operations  36.5 us (10%)
  local copies, waits for them, and re-layouts  26.2 us (7%)
  blocking collectives  13.4 us (4%)
    ppermute x7, waiting for transfers between devices, ring_scatter(): got_left = lax.ppermute(send_left.astype(jnp.bfloat16), axis, forward)  65.7 us
    ppermute x7, waiting for transfers between devices, advance(): lax.ppermute(send_left.astype(jnp.bfloat16), self.axis, self.forward)  28.2 us
    ppermute x7, waiting for transfers between devices, direct_gather(): got[count - shift] = lax.ppermute(value, axis, pairs)  16.1 us
    dot_general x4, matrix products, against(): lax.dot_general(left, right, (((1,), (1,)), ((), ())), preferred_element_...  14.9 us
    ppermute x7, waiting for transfers between devices, advance(): lax.ppermute(send_right.astype(jnp.bfloat16), self.axis, self.backward)  13.7 us
    ppermute x7, starting transfers between devices, direct_scatter(): lax.ppermute(blocks[shift].astype(jnp.bfloat16), axis, pairs)  12.3 us
    ppermute x7, starting transfers between devices, direct_gather(): got[count - shift] = lax.ppermute(value, axis, pairs)  12.2 us
    ppermute x7, starting transfers between devices, advance(): lax.ppermute(send_left.astype(jnp.bfloat16), self.axis, self.forward)  9.58 us
  transfers between devices with their start and end apart: 50, of which 24 were waited for; matrix products, arithmetic and copies ran while one was open for 18% of the time, Pallas kernels for 0%

profile of v13, /device:TPU:0, one launch (start us, length us, event | category | flops | bytes accessed | tf_op | source)
XLA Modules:
  0.0 349.8 jit_solution(8608705636697521120)
XLA Ops:
  2.2 6.9 %fusion.70 = f32[256,1280]{1,0:T(8,128)S(1)} fusion(bf16[256,4096]{1,0:T(8,128)(2,1)S(1)} %copy-done, bf16[1280,4096]{1,0:T(8,128)(2,1)} %param.13), kind=kOutput, calls=%fused_computation.172 | convolution fusion | flops 2684354560 | bytes 13893632 | tf_op jit(solution)/shard_map/dot_general | solution.py:35
  9.6 6.4 %convolution_convert_fusion.2 = bf16[256,1024]{1,0:T(8,128)(2,1)S(1)} fusion(bf16[256,4096]{1,0:T(8,128)(2,1)} %param.15, bf16[1024,4096]{1,0:T(8,128)(2,1)} %param.14), kind=kOutput, calls=%fused_computation.45 | convolution fusion | flops 2147745792 | bytes 11010048 | tf_op jit(solution)/shard_map/dot_general | solution.py:35
  17.6 2.6 collective-permute-start.11
  59.7 4.2 %collective-permute-done.1 = f32[128,256]{1,0:T(8,128)S(1)} collective-permute-done((f32[128,256]{1,0:T(8,128)S(1)}, f32[128,256]{1,0:T(8,128)S(1)}, u32[]{:S(2)}, u32[]{:S(2)}) %collective-permute-start.1) | collective-permute-done | bytes 131104 | tf_op jit(solution)/shard_map/ppermute | solution.py:197
  66.1 4.6 %collective-permute-start.3 = (bf16[259,256]{1,0:T(8,128)(2,1)S(1)}, bf16[259,256]{1,0:T(8,128)(2,1)S(1)}, u32[]{:S(2)}, u32[]{:S(2)}) collective-permute-start(bf16[259,256]{1,0:T(8,128)(2,1)S(1)} %get-tuple-element.13), channel_id=1, source_target_pairs={{0,28},{4,0},{8,4},{12,8},{16,12},{20,16},{24,20},{28,24},{1,29},{... | collective-permute-start | bytes 397832 | tf_op jit(solution)/shard_map/ppermute | solution.py:226
  71.1 3.0 collective-permute-start.6
  80.5 13.5 %collective-permute-done.6 = bf16[259,256]{1,0:T(8,128)(2,1)S(1)} collective-permute-done((bf16[259,256]{1,0:T(8,128)(2,1)S(1)}, bf16[259,256]{1,0:T(8,128)(2,1)S(1)}, u32[]{:S(2)}, u32[]{:S(2)}) %collective-permute-start.6) | collective-permute-done | bytes 132640 | tf_op jit(solution)/shard_map/ppermute | solution.py:226
  102.7 6.7 %all_gather.6 = bf16[256,1024]{1,0:T(8,128)(2,1)S(1)} all-gather(bf16[64,1024]{1,0:T(8,128)(2,1)S(1)} %bitcast.246), channel_id=1, replica_groups=mesh['ctx'=8,'tp'=4] {'tp'}, dimensions={0}, use_global_device_ids=true | all-gather | bytes 655360 | tf_op jit(solution)/shard_map/all_gather | solution.py:332
  109.4 2.4 fusion.71
  111.8 7.1 %convolution_convert_fusion = bf16[256,4096]{1,0:T(8,128)(2,1)} fusion(bf16[256,1024]{1,0:T(8,128)(2,1)S(1)} %all_gather.6, bf16[1024,4096]{1,0:T(8,128)(2,1)} %param.14), kind=kOutput, calls=%fused_computation.3 | convolution fusion | flops 2148532224 | bytes 11010048 | tf_op jit(solution)/shard_map/dot_general | solution.py:333
  121.0 2.8 collective-permute-start.19
  126.7 6.4 %fusion.65 = (f32[8,128,2048]{2,1,0:T(8,128)}, f32[8,128,2048]{2,1,0:T(8,128)}) fusion(f32[8,128,4096]{2,1,0:T(8,128)S(1)} %bitcast.233), kind=kLoop, calls=%fused_computation.167 | loop fusion | bytes 33554432 | tf_op jit(solution)/shard_map/slice | solution.py:157
  134.4 2.5 collective-permute-start.22
  136.9 2.9 collective-permute-start.23
  148.2 10.1 %collective-permute-done.15 = bf16[128,2048]{1,0:T(8,128)(2,1)S(1)} collective-permute-done((bf16[128,2048]{1,0:T(8,128)(2,1)S(1)}, bf16[128,2048]{1,0:T(8,128)(2,1)S(1)}, u32[]{:S(2)}, u32[]{:S(2)}) %collective-permute-start.15) | collective-permute-done | bytes 524320 | tf_op jit(solution)/shard_map/ppermute | solution.py:172
  163.1 6.7 %all_gather.7 = bf16[256,1024]{1,0:T(8,128)(2,1)S(1)} all-gather(bf16[64,1024]{1,0:T(8,128)(2,1)S(1)} %copy_bitcast_fusion.1), channel_id=1, replica_groups=mesh['ctx'=8,'tp'=4] {'tp'}, dimensions={0}, use_global_device_ids=true | all-gather | bytes 655360 | tf_op jit(solution)/shard_map/all_gather | solution.py:356
  169.8 3.6 %collective-permute-done.16 = bf16[128,2048]{1,0:T(8,128)(2,1)S(1)} collective-permute-done((bf16[128,2048]{1,0:T(8,128)(2,1)S(1)}, bf16[128,2048]{1,0:T(8,128)(2,1)S(1)}, u32[]{:S(2)}, u32[]{:S(2)}) %collective-permute-start.16) | collective-permute-done | bytes 524320 | tf_op jit(solution)/shard_map/ppermute | solution.py:172
  175.5 2.1 bitcast_add_fusion.26
  178.5 2.9 fusion.73
  181.5 8.1 %convolution_convert_fusion.1 = bf16[256,4096]{1,0:T(8,128)(2,1)} fusion(bf16[256,1280]{1,0:T(8,128)(2,1)S(1)} %concatenate.45, bf16[1280,4096]{1,0:T(8,128)(2,1)} %param.13), kind=kOutput, calls=%fused_computation.4 | convolution fusion | flops 2685403136 | bytes 13238272 | tf_op jit(solution)/shard_map/dot_general | solution.py:361
  191.6 8.1 %fusion.64 = (f32[8,160,2048]{2,1,0:T(8,128)}, f32[8,160,2048]{2,1,0:T(8,128)}) fusion(f32[8,160,4096]{2,1,0:T(8,128)S(1)} %bitcast.232), kind=kLoop, calls=%fused_computation.166 | loop fusion | bytes 41943040 | tf_op jit(solution)/shard_map/slice | solution.py:83
  209.6 9.4 %collective-permute-done.26 = bf16[160,2048]{1,0:T(8,128)(2,1)S(1)} collective-permute-done((bf16[160,2048]{1,0:T(8,128)(2,1)S(1)}, bf16[160,2048]{1,0:T(8,128)(2,1)S(1)}, u32[]{:S(2)}, u32[]{:S(2)}) %collective-permute-start.26) | collective-permute-done | bytes 655392 | tf_op jit(solution)/shard_map/ppermute | solution.py:94
  224.4 5.8 %collective-permute-done.41 = bf16[128,2048]{1,0:T(8,128)(2,1)S(1)} collective-permute-done((bf16[128,2048]{1,0:T(8,128)(2,1)S(1)}, bf16[128,2048]{1,0:T(8,128)(2,1)S(1)}, u32[]{:S(2)}, u32[]{:S(2)}) %collective-permute-start.41) | collective-permute-done | bytes 524320 | tf_op jit(solution)/shard_map/ppermute | solution.py:171
  235.1 9.2 %collective-permute-done.27 = bf16[160,2048]{1,0:T(8,128)(2,1)S(1)} collective-permute-done((bf16[160,2048]{1,0:T(8,128)(2,1)S(1)}, bf16[160,2048]{1,0:T(8,128)(2,1)S(1)}, u32[]{:S(2)}, u32[]{:S(2)}) %collective-permute-start.27) | collective-permute-done | bytes 655392 | tf_op jit(solution)/shard_map/ppermute | solution.py:94
  248.1 7.4 %collective-permute-done.42 = bf16[128,2048]{1,0:T(8,128)(2,1)S(1)} collective-permute-done((bf16[128,2048]{1,0:T(8,128)(2,1)S(1)}, bf16[128,2048]{1,0:T(8,128)(2,1)S(1)}, u32[]{:S(2)}, u32[]{:S(2)}) %collective-permute-start.42) | collective-permute-done | bytes 524320 | tf_op jit(solution)/shard_map/ppermute | solution.py:171
  260.4 9.2 %collective-permute-done.28 = bf16[160,2048]{1,0:T(8,128)(2,1)S(1)} collective-permute-done((bf16[160,2048]{1,0:T(8,128)(2,1)S(1)}, bf16[160,2048]{1,0:T(8,128)(2,1)S(1)}, u32[]{:S(2)}, u32[]{:S(2)}) %collective-permute-start.28) | collective-permute-done | bytes 655392 | tf_op jit(solution)/shard_map/ppermute | solution.py:94
  273.4 7.4 %collective-permute-done.43 = bf16[128,2048]{1,0:T(8,128)(2,1)S(1)} collective-permute-done((bf16[128,2048]{1,0:T(8,128)(2,1)S(1)}, bf16[128,2048]{1,0:T(8,128)(2,1)S(1)}, u32[]{:S(2)}, u32[]{:S(2)}) %collective-permute-start.43) | collective-permute-done | bytes 524320 | tf_op jit(solution)/shard_map/ppermute | solution.py:171
  285.9 8.9 %collective-permute-done.29 = bf16[160,2048]{1,0:T(8,128)(2,1)S(1)} collective-permute-done((bf16[160,2048]{1,0:T(8,128)(2,1)S(1)}, bf16[160,2048]{1,0:T(8,128)(2,1)S(1)}, u32[]{:S(2)}, u32[]{:S(2)}) %collective-permute-start.29) | collective-permute-done | bytes 655392 | tf_op jit(solution)/shard_map/ppermute | solution.py:94
  298.6 7.5 %collective-permute-done.44 = bf16[128,2048]{1,0:T(8,128)(2,1)S(1)} collective-permute-done((bf16[128,2048]{1,0:T(8,128)(2,1)S(1)}, bf16[128,2048]{1,0:T(8,128)(2,1)S(1)}, u32[]{:S(2)}, u32[]{:S(2)}) %collective-permute-start.44) | collective-permute-done | bytes 524320 | tf_op jit(solution)/shard_map/ppermute | solution.py:171
  307.4 10.2 %collective-permute-done.30 = bf16[160,2048]{1,0:T(8,128)(2,1)S(1)} collective-permute-done((bf16[160,2048]{1,0:T(8,128)(2,1)S(1)}, bf16[160,2048]{1,0:T(8,128)(2,1)S(1)}, u32[]{:S(2)}, u32[]{:S(2)}) %collective-permute-start.30) | collective-permute-done | bytes 655392 | tf_op jit(solution)/shard_map/ppermute | solution.py:94
  322.4 10.2 %collective-permute-done.31 = bf16[160,2048]{1,0:T(8,128)(2,1)S(1)} collective-permute-done((bf16[160,2048]{1,0:T(8,128)(2,1)S(1)}, bf16[160,2048]{1,0:T(8,128)(2,1)S(1)}, u32[]{:S(2)}, u32[]{:S(2)}) %collective-permute-start.31) | collective-permute-done | bytes 655392 | tf_op jit(solution)/shard_map/ppermute | solution.py:94
  337.4 8.7 %collective-permute-done.32 = bf16[160,2048]{1,0:T(8,128)(2,1)S(1)} collective-permute-done((bf16[160,2048]{1,0:T(8,128)(2,1)S(1)}, bf16[160,2048]{1,0:T(8,128)(2,1)S(1)}, u32[]{:S(2)}, u32[]{:S(2)}) %collective-permute-start.32) | collective-permute-done | bytes 655392 | tf_op jit(solution)/shard_map/ppermute | solution.py:94
  (207 shorter events, 105.9 us)
Async XLA Ops:
  9.1 47.6 %collective-permute-start = (f32[256,1280]{1,0:T(8,128)S(1)}, f32[256,1280]{1,0:T(8,128)}, u32[]{:S(2)}, u32[]{:S(2)}) collective-permute-start(f32[256,1280]{1,0:T(8,128)S(1)} %fusion.70), channel_id=1, source_target_pairs={{0,1},{1,0},{2,3},{3,2},{4,5},{5,4},{6,7},{7,6},{8,9},{9,8},{10,11... | collective-permute-start | bytes 3932168 | tf_op jit(solution)/shard_map/ppermute | solution.py:189
  17.6 40.7 %collective-permute-start.11 = (bf16[128,1024]{1,0:T(8,128)(2,1)}, bf16[128,1024]{1,0:T(8,128)(2,1)}, u32[]{:S(2)}, u32[]{:S(2)}) collective-permute-start(bf16[128,1024]{1,0:T(8,128)(2,1)} %constant_dynamic-slice_fusion), channel_id=1, source_target_pairs={{0,2},{1,3},{2,0},{3,1},{4,6},{5,7},{6,4},{7,5},{8,10},{9,11},{10,... | collective-permute-start | bytes 786440 | tf_op jit(solution)/shard_map/ppermute | solution.py:212
  71.1 22.9 %collective-permute-start.6 = (bf16[259,256]{1,0:T(8,128)(2,1)S(1)}, bf16[259,256]{1,0:T(8,128)(2,1)S(1)}, u32[]{:S(2)}, u32[]{:S(2)}) collective-permute-start(bf16[259,256]{1,0:T(8,128)(2,1)S(1)} %get-tuple-element.13), channel_id=1, source_target_pairs={{0,16},{4,20},{8,24},{12,28},{16,0},{20,4},{24,8},{28,12},{1,17},{... | collective-permute-start | bytes 397832 | tf_op jit(solution)/shard_map/ppermute | solution.py:226
  74.8 20.7 %collective-permute-start.7 = (bf16[259,256]{1,0:T(8,128)(2,1)S(1)}, bf16[259,256]{1,0:T(8,128)(2,1)S(1)}, u32[]{:S(2)}, u32[]{:S(2)}) collective-permute-start(bf16[259,256]{1,0:T(8,128)(2,1)S(1)} %get-tuple-element.13), channel_id=1, source_target_pairs={{0,12},{4,16},{8,20},{12,24},{16,28},{20,0},{24,4},{28,8},{1,13},{... | collective-permute-start | bytes 397832 | tf_op jit(solution)/shard_map/ppermute | solution.py:226
  75.9 19.6 %collective-permute-start.8 = (bf16[259,256]{1,0:T(8,128)(2,1)S(1)}, bf16[259,256]{1,0:T(8,128)(2,1)S(1)}, u32[]{:S(2)}, u32[]{:S(2)}) collective-permute-start(bf16[259,256]{1,0:T(8,128)(2,1)S(1)} %get-tuple-element.13), channel_id=1, source_target_pairs={{0,8},{4,12},{8,16},{12,20},{16,24},{20,28},{24,0},{28,4},{1,9},{5... | collective-permute-start | bytes 397832 | tf_op jit(solution)/shard_map/ppermute | solution.py:226
  77.6 17.9 %collective-permute-start.9 = (bf16[259,256]{1,0:T(8,128)(2,1)S(1)}, bf16[259,256]{1,0:T(8,128)(2,1)S(1)}, u32[]{:S(2)}, u32[]{:S(2)}) collective-permute-start(bf16[259,256]{1,0:T(8,128)(2,1)S(1)} %get-tuple-element.13), channel_id=1, source_target_pairs={{0,4},{4,8},{8,12},{12,16},{16,20},{20,24},{24,28},{28,0},{1,5},{5... | collective-permute-start | bytes 397832 | tf_op jit(solution)/shard_map/ppermute | solution.py:226
  119.9 17.1 %collective-permute-start.18 = (bf16[256,256]{1,0:T(8,128)(2,1)S(1)}, bf16[256,256]{1,0:T(8,128)(2,1)S(1)}, u32[]{:S(2)}, u32[]{:S(2)}) collective-permute-start(bf16[256,256]{1,0:T(8,128)(2,1)S(1)} %get-tuple-element.30), channel_id=1, source_target_pairs={{0,8},{4,12},{8,16},{12,20},{16,24},{20,28},{24,0},{28,4},{1,9},{5... | collective-permute-start | bytes 393224 | tf_op jit(solution)/shard_map/ppermute | solution.py:237
  121.0 20.1 %collective-permute-start.19 = (bf16[256,256]{1,0:T(8,128)(2,1)S(1)}, bf16[256,256]{1,0:T(8,128)(2,1)S(1)}, u32[]{:S(2)}, u32[]{:S(2)}) collective-permute-start(bf16[256,256]{1,0:T(8,128)(2,1)S(1)} %get-tuple-element.29), channel_id=1, source_target_pairs={{0,12},{4,16},{8,20},{12,24},{16,28},{20,0},{24,4},{28,8},{1,13},{... | collective-permute-start | bytes 393224 | tf_op jit(solution)/shard_map/ppermute | solution.py:237
  123.8 17.4 %collective-permute-start.20 = (bf16[256,256]{1,0:T(8,128)(2,1)S(1)}, bf16[256,256]{1,0:T(8,128)(2,1)}, u32[]{:S(2)}, u32[]{:S(2)}) collective-permute-start(bf16[256,256]{1,0:T(8,128)(2,1)S(1)} %get-tuple-element.28), channel_id=1, source_target_pairs={{0,16},{4,20},{8,24},{12,28},{16,0},{20,4},{24,8},{28,12},{1,17},{... | collective-permute-start | bytes 393224 | tf_op jit(solution)/shard_map/ppermute | solution.py:237
  125.4 17.8 %collective-permute-start.21 = (bf16[256,256]{1,0:T(8,128)(2,1)S(1)}, bf16[256,256]{1,0:T(8,128)(2,1)}, u32[]{:S(2)}, u32[]{:S(2)}) collective-permute-start(bf16[256,256]{1,0:T(8,128)(2,1)S(1)} %get-tuple-element.27), channel_id=1, source_target_pairs={{0,20},{4,24},{8,28},{12,0},{16,4},{20,8},{24,12},{28,16},{1,21},{... | collective-permute-start | bytes 393224 | tf_op jit(solution)/shard_map/ppermute | solution.py:237
  141.1 17.2 %collective-permute-start.15 = (bf16[128,2048]{1,0:T(8,128)(2,1)S(1)}, bf16[128,2048]{1,0:T(8,128)(2,1)S(1)}, u32[]{:S(2)}, u32[]{:S(2)}) collective-permute-start(bf16[128,2048]{1,0:T(8,128)(2,1)S(1)} %fusion.31), channel_id=1, source_target_pairs={{0,4},{8,0},{16,8},{24,16},{28,24},{20,28},{12,20},{4,12},{1,5},{9... | collective-permute-start | bytes 1572872 | tf_op jit(solution)/shard_map/ppermute | solution.py:172
  141.2 18.5 %collective-permute-start.13 = (bf16[128,2048]{1,0:T(8,128)(2,1)S(1)}, bf16[128,2048]{1,0:T(8,128)(2,1)S(1)}, u32[]{:S(2)}, u32[]{:S(2)}) collective-permute-start(bf16[128,2048]{1,0:T(8,128)(2,1)S(1)} %fusion.30), channel_id=1, source_target_pairs={{0,8},{8,16},{16,24},{24,28},{28,20},{20,12},{12,4},{4,0},{1,9},{9... | collective-permute-start | bytes 1572872 | tf_op jit(solution)/shard_map/ppermute | solution.py:171
  147.1 22.6 %collective-permute-start.25 = (f32[256,256]{1,0:T(8,128)S(1)}, f32[256,256]{1,0:T(8,128)S(1)}, u32[]{:S(2)}, u32[]{:S(2)}) collective-permute-start(f32[256,256]{1,0:T(8,128)S(1)} %add.689), channel_id=1, source_target_pairs={{0,2},{1,3},{2,0},{3,1},{4,6},{5,7},{6,4},{7,5},{8,10},{9,11},{10,... | collective-permute-start | bytes 786440 | tf_op jit(solution)/shard_map/ppermute | solution.py:248
  190.6 16.6 %collective-permute-start.45 = (bf16[128,2048]{1,0:T(8,128)(2,1)S(1)}, bf16[128,2048]{1,0:T(8,128)(2,1)S(1)}, u32[]{:S(2)}, u32[]{:S(2)}) collective-permute-start(bf16[128,2048]{1,0:T(8,128)(2,1)S(1)} %copy-done.4), channel_id=1, source_target_pairs={{0,4},{8,0},{16,8},{24,16},{28,24},{20,28},{12,20},{4,12},{1,5},{9... | collective-permute-start | bytes 1572872 | tf_op jit(solution)/shard_map/ppermute | solution.py:172
  201.3 17.7 %collective-permute-start.26 = (bf16[160,2048]{1,0:T(8,128)(2,1)S(1)}, bf16[160,2048]{1,0:T(8,128)(2,1)S(1)}, u32[]{:S(2)}, u32[]{:S(2)}) collective-permute-start(bf16[160,2048]{1,0:T(8,128)(2,1)S(1)} %fusion.28), channel_id=1, source_target_pairs={{0,8},{8,16},{16,24},{24,28},{28,20},{20,12},{12,4},{4,0},{1,9},{9... | collective-permute-start | bytes 1966088 | tf_op jit(solution)/shard_map/ppermute | solution.py:94
  203.7 18.0 %collective-permute-start.33 = (bf16[160,2048]{1,0:T(8,128)(2,1)S(1)}, bf16[160,2048]{1,0:T(8,128)(2,1)S(1)}, u32[]{:S(2)}, u32[]{:S(2)}) collective-permute-start(bf16[160,2048]{1,0:T(8,128)(2,1)S(1)} %fusion.29), channel_id=1, source_target_pairs={{0,4},{8,0},{16,8},{24,16},{28,24},{20,28},{12,20},{4,12},{1,5},{9... | collective-permute-start | bytes 1966088 | tf_op jit(solution)/shard_map/ppermute | solution.py:95
  206.2 24.1 %collective-permute-start.41 = (bf16[128,2048]{1,0:T(8,128)(2,1)S(1)}, bf16[128,2048]{1,0:T(8,128)(2,1)S(1)}, u32[]{:S(2)}, u32[]{:S(2)}) collective-permute-start(bf16[128,2048]{1,0:T(8,128)(2,1)S(1)} %fusion.25), channel_id=1, source_target_pairs={{0,8},{8,16},{16,24},{24,28},{28,20},{20,12},{12,4},{4,0},{1,9},{9... | collective-permute-start | bytes 1572872 | tf_op jit(solution)/shard_map/ppermute | solution.py:171
  208.6 24.1 %collective-permute-start.46 = (bf16[128,2048]{1,0:T(8,128)(2,1)S(1)}, bf16[128,2048]{1,0:T(8,128)(2,1)S(1)}, u32[]{:S(2)}, u32[]{:S(2)}) collective-permute-start(bf16[128,2048]{1,0:T(8,128)(2,1)S(1)} %fusion.21), channel_id=1, source_target_pairs={{0,4},{8,0},{16,8},{24,16},{28,24},{20,28},{12,20},{4,12},{1,5},{9... | collective-permute-start | bytes 1572872 | tf_op jit(solution)/shard_map/ppermute | solution.py:172
  220.7 23.6 %collective-permute-start.27 = (bf16[160,2048]{1,0:T(8,128)(2,1)S(1)}, bf16[160,2048]{1,0:T(8,128)(2,1)S(1)}, u32[]{:S(2)}, u32[]{:S(2)}) collective-permute-start(bf16[160,2048]{1,0:T(8,128)(2,1)S(1)} %fusion.16), channel_id=1, source_target_pairs={{0,8},{8,16},{16,24},{24,28},{28,20},{20,12},{12,4},{4,0},{1,9},{9... | collective-permute-start | bytes 1966088 | tf_op jit(solution)/shard_map/ppermute | solution.py:94
  223.8 23.0 %collective-permute-start.34 = (bf16[160,2048]{1,0:T(8,128)(2,1)S(1)}, bf16[160,2048]{1,0:T(8,128)(2,1)S(1)}, u32[]{:S(2)}, u32[]{:S(2)}) collective-permute-start(bf16[160,2048]{1,0:T(8,128)(2,1)S(1)} %fusion.10), channel_id=1, source_target_pairs={{0,4},{8,0},{16,8},{24,16},{28,24},{20,28},{12,20},{4,12},{1,5},{9... | collective-permute-start | bytes 1966088 | tf_op jit(solution)/shard_map/ppermute | solution.py:95
  231.6 23.9 %collective-permute-start.42 = (bf16[128,2048]{1,0:T(8,128)(2,1)S(1)}, bf16[128,2048]{1,0:T(8,128)(2,1)S(1)}, u32[]{:S(2)}, u32[]{:S(2)}) collective-permute-start(bf16[128,2048]{1,0:T(8,128)(2,1)S(1)} %fusion.24), channel_id=1, source_target_pairs={{0,8},{8,16},{16,24},{24,28},{28,20},{20,12},{12,4},{4,0},{1,9},{9... | collective-permute-start | bytes 1572872 | tf_op jit(solution)/shard_map/ppermute | solution.py:171
  234.1 23.9 %collective-permute-start.47 = (bf16[128,2048]{1,0:T(8,128)(2,1)S(1)}, bf16[128,2048]{1,0:T(8,128)(2,1)S(1)}, u32[]{:S(2)}, u32[]{:S(2)}) collective-permute-start(bf16[128,2048]{1,0:T(8,128)(2,1)S(1)} %fusion.20), channel_id=1, source_target_pairs={{0,4},{8,0},{16,8},{24,16},{28,24},{20,28},{12,20},{4,12},{1,5},{9... | collective-permute-start | bytes 1572872 | tf_op jit(solution)/shard_map/ppermute | solution.py:172
  245.8 23.8 %collective-permute-start.28 = (bf16[160,2048]{1,0:T(8,128)(2,1)S(1)}, bf16[160,2048]{1,0:T(8,128)(2,1)S(1)}, u32[]{:S(2)}, u32[]{:S(2)}) collective-permute-start(bf16[160,2048]{1,0:T(8,128)(2,1)S(1)} %fusion.15), channel_id=1, source_target_pairs={{0,8},{8,16},{16,24},{24,28},{28,20},{20,12},{12,4},{4,0},{1,9},{9... | collective-permute-start | bytes 1966088 | tf_op jit(solution)/shard_map/ppermute | solution.py:94
  247.1 25.1 %collective-permute-start.35 = (bf16[160,2048]{1,0:T(8,128)(2,1)S(1)}, bf16[160,2048]{1,0:T(8,128)(2,1)S(1)}, u32[]{:S(2)}, u32[]{:S(2)}) collective-permute-start(bf16[160,2048]{1,0:T(8,128)(2,1)S(1)} %fusion.9), channel_id=1, source_target_pairs={{0,4},{8,0},{16,8},{24,16},{28,24},{20,28},{12,20},{4,12},{1,5},{9... | collective-permute-start | bytes 1966088 | tf_op jit(solution)/shard_map/ppermute | solution.py:95
  256.9 23.9 %collective-permute-start.43 = (bf16[128,2048]{1,0:T(8,128)(2,1)S(1)}, bf16[128,2048]{1,0:T(8,128)(2,1)S(1)}, u32[]{:S(2)}, u32[]{:S(2)}) collective-permute-start(bf16[128,2048]{1,0:T(8,128)(2,1)S(1)} %fusion.23), channel_id=1, source_target_pairs={{0,8},{8,16},{16,24},{24,28},{28,20},{20,12},{12,4},{4,0},{1,9},{9... | collective-permute-start | bytes 1572872 | tf_op jit(solution)/shard_map/ppermute | solution.py:171
  259.3 24.1 %collective-permute-start.48 = (bf16[128,2048]{1,0:T(8,128)(2,1)S(1)}, bf16[128,2048]{1,0:T(8,128)(2,1)S(1)}, u32[]{:S(2)}, u32[]{:S(2)}) collective-permute-start(bf16[128,2048]{1,0:T(8,128)(2,1)S(1)} %fusion.19), channel_id=1, source_target_pairs={{0,4},{8,0},{16,8},{24,16},{28,24},{20,28},{12,20},{4,12},{1,5},{9... | collective-permute-start | bytes 1572872 | tf_op jit(solution)/shard_map/ppermute | solution.py:172
  271.1 23.8 %collective-permute-start.29 = (bf16[160,2048]{1,0:T(8,128)(2,1)S(1)}, bf16[160,2048]{1,0:T(8,128)(2,1)S(1)}, u32[]{:S(2)}, u32[]{:S(2)}) collective-permute-start(bf16[160,2048]{1,0:T(8,128)(2,1)S(1)} %fusion.14), channel_id=1, source_target_pairs={{0,8},{8,16},{16,24},{24,28},{28,20},{20,12},{12,4},{4,0},{1,9},{9... | collective-permute-start | bytes 1966088 | tf_op jit(solution)/shard_map/ppermute | solution.py:94
  272.3 25.0 %collective-permute-start.36 = (bf16[160,2048]{1,0:T(8,128)(2,1)S(1)}, bf16[160,2048]{1,0:T(8,128)(2,1)S(1)}, u32[]{:S(2)}, u32[]{:S(2)}) collective-permute-start(bf16[160,2048]{1,0:T(8,128)(2,1)S(1)} %fusion.8), channel_id=1, source_target_pairs={{0,4},{8,0},{16,8},{24,16},{28,24},{20,28},{12,20},{4,12},{1,5},{9... | collective-permute-start | bytes 1966088 | tf_op jit(solution)/shard_map/ppermute | solution.py:95
  282.2 23.9 %collective-permute-start.44 = (bf16[128,2048]{1,0:T(8,128)(2,1)S(1)}, bf16[128,2048]{1,0:T(8,128)(2,1)S(1)}, u32[]{:S(2)}, u32[]{:S(2)}) collective-permute-start(bf16[128,2048]{1,0:T(8,128)(2,1)S(1)} %fusion.22), channel_id=1, source_target_pairs={{0,8},{8,16},{16,24},{24,28},{28,20},{20,12},{12,4},{4,0},{1,9},{9... | collective-permute-start | bytes 1572872 | tf_op jit(solution)/shard_map/ppermute | solution.py:171
  284.8 36.2 %collective-permute-start.49 = (bf16[128,2048]{1,0:T(8,128)(2,1)S(1)}, bf16[128,2048]{1,0:T(8,128)(2,1)S(1)}, u32[]{:S(2)}, u32[]{:S(2)}) collective-permute-start(bf16[128,2048]{1,0:T(8,128)(2,1)S(1)} %fusion.18), channel_id=1, source_target_pairs={{0,4},{8,0},{16,8},{24,16},{28,24},{20,28},{12,20},{4,12},{1,5},{9... | collective-permute-start | bytes 1572872 | tf_op jit(solution)/shard_map/ppermute | solution.py:172
  295.0 22.6 %collective-permute-start.30 = (bf16[160,2048]{1,0:T(8,128)(2,1)S(1)}, bf16[160,2048]{1,0:T(8,128)(2,1)S(1)}, u32[]{:S(2)}, u32[]{:S(2)}) collective-permute-start(bf16[160,2048]{1,0:T(8,128)(2,1)S(1)} %fusion.13), channel_id=1, source_target_pairs={{0,8},{8,16},{16,24},{24,28},{28,20},{20,12},{12,4},{4,0},{1,9},{9... | collective-permute-start | bytes 1966088 | tf_op jit(solution)/shard_map/ppermute | solution.py:94
  297.5 22.1 %collective-permute-start.37 = (bf16[160,2048]{1,0:T(8,128)(2,1)S(1)}, bf16[160,2048]{1,0:T(8,128)(2,1)S(1)}, u32[]{:S(2)}, u32[]{:S(2)}) collective-permute-start(bf16[160,2048]{1,0:T(8,128)(2,1)S(1)} %fusion.7), channel_id=1, source_target_pairs={{0,4},{8,0},{16,8},{24,16},{28,24},{20,28},{12,20},{4,12},{1,5},{9... | collective-permute-start | bytes 1966088 | tf_op jit(solution)/shard_map/ppermute | solution.py:95
  (34 other events, 515.5 us)

commit v14 on v10

--- a/solution.py
+++ b/solution.py
@@ -291,7 +291,7 @@
     info = info.reshape(info_rows, pair_width).astype(jnp.bfloat16)
     packed = jnp.concatenate([keys, values], axis=1)
     packed = jnp.concatenate([packed, info], axis=0)
-    gathered = direct_gather(packed, "ctx")
+    gathered = ring_gather(packed, ring, "ctx")
     if tp_size == 4 and rows_ctx % (2 * tp_size) == 0:
         grad_rows = tp_scatter(grad_part, rows_mine, "tp").astype(jnp.bfloat16)
     else:
@@ -345,7 +345,7 @@
     value_part = across(prob.astype(jnp.bfloat16), grad_stack)
     pair_all = jnp.concatenate([key_part, value_part], axis=1)
     out_ring = Ring(out_weight_grad, ring, "ctx").advance(len(ring) // 4)
-    pair_grad = butterfly_sum(direct_scatter(pair_all, "ctx"), "tp")
+    pair_grad = butterfly_sum(ring_scatter_relative(pair_all, ring, "ctx"), "tp")
     out_ring.state, pair_grad = lax.optimization_barrier((out_ring.state, pair_grad))
 
     key_raw = rotate(pair_grad[:, :head_dim], cosine_all, -sine_all)

time: 348 us -> 362 us (1.040)
  waiting for transfers between devices: 122 us -> 136 us
  other arithmetic: 50 us -> 53.8 us
  starting transfers between devices: 57.5 us -> 53.7 us
    ppermute x14 -> x21, waiting for transfers between devices: 17.1 us -> 25 us  [the longest x7 9.28 us: ring_scatter_relative(): got_right = lax.ppermute(send_right.astype(jnp.bfloat16), axis, backward)]
    ppermute x7, starting transfers between devices: 9.87 us -> 2.67 us  [ring_scatter(): got_right = lax.ppermute(send_right.astype(jnp.bfloat16), axis, backward)]
    ppermute x1, waiting for transfers between devices: 0.01 us -> 5.6 us  [tp_scatter(): lax.ppermute(sent.astype(jnp.bfloat16), axis, far).astype(jnp.float32)]
    ppermute x7, waiting for transfers between devices: 4.23 us -> 8.85 us  [ring_scatter(): got_right = lax.ppermute(send_right.astype(jnp.bfloat16), axis, backward)]
    ppermute x7, starting transfers between devices: 5.27 us -> 9.24 us  [ring_scatter(): got_left = lax.ppermute(send_left.astype(jnp.bfloat16), axis, forward)]
    ppermute x14 -> x21, starting transfers between devices: 24.1 us -> 21.1 us  [the longest x7 11 us: ring_scatter_relative(): got_left = lax.ppermute(send_left.astype(jnp.bfloat16), axis, forward)]
  transfers between devices with their start and end apart: 50 -> 57, of which waited for: 28 -> 34; matrix products, arithmetic and copies ran while one was open for 24% -> 22% of each run, Pallas kernels for 0% -> 0%
where the time goes in v14:
time: 362 us; the launch traced here: 360 us
  waiting for transfers between devices  136 us (38%)
  other arithmetic  53.8 us (15%)
  starting transfers between devices  53.7 us (15%)
  between operations  36.6 us (10%)
  matrix products  34.2 us (9%)
  local copies, waits for them, and re-layouts  30.9 us (9%)
  blocking collectives  14.9 us (4%)
    ppermute x7, waiting for transfers between devices, ring_scatter(): got_left = lax.ppermute(send_left.astype(jnp.bfloat16), axis, forward)  56.4 us
    ppermute x7, waiting for transfers between devices, advance(): lax.ppermute(send_right.astype(jnp.bfloat16), self.axis, self.backward)  33.7 us
    dot_general x4, matrix products, against(): lax.dot_general(left, right, (((1,), (1,)), ((), ())), preferred_element_...  14.9 us
    ppermute x7, starting transfers between devices, ring_scatter_relative(): got_left = lax.ppermute(send_left.astype(jnp.bfloat16), axis, forward)  11 us
    ppermute x7, starting transfers between devices, advance(): lax.ppermute(send_left.astype(jnp.bfloat16), self.axis, self.forward)  9.37 us
    ppermute x7, waiting for transfers between devices, ring_scatter_relative(): got_right = lax.ppermute(send_right.astype(jnp.bfloat16), axis, backward)  9.28 us
    ppermute x7, starting transfers between devices, ring_scatter(): got_left = lax.ppermute(send_left.astype(jnp.bfloat16), axis, forward)  9.24 us
    ppermute x4, waiting for transfers between devices, ring_gather(): from_left = lax.ppermute(from_left, axis, forward)  9.23 us
  transfers between devices with their start and end apart: 57, of which 34 were waited for; matrix products, arithmetic and copies ran while one was open for 22% of the time, Pallas kernels for 0%

profile of v14, /device:TPU:0, one launch (start us, length us, event | category | flops | bytes accessed | tf_op | source)
XLA Modules:
  0.0 359.8 jit_solution(6723667223295949434)
XLA Ops:
  2.2 6.9 %fusion.87 = f32[256,1280]{1,0:T(8,128)S(1)} fusion(bf16[256,4096]{1,0:T(8,128)(2,1)S(1)} %copy-done, bf16[1280,4096]{1,0:T(8,128)(2,1)} %param.13), kind=kOutput, calls=%fused_computation.204 | convolution fusion | flops 2684354560 | bytes 13893632 | tf_op jit(solution)/shard_map/dot_general | solution.py:35
  9.6 6.4 %convolution_convert_fusion.2 = bf16[256,1024]{1,0:T(8,128)(2,1)S(1)} fusion(bf16[256,4096]{1,0:T(8,128)(2,1)} %param.15, bf16[1024,4096]{1,0:T(8,128)(2,1)} %param.14), kind=kOutput, calls=%fused_computation.42 | convolution fusion | flops 2147745792 | bytes 11010048 | tf_op jit(solution)/shard_map/dot_general | solution.py:35
  17.6 2.6 collective-permute-start.11
  22.0 5.6 %collective-permute-done.11 = bf16[128,1024]{1,0:T(8,128)(2,1)} collective-permute-done((bf16[128,1024]{1,0:T(8,128)(2,1)}, bf16[128,1024]{1,0:T(8,128)(2,1)}, u32[]{:S(2)}, u32[]{:S(2)}) %collective-permute-start.11) | collective-permute-done | bytes 262176 | tf_op jit(solution)/shard_map/ppermute | solution.py:212
  35.7 3.4 collective-permute-done.10
  41.7 3.2 collective-permute-done.4
  46.9 4.6 %collective-permute-done.8 = bf16[259,256]{1,0:T(8,128)(2,1)S(1)} collective-permute-done((bf16[259,256]{1,0:T(8,128)(2,1)S(1)}, bf16[259,256]{1,0:T(8,128)(2,1)S(1)}, u32[]{:S(2)}, u32[]{:S(2)}) %collective-permute-start.8) | collective-permute-done | bytes 132640 | tf_op jit(solution)/shard_map/ppermute | solution.py:119
  52.0 4.6 %collective-permute-done.9 = bf16[259,256]{1,0:T(8,128)(2,1)S(1)} collective-permute-done((bf16[259,256]{1,0:T(8,128)(2,1)S(1)}, bf16[259,256]{1,0:T(8,128)(2,1)S(1)}, u32[]{:S(2)}, u32[]{:S(2)}) %collective-permute-start.9) | collective-permute-done | bytes 132640 | tf_op jit(solution)/shard_map/ppermute | solution.py:119
  65.4 2.9 copy.27
  72.1 2.7 collective-permute-done.17
  99.3 7.5 %all_gather.6 = bf16[256,1024]{1,0:T(8,128)(2,1)S(1)} all-gather(bf16[64,1024]{1,0:T(8,128)(2,1)S(1)} %bitcast.337), channel_id=1, replica_groups=mesh['ctx'=8,'tp'=4] {'tp'}, dimensions={0}, use_global_device_ids=true | all-gather | bytes 655360 | tf_op jit(solution)/shard_map/all_gather | solution.py:332
  110.0 2.4 fusion.88
  116.0 6.3 %fusion.83 = (f32[8,128,2048]{2,1,0:T(8,128)}, f32[8,128,2048]{2,1,0:T(8,128)}) fusion(f32[8,128,4096]{2,1,0:T(8,128)S(1)} %bitcast.318), kind=kLoop, calls=%fused_computation.200 | loop fusion | bytes 33554432 | tf_op jit(solution)/shard_map/slice | solution.py:157
  126.6 2.3 collective-permute-done.29
  134.0 5.4 %collective-permute-done.30 = bf16[256,128]{1,0:T(8,128)(2,1)S(1)} collective-permute-done((bf16[256,128]{1,0:T(8,128)(2,1)S(1)}, bf16[256,128]{1,0:T(8,128)(2,1)S(1)}, u32[]{:S(2)}, u32[]{:S(2)}) %collective-permute-start.30) | collective-permute-done | bytes 65568 | tf_op jit(solution)/shard_map/ppermute | solution.py:140
  139.6 2.1 fusion.25
  172.3 10.5 %collective-permute-done.38 = bf16[128,2048]{1,0:T(8,128)(2,1)S(1)} collective-permute-done((bf16[128,2048]{1,0:T(8,128)(2,1)S(1)}, bf16[128,2048]{1,0:T(8,128)(2,1)S(1)}, u32[]{:S(2)}, u32[]{:S(2)}) %collective-permute-start.38) | collective-permute-done | bytes 524320 | tf_op jit(solution)/shard_map/ppermute | solution.py:172
  187.8 9.0 %collective-permute-done.39 = bf16[128,2048]{1,0:T(8,128)(2,1)S(1)} collective-permute-done((bf16[128,2048]{1,0:T(8,128)(2,1)S(1)}, bf16[128,2048]{1,0:T(8,128)(2,1)S(1)}, u32[]{:S(2)}, u32[]{:S(2)}) %collective-permute-start.39) | collective-permute-done | bytes 524320 | tf_op jit(solution)/shard_map/ppermute | solution.py:172
  201.6 7.3 %all_gather.7 = bf16[256,1024]{1,0:T(8,128)(2,1)} all-gather(bf16[64,1024]{1,0:T(8,128)(2,1)S(1)} %copy_bitcast_fusion.1), channel_id=1, replica_groups=mesh['ctx'=8,'tp'=4] {'tp'}, dimensions={0}, use_global_device_ids=true | all-gather | bytes 655360 | tf_op jit(solution)/shard_map/all_gather | solution.py:356
  217.9 7.6 %collective-permute-done.41 = bf16[128,2048]{1,0:T(8,128)(2,1)} collective-permute-done((bf16[128,2048]{1,0:T(8,128)(2,1)}, bf16[128,2048]{1,0:T(8,128)(2,1)}, u32[]{:S(2)}, u32[]{:S(2)}) %collective-permute-start.41) | collective-permute-done | bytes 524320 | tf_op jit(solution)/shard_map/ppermute | solution.py:172
  230.9 2.9 fusion.90
  233.9 5.5 %collective-permute-done.42 = bf16[128,2048]{1,0:T(8,128)(2,1)S(1)} collective-permute-done((bf16[128,2048]{1,0:T(8,128)(2,1)S(1)}, bf16[128,2048]{1,0:T(8,128)(2,1)S(1)}, u32[]{:S(2)}, u32[]{:S(2)}) %collective-permute-start.42) | collective-permute-done | bytes 524320 | tf_op jit(solution)/shard_map/ppermute | solution.py:172
  243.1 8.1 %fusion.82 = (f32[8,160,2048]{2,1,0:T(8,128)}, f32[8,160,2048]{2,1,0:T(8,128)}) fusion(f32[8,160,4096]{2,1,0:T(8,128)S(1)} %bitcast.317), kind=kLoop, calls=%fused_computation.199 | loop fusion | bytes 41943040 | tf_op jit(solution)/shard_map/slice | solution.py:83
  256.8 9.9 %collective-permute-done.43 = bf16[160,2048]{1,0:T(8,128)(2,1)S(1)} collective-permute-done((bf16[160,2048]{1,0:T(8,128)(2,1)S(1)}, bf16[160,2048]{1,0:T(8,128)(2,1)S(1)}, u32[]{:S(2)}, u32[]{:S(2)}) %collective-permute-start.43) | collective-permute-done | bytes 655392 | tf_op jit(solution)/shard_map/ppermute | solution.py:94
  271.8 9.7 %collective-permute-done.44 = bf16[160,2048]{1,0:T(8,128)(2,1)S(1)} collective-permute-done((bf16[160,2048]{1,0:T(8,128)(2,1)S(1)}, bf16[160,2048]{1,0:T(8,128)(2,1)S(1)}, u32[]{:S(2)}, u32[]{:S(2)}) %collective-permute-start.44) | collective-permute-done | bytes 655392 | tf_op jit(solution)/shard_map/ppermute | solution.py:94
  286.5 10.0 %collective-permute-done.45 = bf16[160,2048]{1,0:T(8,128)(2,1)S(1)} collective-permute-done((bf16[160,2048]{1,0:T(8,128)(2,1)S(1)}, bf16[160,2048]{1,0:T(8,128)(2,1)S(1)}, u32[]{:S(2)}, u32[]{:S(2)}) %collective-permute-start.45) | collective-permute-done | bytes 655392 | tf_op jit(solution)/shard_map/ppermute | solution.py:94
  301.4 10.0 %collective-permute-done.46 = bf16[160,2048]{1,0:T(8,128)(2,1)S(1)} collective-permute-done((bf16[160,2048]{1,0:T(8,128)(2,1)S(1)}, bf16[160,2048]{1,0:T(8,128)(2,1)S(1)}, u32[]{:S(2)}, u32[]{:S(2)}) %collective-permute-start.46) | collective-permute-done | bytes 655392 | tf_op jit(solution)/shard_map/ppermute | solution.py:94
  316.3 7.4 %convolution_convert_fusion = bf16[256,4096]{1,0:T(8,128)(2,1)} fusion(bf16[256,1024]{1,0:T(8,128)(2,1)S(1)} %all_gather.6, bf16[1024,4096]{1,0:T(8,128)(2,1)} %param.14), kind=kOutput, calls=%fused_computation.3 | convolution fusion | flops 2148532224 | bytes 11010048 | tf_op jit(solution)/shard_map/dot_general | solution.py:333
  323.6 3.0 collective-permute-done.47
  331.3 4.1 %convolution_convert_fusion.1 = bf16[256,4096]{1,0:T(8,128)(2,1)} fusion(bf16[256,1280]{1,0:T(8,128)(2,1)S(1)} %concatenate.49, bf16[1280,4096]{1,0:T(8,128)(2,1)S(1)} %bitcast.344), kind=kOutput, calls=%fused_computation.4 | convolution fusion | flops 2685403136 | bytes 13238272 | tf_op jit(solution)/shard_map/dot_general | solution.py:361
  335.4 7.3 %collective-permute-done.48 = bf16[160,2048]{1,0:T(8,128)(2,1)S(1)} collective-permute-done((bf16[160,2048]{1,0:T(8,128)(2,1)S(1)}, bf16[160,2048]{1,0:T(8,128)(2,1)S(1)}, u32[]{:S(2)}, u32[]{:S(2)}) %collective-permute-start.48) | collective-permute-done | bytes 655392 | tf_op jit(solution)/shard_map/ppermute | solution.py:94
  348.5 6.3 %collective-permute-done.49 = bf16[160,2048]{1,0:T(8,128)(2,1)S(1)} collective-permute-done((bf16[160,2048]{1,0:T(8,128)(2,1)S(1)}, bf16[160,2048]{1,0:T(8,128)(2,1)S(1)}, u32[]{:S(2)}, u32[]{:S(2)}) %collective-permute-start.49) | collective-permute-done | bytes 655392 | tf_op jit(solution)/shard_map/ppermute | solution.py:94
  (236 shorter events, 135.3 us)
Async XLA Ops:
  9.1 11.2 %collective-permute-start = (f32[256,1280]{1,0:T(8,128)S(1)}, f32[256,1280]{1,0:T(8,128)}, u32[]{:S(2)}, u32[]{:S(2)}) collective-permute-start(f32[256,1280]{1,0:T(8,128)S(1)} %fusion.87), channel_id=1, source_target_pairs={{0,1},{1,0},{2,3},{3,2},{4,5},{5,4},{6,7},{7,6},{8,9},{9,8},{10,11... | collective-permute-start | bytes 3932168 | tf_op jit(solution)/shard_map/ppermute | solution.py:189
  75.8 20.3 %collective-permute-start.18 = (bf16[256,128]{1,0:T(8,128)(2,1)S(1)}, bf16[256,128]{1,0:T(8,128)(2,1)S(1)}, u32[]{:S(2)}, u32[]{:S(2)}) collective-permute-start(bf16[256,128]{1,0:T(8,128)(2,1)S(1)} %get-tuple-element.40), channel_id=1, source_target_pairs={{0,8},{8,16},{16,24},{24,28},{28,20},{20,12},{12,4},{4,0},{1,9},{9... | collective-permute-start | bytes 196616 | tf_op jit(solution)/shard_map/ppermute | solution.py:139
  77.9 18.2 %collective-permute-start.25 = (bf16[256,128]{1,0:T(8,128)(2,1)S(1)}, bf16[256,128]{1,0:T(8,128)(2,1)S(1)}, u32[]{:S(2)}, u32[]{:S(2)}) collective-permute-start(bf16[256,128]{1,0:T(8,128)(2,1)S(1)} %get-tuple-element.41), channel_id=1, source_target_pairs={{0,4},{8,0},{16,8},{24,16},{28,24},{20,28},{12,20},{4,12},{1,5},{9... | collective-permute-start | bytes 196616 | tf_op jit(solution)/shard_map/ppermute | solution.py:140
  125.7 13.9 %collective-permute-start.15 = (bf16[128,2048]{1,0:T(8,128)(2,1)S(1)}, bf16[128,2048]{1,0:T(8,128)(2,1)S(1)}, u32[]{:S(2)}, u32[]{:S(2)}) collective-permute-start(bf16[128,2048]{1,0:T(8,128)(2,1)S(1)} %fusion.30), channel_id=1, source_target_pairs={{0,4},{8,0},{16,8},{24,16},{28,24},{20,28},{12,20},{4,12},{1,5},{9... | collective-permute-start | bytes 1572872 | tf_op jit(solution)/shard_map/ppermute | solution.py:172
  132.3 11.1 %collective-permute-start.13 = (bf16[128,2048]{1,0:T(8,128)(2,1)S(1)}, bf16[128,2048]{1,0:T(8,128)(2,1)S(1)}, u32[]{:S(2)}, u32[]{:S(2)}) collective-permute-start(bf16[128,2048]{1,0:T(8,128)(2,1)S(1)} %fusion.29), channel_id=1, source_target_pairs={{0,8},{8,16},{16,24},{24,28},{28,20},{20,12},{12,4},{4,0},{1,9},{9... | collective-permute-start | bytes 1572872 | tf_op jit(solution)/shard_map/ppermute | solution.py:171
  141.8 24.4 %collective-permute-start.16 = (bf16[128,2048]{1,0:T(8,128)(2,1)}, bf16[128,2048]{1,0:T(8,128)(2,1)}, u32[]{:S(2)}, u32[]{:S(2)}) collective-permute-start(bf16[128,2048]{1,0:T(8,128)(2,1)} %fusion.25), channel_id=1, source_target_pairs={{0,4},{8,0},{16,8},{24,16},{28,24},{20,28},{12,20},{4,12},{1,5},{9... | collective-permute-start | bytes 1572872 | tf_op jit(solution)/shard_map/ppermute | solution.py:172
  142.6 22.6 %collective-permute-start.32 = (f32[256,256]{1,0:T(8,128)S(1)}, f32[256,256]{1,0:T(8,128)}, u32[]{:S(2)}, u32[]{:S(2)}) collective-permute-start(f32[256,256]{1,0:T(8,128)S(1)} %fusion.80), channel_id=1, source_target_pairs={{0,2},{1,3},{2,0},{3,1},{4,6},{5,7},{6,4},{7,5},{8,10},{9,11},{10,... | collective-permute-start | bytes 786440 | tf_op jit(solution)/shard_map/ppermute | solution.py:248
  145.6 22.3 %collective-permute-start.14 = (bf16[128,2048]{1,0:T(8,128)(2,1)}, bf16[128,2048]{1,0:T(8,128)(2,1)}, u32[]{:S(2)}, u32[]{:S(2)}) collective-permute-start(bf16[128,2048]{1,0:T(8,128)(2,1)} %fusion.26), channel_id=1, source_target_pairs={{0,8},{8,16},{16,24},{24,28},{28,20},{20,12},{12,4},{4,0},{1,9},{9... | collective-permute-start | bytes 1572872 | tf_op jit(solution)/shard_map/ppermute | solution.py:171
  169.3 13.5 %collective-permute-start.38 = (bf16[128,2048]{1,0:T(8,128)(2,1)S(1)}, bf16[128,2048]{1,0:T(8,128)(2,1)S(1)}, u32[]{:S(2)}, u32[]{:S(2)}) collective-permute-start(bf16[128,2048]{1,0:T(8,128)(2,1)S(1)} %bitcast_add_fusion.24), channel_id=1, source_target_pairs={{0,4},{8,0},{16,8},{24,16},{28,24},{20,28},{12,20},{4,12},{1,5},{9... | collective-permute-start | bytes 1572872 | tf_op jit(solution)/shard_map/ppermute | solution.py:172
  170.8 14.2 %collective-permute-start.33 = (bf16[128,2048]{1,0:T(8,128)(2,1)S(1)}, bf16[128,2048]{1,0:T(8,128)(2,1)S(1)}, u32[]{:S(2)}, u32[]{:S(2)}) collective-permute-start(bf16[128,2048]{1,0:T(8,128)(2,1)S(1)} %bitcast_add_fusion.26), channel_id=1, source_target_pairs={{0,8},{8,16},{16,24},{24,28},{28,20},{20,12},{12,4},{4,0},{1,9},{9... | collective-permute-start | bytes 1572872 | tf_op jit(solution)/shard_map/ppermute | solution.py:171
  184.2 12.6 %collective-permute-start.39 = (bf16[128,2048]{1,0:T(8,128)(2,1)S(1)}, bf16[128,2048]{1,0:T(8,128)(2,1)S(1)}, u32[]{:S(2)}, u32[]{:S(2)}) collective-permute-start(bf16[128,2048]{1,0:T(8,128)(2,1)S(1)} %fusion.20), channel_id=1, source_target_pairs={{0,4},{8,0},{16,8},{24,16},{28,24},{20,28},{12,20},{4,12},{1,5},{9... | collective-permute-start | bytes 1572872 | tf_op jit(solution)/shard_map/ppermute | solution.py:172
  186.3 12.6 %collective-permute-start.34 = (bf16[128,2048]{1,0:T(8,128)(2,1)S(1)}, bf16[128,2048]{1,0:T(8,128)(2,1)S(1)}, u32[]{:S(2)}, u32[]{:S(2)}) collective-permute-start(bf16[128,2048]{1,0:T(8,128)(2,1)S(1)} %fusion.24), channel_id=1, source_target_pairs={{0,8},{8,16},{16,24},{24,28},{28,20},{20,12},{12,4},{4,0},{1,9},{9... | collective-permute-start | bytes 1572872 | tf_op jit(solution)/shard_map/ppermute | solution.py:171
  198.1 11.7 %collective-permute-start.40 = (bf16[128,2048]{1,0:T(8,128)(2,1)S(1)}, bf16[128,2048]{1,0:T(8,128)(2,1)S(1)}, u32[]{:S(2)}, u32[]{:S(2)}) collective-permute-start(bf16[128,2048]{1,0:T(8,128)(2,1)S(1)} %fusion.19), channel_id=1, source_target_pairs={{0,4},{8,0},{16,8},{24,16},{28,24},{20,28},{12,20},{4,12},{1,5},{9... | collective-permute-start | bytes 1572872 | tf_op jit(solution)/shard_map/ppermute | solution.py:172
  200.3 12.4 %collective-permute-start.35 = (bf16[128,2048]{1,0:T(8,128)(2,1)S(1)}, bf16[128,2048]{1,0:T(8,128)(2,1)S(1)}, u32[]{:S(2)}, u32[]{:S(2)}) collective-permute-start(bf16[128,2048]{1,0:T(8,128)(2,1)S(1)} %fusion.23), channel_id=1, source_target_pairs={{0,8},{8,16},{16,24},{24,28},{28,20},{20,12},{12,4},{4,0},{1,9},{9... | collective-permute-start | bytes 1572872 | tf_op jit(solution)/shard_map/ppermute | solution.py:171
  212.0 13.6 %collective-permute-start.41 = (bf16[128,2048]{1,0:T(8,128)(2,1)}, bf16[128,2048]{1,0:T(8,128)(2,1)}, u32[]{:S(2)}, u32[]{:S(2)}) collective-permute-start(bf16[128,2048]{1,0:T(8,128)(2,1)} %fusion.18), channel_id=1, source_target_pairs={{0,4},{8,0},{16,8},{24,16},{28,24},{20,28},{12,20},{4,12},{1,5},{9... | collective-permute-start | bytes 1572872 | tf_op jit(solution)/shard_map/ppermute | solution.py:172
  214.9 13.3 %collective-permute-start.36 = (bf16[128,2048]{1,0:T(8,128)(2,1)}, bf16[128,2048]{1,0:T(8,128)(2,1)}, u32[]{:S(2)}, u32[]{:S(2)}) collective-permute-start(bf16[128,2048]{1,0:T(8,128)(2,1)} %fusion.22), channel_id=1, source_target_pairs={{0,8},{8,16},{16,24},{24,28},{28,20},{20,12},{12,4},{4,0},{1,9},{9... | collective-permute-start | bytes 1572872 | tf_op jit(solution)/shard_map/ppermute | solution.py:171
  227.0 12.4 %collective-permute-start.42 = (bf16[128,2048]{1,0:T(8,128)(2,1)S(1)}, bf16[128,2048]{1,0:T(8,128)(2,1)S(1)}, u32[]{:S(2)}, u32[]{:S(2)}) collective-permute-start(bf16[128,2048]{1,0:T(8,128)(2,1)S(1)} %fusion.17), channel_id=1, source_target_pairs={{0,4},{8,0},{16,8},{24,16},{28,24},{20,28},{12,20},{4,12},{1,5},{9... | collective-permute-start | bytes 1572872 | tf_op jit(solution)/shard_map/ppermute | solution.py:172
  229.6 12.1 %collective-permute-start.37 = (bf16[128,2048]{1,0:T(8,128)(2,1)S(1)}, bf16[128,2048]{1,0:T(8,128)(2,1)S(1)}, u32[]{:S(2)}, u32[]{:S(2)}) collective-permute-start(bf16[128,2048]{1,0:T(8,128)(2,1)S(1)} %fusion.21), channel_id=1, source_target_pairs={{0,8},{8,16},{16,24},{24,28},{28,20},{20,12},{12,4},{4,0},{1,9},{9... | collective-permute-start | bytes 1572872 | tf_op jit(solution)/shard_map/ppermute | solution.py:171
  252.7 14.0 %collective-permute-start.43 = (bf16[160,2048]{1,0:T(8,128)(2,1)S(1)}, bf16[160,2048]{1,0:T(8,128)(2,1)S(1)}, u32[]{:S(2)}, u32[]{:S(2)}) collective-permute-start(bf16[160,2048]{1,0:T(8,128)(2,1)S(1)} %fusion.27), channel_id=1, source_target_pairs={{0,8},{8,16},{16,24},{24,28},{28,20},{20,12},{12,4},{4,0},{1,9},{9... | collective-permute-start | bytes 1966088 | tf_op jit(solution)/shard_map/ppermute | solution.py:94
  255.9 13.9 %collective-permute-start.50 = (bf16[160,2048]{1,0:T(8,128)(2,1)S(1)}, bf16[160,2048]{1,0:T(8,128)(2,1)S(1)}, u32[]{:S(2)}, u32[]{:S(2)}) collective-permute-start(bf16[160,2048]{1,0:T(8,128)(2,1)S(1)} %fusion.28), channel_id=1, source_target_pairs={{0,4},{8,0},{16,8},{24,16},{28,24},{20,28},{12,20},{4,12},{1,5},{9... | collective-permute-start | bytes 1966088 | tf_op jit(solution)/shard_map/ppermute | solution.py:95
  268.2 13.4 %collective-permute-start.44 = (bf16[160,2048]{1,0:T(8,128)(2,1)S(1)}, bf16[160,2048]{1,0:T(8,128)(2,1)S(1)}, u32[]{:S(2)}, u32[]{:S(2)}) collective-permute-start(bf16[160,2048]{1,0:T(8,128)(2,1)S(1)} %fusion.15), channel_id=1, source_target_pairs={{0,8},{8,16},{16,24},{24,28},{28,20},{20,12},{12,4},{4,0},{1,9},{9... | collective-permute-start | bytes 1966088 | tf_op jit(solution)/shard_map/ppermute | solution.py:94
  271.3 14.7 %collective-permute-start.51 = (bf16[160,2048]{1,0:T(8,128)(2,1)S(1)}, bf16[160,2048]{1,0:T(8,128)(2,1)S(1)}, u32[]{:S(2)}, u32[]{:S(2)}) collective-permute-start(bf16[160,2048]{1,0:T(8,128)(2,1)S(1)} %fusion.9), channel_id=1, source_target_pairs={{0,4},{8,0},{16,8},{24,16},{28,24},{20,28},{12,20},{4,12},{1,5},{9... | collective-permute-start | bytes 1966088 | tf_op jit(solution)/shard_map/ppermute | solution.py:95
  283.1 13.4 %collective-permute-start.45 = (bf16[160,2048]{1,0:T(8,128)(2,1)S(1)}, bf16[160,2048]{1,0:T(8,128)(2,1)S(1)}, u32[]{:S(2)}, u32[]{:S(2)}) collective-permute-start(bf16[160,2048]{1,0:T(8,128)(2,1)S(1)} %fusion.14), channel_id=1, source_target_pairs={{0,8},{8,16},{16,24},{24,28},{28,20},{20,12},{12,4},{4,0},{1,9},{9... | collective-permute-start | bytes 1966088 | tf_op jit(solution)/shard_map/ppermute | solution.py:94
  286.2 14.7 %collective-permute-start.52 = (bf16[160,2048]{1,0:T(8,128)(2,1)S(1)}, bf16[160,2048]{1,0:T(8,128)(2,1)S(1)}, u32[]{:S(2)}, u32[]{:S(2)}) collective-permute-start(bf16[160,2048]{1,0:T(8,128)(2,1)S(1)} %fusion.8), channel_id=1, source_target_pairs={{0,4},{8,0},{16,8},{24,16},{28,24},{20,28},{12,20},{4,12},{1,5},{9... | collective-permute-start | bytes 1966088 | tf_op jit(solution)/shard_map/ppermute | solution.py:95
  298.0 13.4 %collective-permute-start.46 = (bf16[160,2048]{1,0:T(8,128)(2,1)S(1)}, bf16[160,2048]{1,0:T(8,128)(2,1)S(1)}, u32[]{:S(2)}, u32[]{:S(2)}) collective-permute-start(bf16[160,2048]{1,0:T(8,128)(2,1)S(1)} %fusion.13), channel_id=1, source_target_pairs={{0,8},{8,16},{16,24},{24,28},{28,20},{20,12},{12,4},{4,0},{1,9},{9... | collective-permute-start | bytes 1966088 | tf_op jit(solution)/shard_map/ppermute | solution.py:94
  301.1 14.5 %collective-permute-start.53 = (bf16[160,2048]{1,0:T(8,128)(2,1)S(1)}, bf16[160,2048]{1,0:T(8,128)(2,1)S(1)}, u32[]{:S(2)}, u32[]{:S(2)}) collective-permute-start(bf16[160,2048]{1,0:T(8,128)(2,1)S(1)} %fusion.7), channel_id=1, source_target_pairs={{0,4},{8,0},{16,8},{24,16},{28,24},{20,28},{12,20},{4,12},{1,5},{9... | collective-permute-start | bytes 1966088 | tf_op jit(solution)/shard_map/ppermute | solution.py:95
  312.9 13.8 %collective-permute-start.47 = (bf16[160,2048]{1,0:T(8,128)(2,1)S(1)}, bf16[160,2048]{1,0:T(8,128)(2,1)S(1)}, u32[]{:S(2)}, u32[]{:S(2)}) collective-permute-start(bf16[160,2048]{1,0:T(8,128)(2,1)S(1)} %fusion.12), channel_id=1, source_target_pairs={{0,8},{8,16},{16,24},{24,28},{28,20},{20,12},{12,4},{4,0},{1,9},{9... | collective-permute-start | bytes 1966088 | tf_op jit(solution)/shard_map/ppermute | solution.py:94
  315.7 15.1 %collective-permute-start.54 = (bf16[160,2048]{1,0:T(8,128)(2,1)S(1)}, bf16[160,2048]{1,0:T(8,128)(2,1)S(1)}, u32[]{:S(2)}, u32[]{:S(2)}) collective-permute-start(bf16[160,2048]{1,0:T(8,128)(2,1)S(1)} %fusion.6), channel_id=1, source_target_pairs={{0,4},{8,0},{16,8},{24,16},{28,24},{20,28},{12,20},{4,12},{1,5},{9... | collective-permute-start | bytes 1966088 | tf_op jit(solution)/shard_map/ppermute | solution.py:95
  328.1 14.6 %collective-permute-start.48 = (bf16[160,2048]{1,0:T(8,128)(2,1)S(1)}, bf16[160,2048]{1,0:T(8,128)(2,1)S(1)}, u32[]{:S(2)}, u32[]{:S(2)}) collective-permute-start(bf16[160,2048]{1,0:T(8,128)(2,1)S(1)} %fusion.11), channel_id=1, source_target_pairs={{0,8},{8,16},{16,24},{24,28},{28,20},{20,12},{12,4},{4,0},{1,9},{9... | collective-permute-start | bytes 1966088 | tf_op jit(solution)/shard_map/ppermute | solution.py:94
  331.1 15.7 %collective-permute-start.55 = (bf16[160,2048]{1,0:T(8,128)(2,1)S(1)}, bf16[160,2048]{1,0:T(8,128)(2,1)S(1)}, u32[]{:S(2)}, u32[]{:S(2)}) collective-permute-start(bf16[160,2048]{1,0:T(8,128)(2,1)S(1)} %fusion.5), channel_id=1, source_target_pairs={{0,4},{8,0},{16,8},{24,16},{28,24},{20,28},{12,20},{4,12},{1,5},{9... | collective-permute-start | bytes 1966088 | tf_op jit(solution)/shard_map/ppermute | solution.py:95
  344.2 10.6 %collective-permute-start.49 = (bf16[160,2048]{1,0:T(8,128)(2,1)S(1)}, bf16[160,2048]{1,0:T(8,128)(2,1)S(1)}, u32[]{:S(2)}, u32[]{:S(2)}) collective-permute-start(bf16[160,2048]{1,0:T(8,128)(2,1)S(1)} %fusion.10), channel_id=1, source_target_pairs={{0,8},{8,16},{16,24},{24,28},{28,20},{20,12},{12,4},{4,0},{1,9},{9... | collective-permute-start | bytes 1966088 | tf_op jit(solution)/shard_map/ppermute | solution.py:94
  346.9 10.6 %collective-permute-start.56 = (bf16[160,2048]{1,0:T(8,128)(2,1)S(1)}, bf16[160,2048]{1,0:T(8,128)(2,1)S(1)}, u32[]{:S(2)}, u32[]{:S(2)}) collective-permute-start(bf16[160,2048]{1,0:T(8,128)(2,1)S(1)} %fusion.4), channel_id=1, source_target_pairs={{0,4},{8,0},{16,8},{24,16},{28,24},{20,28},{12,20},{4,12},{1,5},{9... | collective-permute-start | bytes 1966088 | tf_op jit(solution)/shard_map/ppermute | solution.py:95
  (44 other events, 340.4 us)

commit v15 on v10

--- a/solution.py
+++ b/solution.py
@@ -333,6 +333,7 @@
     out = jnp.dot(piece, w_out, preferred_element_type=jnp.float32).astype(jnp.bfloat16)
     out_weight_grad = across(piece, grad_out)
 
+    out, grad_rows = lax.optimization_barrier((out, grad_rows))
     grad_stack = jnp.transpose(grad_rows.reshape(rows_mine, heads, head_dim), (1, 0, 2)).reshape(
         stacked, head_dim
     )

time: 348 us -> 357 us (1.026)
  waiting for transfers between devices: 122 us -> 136 us
    ppermute x7, waiting for transfers between devices: 4.23 us -> 9.39 us  [ring_scatter(): got_right = lax.ppermute(send_right.astype(jnp.bfloat16), axis, backward)]
    ppermute x7, starting transfers between devices: 9.87 us -> 4.99 us  [ring_scatter(): got_right = lax.ppermute(send_right.astype(jnp.bfloat16), axis, backward)]
    dot_general x1, matrix products: 7.8 us -> 3.72 us  [shards(): jnp.dot(piece, w_out, preferred_element_type=jnp.float32)]
    dot_general x1, matrix products: 4.12 us -> 8.03 us  [shards(): jnp.dot(d_qkv, w_qkv, preferred_element_type=jnp.float32)]
  transfers between devices with their start and end apart: 50 -> 50, of which waited for: 28 -> 29; matrix products, arithmetic and copies ran while one was open for 24% -> 21% of each run, Pallas kernels for 0% -> 0%
where the time goes in v15:
time: 357 us; the launch traced here: 355 us
  waiting for transfers between devices  136 us (38%)
  starting transfers between devices  57.6 us (16%)
  other arithmetic  47.8 us (13%)
  between operations  37.4 us (10%)
  matrix products  34.9 us (10%)
  local copies, waits for them, and re-layouts  28.3 us (8%)
  blocking collectives  13.6 us (4%)
    ppermute x7, waiting for transfers between devices, ring_scatter(): got_left = lax.ppermute(send_left.astype(jnp.bfloat16), axis, forward)  59.2 us
    ppermute x7, waiting for transfers between devices, advance(): lax.ppermute(send_right.astype(jnp.bfloat16), self.axis, self.backward)  34.6 us
    ppermute x7, waiting for transfers between devices, direct_gather(): got[count - shift] = lax.ppermute(value, axis, pairs)  16.3 us
    dot_general x4, matrix products, against(): lax.dot_general(left, right, (((1,), (1,)), ((), ())), preferred_element_...  14.9 us
    ppermute x7, starting transfers between devices, direct_gather(): got[count - shift] = lax.ppermute(value, axis, pairs)  12.6 us
    ppermute x7, starting transfers between devices, direct_scatter(): lax.ppermute(blocks[shift].astype(jnp.bfloat16), axis, pairs)  12.2 us
    ppermute x7, waiting for transfers between devices, ring_scatter(): got_right = lax.ppermute(send_right.astype(jnp.bfloat16), axis, backward)  9.39 us
    convert_element_type x6, other arithmetic, ring_scatter(): got_left = lax.ppermute(send_left.astype(jnp.bfloat16), axis, forward)  8.9 us
  transfers between devices with their start and end apart: 50, of which 29 were waited for; matrix products, arithmetic and copies ran while one was open for 21% of the time, Pallas kernels for 0%

profile of v15, /device:TPU:0, one launch (start us, length us, event | category | flops | bytes accessed | tf_op | source)
XLA Modules:
  0.0 355.4 jit_solution(8855948464437863124)
XLA Ops:
  2.2 6.9 %fusion.69 = f32[256,1280]{1,0:T(8,128)S(1)} fusion(bf16[256,4096]{1,0:T(8,128)(2,1)S(1)} %copy-done, bf16[1280,4096]{1,0:T(8,128)(2,1)} %param.13), kind=kOutput, calls=%fused_computation.171 | convolution fusion | flops 2684354560 | bytes 13893632 | tf_op jit(solution)/shard_map/dot_general | solution.py:35
  9.6 6.4 %convolution_convert_fusion.2 = bf16[256,1024]{1,0:T(8,128)(2,1)S(1)} fusion(bf16[256,4096]{1,0:T(8,128)(2,1)} %param.15, bf16[1024,4096]{1,0:T(8,128)(2,1)} %param.14), kind=kOutput, calls=%fused_computation.45 | convolution fusion | flops 2147745792 | bytes 11010048 | tf_op jit(solution)/shard_map/dot_general | solution.py:35
  17.6 2.6 collective-permute-start.11
  37.9 4.2 %collective-permute-done.1 = f32[128,256]{1,0:T(8,128)S(1)} collective-permute-done((f32[128,256]{1,0:T(8,128)S(1)}, f32[128,256]{1,0:T(8,128)S(1)}, u32[]{:S(2)}, u32[]{:S(2)}) %collective-permute-start.1) | collective-permute-done | bytes 131104 | tf_op jit(solution)/shard_map/ppermute | solution.py:197
  44.4 4.6 %collective-permute-start.3 = (bf16[259,256]{1,0:T(8,128)(2,1)S(1)}, bf16[259,256]{1,0:T(8,128)(2,1)S(1)}, u32[]{:S(2)}, u32[]{:S(2)}) collective-permute-start(bf16[259,256]{1,0:T(8,128)(2,1)S(1)} %get-tuple-element.23), channel_id=1, source_target_pairs={{0,28},{4,0},{8,4},{12,8},{16,12},{20,16},{24,20},{28,24},{1,29},{... | collective-permute-start | bytes 397832 | tf_op jit(solution)/shard_map/ppermute | solution.py:226
  49.4 3.0 collective-permute-start.6
  58.8 13.5 %collective-permute-done.6 = bf16[259,256]{1,0:T(8,128)(2,1)S(1)} collective-permute-done((bf16[259,256]{1,0:T(8,128)(2,1)S(1)}, bf16[259,256]{1,0:T(8,128)(2,1)S(1)}, u32[]{:S(2)}, u32[]{:S(2)}) %collective-permute-start.6) | collective-permute-done | bytes 132640 | tf_op jit(solution)/shard_map/ppermute | solution.py:226
  77.5 6.9 %all_gather.6 = bf16[256,1024]{1,0:T(8,128)(2,1)S(1)} all-gather(bf16[64,1024]{1,0:T(8,128)(2,1)S(1)} %bitcast.244), channel_id=1, replica_groups=mesh['ctx'=8,'tp'=4] {'tp'}, dimensions={0}, use_global_device_ids=true | all-gather | bytes 655360 | tf_op jit(solution)/shard_map/all_gather | solution.py:332
  84.4 3.7 %convolution_convert_fusion = bf16[256,4096]{1,0:T(8,128)(2,1)} fusion(bf16[256,1024]{1,0:T(8,128)(2,1)S(1)} %all_gather.6, bf16[1024,4096]{1,0:T(8,128)(2,1)S(1)} %bitcast.251), kind=kOutput, calls=%fused_computation.3 | convolution fusion | flops 2148532224 | bytes 11010048 | tf_op jit(solution)/shard_map/dot_general | solution.py:333
  88.1 2.4 fusion.70
  96.0 2.8 collective-permute-start.19
  101.7 6.3 %fusion.64 = (f32[8,128,2048]{2,1,0:T(8,128)}, f32[8,128,2048]{2,1,0:T(8,128)}) fusion(f32[8,128,4096]{2,1,0:T(8,128)S(1)} %bitcast.233), kind=kLoop, calls=%fused_computation.166 | loop fusion | bytes 33554432 | tf_op jit(solution)/shard_map/slice | solution.py:157
  108.1 2.4 collective-permute-start.22
  110.5 2.8 collective-permute-start.23
  115.4 3.6 %collective-permute-done.22 = bf16[256,256]{1,0:T(8,128)(2,1)S(1)} collective-permute-done((bf16[256,256]{1,0:T(8,128)(2,1)S(1)}, bf16[256,256]{1,0:T(8,128)(2,1)S(1)}, u32[]{:S(2)}, u32[]{:S(2)}) %collective-permute-start.22) | collective-permute-done | bytes 131104 | tf_op jit(solution)/shard_map/ppermute | solution.py:237
  122.5 3.5 collective-permute-start.13
  133.7 5.9 %collective-permute-done.13 = bf16[128,2048]{1,0:T(8,128)(2,1)} collective-permute-done((bf16[128,2048]{1,0:T(8,128)(2,1)}, bf16[128,2048]{1,0:T(8,128)(2,1)}, u32[]{:S(2)}, u32[]{:S(2)}) %collective-permute-start.13) | collective-permute-done | bytes 524320 | tf_op jit(solution)/shard_map/ppermute | solution.py:171
  169.0 10.3 %collective-permute-done.31 = bf16[128,2048]{1,0:T(8,128)(2,1)S(1)} collective-permute-done((bf16[128,2048]{1,0:T(8,128)(2,1)S(1)}, bf16[128,2048]{1,0:T(8,128)(2,1)S(1)}, u32[]{:S(2)}, u32[]{:S(2)}) %collective-permute-start.31) | collective-permute-done | bytes 524320 | tf_op jit(solution)/shard_map/ppermute | solution.py:172
  184.4 8.8 %collective-permute-done.32 = bf16[128,2048]{1,0:T(8,128)(2,1)S(1)} collective-permute-done((bf16[128,2048]{1,0:T(8,128)(2,1)S(1)}, bf16[128,2048]{1,0:T(8,128)(2,1)S(1)}, u32[]{:S(2)}, u32[]{:S(2)}) %collective-permute-start.32) | collective-permute-done | bytes 524320 | tf_op jit(solution)/shard_map/ppermute | solution.py:172
  198.0 6.7 %all_gather.7 = bf16[256,1024]{1,0:T(8,128)(2,1)S(1)} all-gather(bf16[64,1024]{1,0:T(8,128)(2,1)S(1)} %copy_bitcast_fusion.1), channel_id=1, replica_groups=mesh['ctx'=8,'tp'=4] {'tp'}, dimensions={0}, use_global_device_ids=true | all-gather | bytes 655360 | tf_op jit(solution)/shard_map/all_gather | solution.py:357
  213.3 8.1 %collective-permute-done.34 = bf16[128,2048]{1,0:T(8,128)(2,1)} collective-permute-done((bf16[128,2048]{1,0:T(8,128)(2,1)}, bf16[128,2048]{1,0:T(8,128)(2,1)}, u32[]{:S(2)}, u32[]{:S(2)}) %collective-permute-start.34) | collective-permute-done | bytes 524320 | tf_op jit(solution)/shard_map/ppermute | solution.py:172
  226.7 2.9 fusion.72
  229.6 5.1 %collective-permute-done.35 = bf16[128,2048]{1,0:T(8,128)(2,1)S(1)} collective-permute-done((bf16[128,2048]{1,0:T(8,128)(2,1)S(1)}, bf16[128,2048]{1,0:T(8,128)(2,1)S(1)}, u32[]{:S(2)}, u32[]{:S(2)}) %collective-permute-start.35) | collective-permute-done | bytes 524320 | tf_op jit(solution)/shard_map/ppermute | solution.py:172
  238.9 8.0 %fusion.63 = (f32[8,160,2048]{2,1,0:T(8,128)}, f32[8,160,2048]{2,1,0:T(8,128)}) fusion(f32[8,160,4096]{2,1,0:T(8,128)S(1)} %bitcast.232), kind=kLoop, calls=%fused_computation.165 | loop fusion | bytes 41943040 | tf_op jit(solution)/shard_map/slice | solution.py:83
  252.5 9.4 %collective-permute-done.36 = bf16[160,2048]{1,0:T(8,128)(2,1)S(1)} collective-permute-done((bf16[160,2048]{1,0:T(8,128)(2,1)S(1)}, bf16[160,2048]{1,0:T(8,128)(2,1)S(1)}, u32[]{:S(2)}, u32[]{:S(2)}) %collective-permute-start.36) | collective-permute-done | bytes 655392 | tf_op jit(solution)/shard_map/ppermute | solution.py:94
  267.0 9.8 %collective-permute-done.37 = bf16[160,2048]{1,0:T(8,128)(2,1)S(1)} collective-permute-done((bf16[160,2048]{1,0:T(8,128)(2,1)S(1)}, bf16[160,2048]{1,0:T(8,128)(2,1)S(1)}, u32[]{:S(2)}, u32[]{:S(2)}) %collective-permute-start.37) | collective-permute-done | bytes 655392 | tf_op jit(solution)/shard_map/ppermute | solution.py:94
  281.8 9.9 %collective-permute-done.38 = bf16[160,2048]{1,0:T(8,128)(2,1)S(1)} collective-permute-done((bf16[160,2048]{1,0:T(8,128)(2,1)S(1)}, bf16[160,2048]{1,0:T(8,128)(2,1)S(1)}, u32[]{:S(2)}, u32[]{:S(2)}) %collective-permute-start.38) | collective-permute-done | bytes 655392 | tf_op jit(solution)/shard_map/ppermute | solution.py:94
  296.6 9.9 %collective-permute-done.39 = bf16[160,2048]{1,0:T(8,128)(2,1)S(1)} collective-permute-done((bf16[160,2048]{1,0:T(8,128)(2,1)S(1)}, bf16[160,2048]{1,0:T(8,128)(2,1)S(1)}, u32[]{:S(2)}, u32[]{:S(2)}) %collective-permute-start.39) | collective-permute-done | bytes 655392 | tf_op jit(solution)/shard_map/ppermute | solution.py:94
  311.6 10.6 %collective-permute-done.40 = bf16[160,2048]{1,0:T(8,128)(2,1)S(1)} collective-permute-done((bf16[160,2048]{1,0:T(8,128)(2,1)S(1)}, bf16[160,2048]{1,0:T(8,128)(2,1)S(1)}, u32[]{:S(2)}, u32[]{:S(2)}) %collective-permute-start.40) | collective-permute-done | bytes 655392 | tf_op jit(solution)/shard_map/ppermute | solution.py:94
  327.0 8.0 %convolution_convert_fusion.1 = bf16[256,4096]{1,0:T(8,128)(2,1)} fusion(bf16[256,1280]{1,0:T(8,128)(2,1)S(1)} %concatenate.45, bf16[1280,4096]{1,0:T(8,128)(2,1)} %param.13), kind=kOutput, calls=%fused_computation.4 | convolution fusion | flops 2685403136 | bytes 13238272 | tf_op jit(solution)/shard_map/dot_general | solution.py:362
  335.0 3.6 %collective-permute-done.41 = bf16[160,2048]{1,0:T(8,128)(2,1)S(1)} collective-permute-done((bf16[160,2048]{1,0:T(8,128)(2,1)S(1)}, bf16[160,2048]{1,0:T(8,128)(2,1)S(1)}, u32[]{:S(2)}, u32[]{:S(2)}) %collective-permute-start.41) | collective-permute-done | bytes 655392 | tf_op jit(solution)/shard_map/ppermute | solution.py:94
  344.8 6.0 %collective-permute-done.42 = bf16[160,2048]{1,0:T(8,128)(2,1)S(1)} collective-permute-done((bf16[160,2048]{1,0:T(8,128)(2,1)S(1)}, bf16[160,2048]{1,0:T(8,128)(2,1)S(1)}, u32[]{:S(2)}, u32[]{:S(2)}) %collective-permute-start.42) | collective-permute-done | bytes 655392 | tf_op jit(solution)/shard_map/ppermute | solution.py:94
  (203 shorter events, 119.2 us)
Async XLA Ops:
  9.1 25.8 %collective-permute-start = (f32[256,1280]{1,0:T(8,128)S(1)}, f32[256,1280]{1,0:T(8,128)}, u32[]{:S(2)}, u32[]{:S(2)}) collective-permute-start(f32[256,1280]{1,0:T(8,128)S(1)} %fusion.69), channel_id=1, source_target_pairs={{0,1},{1,0},{2,3},{3,2},{4,5},{5,4},{6,7},{7,6},{8,9},{9,8},{10,11... | collective-permute-start | bytes 3932168 | tf_op jit(solution)/shard_map/ppermute | solution.py:189
  17.6 19.0 %collective-permute-start.11 = (bf16[128,1024]{1,0:T(8,128)(2,1)}, bf16[128,1024]{1,0:T(8,128)(2,1)}, u32[]{:S(2)}, u32[]{:S(2)}) collective-permute-start(bf16[128,1024]{1,0:T(8,128)(2,1)} %constant_dynamic-slice_fusion), channel_id=1, source_target_pairs={{0,2},{1,3},{2,0},{3,1},{4,6},{5,7},{6,4},{7,5},{8,10},{9,11},{10,... | collective-permute-start | bytes 786440 | tf_op jit(solution)/shard_map/ppermute | solution.py:212
  49.4 22.9 %collective-permute-start.6 = (bf16[259,256]{1,0:T(8,128)(2,1)S(1)}, bf16[259,256]{1,0:T(8,128)(2,1)S(1)}, u32[]{:S(2)}, u32[]{:S(2)}) collective-permute-start(bf16[259,256]{1,0:T(8,128)(2,1)S(1)} %get-tuple-element.23), channel_id=1, source_target_pairs={{0,16},{4,20},{8,24},{12,28},{16,0},{20,4},{24,8},{28,12},{1,17},{... | collective-permute-start | bytes 397832 | tf_op jit(solution)/shard_map/ppermute | solution.py:226
  52.4 21.4 %collective-permute-start.7 = (bf16[259,256]{1,0:T(8,128)(2,1)S(1)}, bf16[259,256]{1,0:T(8,128)(2,1)S(1)}, u32[]{:S(2)}, u32[]{:S(2)}) collective-permute-start(bf16[259,256]{1,0:T(8,128)(2,1)S(1)} %get-tuple-element.23), channel_id=1, source_target_pairs={{0,12},{4,16},{8,20},{12,24},{16,28},{20,0},{24,4},{28,8},{1,13},{... | collective-permute-start | bytes 397832 | tf_op jit(solution)/shard_map/ppermute | solution.py:226
  54.2 19.6 %collective-permute-start.8 = (bf16[259,256]{1,0:T(8,128)(2,1)S(1)}, bf16[259,256]{1,0:T(8,128)(2,1)S(1)}, u32[]{:S(2)}, u32[]{:S(2)}) collective-permute-start(bf16[259,256]{1,0:T(8,128)(2,1)S(1)} %get-tuple-element.23), channel_id=1, source_target_pairs={{0,8},{4,12},{8,16},{12,20},{16,24},{20,28},{24,0},{28,4},{1,9},{5... | collective-permute-start | bytes 397832 | tf_op jit(solution)/shard_map/ppermute | solution.py:226
  55.9 17.9 %collective-permute-start.9 = (bf16[259,256]{1,0:T(8,128)(2,1)S(1)}, bf16[259,256]{1,0:T(8,128)(2,1)S(1)}, u32[]{:S(2)}, u32[]{:S(2)}) collective-permute-start(bf16[259,256]{1,0:T(8,128)(2,1)S(1)} %get-tuple-element.23), channel_id=1, source_target_pairs={{0,4},{4,8},{8,12},{12,16},{16,20},{20,24},{24,28},{28,0},{1,5},{5... | collective-permute-start | bytes 397832 | tf_op jit(solution)/shard_map/ppermute | solution.py:226
  94.8 13.3 %collective-permute-start.17 = (bf16[256,256]{1,0:T(8,128)(2,1)S(1)}, bf16[256,256]{1,0:T(8,128)(2,1)}, u32[]{:S(2)}, u32[]{:S(2)}) collective-permute-start(bf16[256,256]{1,0:T(8,128)(2,1)S(1)} %get-tuple-element.34), channel_id=1, source_target_pairs={{0,4},{4,8},{8,12},{12,16},{16,20},{20,24},{24,28},{28,0},{1,5},{5... | collective-permute-start | bytes 393224 | tf_op jit(solution)/shard_map/ppermute | solution.py:237
  94.9 15.6 %collective-permute-start.18 = (bf16[256,256]{1,0:T(8,128)(2,1)S(1)}, bf16[256,256]{1,0:T(8,128)(2,1)}, u32[]{:S(2)}, u32[]{:S(2)}) collective-permute-start(bf16[256,256]{1,0:T(8,128)(2,1)S(1)} %get-tuple-element.40), channel_id=1, source_target_pairs={{0,8},{4,12},{8,16},{12,20},{16,24},{20,28},{24,0},{28,4},{1,9},{5... | collective-permute-start | bytes 393224 | tf_op jit(solution)/shard_map/ppermute | solution.py:237
  96.0 19.5 %collective-permute-start.19 = (bf16[256,256]{1,0:T(8,128)(2,1)S(1)}, bf16[256,256]{1,0:T(8,128)(2,1)}, u32[]{:S(2)}, u32[]{:S(2)}) collective-permute-start(bf16[256,256]{1,0:T(8,128)(2,1)S(1)} %get-tuple-element.39), channel_id=1, source_target_pairs={{0,12},{4,16},{8,20},{12,24},{16,28},{20,0},{24,4},{28,8},{1,13},{... | collective-permute-start | bytes 393224 | tf_op jit(solution)/shard_map/ppermute | solution.py:237
  98.8 16.6 %collective-permute-start.20 = (bf16[256,256]{1,0:T(8,128)(2,1)S(1)}, bf16[256,256]{1,0:T(8,128)(2,1)}, u32[]{:S(2)}, u32[]{:S(2)}) collective-permute-start(bf16[256,256]{1,0:T(8,128)(2,1)S(1)} %get-tuple-element.38), channel_id=1, source_target_pairs={{0,16},{4,20},{8,24},{12,28},{16,0},{20,4},{24,8},{28,12},{1,17},{... | collective-permute-start | bytes 393224 | tf_op jit(solution)/shard_map/ppermute | solution.py:237
  100.4 15.0 %collective-permute-start.21 = (bf16[256,256]{1,0:T(8,128)(2,1)S(1)}, bf16[256,256]{1,0:T(8,128)(2,1)}, u32[]{:S(2)}, u32[]{:S(2)}) collective-permute-start(bf16[256,256]{1,0:T(8,128)(2,1)S(1)} %get-tuple-element.37), channel_id=1, source_target_pairs={{0,20},{4,24},{8,28},{12,0},{16,4},{20,8},{24,12},{28,16},{1,21},{... | collective-permute-start | bytes 393224 | tf_op jit(solution)/shard_map/ppermute | solution.py:237
  115.4 16.4 %collective-permute-start.15 = (bf16[128,2048]{1,0:T(8,128)(2,1)}, bf16[128,2048]{1,0:T(8,128)(2,1)}, u32[]{:S(2)}, u32[]{:S(2)}) collective-permute-start(bf16[128,2048]{1,0:T(8,128)(2,1)} %fusion.31), channel_id=1, source_target_pairs={{0,4},{8,0},{16,8},{24,16},{28,24},{20,28},{12,20},{4,12},{1,5},{9... | collective-permute-start | bytes 1572872 | tf_op jit(solution)/shard_map/ppermute | solution.py:172
  122.5 17.2 %collective-permute-start.13 = (bf16[128,2048]{1,0:T(8,128)(2,1)}, bf16[128,2048]{1,0:T(8,128)(2,1)}, u32[]{:S(2)}, u32[]{:S(2)}) collective-permute-start(bf16[128,2048]{1,0:T(8,128)(2,1)} %fusion.30), channel_id=1, source_target_pairs={{0,8},{8,16},{16,24},{24,28},{28,20},{20,12},{12,4},{4,0},{1,9},{9... | collective-permute-start | bytes 1572872 | tf_op jit(solution)/shard_map/ppermute | solution.py:171
  129.8 32.0 %collective-permute-start.25 = (f32[256,256]{1,0:T(8,128)S(1)}, f32[256,256]{1,0:T(8,128)}, u32[]{:S(2)}, u32[]{:S(2)}) collective-permute-start(f32[256,256]{1,0:T(8,128)S(1)} %add.689), channel_id=1, source_target_pairs={{0,2},{1,3},{2,0},{3,1},{4,6},{5,7},{6,4},{7,5},{8,10},{9,11},{10,... | collective-permute-start | bytes 786440 | tf_op jit(solution)/shard_map/ppermute | solution.py:248
  133.3 29.5 %collective-permute-start.16 = (bf16[128,2048]{1,0:T(8,128)(2,1)S(1)}, bf16[128,2048]{1,0:T(8,128)(2,1)}, u32[]{:S(2)}, u32[]{:S(2)}) collective-permute-start(bf16[128,2048]{1,0:T(8,128)(2,1)S(1)} %fusion.26), channel_id=1, source_target_pairs={{0,4},{8,0},{16,8},{24,16},{28,24},{20,28},{12,20},{4,12},{1,5},{9... | collective-permute-start | bytes 1572872 | tf_op jit(solution)/shard_map/ppermute | solution.py:172
  141.9 22.6 %collective-permute-start.14 = (bf16[128,2048]{1,0:T(8,128)(2,1)}, bf16[128,2048]{1,0:T(8,128)(2,1)}, u32[]{:S(2)}, u32[]{:S(2)}) collective-permute-start(bf16[128,2048]{1,0:T(8,128)(2,1)} %fusion.27), channel_id=1, source_target_pairs={{0,8},{8,16},{16,24},{24,28},{28,20},{20,12},{12,4},{4,0},{1,9},{9... | collective-permute-start | bytes 1572872 | tf_op jit(solution)/shard_map/ppermute | solution.py:171
  166.0 13.3 %collective-permute-start.31 = (bf16[128,2048]{1,0:T(8,128)(2,1)S(1)}, bf16[128,2048]{1,0:T(8,128)(2,1)S(1)}, u32[]{:S(2)}, u32[]{:S(2)}) collective-permute-start(bf16[128,2048]{1,0:T(8,128)(2,1)S(1)} %bitcast_add_fusion.24), channel_id=1, source_target_pairs={{0,4},{8,0},{16,8},{24,16},{28,24},{20,28},{12,20},{4,12},{1,5},{9... | collective-permute-start | bytes 1572872 | tf_op jit(solution)/shard_map/ppermute | solution.py:172
  167.7 14.4 %collective-permute-start.26 = (bf16[128,2048]{1,0:T(8,128)(2,1)S(1)}, bf16[128,2048]{1,0:T(8,128)(2,1)S(1)}, u32[]{:S(2)}, u32[]{:S(2)}) collective-permute-start(bf16[128,2048]{1,0:T(8,128)(2,1)S(1)} %bitcast_add_fusion.26), channel_id=1, source_target_pairs={{0,8},{8,16},{16,24},{24,28},{28,20},{20,12},{12,4},{4,0},{1,9},{9... | collective-permute-start | bytes 1572872 | tf_op jit(solution)/shard_map/ppermute | solution.py:171
  208.2 13.1 %collective-permute-start.34 = (bf16[128,2048]{1,0:T(8,128)(2,1)}, bf16[128,2048]{1,0:T(8,128)(2,1)}, u32[]{:S(2)}, u32[]{:S(2)}) collective-permute-start(bf16[128,2048]{1,0:T(8,128)(2,1)} %fusion.19), channel_id=1, source_target_pairs={{0,4},{8,0},{16,8},{24,16},{28,24},{20,28},{12,20},{4,12},{1,5},{9... | collective-permute-start | bytes 1572872 | tf_op jit(solution)/shard_map/ppermute | solution.py:172
  211.9 12.7 %collective-permute-start.29 = (bf16[128,2048]{1,0:T(8,128)(2,1)}, bf16[128,2048]{1,0:T(8,128)(2,1)}, u32[]{:S(2)}, u32[]{:S(2)}) collective-permute-start(bf16[128,2048]{1,0:T(8,128)(2,1)} %fusion.23), channel_id=1, source_target_pairs={{0,8},{8,16},{16,24},{24,28},{28,20},{20,12},{12,4},{4,0},{1,9},{9... | collective-permute-start | bytes 1572872 | tf_op jit(solution)/shard_map/ppermute | solution.py:171
  248.5 13.4 %collective-permute-start.36 = (bf16[160,2048]{1,0:T(8,128)(2,1)S(1)}, bf16[160,2048]{1,0:T(8,128)(2,1)S(1)}, u32[]{:S(2)}, u32[]{:S(2)}) collective-permute-start(bf16[160,2048]{1,0:T(8,128)(2,1)S(1)} %fusion.28), channel_id=1, source_target_pairs={{0,8},{8,16},{16,24},{24,28},{28,20},{20,12},{12,4},{4,0},{1,9},{9... | collective-permute-start | bytes 1966088 | tf_op jit(solution)/shard_map/ppermute | solution.py:94
  251.3 13.4 %collective-permute-start.43 = (bf16[160,2048]{1,0:T(8,128)(2,1)S(1)}, bf16[160,2048]{1,0:T(8,128)(2,1)S(1)}, u32[]{:S(2)}, u32[]{:S(2)}) collective-permute-start(bf16[160,2048]{1,0:T(8,128)(2,1)S(1)} %fusion.29), channel_id=1, source_target_pairs={{0,4},{8,0},{16,8},{24,16},{28,24},{20,28},{12,20},{4,12},{1,5},{9... | collective-permute-start | bytes 1966088 | tf_op jit(solution)/shard_map/ppermute | solution.py:95
  263.3 13.4 %collective-permute-start.37 = (bf16[160,2048]{1,0:T(8,128)(2,1)S(1)}, bf16[160,2048]{1,0:T(8,128)(2,1)S(1)}, u32[]{:S(2)}, u32[]{:S(2)}) collective-permute-start(bf16[160,2048]{1,0:T(8,128)(2,1)S(1)} %fusion.16), channel_id=1, source_target_pairs={{0,8},{8,16},{16,24},{24,28},{28,20},{20,12},{12,4},{4,0},{1,9},{9... | collective-permute-start | bytes 1966088 | tf_op jit(solution)/shard_map/ppermute | solution.py:94
  266.2 14.7 %collective-permute-start.44 = (bf16[160,2048]{1,0:T(8,128)(2,1)S(1)}, bf16[160,2048]{1,0:T(8,128)(2,1)S(1)}, u32[]{:S(2)}, u32[]{:S(2)}) collective-permute-start(bf16[160,2048]{1,0:T(8,128)(2,1)S(1)} %fusion.10), channel_id=1, source_target_pairs={{0,4},{8,0},{16,8},{24,16},{28,24},{20,28},{12,20},{4,12},{1,5},{9... | collective-permute-start | bytes 1966088 | tf_op jit(solution)/shard_map/ppermute | solution.py:95
  278.2 13.4 %collective-permute-start.38 = (bf16[160,2048]{1,0:T(8,128)(2,1)S(1)}, bf16[160,2048]{1,0:T(8,128)(2,1)S(1)}, u32[]{:S(2)}, u32[]{:S(2)}) collective-permute-start(bf16[160,2048]{1,0:T(8,128)(2,1)S(1)} %fusion.15), channel_id=1, source_target_pairs={{0,8},{8,16},{16,24},{24,28},{28,20},{20,12},{12,4},{4,0},{1,9},{9... | collective-permute-start | bytes 1966088 | tf_op jit(solution)/shard_map/ppermute | solution.py:94
  281.1 14.7 %collective-permute-start.45 = (bf16[160,2048]{1,0:T(8,128)(2,1)S(1)}, bf16[160,2048]{1,0:T(8,128)(2,1)S(1)}, u32[]{:S(2)}, u32[]{:S(2)}) collective-permute-start(bf16[160,2048]{1,0:T(8,128)(2,1)S(1)} %fusion.9), channel_id=1, source_target_pairs={{0,4},{8,0},{16,8},{24,16},{28,24},{20,28},{12,20},{4,12},{1,5},{9... | collective-permute-start | bytes 1966088 | tf_op jit(solution)/shard_map/ppermute | solution.py:95
  293.1 13.4 %collective-permute-start.39 = (bf16[160,2048]{1,0:T(8,128)(2,1)S(1)}, bf16[160,2048]{1,0:T(8,128)(2,1)S(1)}, u32[]{:S(2)}, u32[]{:S(2)}) collective-permute-start(bf16[160,2048]{1,0:T(8,128)(2,1)S(1)} %fusion.14), channel_id=1, source_target_pairs={{0,8},{8,16},{16,24},{24,28},{28,20},{20,12},{12,4},{4,0},{1,9},{9... | collective-permute-start | bytes 1966088 | tf_op jit(solution)/shard_map/ppermute | solution.py:94
  296.0 14.7 %collective-permute-start.46 = (bf16[160,2048]{1,0:T(8,128)(2,1)S(1)}, bf16[160,2048]{1,0:T(8,128)(2,1)S(1)}, u32[]{:S(2)}, u32[]{:S(2)}) collective-permute-start(bf16[160,2048]{1,0:T(8,128)(2,1)S(1)} %fusion.8), channel_id=1, source_target_pairs={{0,4},{8,0},{16,8},{24,16},{28,24},{20,28},{12,20},{4,12},{1,5},{9... | collective-permute-start | bytes 1966088 | tf_op jit(solution)/shard_map/ppermute | solution.py:95
  308.0 14.2 %collective-permute-start.40 = (bf16[160,2048]{1,0:T(8,128)(2,1)S(1)}, bf16[160,2048]{1,0:T(8,128)(2,1)S(1)}, u32[]{:S(2)}, u32[]{:S(2)}) collective-permute-start(bf16[160,2048]{1,0:T(8,128)(2,1)S(1)} %fusion.13), channel_id=1, source_target_pairs={{0,8},{8,16},{16,24},{24,28},{28,20},{20,12},{12,4},{4,0},{1,9},{9... | collective-permute-start | bytes 1966088 | tf_op jit(solution)/shard_map/ppermute | solution.py:94
  310.8 15.5 %collective-permute-start.47 = (bf16[160,2048]{1,0:T(8,128)(2,1)S(1)}, bf16[160,2048]{1,0:T(8,128)(2,1)S(1)}, u32[]{:S(2)}, u32[]{:S(2)}) collective-permute-start(bf16[160,2048]{1,0:T(8,128)(2,1)S(1)} %fusion.7), channel_id=1, source_target_pairs={{0,4},{8,0},{16,8},{24,16},{28,24},{20,28},{12,20},{4,12},{1,5},{9... | collective-permute-start | bytes 1966088 | tf_op jit(solution)/shard_map/ppermute | solution.py:95
  323.7 15.0 %collective-permute-start.41 = (bf16[160,2048]{1,0:T(8,128)(2,1)S(1)}, bf16[160,2048]{1,0:T(8,128)(2,1)S(1)}, u32[]{:S(2)}, u32[]{:S(2)}) collective-permute-start(bf16[160,2048]{1,0:T(8,128)(2,1)S(1)} %fusion.12), channel_id=1, source_target_pairs={{0,8},{8,16},{16,24},{24,28},{28,20},{20,12},{12,4},{4,0},{1,9},{9... | collective-permute-start | bytes 1966088 | tf_op jit(solution)/shard_map/ppermute | solution.py:94
  326.4 16.3 %collective-permute-start.48 = (bf16[160,2048]{1,0:T(8,128)(2,1)S(1)}, bf16[160,2048]{1,0:T(8,128)(2,1)S(1)}, u32[]{:S(2)}, u32[]{:S(2)}) collective-permute-start(bf16[160,2048]{1,0:T(8,128)(2,1)S(1)} %fusion.6), channel_id=1, source_target_pairs={{0,4},{8,0},{16,8},{24,16},{28,24},{20,28},{12,20},{4,12},{1,5},{9... | collective-permute-start | bytes 1966088 | tf_op jit(solution)/shard_map/ppermute | solution.py:95
  (31 other events, 289.3 us)

commit v16 on v10

--- a/solution.py
+++ b/solution.py
@@ -345,8 +345,8 @@
     value_part = across(prob.astype(jnp.bfloat16), grad_stack)
     pair_all = jnp.concatenate([key_part, value_part], axis=1)
     out_ring = Ring(out_weight_grad, ring, "ctx").advance(len(ring) // 4)
+    out_ring.state, pair_all = lax.optimization_barrier((out_ring.state, pair_all))
     pair_grad = butterfly_sum(direct_scatter(pair_all, "ctx"), "tp")
-    out_ring.state, pair_grad = lax.optimization_barrier((out_ring.state, pair_grad))
 
     key_raw = rotate(pair_grad[:, :head_dim], cosine_all, -sine_all)
     query_grad = jnp.transpose((query_sum * factor).reshape(heads, rows_mine, head_dim), (1, 0, 2))

time: 348 us -> 370 us (1.063)
  waiting for transfers between devices: 122 us -> 153 us
  other arithmetic: 50 us -> 34 us
  starting transfers between devices: 57.5 us -> 66 us
    ppermute x7, waiting for transfers between devices: 1.05 us -> 18 us  [direct_scatter(): lax.ppermute(blocks[shift].astype(jnp.bfloat16), axis, pairs)]
    ppermute x7, starting transfers between devices: 5.27 us -> 17.7 us  [ring_scatter(): got_left = lax.ppermute(send_left.astype(jnp.bfloat16), axis, forward)]
    ppermute x7, waiting for transfers between devices: 4.4 us -> 15.1 us  [advance(): lax.ppermute(send_left.astype(jnp.bfloat16), self.axis, self.forward)]
    ppermute x7, starting transfers between devices: 9.87 us -> 0.91 us  [ring_scatter(): got_right = lax.ppermute(send_right.astype(jnp.bfloat16), axis, backward)]
    ppermute x7, starting transfers between devices: 6.65 us -> 12.6 us  [advance(): lax.ppermute(send_right.astype(jnp.bfloat16), self.axis, self.backward)]
    convert_element_type x5, other arithmetic: 8.51 us -> 2.73 us  [advance(): send_left.astype(jnp.bfloat16)]
    convert_element_type x5, other arithmetic: 8.5 us -> 2.74 us  [advance(): send_right.astype(jnp.bfloat16)]
    ppermute x7, waiting for transfers between devices: 55.9 us -> 60.5 us  [ring_scatter(): got_left = lax.ppermute(send_left.astype(jnp.bfloat16), axis, forward)]
  transfers between devices with their start and end apart: 50 -> 50, of which waited for: 28 -> 26; matrix products, arithmetic and copies ran while one was open for 24% -> 16% of each run, Pallas kernels for 0% -> 0%
where the time goes in v16:
time: 370 us; the launch traced here: 368 us
  waiting for transfers between devices  153 us (41%)
  starting transfers between devices  66 us (18%)
  between operations  37.2 us (10%)
  matrix products  37 us (10%)
  other arithmetic  34 us (9%)
  local copies, waits for them, and re-layouts  27 us (7%)
  blocking collectives  13.9 us (4%)
    ppermute x7, waiting for transfers between devices, ring_scatter(): got_left = lax.ppermute(send_left.astype(jnp.bfloat16), axis, forward)  60.5 us
    ppermute x7, waiting for transfers between devices, advance(): lax.ppermute(send_right.astype(jnp.bfloat16), self.axis, self.backward)  37.4 us
    ppermute x7, waiting for transfers between devices, direct_scatter(): lax.ppermute(blocks[shift].astype(jnp.bfloat16), axis, pairs)  18 us
    ppermute x7, starting transfers between devices, ring_scatter(): got_left = lax.ppermute(send_left.astype(jnp.bfloat16), axis, forward)  17.7 us
    dot_general x4, matrix products, against(): lax.dot_general(left, right, (((1,), (1,)), ((), ())), preferred_element_...  17.3 us
    ppermute x7, waiting for transfers between devices, direct_gather(): got[count - shift] = lax.ppermute(value, axis, pairs)  16.1 us
    ppermute x7, waiting for transfers between devices, advance(): lax.ppermute(send_left.astype(jnp.bfloat16), self.axis, self.forward)  15.1 us
    ppermute x7, starting transfers between devices, direct_gather(): got[count - shift] = lax.ppermute(value, axis, pairs)  12.8 us
  transfers between devices with their start and end apart: 50, of which 26 were waited for; matrix products, arithmetic and copies ran while one was open for 16% of the time, Pallas kernels for 0%

profile of v16, /device:TPU:0, one launch (start us, length us, event | category | flops | bytes accessed | tf_op | source)
XLA Modules:
  0.0 368.3 jit_solution(17781540808524960862)
XLA Ops:
  2.2 6.9 %fusion.61 = f32[256,1280]{1,0:T(8,128)S(1)} fusion(bf16[256,4096]{1,0:T(8,128)(2,1)S(1)} %copy-done, bf16[1280,4096]{1,0:T(8,128)(2,1)} %param.13), kind=kOutput, calls=%fused_computation.162 | convolution fusion | flops 2684354560 | bytes 13893632 | tf_op jit(solution)/shard_map/dot_general | solution.py:35
  9.6 6.4 %convolution_convert_fusion.2 = bf16[256,1024]{1,0:T(8,128)(2,1)S(1)} fusion(bf16[256,4096]{1,0:T(8,128)(2,1)} %param.15, bf16[1024,4096]{1,0:T(8,128)(2,1)} %param.14), kind=kOutput, calls=%fused_computation.42 | convolution fusion | flops 2147745792 | bytes 11010048 | tf_op jit(solution)/shard_map/dot_general | solution.py:35
  60.3 4.2 %collective-permute-done.1 = f32[128,256]{1,0:T(8,128)S(1)} collective-permute-done((f32[128,256]{1,0:T(8,128)S(1)}, f32[128,256]{1,0:T(8,128)S(1)}, u32[]{:S(2)}, u32[]{:S(2)}) %collective-permute-start.1) | collective-permute-done | bytes 131104 | tf_op jit(solution)/shard_map/ppermute | solution.py:197
  66.7 4.6 %collective-permute-start.3 = (bf16[259,256]{1,0:T(8,128)(2,1)S(1)}, bf16[259,256]{1,0:T(8,128)(2,1)S(1)}, u32[]{:S(2)}, u32[]{:S(2)}) collective-permute-start(bf16[259,256]{1,0:T(8,128)(2,1)S(1)} %get-tuple-element.19), channel_id=1, source_target_pairs={{0,28},{4,0},{8,4},{12,8},{16,12},{20,16},{24,20},{28,24},{1,29},{... | collective-permute-start | bytes 397832 | tf_op jit(solution)/shard_map/ppermute | solution.py:226
  81.2 13.5 %collective-permute-done.6 = bf16[259,256]{1,0:T(8,128)(2,1)S(1)} collective-permute-done((bf16[259,256]{1,0:T(8,128)(2,1)S(1)}, bf16[259,256]{1,0:T(8,128)(2,1)S(1)}, u32[]{:S(2)}, u32[]{:S(2)}) %collective-permute-start.6) | collective-permute-done | bytes 132640 | tf_op jit(solution)/shard_map/ppermute | solution.py:226
  99.1 3.2 fusion.1
  103.2 6.7 %all_gather.6 = bf16[256,1024]{1,0:T(8,128)(2,1)S(1)} all-gather(bf16[64,1024]{1,0:T(8,128)(2,1)S(1)} %bitcast.246), channel_id=1, replica_groups=mesh['ctx'=8,'tp'=4] {'tp'}, dimensions={0}, use_global_device_ids=true | all-gather | bytes 655360 | tf_op jit(solution)/shard_map/all_gather | solution.py:332
  112.3 6.4 %fusion.56 = (f32[8,128,2048]{2,1,0:T(8,128)}, f32[8,128,2048]{2,1,0:T(8,128)}) fusion(f32[8,128,4096]{2,1,0:T(8,128)S(1)} %bitcast.233), kind=kLoop, calls=%fused_computation.157 | loop fusion | bytes 33554432 | tf_op jit(solution)/shard_map/slice | solution.py:157
  128.0 6.2 %collective-permute-done.15 = bf16[128,2048]{1,0:T(8,128)(2,1)S(1)} collective-permute-done((bf16[128,2048]{1,0:T(8,128)(2,1)S(1)}, bf16[128,2048]{1,0:T(8,128)(2,1)S(1)}, u32[]{:S(2)}, u32[]{:S(2)}) %collective-permute-start.15) | collective-permute-done | bytes 524320 | tf_op jit(solution)/shard_map/ppermute | solution.py:172
  137.6 10.1 %collective-permute-done.16 = bf16[128,2048]{1,0:T(8,128)(2,1)S(1)} collective-permute-done((bf16[128,2048]{1,0:T(8,128)(2,1)S(1)}, bf16[128,2048]{1,0:T(8,128)(2,1)S(1)}, u32[]{:S(2)}, u32[]{:S(2)}) %collective-permute-start.16) | collective-permute-done | bytes 524320 | tf_op jit(solution)/shard_map/ppermute | solution.py:172
  151.0 3.9 %collective-permute-start.19 = (bf16[256,256]{1,0:T(8,128)(2,1)S(1)}, bf16[256,256]{1,0:T(8,128)(2,1)S(1)}, u32[]{:S(2)}, u32[]{:S(2)}) collective-permute-start(bf16[256,256]{1,0:T(8,128)(2,1)S(1)} %get-tuple-element.35), channel_id=1, source_target_pairs={{0,12},{4,16},{8,20},{12,24},{16,28},{20,0},{24,4},{28,8},{1,13},{... | collective-permute-start | bytes 393224 | tf_op jit(solution)/shard_map/ppermute | solution.py:237
  159.0 3.4 collective-permute-start.22
  162.5 5.2 %collective-permute-done.19 = bf16[256,256]{1,0:T(8,128)(2,1)S(1)} collective-permute-done((bf16[256,256]{1,0:T(8,128)(2,1)S(1)}, bf16[256,256]{1,0:T(8,128)(2,1)S(1)}, u32[]{:S(2)}, u32[]{:S(2)}) %collective-permute-start.19) | collective-permute-done | bytes 131104 | tf_op jit(solution)/shard_map/ppermute | solution.py:237
  167.8 11.7 %collective-permute-done.20 = bf16[256,256]{1,0:T(8,128)(2,1)S(1)} collective-permute-done((bf16[256,256]{1,0:T(8,128)(2,1)S(1)}, bf16[256,256]{1,0:T(8,128)(2,1)S(1)}, u32[]{:S(2)}, u32[]{:S(2)}) %collective-permute-start.20) | collective-permute-done | bytes 131104 | tf_op jit(solution)/shard_map/ppermute | solution.py:237
  179.9 4.3 %collective-permute-start.32 = (bf16[128,2048]{1,0:T(8,128)(2,1)S(1)}, bf16[128,2048]{1,0:T(8,128)(2,1)S(1)}, u32[]{:S(2)}, u32[]{:S(2)}) collective-permute-start(bf16[128,2048]{1,0:T(8,128)(2,1)S(1)} %fusion.20), channel_id=1, source_target_pairs={{0,4},{8,0},{16,8},{24,16},{28,24},{20,28},{12,20},{4,12},{1,5},{9... | collective-permute-start | bytes 1572872 | tf_op jit(solution)/shard_map/ppermute | solution.py:172
  184.2 8.4 %collective-permute-done.26 = bf16[128,2048]{1,0:T(8,128)(2,1)S(1)} collective-permute-done((bf16[128,2048]{1,0:T(8,128)(2,1)S(1)}, bf16[128,2048]{1,0:T(8,128)(2,1)S(1)}, u32[]{:S(2)}, u32[]{:S(2)}) %collective-permute-start.26) | collective-permute-done | bytes 524320 | tf_op jit(solution)/shard_map/ppermute | solution.py:171
  194.2 4.4 %collective-permute-done.32 = bf16[128,2048]{1,0:T(8,128)(2,1)S(1)} collective-permute-done((bf16[128,2048]{1,0:T(8,128)(2,1)S(1)}, bf16[128,2048]{1,0:T(8,128)(2,1)S(1)}, u32[]{:S(2)}, u32[]{:S(2)}) %collective-permute-start.32) | collective-permute-done | bytes 524320 | tf_op jit(solution)/shard_map/ppermute | solution.py:172
  198.8 3.1 collective-permute-start.33
  201.9 4.4 %collective-permute-done.27 = bf16[128,2048]{1,0:T(8,128)(2,1)S(1)} collective-permute-done((bf16[128,2048]{1,0:T(8,128)(2,1)S(1)}, bf16[128,2048]{1,0:T(8,128)(2,1)S(1)}, u32[]{:S(2)}, u32[]{:S(2)}) %collective-permute-start.27) | collective-permute-done | bytes 524320 | tf_op jit(solution)/shard_map/ppermute | solution.py:171
  206.5 7.2 %all_gather.7 = bf16[256,1024]{1,0:T(8,128)(2,1)} all-gather(bf16[64,1024]{1,0:T(8,128)(2,1)S(1)} %copy_bitcast_fusion.1), channel_id=1, replica_groups=mesh['ctx'=8,'tp'=4] {'tp'}, dimensions={0}, use_global_device_ids=true | all-gather | bytes 655360 | tf_op jit(solution)/shard_map/all_gather | solution.py:356
  219.9 9.3 %collective-permute-done.34 = bf16[128,2048]{1,0:T(8,128)(2,1)} collective-permute-done((bf16[128,2048]{1,0:T(8,128)(2,1)}, bf16[128,2048]{1,0:T(8,128)(2,1)}, u32[]{:S(2)}, u32[]{:S(2)}) %collective-permute-start.34) | collective-permute-done | bytes 524320 | tf_op jit(solution)/shard_map/ppermute | solution.py:172
  239.0 7.4 %collective-permute-done.35 = bf16[128,2048]{1,0:T(8,128)(2,1)S(1)} collective-permute-done((bf16[128,2048]{1,0:T(8,128)(2,1)S(1)}, bf16[128,2048]{1,0:T(8,128)(2,1)S(1)}, u32[]{:S(2)}, u32[]{:S(2)}) %collective-permute-start.35) | collective-permute-done | bytes 524320 | tf_op jit(solution)/shard_map/ppermute | solution.py:172
  249.0 8.1 %fusion.55 = (f32[8,160,2048]{2,1,0:T(8,128)}, f32[8,160,2048]{2,1,0:T(8,128)}) fusion(f32[8,160,4096]{2,1,0:T(8,128)S(1)} %bitcast.232), kind=kLoop, calls=%fused_computation.156 | loop fusion | bytes 41943040 | tf_op jit(solution)/shard_map/slice | solution.py:83
  262.7 11.9 %collective-permute-done.36 = bf16[160,2048]{1,0:T(8,128)(2,1)S(1)} collective-permute-done((bf16[160,2048]{1,0:T(8,128)(2,1)S(1)}, bf16[160,2048]{1,0:T(8,128)(2,1)S(1)}, u32[]{:S(2)}, u32[]{:S(2)}) %collective-permute-start.36) | collective-permute-done | bytes 655392 | tf_op jit(solution)/shard_map/ppermute | solution.py:94
  280.2 10.9 %collective-permute-done.37 = bf16[160,2048]{1,0:T(8,128)(2,1)S(1)} collective-permute-done((bf16[160,2048]{1,0:T(8,128)(2,1)S(1)}, bf16[160,2048]{1,0:T(8,128)(2,1)S(1)}, u32[]{:S(2)}, u32[]{:S(2)}) %collective-permute-start.37) | collective-permute-done | bytes 655392 | tf_op jit(solution)/shard_map/ppermute | solution.py:94
  295.5 11.0 %collective-permute-done.38 = bf16[160,2048]{1,0:T(8,128)(2,1)S(1)} collective-permute-done((bf16[160,2048]{1,0:T(8,128)(2,1)S(1)}, bf16[160,2048]{1,0:T(8,128)(2,1)S(1)}, u32[]{:S(2)}, u32[]{:S(2)}) %collective-permute-start.38) | collective-permute-done | bytes 655392 | tf_op jit(solution)/shard_map/ppermute | solution.py:94
  310.8 10.7 %collective-permute-done.39 = bf16[160,2048]{1,0:T(8,128)(2,1)S(1)} collective-permute-done((bf16[160,2048]{1,0:T(8,128)(2,1)S(1)}, bf16[160,2048]{1,0:T(8,128)(2,1)S(1)}, u32[]{:S(2)}, u32[]{:S(2)}) %collective-permute-start.39) | collective-permute-done | bytes 655392 | tf_op jit(solution)/shard_map/ppermute | solution.py:94
  326.0 7.3 %convolution_convert_fusion = bf16[256,4096]{1,0:T(8,128)(2,1)} fusion(bf16[256,1024]{1,0:T(8,128)(2,1)S(1)} %all_gather.6, bf16[1024,4096]{1,0:T(8,128)(2,1)} %param.14), kind=kOutput, calls=%fused_computation.3 | convolution fusion | flops 2148532224 | bytes 11010048 | tf_op jit(solution)/shard_map/dot_general | solution.py:333
  333.3 3.1 collective-permute-done.40
  340.7 4.1 %convolution_convert_fusion.1 = bf16[256,4096]{1,0:T(8,128)(2,1)} fusion(bf16[256,1280]{1,0:T(8,128)(2,1)S(1)} %concatenate.45, bf16[1280,4096]{1,0:T(8,128)(2,1)S(1)} %bitcast.253), kind=kOutput, calls=%fused_computation.4 | convolution fusion | flops 2685403136 | bytes 13238272 | tf_op jit(solution)/shard_map/dot_general | solution.py:361
  344.8 6.5 %collective-permute-done.41 = bf16[160,2048]{1,0:T(8,128)(2,1)S(1)} collective-permute-done((bf16[160,2048]{1,0:T(8,128)(2,1)S(1)}, bf16[160,2048]{1,0:T(8,128)(2,1)S(1)}, u32[]{:S(2)}, u32[]{:S(2)}) %collective-permute-start.41) | collective-permute-done | bytes 655392 | tf_op jit(solution)/shard_map/ppermute | solution.py:94
  357.0 6.4 %collective-permute-done.42 = bf16[160,2048]{1,0:T(8,128)(2,1)S(1)} collective-permute-done((bf16[160,2048]{1,0:T(8,128)(2,1)S(1)}, bf16[160,2048]{1,0:T(8,128)(2,1)S(1)}, u32[]{:S(2)}, u32[]{:S(2)}) %collective-permute-start.42) | collective-permute-done | bytes 655392 | tf_op jit(solution)/shard_map/ppermute | solution.py:94
  (213 shorter events, 110.3 us)
Async XLA Ops:
  9.1 48.2 %collective-permute-start = (f32[256,1280]{1,0:T(8,128)S(1)}, f32[256,1280]{1,0:T(8,128)}, u32[]{:S(2)}, u32[]{:S(2)}) collective-permute-start(f32[256,1280]{1,0:T(8,128)S(1)} %fusion.61), channel_id=1, source_target_pairs={{0,1},{1,0},{2,3},{3,2},{4,5},{5,4},{6,7},{7,6},{8,9},{9,8},{10,11... | collective-permute-start | bytes 3932168 | tf_op jit(solution)/shard_map/ppermute | solution.py:189
  17.6 41.4 %collective-permute-start.11 = (bf16[128,1024]{1,0:T(8,128)(2,1)}, bf16[128,1024]{1,0:T(8,128)(2,1)}, u32[]{:S(2)}, u32[]{:S(2)}) collective-permute-start(bf16[128,1024]{1,0:T(8,128)(2,1)} %constant_dynamic-slice_fusion), channel_id=1, source_target_pairs={{0,2},{1,3},{2,0},{3,1},{4,6},{5,7},{6,4},{7,5},{8,10},{9,11},{10,... | collective-permute-start | bytes 786440 | tf_op jit(solution)/shard_map/ppermute | solution.py:212
  71.8 22.9 %collective-permute-start.6 = (bf16[259,256]{1,0:T(8,128)(2,1)S(1)}, bf16[259,256]{1,0:T(8,128)(2,1)S(1)}, u32[]{:S(2)}, u32[]{:S(2)}) collective-permute-start(bf16[259,256]{1,0:T(8,128)(2,1)S(1)} %get-tuple-element.19), channel_id=1, source_target_pairs={{0,16},{4,20},{8,24},{12,28},{16,0},{20,4},{24,8},{28,12},{1,17},{... | collective-permute-start | bytes 397832 | tf_op jit(solution)/shard_map/ppermute | solution.py:226
  74.8 21.3 %collective-permute-start.7 = (bf16[259,256]{1,0:T(8,128)(2,1)S(1)}, bf16[259,256]{1,0:T(8,128)(2,1)S(1)}, u32[]{:S(2)}, u32[]{:S(2)}) collective-permute-start(bf16[259,256]{1,0:T(8,128)(2,1)S(1)} %get-tuple-element.19), channel_id=1, source_target_pairs={{0,12},{4,16},{8,20},{12,24},{16,28},{20,0},{24,4},{28,8},{1,13},{... | collective-permute-start | bytes 397832 | tf_op jit(solution)/shard_map/ppermute | solution.py:226
  76.6 19.6 %collective-permute-start.8 = (bf16[259,256]{1,0:T(8,128)(2,1)S(1)}, bf16[259,256]{1,0:T(8,128)(2,1)S(1)}, u32[]{:S(2)}, u32[]{:S(2)}) collective-permute-start(bf16[259,256]{1,0:T(8,128)(2,1)S(1)} %get-tuple-element.19), channel_id=1, source_target_pairs={{0,8},{4,12},{8,16},{12,20},{16,24},{20,28},{24,0},{28,4},{1,9},{5... | collective-permute-start | bytes 397832 | tf_op jit(solution)/shard_map/ppermute | solution.py:226
  78.2 17.9 %collective-permute-start.9 = (bf16[259,256]{1,0:T(8,128)(2,1)S(1)}, bf16[259,256]{1,0:T(8,128)(2,1)S(1)}, u32[]{:S(2)}, u32[]{:S(2)}) collective-permute-start(bf16[259,256]{1,0:T(8,128)(2,1)S(1)} %get-tuple-element.19), channel_id=1, source_target_pairs={{0,4},{4,8},{8,12},{12,16},{16,20},{20,24},{24,28},{28,0},{1,5},{5... | collective-permute-start | bytes 397832 | tf_op jit(solution)/shard_map/ppermute | solution.py:226
  120.0 14.2 %collective-permute-start.15 = (bf16[128,2048]{1,0:T(8,128)(2,1)S(1)}, bf16[128,2048]{1,0:T(8,128)(2,1)S(1)}, u32[]{:S(2)}, u32[]{:S(2)}) collective-permute-start(bf16[128,2048]{1,0:T(8,128)(2,1)S(1)} %fusion.30), channel_id=1, source_target_pairs={{0,4},{8,0},{16,8},{24,16},{28,24},{20,28},{12,20},{4,12},{1,5},{9... | collective-permute-start | bytes 1572872 | tf_op jit(solution)/shard_map/ppermute | solution.py:172
  121.4 14.2 %collective-permute-start.13 = (bf16[128,2048]{1,0:T(8,128)(2,1)S(1)}, bf16[128,2048]{1,0:T(8,128)(2,1)S(1)}, u32[]{:S(2)}, u32[]{:S(2)}) collective-permute-start(bf16[128,2048]{1,0:T(8,128)(2,1)S(1)} %fusion.29), channel_id=1, source_target_pairs={{0,8},{8,16},{16,24},{24,28},{28,20},{20,12},{12,4},{4,0},{1,9},{9... | collective-permute-start | bytes 1572872 | tf_op jit(solution)/shard_map/ppermute | solution.py:171
  151.0 16.7 %collective-permute-start.19 = (bf16[256,256]{1,0:T(8,128)(2,1)S(1)}, bf16[256,256]{1,0:T(8,128)(2,1)S(1)}, u32[]{:S(2)}, u32[]{:S(2)}) collective-permute-start(bf16[256,256]{1,0:T(8,128)(2,1)S(1)} %get-tuple-element.35), channel_id=1, source_target_pairs={{0,12},{4,16},{8,20},{12,24},{16,28},{20,0},{24,4},{28,8},{1,13},{... | collective-permute-start | bytes 393224 | tf_op jit(solution)/shard_map/ppermute | solution.py:237
  154.9 24.8 %collective-permute-start.31 = (bf16[128,2048]{1,0:T(8,128)(2,1)S(1)}, bf16[128,2048]{1,0:T(8,128)(2,1)S(1)}, u32[]{:S(2)}, u32[]{:S(2)}) collective-permute-start(bf16[128,2048]{1,0:T(8,128)(2,1)S(1)} %bitcast_add_fusion.24), channel_id=1, source_target_pairs={{0,4},{8,0},{16,8},{24,16},{28,24},{20,28},{12,20},{4,12},{1,5},{9... | collective-permute-start | bytes 1572872 | tf_op jit(solution)/shard_map/ppermute | solution.py:172
  156.2 23.3 %collective-permute-start.20 = (bf16[256,256]{1,0:T(8,128)(2,1)S(1)}, bf16[256,256]{1,0:T(8,128)(2,1)S(1)}, u32[]{:S(2)}, u32[]{:S(2)}) collective-permute-start(bf16[256,256]{1,0:T(8,128)(2,1)S(1)} %get-tuple-element.34), channel_id=1, source_target_pairs={{0,16},{4,20},{8,24},{12,28},{16,0},{20,4},{24,8},{28,12},{1,17},{... | collective-permute-start | bytes 393224 | tf_op jit(solution)/shard_map/ppermute | solution.py:237
  158.7 20.8 %collective-permute-start.21 = (bf16[256,256]{1,0:T(8,128)(2,1)S(1)}, bf16[256,256]{1,0:T(8,128)(2,1)S(1)}, u32[]{:S(2)}, u32[]{:S(2)}) collective-permute-start(bf16[256,256]{1,0:T(8,128)(2,1)S(1)} %get-tuple-element.33), channel_id=1, source_target_pairs={{0,20},{4,24},{8,28},{12,0},{16,4},{20,8},{24,12},{28,16},{1,21},{... | collective-permute-start | bytes 393224 | tf_op jit(solution)/shard_map/ppermute | solution.py:237
  159.0 20.5 %collective-permute-start.22 = (bf16[256,256]{1,0:T(8,128)(2,1)S(1)}, bf16[256,256]{1,0:T(8,128)(2,1)S(1)}, u32[]{:S(2)}, u32[]{:S(2)}) collective-permute-start(bf16[256,256]{1,0:T(8,128)(2,1)S(1)} %get-tuple-element.32), channel_id=1, source_target_pairs={{0,24},{4,28},{8,0},{12,4},{16,8},{20,12},{24,16},{28,20},{1,25},{... | collective-permute-start | bytes 393224 | tf_op jit(solution)/shard_map/ppermute | solution.py:237
  179.6 13.5 %collective-permute-start.24 = (f32[256,256]{1,0:T(8,128)S(1)}, f32[256,256]{1,0:T(8,128)S(1)}, u32[]{:S(2)}, u32[]{:S(2)}) collective-permute-start(f32[256,256]{1,0:T(8,128)S(1)} %convert_add_fusion.1), channel_id=1, source_target_pairs={{0,1},{1,0},{2,3},{3,2},{4,5},{5,4},{6,7},{7,6},{8,9},{9,8},{10,11... | collective-permute-start | bytes 786440 | tf_op jit(solution)/shard_map/ppermute | solution.py:248
  179.9 18.8 %collective-permute-start.32 = (bf16[128,2048]{1,0:T(8,128)(2,1)S(1)}, bf16[128,2048]{1,0:T(8,128)(2,1)S(1)}, u32[]{:S(2)}, u32[]{:S(2)}) collective-permute-start(bf16[128,2048]{1,0:T(8,128)(2,1)S(1)} %fusion.20), channel_id=1, source_target_pairs={{0,4},{8,0},{16,8},{24,16},{28,24},{20,28},{12,20},{4,12},{1,5},{9... | collective-permute-start | bytes 1572872 | tf_op jit(solution)/shard_map/ppermute | solution.py:172
  192.7 13.6 %collective-permute-start.27 = (bf16[128,2048]{1,0:T(8,128)(2,1)S(1)}, bf16[128,2048]{1,0:T(8,128)(2,1)S(1)}, u32[]{:S(2)}, u32[]{:S(2)}) collective-permute-start(bf16[128,2048]{1,0:T(8,128)(2,1)S(1)} %fusion.24), channel_id=1, source_target_pairs={{0,8},{8,16},{16,24},{24,28},{28,20},{20,12},{12,4},{4,0},{1,9},{9... | collective-permute-start | bytes 1572872 | tf_op jit(solution)/shard_map/ppermute | solution.py:171
  193.2 20.5 %collective-permute-start.25 = (f32[256,256]{1,0:T(8,128)S(1)}, f32[256,256]{1,0:T(8,128)S(1)}, u32[]{:S(2)}, u32[]{:S(2)}) collective-permute-start(f32[256,256]{1,0:T(8,128)S(1)} %add.689), channel_id=1, source_target_pairs={{0,2},{1,3},{2,0},{3,1},{4,6},{5,7},{6,4},{7,5},{8,10},{9,11},{10,... | collective-permute-start | bytes 786440 | tf_op jit(solution)/shard_map/ppermute | solution.py:248
  198.8 14.9 %collective-permute-start.33 = (bf16[128,2048]{1,0:T(8,128)(2,1)S(1)}, bf16[128,2048]{1,0:T(8,128)(2,1)S(1)}, u32[]{:S(2)}, u32[]{:S(2)}) collective-permute-start(bf16[128,2048]{1,0:T(8,128)(2,1)S(1)} %fusion.19), channel_id=1, source_target_pairs={{0,4},{8,0},{16,8},{24,16},{28,24},{20,28},{12,20},{4,12},{1,5},{9... | collective-permute-start | bytes 1572872 | tf_op jit(solution)/shard_map/ppermute | solution.py:172
  214.6 14.5 %collective-permute-start.34 = (bf16[128,2048]{1,0:T(8,128)(2,1)}, bf16[128,2048]{1,0:T(8,128)(2,1)}, u32[]{:S(2)}, u32[]{:S(2)}) collective-permute-start(bf16[128,2048]{1,0:T(8,128)(2,1)} %fusion.18), channel_id=1, source_target_pairs={{0,4},{8,0},{16,8},{24,16},{28,24},{20,28},{12,20},{4,12},{1,5},{9... | collective-permute-start | bytes 1572872 | tf_op jit(solution)/shard_map/ppermute | solution.py:172
  217.8 14.9 %collective-permute-start.29 = (bf16[128,2048]{1,0:T(8,128)(2,1)}, bf16[128,2048]{1,0:T(8,128)(2,1)}, u32[]{:S(2)}, u32[]{:S(2)}) collective-permute-start(bf16[128,2048]{1,0:T(8,128)(2,1)} %fusion.22), channel_id=1, source_target_pairs={{0,8},{8,16},{16,24},{24,28},{28,20},{20,12},{12,4},{4,0},{1,9},{9... | collective-permute-start | bytes 1572872 | tf_op jit(solution)/shard_map/ppermute | solution.py:171
  230.6 15.7 %collective-permute-start.35 = (bf16[128,2048]{1,0:T(8,128)(2,1)S(1)}, bf16[128,2048]{1,0:T(8,128)(2,1)S(1)}, u32[]{:S(2)}, u32[]{:S(2)}) collective-permute-start(bf16[128,2048]{1,0:T(8,128)(2,1)S(1)} %fusion.17), channel_id=1, source_target_pairs={{0,4},{8,0},{16,8},{24,16},{28,24},{20,28},{12,20},{4,12},{1,5},{9... | collective-permute-start | bytes 1572872 | tf_op jit(solution)/shard_map/ppermute | solution.py:172
  234.2 13.5 %collective-permute-start.30 = (bf16[128,2048]{1,0:T(8,128)(2,1)S(1)}, bf16[128,2048]{1,0:T(8,128)(2,1)S(1)}, u32[]{:S(2)}, u32[]{:S(2)}) collective-permute-start(bf16[128,2048]{1,0:T(8,128)(2,1)S(1)} %fusion.21), channel_id=1, source_target_pairs={{0,8},{8,16},{16,24},{24,28},{28,20},{20,12},{12,4},{4,0},{1,9},{9... | collective-permute-start | bytes 1572872 | tf_op jit(solution)/shard_map/ppermute | solution.py:171
  258.7 15.9 %collective-permute-start.36 = (bf16[160,2048]{1,0:T(8,128)(2,1)S(1)}, bf16[160,2048]{1,0:T(8,128)(2,1)S(1)}, u32[]{:S(2)}, u32[]{:S(2)}) collective-permute-start(bf16[160,2048]{1,0:T(8,128)(2,1)S(1)} %fusion.27), channel_id=1, source_target_pairs={{0,8},{8,16},{16,24},{24,28},{28,20},{20,12},{12,4},{4,0},{1,9},{9... | collective-permute-start | bytes 1966088 | tf_op jit(solution)/shard_map/ppermute | solution.py:94
  262.6 16.0 %collective-permute-start.43 = (bf16[160,2048]{1,0:T(8,128)(2,1)S(1)}, bf16[160,2048]{1,0:T(8,128)(2,1)S(1)}, u32[]{:S(2)}, u32[]{:S(2)}) collective-permute-start(bf16[160,2048]{1,0:T(8,128)(2,1)S(1)} %fusion.28), channel_id=1, source_target_pairs={{0,4},{8,0},{16,8},{24,16},{28,24},{20,28},{12,20},{4,12},{1,5},{9... | collective-permute-start | bytes 1966088 | tf_op jit(solution)/shard_map/ppermute | solution.py:95
  276.1 15.0 %collective-permute-start.37 = (bf16[160,2048]{1,0:T(8,128)(2,1)S(1)}, bf16[160,2048]{1,0:T(8,128)(2,1)S(1)}, u32[]{:S(2)}, u32[]{:S(2)}) collective-permute-start(bf16[160,2048]{1,0:T(8,128)(2,1)S(1)} %fusion.15), channel_id=1, source_target_pairs={{0,8},{8,16},{16,24},{24,28},{28,20},{20,12},{12,4},{4,0},{1,9},{9... | collective-permute-start | bytes 1966088 | tf_op jit(solution)/shard_map/ppermute | solution.py:94
  280.1 15.0 %collective-permute-start.44 = (bf16[160,2048]{1,0:T(8,128)(2,1)S(1)}, bf16[160,2048]{1,0:T(8,128)(2,1)S(1)}, u32[]{:S(2)}, u32[]{:S(2)}) collective-permute-start(bf16[160,2048]{1,0:T(8,128)(2,1)S(1)} %fusion.9), channel_id=1, source_target_pairs={{0,4},{8,0},{16,8},{24,16},{28,24},{20,28},{12,20},{4,12},{1,5},{9... | collective-permute-start | bytes 1966088 | tf_op jit(solution)/shard_map/ppermute | solution.py:95
  292.5 14.1 %collective-permute-start.38 = (bf16[160,2048]{1,0:T(8,128)(2,1)S(1)}, bf16[160,2048]{1,0:T(8,128)(2,1)S(1)}, u32[]{:S(2)}, u32[]{:S(2)}) collective-permute-start(bf16[160,2048]{1,0:T(8,128)(2,1)S(1)} %fusion.14), channel_id=1, source_target_pairs={{0,8},{8,16},{16,24},{24,28},{28,20},{20,12},{12,4},{4,0},{1,9},{9... | collective-permute-start | bytes 1966088 | tf_op jit(solution)/shard_map/ppermute | solution.py:94
  295.2 15.4 %collective-permute-start.45 = (bf16[160,2048]{1,0:T(8,128)(2,1)S(1)}, bf16[160,2048]{1,0:T(8,128)(2,1)S(1)}, u32[]{:S(2)}, u32[]{:S(2)}) collective-permute-start(bf16[160,2048]{1,0:T(8,128)(2,1)S(1)} %fusion.8), channel_id=1, source_target_pairs={{0,4},{8,0},{16,8},{24,16},{28,24},{20,28},{12,20},{4,12},{1,5},{9... | collective-permute-start | bytes 1966088 | tf_op jit(solution)/shard_map/ppermute | solution.py:95
  310.8 14.7 %collective-permute-start.46 = (bf16[160,2048]{1,0:T(8,128)(2,1)S(1)}, bf16[160,2048]{1,0:T(8,128)(2,1)S(1)}, u32[]{:S(2)}, u32[]{:S(2)}) collective-permute-start(bf16[160,2048]{1,0:T(8,128)(2,1)S(1)} %fusion.7), channel_id=1, source_target_pairs={{0,4},{8,0},{16,8},{24,16},{28,24},{20,28},{12,20},{4,12},{1,5},{9... | collective-permute-start | bytes 1966088 | tf_op jit(solution)/shard_map/ppermute | solution.py:95
  323.0 13.4 %collective-permute-start.40 = (bf16[160,2048]{1,0:T(8,128)(2,1)S(1)}, bf16[160,2048]{1,0:T(8,128)(2,1)S(1)}, u32[]{:S(2)}, u32[]{:S(2)}) collective-permute-start(bf16[160,2048]{1,0:T(8,128)(2,1)S(1)} %fusion.12), channel_id=1, source_target_pairs={{0,8},{8,16},{16,24},{24,28},{28,20},{20,12},{12,4},{4,0},{1,9},{9... | collective-permute-start | bytes 1966088 | tf_op jit(solution)/shard_map/ppermute | solution.py:94
  325.7 14.7 %collective-permute-start.47 = (bf16[160,2048]{1,0:T(8,128)(2,1)S(1)}, bf16[160,2048]{1,0:T(8,128)(2,1)S(1)}, u32[]{:S(2)}, u32[]{:S(2)}) collective-permute-start(bf16[160,2048]{1,0:T(8,128)(2,1)S(1)} %fusion.6), channel_id=1, source_target_pairs={{0,4},{8,0},{16,8},{24,16},{28,24},{20,28},{12,20},{4,12},{1,5},{9... | collective-permute-start | bytes 1966088 | tf_op jit(solution)/shard_map/ppermute | solution.py:95
  340.6 14.7 %collective-permute-start.48 = (bf16[160,2048]{1,0:T(8,128)(2,1)S(1)}, bf16[160,2048]{1,0:T(8,128)(2,1)S(1)}, u32[]{:S(2)}, u32[]{:S(2)}) collective-permute-start(bf16[160,2048]{1,0:T(8,128)(2,1)S(1)} %fusion.5), channel_id=1, source_target_pairs={{0,4},{8,0},{16,8},{24,16},{28,24},{20,28},{12,20},{4,12},{1,5},{9... | collective-permute-start | bytes 1966088 | tf_op jit(solution)/shard_map/ppermute | solution.py:95
  (36 other events, 368.1 us)
